TPU v7x, 128 devices: a whole 4x4x4 slice. The times are simulated.
128 devices in a mesh: row: 8 (over z_lo, y), col: 16 (over x, z_hi, core).
Axes of the slice: x: 4, y: 4, z: 4 (z_hi: 2, z_lo: 2; z = z_hi * 2 + z_lo), core: 2. Of those that a mesh axis runs over, the one named last changes fastest.
Arguments:
- factors: bfloat16 [10240, 3, 2048], P(('row', 'col')), may hold values from -0.59765625 to 0.59765625
- occ_energy: float32 [300], replicated, may hold values from -3 to -0.5
- vir_energy: float32 [2048], replicated, may hold values from 0.3 to 4
- slab_orbitals: int32 [3], replicated, may hold values from 0 to 299
- pair_list: int32 [16, 2], replicated, may hold values from 0 to 2
- pair_state: int32 [16], replicated, may hold values from 0 to 3
- state_shift: float32 [4], replicated, may hold values from 0.1 to 1
Outputs:
- amplitudes: float32 [16, 2048, 2048], P(None, 'row', 'col')
All inputs are finite; a program needn't handle non-finite values.
Results may differ from a plain program's by a relative error of at most 0.0003.
Values may be sent and summed in bfloat16 or wider, within the bound.
No kernel may reach another device: no remote copies, remote signals or barrier semaphores. Data moves between devices by JAX's collectives and lax.ppermute only.
A program may use at most 192 MiB of HBM per device.

v0:
```python
import jax
import jax.numpy as jnp
from jax import lax
from jax.sharding import PartitionSpec as P


def shards(factors, occ_energy, vir_energy, slab_orbitals, pair_list, pair_state, state_shift):
    n_row = lax.axis_size("row")
    n_col = lax.axis_size("col")
    local_aux, nocc, nvir = factors.shape
    rows_a = nvir // n_row
    cols_b = nvir // n_col
    spread_a = lax.all_to_all(
        factors.reshape(local_aux, nocc, n_row, rows_a), "row", split_axis=2, concat_axis=0, tiled=True
    ).reshape(n_row * local_aux, nocc, rows_a)
    block_a = lax.all_gather(spread_a, "col", axis=0, tiled=True)
    spread_b = lax.all_to_all(
        factors.reshape(local_aux, nocc, n_col, cols_b), "col", split_axis=2, concat_axis=0, tiled=True
    ).reshape(n_col * local_aux, nocc, cols_b)
    block_b = lax.all_gather(spread_b, "row", axis=0, tiled=True)
    block_a = block_a.reshape(n_col, n_row, local_aux, nocc, rows_a)
    block_b = block_b.reshape(n_row, n_col, local_aux, nocc, cols_b)
    gram = jnp.einsum(
        "crpia,rcpjb->ijab", block_a, block_b, preferred_element_type=jnp.float32
    ).reshape(nocc * nocc, rows_a, cols_b)
    first = pair_list[:, 0]
    second = pair_list[:, 1]
    kernel = jnp.take(gram, first * nocc + second, axis=0)
    vir_a = lax.dynamic_slice_in_dim(vir_energy, lax.axis_index("row") * rows_a, rows_a)
    vir_b = lax.dynamic_slice_in_dim(vir_energy, lax.axis_index("col") * cols_b, cols_b)
    e_first = occ_energy[slab_orbitals[first]]
    e_second = occ_energy[slab_orbitals[second]]
    shift = state_shift[pair_state]
    denom = (
        (vir_a[None, :, None] + vir_b[None, None, :])
        - e_first[:, None, None]
        - e_second[:, None, None]
        + shift[:, None, None]
    )
    return -kernel / denom


def solution(mesh):
    placed = (P(("row", "col"), None, None), P(), P(), P(), P(), P(), P())
    return jax.shard_map(
        shards, mesh=mesh, in_specs=placed, out_specs=P(None, "row", "col"), check_vma=False
    )
```

profile of v0, /device:TPU:1, one launch (start us, length us, event | category | flops | bytes accessed | tf_op | source)
XLA Modules:
  0.0 253.7 jit_solution(9331506585385530803)
XLA Ops:
  6.5 0.0 copy-start
  6.5 0.0 all-gather.3.cloned.1.call-start
  6.5 1.4 copy_bitcast_fusion.1
  7.9 0.0 copy-start.2
  7.9 25.3 %all_to_all.30 = bf16[80,3,16,128]{3,0,1,2:T(8,128)(2,1)S(1)} all-to-all(bf16[80,3,16,128]{3,0,1,2:T(8,128)(2,1)S(1)} %copy_bitcast_fusion.1), channel_id=1, replica_groups=mesh['row'=8,'col'=16] {'col'}, dimensions={2} | all-to-all | bytes 1966080 | tf_op jit(solution)/shard_map/all_to_all | solution.py:17
  33.3 1.0 copy.21
  34.3 0.0 all-gather.3.cloned.1.call-update
  34.3 0.0 all-gather.5.cloned.1.call-start
  34.4 0.0 copy-done.2
  34.4 0.1 copy.38
  34.5 0.0 copy-start.3
  34.5 0.0 copy-start.4
  34.5 25.2 %all_to_all.31 = bf16[80,3,8,256]{3,0,1,2:T(8,128)(2,1)S(1)} all-to-all(bf16[80,3,8,256]{3,0,1,2:T(8,128)(2,1)S(1)} %bitcast.47), channel_id=1, replica_groups=mesh['row'=8,'col'=16] {'row'}, dimensions={2} | all-to-all | bytes 1966080 | tf_op jit(solution)/shard_map/all_to_all | solution.py:13
  59.7 0.0 copy-start.5
  59.7 0.0 copy-start.1
  59.7 1.0 copy.23
  60.7 0.0 all-gather.5.cloned.1.call-update
  60.7 0.0 copy-done.3
  60.8 0.7 fusion.7
  61.4 0.0 copy-done.4
  61.4 1.9 fusion.5
  63.3 0.0 copy-done
  63.3 0.7 gather_fusion.2
  64.0 0.7 gather_fusion.1
  64.7 0.8 dynamic_slice.7
  65.4 0.8 dynamic_slice.6
  66.2 0.0 copy-done.5
  66.2 0.0 copy-done.1
  66.2 0.7 gather_fusion.3
  66.9 0.1 broadcast_add_fusion
  67.0 61.6 %all-gather.3.cloned.1.call-done = bf16[10240,3,128]{2,0,1:T(8,128)(2,1)} async-done(((bf16[1280,3,128]{2,0,1:T(8,128)(2,1)}), bf16[10240,3,128]{2,0,1:T(8,128)(2,1)}) %all-gather.3.cloned.1.call-update) | async-done | bytes 7864336 | tf_op jit(solution)/shard_map/all_gather | solution.py:20
  128.6 103.5 %all-gather.5.cloned.1.call-done = bf16[10240,3,256]{2,0,1:T(8,128)(2,1)} async-done(((bf16[640,3,256]{2,0,1:T(8,128)(2,1)}), bf16[10240,3,256]{2,0,1:T(8,128)(2,1)}) %all-gather.5.cloned.1.call-update) | async-done | bytes 15728656 | tf_op jit(solution)/shard_map/all_gather | solution.py:16
  232.1 11.8 %fusion.2 = f32[3,3,256,128]{2,3,0,1:T(8,128)S(1)} fusion(bf16[16,8,80,3,256,1]{4,2,1,0,3,5:T(8,128)(2,1)} %bitcast.49, bf16[8,16,80,3,128,1]{4,2,1,0,3,5:T(8,128)(2,1)} %bitcast.50), kind=kOutput, calls=%fused_computation.7 | convolution fusion | flops 6039797760 | bytes 24772608 | tf_op jit(solution)/shard_map/crpia,rcpjb->ijab/dot_general | solution.py:23
  243.8 0.4 copy.25
  244.2 0.7 gather_fusion
  244.9 1.9 add_divide_fusion
  (5 shorter events, 0.0 us)
Async XLA Ops:
  6.5 56.8 %copy-start = (f32[300]{0:T(512)S(1)}, f32[300]{0:T(512)}, u32[]{:S(2)}) copy-start(f32[300]{0:T(512)} %param.8) | copy-start | bytes 3604
  6.5 122.0 %all-gather.3.cloned.1.call-start = ((), (), s32[]{:S(2)}) async-start(), calls=%async_computation.2 | async-start | bytes 8847360 | tf_op jit(solution)/shard_map/all_gather | solution.py:20
  7.9 26.5 %copy-start.2 = (bf16[80,3,2048]{2,0,1:T(8,128)(2,1)S(1)}, bf16[80,3,2048]{2,0,1:T(8,128)(2,1)}, u32[]{:S(2)}) copy-start(bf16[80,3,2048]{2,0,1:T(8,128)(2,1)} %param.7) | copy-start | bytes 2949124
  34.3 197.7 %all-gather.5.cloned.1.call-start = ((), (), s32[]{:S(2)}) async-start(), calls=%async_computation.3 | async-start | bytes 16711680 | tf_op jit(solution)/shard_map/all_gather | solution.py:16
  34.5 26.3 %copy-start.3 = (s32[3]{0:T(128)S(1)}, s32[3]{0:T(128)}, u32[]{:S(2)}) copy-start(s32[3]{0:T(128)} %param.10) | copy-start | bytes 40
  34.5 26.9 %copy-start.4 = (s32[16,2]{0,1:T(2,128)S(1)}, s32[16,2]{0,1:T(2,128)}, u32[]{:S(2)}) copy-start(s32[16,2]{0,1:T(2,128)} %param.11) | copy-start | bytes 388
  59.7 6.5 %copy-start.5 = (s32[16]{0:T(128)S(1)}, s32[16]{0:T(128)}, u32[]{:S(2)}) copy-start(s32[16]{0:T(128)} %param.12) | copy-start | bytes 196
  59.7 6.5 %copy-start.1 = (f32[4]{0:T(128)S(1)}, f32[4]{0:T(128)}, u32[]{:S(2)}) copy-start(f32[4]{0:T(128)} %param.13) | copy-start | bytes 52
Sparse Core Ops, SparseCore 0:
  34.4 94.0 all-gather.2
  131.0 100.9 all-gather.4
where the time goes:
time: 254 us
  waiting for transfers between devices  165 us (65%)
  blocking collectives  50.5 us (20%)
  between operations  13.5 us (5%)
  matrix products  11.8 us (5%)
  local copies, waits for them, and re-layouts  8.74 us (3%)
  other arithmetic  3.98 us (2%)
    all_gather x1, waiting for transfers between devices, shards(): block_a = lax.all_gather(spread_a, 'col', axis=0, tiled=True)  103 us
    all_gather x1, waiting for transfers between devices, shards(): block_b = lax.all_gather(spread_b, 'row', axis=0, tiled=True)  61.6 us
    all_to_all x1, blocking collectives, shards(): lax.all_to_all(factors.reshape(local_aux, nocc, n_col, cols_b), 'col', sp...  25.3 us
    all_to_all x1, blocking collectives, shards(): lax.all_to_all(factors.reshape(local_aux, nocc, n_row, rows_a), 'row', sp...  25.2 us
    dot_general x1, matrix products, shards(): jnp.einsum('crpia,rcpjb->ijab', block_a, block_b, preferred_element_type=...  11.8 us
  transfers between devices with their start and end apart: 2, of which 2 were waited for; matrix products, arithmetic and copies ran while one was open for 3% of the time, Pallas kernels for 0%

commit v1 on v0

--- a/solution.py
+++ b/solution.py
@@ -2,6 +2,35 @@
 import jax.numpy as jnp
 from jax import lax
 from jax.sharding import PartitionSpec as P
+
+
+def row_ring(n_row):
+    half = n_row // 2
+    return list(range(half)) + [half + y for y in reversed(range(half))]
+
+
+def ring_gather(shard, axis, ring):
+    n = len(ring)
+    position = [0] * n
+    for k, r in enumerate(ring):
+        position[r] = k
+    right = [(ring[k], ring[(k + 1) % n]) for k in range(n)]
+    left = [(ring[k], ring[(k - 1) % n]) for k in range(n)]
+    ring_arr = jnp.array(ring, dtype=jnp.int32)
+    me = lax.axis_index(axis)
+    my_pos = jnp.array(position, dtype=jnp.int32)[me]
+    out = jnp.zeros((n,) + shard.shape, shard.dtype)
+    out = lax.dynamic_update_index_in_dim(out, shard, me, 0)
+    go_right = go_left = shard
+    n_right = n // 2
+    n_left = n - 1 - n_right
+    for step in range(1, n_right + 1):
+        go_right = lax.ppermute(go_right, axis, right)
+        out = lax.dynamic_update_index_in_dim(out, go_right, ring_arr[(my_pos - step) % n], 0)
+        if step <= n_left:
+            go_left = lax.ppermute(go_left, axis, left)
+            out = lax.dynamic_update_index_in_dim(out, go_left, ring_arr[(my_pos + step) % n], 0)
+    return out
 
 
 def shards(factors, occ_energy, vir_energy, slab_orbitals, pair_list, pair_state, state_shift):
@@ -17,7 +46,7 @@
     spread_b = lax.all_to_all(
         factors.reshape(local_aux, nocc, n_col, cols_b), "col", split_axis=2, concat_axis=0, tiled=True
     ).reshape(n_col * local_aux, nocc, cols_b)
-    block_b = lax.all_gather(spread_b, "row", axis=0, tiled=True)
+    block_b = ring_gather(spread_b, "row", row_ring(n_row))
     block_a = block_a.reshape(n_col, n_row, local_aux, nocc, rows_a)
     block_b = block_b.reshape(n_row, n_col, local_aux, nocc, cols_b)
     gram = jnp.einsum(

time: 254 us -> 218 us (0.86)
  waiting for transfers between devices: 165 us -> 111 us
  blocking collectives: 50.5 us -> 20.5 us
  between operations: 13.5 us -> 31.4 us
  local copies, waits for them, and re-layouts: 8.74 us -> 24.3 us
  starting transfers between devices: 0.04 us -> 14.1 us
    all_gather x1, waiting for transfers between devices: 103 us -> 0.01 us  [shards(): block_a = lax.all_gather(spread_a, 'col', axis=0, tiled=True)]
    ppermute x0 -> x7, waiting for transfers between devices: none -> 89.9 us  [the longest x4 89.9 us: ring_gather(): go_right = lax.ppermute(go_right, axis, right)]
    all_gather x1 -> x0, waiting for transfers between devices: 61.6 us -> none  [shards(): block_b = lax.all_gather(spread_b, 'row', axis=0, tiled=True)]
    all_to_all x1 -> x0, blocking collectives: 25.3 us -> none  [shards(): lax.all_to_all(factors.reshape(local_aux, nocc, n_col, cols_b), 'col', sp...]
    all_to_all x0 -> x1, waiting for transfers between devices: none -> 21.4 us  [shards(): lax.all_to_all(factors.reshape(local_aux, nocc, n_col, cols_b), 'col', sp...]
    all_to_all x0 -> x1, starting transfers between devices: none -> 8.97 us  [shards(): lax.all_to_all(factors.reshape(local_aux, nocc, n_col, cols_b), 'col', sp...]
    dynamic_update_slice x0 -> x8, local copies, waits for them, and re-layouts: none -> 8.24 us  [the longest x4 4.1 us: ring_gather(): lax.dynamic_update_index_in_dim(out, go_right, ring_arr[(my_pos - step) %...]
    ppermute x0 -> x7, starting transfers between devices: none -> 5.13 us  [the longest x3 4.64 us: ring_gather(): go_left = lax.ppermute(go_left, axis, left)]
  transfers between devices with their start and end apart: 2 -> 9, of which waited for: 2 -> 4; matrix products, arithmetic and copies ran while one was open for 3% -> 11% of each run, Pallas kernels for 0% -> 0%
where the time goes in v1:
time: 218 us; the launch traced here: 217 us
  waiting for transfers between devices  111 us (51%)
  between operations  31.4 us (14%)
  local copies, waits for them, and re-layouts  24.3 us (11%)
  blocking collectives  20.5 us (9%)
  starting transfers between devices  14.1 us (6%)
  matrix products  11.8 us (5%)
  other arithmetic  3.88 us (2%)
    ppermute x4, waiting for transfers between devices, ring_gather(): go_right = lax.ppermute(go_right, axis, right)  89.9 us
    all_to_all x1, waiting for transfers between devices, shards(): lax.all_to_all(factors.reshape(local_aux, nocc, n_col, cols_b), 'col', sp...  21.4 us
    all_to_all x1, blocking collectives, shards(): lax.all_to_all(factors.reshape(local_aux, nocc, n_row, rows_a), 'row', sp...  20.5 us
    dot_general x1, matrix products, shards(): jnp.einsum('crpia,rcpjb->ijab', block_a, block_b, preferred_element_type=...  11.8 us
    all_to_all x1, starting transfers between devices, shards(): lax.all_to_all(factors.reshape(local_aux, nocc, n_col, cols_b), 'col', sp...  8.97 us
    broadcast_in_dim x1, local copies, waits for them, and re-layouts, ring_gather(): out = jnp.zeros((n,) + shard.shape, shard.dtype)  4.83 us
    ppermute x3, starting transfers between devices, ring_gather(): go_left = lax.ppermute(go_left, axis, left)  4.64 us
  transfers between devices with their start and end apart: 9, of which 4 were waited for; matrix products, arithmetic and copies ran while one was open for 11% of the time, Pallas kernels for 0%

profile of v1, /device:TPU:1, one launch (start us, length us, event | category | flops | bytes accessed | tf_op | source)
XLA Modules:
  0.0 217.3 jit_solution(1795550504822985843)
XLA Ops:
  6.5 0.0 copy-start
  6.5 0.0 copy-start.2
  6.5 0.0 copy-start.3
  6.5 0.0 copy-start.5
  6.5 0.0 copy-start.4
  6.5 0.0 copy-start.1
  6.6 0.0 all-gather.2.cloned.1.call-start
  6.6 1.3 copy.46
  7.9 20.5 %all_to_all.30 = bf16[80,3,8,256]{3,0,1,2:T(8,128)(2,1)S(1)} all-to-all(bf16[80,3,8,256]{3,0,1,2:T(8,128)(2,1)S(1)} %bitcast.79), channel_id=1, replica_groups=mesh['row'=8,'col'=16] {'row'}, dimensions={2} | all-to-all | bytes 1966080 | tf_op jit(solution)/shard_map/all_to_all | solution.py:42
  28.4 1.0 copy.29
  29.4 0.0 all-gather.2.cloned.1.call-update
  29.4 2.3 %copy_bitcast_fusion.1 = bf16[80,3,16,128]{3,0,1,2:T(8,128)(2,1)} fusion(bf16[80,3,2048]{2,0,1:T(8,128)(2,1)} %param.9), kind=kLoop, calls=%fused_computation.9 | loop fusion | bytes 1966080 | tf_op jit(solution)/shard_map/reshape | solution.py:47
  31.7 9.0 %all-to-all-start = ((bf16[80,3,16,128]{3,0,1,2:T(8,128)(2,1)}), bf16[80,3,16,128]{3,0,1,2:T(8,128)(2,1)S(1)}, u32[]{:S(2)}, u32[]{:S(2)}) async-start(bf16[80,3,16,128]{3,0,1,2:T(8,128)(2,1)} %copy_bitcast_fusion.1), calls=%async_computation | async-start | bytes 1966080 | tf_op jit(solution)/shard_map/all_to_all | solution.py:46
  40.7 0.0 copy-done.3
  40.7 0.6 fusion.7
  41.4 0.0 copy-done.5
  41.4 0.0 copy-done.4
  41.4 1.8 fusion.5
  43.2 21.4 %all-to-all-done = bf16[80,3,16,128]{3,0,1,2:T(8,128)(2,1)S(1)} async-done(((bf16[80,3,16,128]{3,0,1,2:T(8,128)(2,1)}), bf16[80,3,16,128]{3,0,1,2:T(8,128)(2,1)S(1)}, u32[]{:S(2)}, u32[]{:S(2)}) %all-to-all-start) | async-done | bytes 983072 | tf_op jit(solution)/shard_map/all_to_all | solution.py:46
  64.5 0.1 copy.27
  64.6 0.3 collective-permute-start
  64.9 1.2 collective-permute-start.1
  66.2 0.0 copy-done.2
  66.2 0.6 dynamic_slice.30
  71.4 0.7 fusion.8
  80.9 0.8 dynamic_slice.38
  81.7 0.8 dynamic_slice.39
  82.5 0.0 copy-done
  82.5 0.7 gather_fusion.1
  83.2 0.7 gather_fusion.2
  88.2 0.0 copy-done.1
  88.2 0.7 gather_fusion.3
  88.9 0.1 broadcast_add_fusion
  89.0 4.8 %broadcast_in_dim.51 = bf16[8,1280,3,128]{3,1,2,0:T(8,128)(2,1)} broadcast(bf16[]{:T(256)} %constant.100.clone.1), dimensions={} | broadcast | bytes 7864322 | tf_op jit(solution)/shard_map/broadcast_in_dim | solution.py:22
  93.9 1.0 constant_dynamic-update-slice_fusion
  94.9 0.0 collective-permute-done
  94.9 0.2 collective-permute-start.2
  95.1 0.0 collective-permute-done.1
  95.1 1.6 collective-permute-start.3
  96.7 1.0 bitcast_dynamic-update-slice_fusion.6
  97.7 1.0 bitcast_dynamic-update-slice_fusion.5
  98.8 40.9 %collective-permute-done.2 = bf16[1280,3,128]{2,0,1:T(8,128)(2,1)S(1)} collective-permute-done((bf16[1280,3,128]{2,0,1:T(8,128)(2,1)S(1)}, bf16[1280,3,128]{2,0,1:T(8,128)(2,1)S(1)}, u32[]{:S(2)}, u32[]{:S(2)}) %collective-permute-start.2) | collective-permute-done | bytes 983072 | tf_op jit(solution)/shard_map/ppermute | solution.py:28
  139.7 0.0 collective-permute-start.4
  139.7 0.0 collective-permute-done.3
  139.7 1.8 collective-permute-start.5
  141.5 1.0 bitcast_dynamic-update-slice_fusion.4
  142.5 1.0 bitcast_dynamic-update-slice_fusion.3
  143.5 28.1 %collective-permute-done.4 = bf16[1280,3,128]{2,0,1:T(8,128)(2,1)S(1)} collective-permute-done((bf16[1280,3,128]{2,0,1:T(8,128)(2,1)S(1)}, bf16[1280,3,128]{2,0,1:T(8,128)(2,1)S(1)}, u32[]{:S(2)}, u32[]{:S(2)}) %collective-permute-start.4) | collective-permute-done | bytes 983072 | tf_op jit(solution)/shard_map/ppermute | solution.py:28
  171.6 0.0 collective-permute-start.6
  171.6 1.0 bitcast_dynamic-update-slice_fusion.2
  172.6 0.0 collective-permute-done.5
  172.6 1.0 bitcast_dynamic-update-slice_fusion.1
  173.7 20.9 %collective-permute-done.6 = bf16[1280,3,128]{2,0,1:T(8,128)(2,1)S(1)} collective-permute-done((bf16[1280,3,128]{2,0,1:T(8,128)(2,1)S(1)}, bf16[1280,3,128]{2,0,1:T(8,128)(2,1)S(1)}, u32[]{:S(2)}, u32[]{:S(2)}) %collective-permute-start.6) | collective-permute-done | bytes 983072 | tf_op jit(solution)/shard_map/ppermute | solution.py:28
  194.6 1.0 bitcast_dynamic-update-slice_fusion
  195.6 0.0 all-gather.2.cloned.1.call-done
  195.6 11.8 %fusion.2 = f32[3,3,256,128]{2,3,1,0:T(8,128)S(1)} fusion(bf16[8,16,80,3,128,1]{4,2,1,3,5,0:T(8,128)(2,1)} %bitcast.30, bf16[16,8,80,3,256,1]{4,2,1,0,3,5:T(8,128)(2,1)} %bitcast.81), kind=kOutput, calls=%fused_computation.7 | convolution fusion | flops 6039797760 | bytes 24772608 | tf_op jit(solution)/shard_map/crpia,rcpjb->ijab/dot_general | solution.py:52
  207.4 0.4 copy.31
  207.8 0.7 gather_fusion
  208.5 1.9 add_divide_fusion
  (5 shorter events, 0.0 us)
Async XLA Ops:
  6.5 76.0 %copy-start = (f32[300]{0:T(512)S(1)}, f32[300]{0:T(512)}, u32[]{:S(2)}) copy-start(f32[300]{0:T(512)} %param.10) | copy-start | bytes 3604
  6.5 59.6 %copy-start.2 = (s32[8]{0:T(128)S(1)}, s32[8]{0:T(128)}, u32[]{:S(2)}) copy-start(s32[8]{0:T(128)} %constant.118.clone) | copy-start | bytes 100
  6.5 34.2 %copy-start.3 = (s32[3]{0:T(128)S(1)}, s32[3]{0:T(128)}, u32[]{:S(2)}) copy-start(s32[3]{0:T(128)} %param.12) | copy-start | bytes 40
  6.5 34.8 %copy-start.5 = (s32[16]{0:T(128)S(1)}, s32[16]{0:T(128)}, u32[]{:S(2)}) copy-start(s32[16]{0:T(128)} %param.14) | copy-start | bytes 196
  6.5 34.8 %copy-start.4 = (s32[16,2]{0,1:T(2,128)S(1)}, s32[16,2]{0,1:T(2,128)}, u32[]{:S(2)}) copy-start(s32[16,2]{0,1:T(2,128)} %param.13) | copy-start | bytes 388
  6.5 81.7 %copy-start.1 = (f32[4]{0:T(128)S(1)}, f32[4]{0:T(128)}, u32[]{:S(2)}) copy-start(f32[4]{0:T(128)} %param.15) | copy-start | bytes 52
  6.6 189.1 %all-gather.2.cloned.1.call-start = ((), (), s32[]{:S(2)}) async-start(), calls=%async_computation.2 | async-start | bytes 16711680 | tf_op jit(solution)/shard_map/all_gather | solution.py:45
  31.7 32.8 %all-to-all-start = ((bf16[80,3,16,128]{3,0,1,2:T(8,128)(2,1)}), bf16[80,3,16,128]{3,0,1,2:T(8,128)(2,1)S(1)}, u32[]{:S(2)}, u32[]{:S(2)}) async-start(bf16[80,3,16,128]{3,0,1,2:T(8,128)(2,1)} %copy_bitcast_fusion.1), calls=%async_computation | async-start | bytes 1966080 | tf_op jit(solution)/shard_map/all_to_all | solution.py:46
  64.6 30.3 %collective-permute-start = (bf16[1280,3,128]{2,0,1:T(8,128)(2,1)S(1)}, bf16[1280,3,128]{2,0,1:T(8,128)(2,1)S(1)}, u32[]{:S(2)}, u32[]{:S(2)}) collective-permute-start(bf16[1280,3,128]{2,0,1:T(8,128)(2,1)S(1)} %bitcast.76), channel_id=1, source_target_pairs={{0,16},{16,32},{32,48},{48,112},{112,96},{96,80},{80,64},{64,0},{1... | collective-permute-start | bytes 2949128 | tf_op jit(solution)/shard_map/ppermute | solution.py:28
  64.9 30.2 %collective-permute-start.1 = (bf16[1280,3,128]{2,0,1:T(8,128)(2,1)S(1)}, bf16[1280,3,128]{2,0,1:T(8,128)(2,1)S(1)}, u32[]{:S(2)}, u32[]{:S(2)}) collective-permute-start(bf16[1280,3,128]{2,0,1:T(8,128)(2,1)S(1)} %bitcast.77), channel_id=1, source_target_pairs={{0,64},{16,0},{32,16},{48,32},{112,48},{96,112},{80,96},{64,80},{1... | collective-permute-start | bytes 2949128 | tf_op jit(solution)/shard_map/ppermute | solution.py:31
  94.9 44.8 %collective-permute-start.2 = (bf16[1280,3,128]{2,0,1:T(8,128)(2,1)S(1)}, bf16[1280,3,128]{2,0,1:T(8,128)(2,1)S(1)}, u32[]{:S(2)}, u32[]{:S(2)}) collective-permute-start(bf16[1280,3,128]{2,0,1:T(8,128)(2,1)S(1)} %collective-permute-done), channel_id=1, source_target_pairs={{0,16},{16,32},{32,48},{48,112},{112,96},{96,80},{80,64},{64,0},{1... | collective-permute-start | bytes 2949128 | tf_op jit(solution)/shard_map/ppermute | solution.py:28
  95.1 44.6 %collective-permute-start.3 = (bf16[1280,3,128]{2,0,1:T(8,128)(2,1)S(1)}, bf16[1280,3,128]{2,0,1:T(8,128)(2,1)S(1)}, u32[]{:S(2)}, u32[]{:S(2)}) collective-permute-start(bf16[1280,3,128]{2,0,1:T(8,128)(2,1)S(1)} %collective-permute-done.1), channel_id=1, source_target_pairs={{0,64},{16,0},{32,16},{48,32},{112,48},{96,112},{80,96},{64,80},{1... | collective-permute-start | bytes 2949128 | tf_op jit(solution)/shard_map/ppermute | solution.py:31
  139.7 31.9 %collective-permute-start.4 = (bf16[1280,3,128]{2,0,1:T(8,128)(2,1)S(1)}, bf16[1280,3,128]{2,0,1:T(8,128)(2,1)S(1)}, u32[]{:S(2)}, u32[]{:S(2)}) collective-permute-start(bf16[1280,3,128]{2,0,1:T(8,128)(2,1)S(1)} %collective-permute-done.2), channel_id=1, source_target_pairs={{0,16},{16,32},{32,48},{48,112},{112,96},{96,80},{80,64},{64,0},{1... | collective-permute-start | bytes 2949128 | tf_op jit(solution)/shard_map/ppermute | solution.py:28
  139.7 33.0 %collective-permute-start.5 = (bf16[1280,3,128]{2,0,1:T(8,128)(2,1)S(1)}, bf16[1280,3,128]{2,0,1:T(8,128)(2,1)S(1)}, u32[]{:S(2)}, u32[]{:S(2)}) collective-permute-start(bf16[1280,3,128]{2,0,1:T(8,128)(2,1)S(1)} %collective-permute-done.3), channel_id=1, source_target_pairs={{0,64},{16,0},{32,16},{48,32},{112,48},{96,112},{80,96},{64,80},{1... | collective-permute-start | bytes 2949128 | tf_op jit(solution)/shard_map/ppermute | solution.py:31
  171.6 23.0 %collective-permute-start.6 = (bf16[1280,3,128]{2,0,1:T(8,128)(2,1)S(1)}, bf16[1280,3,128]{2,0,1:T(8,128)(2,1)S(1)}, u32[]{:S(2)}, u32[]{:S(2)}) collective-permute-start(bf16[1280,3,128]{2,0,1:T(8,128)(2,1)S(1)} %collective-permute-done.4), channel_id=1, source_target_pairs={{0,16},{16,32},{32,48},{48,112},{112,96},{96,80},{80,64},{64,0},{1... | collective-permute-start | bytes 2949128 | tf_op jit(solution)/shard_map/ppermute | solution.py:28
Sparse Core Ops, SparseCore 0:
  29.5 148.5 all-gather.1

commit v2 on v1

--- a/solution.py
+++ b/solution.py
@@ -1,7 +1,7 @@
 import jax
 import jax.numpy as jnp
 from jax import lax
-from jax.sharding import PartitionSpec as P
+from jax.sharding import Mesh, PartitionSpec as P
 
 
 def row_ring(n_row):
@@ -35,28 +35,42 @@
 
 def shards(factors, occ_energy, vir_energy, slab_orbitals, pair_list, pair_state, state_shift):
     n_row = lax.axis_size("row")
-    n_col = lax.axis_size("col")
+    n_colx = lax.axis_size("colx")
+    n_core = lax.axis_size("core")
+    n_col = n_colx * n_core
     local_aux, nocc, nvir = factors.shape
     rows_a = nvir // n_row
     cols_b = nvir // n_col
     spread_a = lax.all_to_all(
         factors.reshape(local_aux, nocc, n_row, rows_a), "row", split_axis=2, concat_axis=0, tiled=True
     ).reshape(n_row * local_aux, nocc, rows_a)
-    block_a = lax.all_gather(spread_a, "col", axis=0, tiled=True)
+    half_a = lax.all_gather(spread_a, "colx", axis=0, tiled=True)
+    other_a = lax.ppermute(half_a, "core", [(k, (k + 1) % n_core) for k in range(n_core)])
     spread_b = lax.all_to_all(
-        factors.reshape(local_aux, nocc, n_col, cols_b), "col", split_axis=2, concat_axis=0, tiled=True
+        factors.reshape(local_aux, nocc, n_col, cols_b), ("colx", "core"), split_axis=2, concat_axis=0, tiled=True
     ).reshape(n_col * local_aux, nocc, cols_b)
     block_b = ring_gather(spread_b, "row", row_ring(n_row))
-    block_a = block_a.reshape(n_col, n_row, local_aux, nocc, rows_a)
-    block_b = block_b.reshape(n_row, n_col, local_aux, nocc, cols_b)
+    block_b = block_b.reshape(n_row, n_colx, n_core, local_aux, nocc, cols_b)
+    me_core = lax.axis_index("core")
+    contract = "xrpia,rxpjb->ijab"
     gram = jnp.einsum(
-        "crpia,rcpjb->ijab", block_a, block_b, preferred_element_type=jnp.float32
-    ).reshape(nocc * nocc, rows_a, cols_b)
+        contract,
+        half_a.reshape(n_colx, n_row, local_aux, nocc, rows_a),
+        lax.dynamic_index_in_dim(block_b, me_core, 2, keepdims=False),
+        preferred_element_type=jnp.float32,
+    ) + jnp.einsum(
+        contract,
+        other_a.reshape(n_colx, n_row, local_aux, nocc, rows_a),
+        lax.dynamic_index_in_dim(block_b, (me_core + n_core - 1) % n_core, 2, keepdims=False),
+        preferred_element_type=jnp.float32,
+    )
+    gram = gram.reshape(nocc * nocc, rows_a, cols_b)
     first = pair_list[:, 0]
     second = pair_list[:, 1]
     kernel = jnp.take(gram, first * nocc + second, axis=0)
     vir_a = lax.dynamic_slice_in_dim(vir_energy, lax.axis_index("row") * rows_a, rows_a)
-    vir_b = lax.dynamic_slice_in_dim(vir_energy, lax.axis_index("col") * cols_b, cols_b)
+    col_index = lax.axis_index("colx") * n_core + me_core
+    vir_b = lax.dynamic_slice_in_dim(vir_energy, col_index * cols_b, cols_b)
     e_first = occ_energy[slab_orbitals[first]]
     e_second = occ_energy[slab_orbitals[second]]
     shift = state_shift[pair_state]
@@ -70,7 +84,9 @@
 
 
 def solution(mesh):
-    placed = (P(("row", "col"), None, None), P(), P(), P(), P(), P(), P())
+    n_row, n_col = mesh.devices.shape
+    sub = Mesh(mesh.devices.reshape(n_row, n_col // 2, 2), ("row", "colx", "core"))
+    placed = (P(("row", "colx", "core"), None, None), P(), P(), P(), P(), P(), P())
     return jax.shard_map(
-        shards, mesh=mesh, in_specs=placed, out_specs=P(None, "row", "col"), check_vma=False
+        shards, mesh=sub, in_specs=placed, out_specs=P(None, "row", ("colx", "core")), check_vma=False
     )

time: 218 us -> 276 us (1.27); the launches traced: 217 us -> 272 us
  waiting for transfers between devices: 111 us -> 175 us
  local copies, waits for them, and re-layouts: 24.3 us -> 16 us
  starting transfers between devices: 14.1 us -> 10.7 us
    all_gather x1, waiting for transfers between devices: 0.01 us -> 104 us  [shards(): half_a = lax.all_gather(spread_a, 'colx', axis=0, tiled=True)]
    ppermute x4, waiting for transfers between devices: 89.9 us -> 57.6 us  [ring_gather(): go_right = lax.ppermute(go_right, axis, right)]
    all_to_all x1, waiting for transfers between devices: 21.4 us -> 13.5 us  [shards(): lax.all_to_all(factors.reshape(local_aux, nocc, n_col, cols_b), ('colx',...]
    all_to_all x1, starting transfers between devices: 8.97 us -> 3.54 us  [shards(): lax.all_to_all(factors.reshape(local_aux, nocc, n_col, cols_b), ('colx',...]
    ppermute x4, starting transfers between devices: 0.49 us -> 4.96 us  [ring_gather(): go_right = lax.ppermute(go_right, axis, right)]
    ppermute x3, starting transfers between devices: 4.64 us -> 0.78 us  [ring_gather(): go_left = lax.ppermute(go_left, axis, left)]
    dynamic_update_slice x4, local copies, waits for them, and re-layouts: 4.1 us -> 0.51 us  [ring_gather(): lax.dynamic_update_index_in_dim(out, go_right, ring_arr[(my_pos - step) %...]
    dynamic_slice x1 -> x2, local copies, waits for them, and re-layouts: 0.76 us -> 4 us  [the longest x1 3.24 us: shards(): lax.dynamic_index_in_dim(block_b, me_core, 2, keepdims=False)]
  transfers between devices with their start and end apart: 9 -> 10, of which waited for: 4 -> 5; matrix products, arithmetic and copies ran while one was open for 11% -> 5% of each run, Pallas kernels for 0% -> 0%
where the time goes in v2:
time: 276 us; the launch traced here: 272 us
  waiting for transfers between devices  175 us (63%)
  between operations  31.7 us (11%)
  blocking collectives  20.5 us (7%)
  local copies, waits for them, and re-layouts  16 us (6%)
  matrix products  14.2 us (5%)
  starting transfers between devices  10.7 us (4%)
  other arithmetic  4.01 us (1%)
    all_gather x1, waiting for transfers between devices, shards(): half_a = lax.all_gather(spread_a, 'colx', axis=0, tiled=True)  104 us
    ppermute x4, waiting for transfers between devices, ring_gather(): go_right = lax.ppermute(go_right, axis, right)  57.6 us
    all_to_all x1, blocking collectives, shards(): lax.all_to_all(factors.reshape(local_aux, nocc, n_row, rows_a), 'row', sp...  20.5 us
    all_to_all x1, waiting for transfers between devices, shards(): lax.all_to_all(factors.reshape(local_aux, nocc, n_col, cols_b), ('colx',...  13.5 us
    dot_general x1, matrix products, shards(): jnp.einsum(contract, other_a.reshape(n_colx, n_row, local_aux, nocc, rows...  7.7 us
    dot_general x1, matrix products, shards(): jnp.einsum(contract, half_a.reshape(n_colx, n_row, local_aux, nocc, rows_...  6.54 us
  transfers between devices with their start and end apart: 10, of which 5 were waited for; matrix products, arithmetic and copies ran while one was open for 5% of the time, Pallas kernels for 0%

profile of v2, /device:TPU:1, one launch (start us, length us, event | category | flops | bytes accessed | tf_op | source)
XLA Modules:
  0.0 272.3 jit_solution(11836928373755230479)
XLA Ops:
  6.5 0.0 copy-start
  6.5 0.0 copy-start.2
  6.5 0.0 all-gather.2.cloned.1.call-start
  6.5 1.4 copy.72
  7.9 20.5 %all_to_all.30 = bf16[80,3,8,256]{3,0,1,2:T(8,128)(2,1)S(1)} all-to-all(bf16[80,3,8,256]{3,0,1,2:T(8,128)(2,1)S(1)} %bitcast.118), channel_id=1, replica_groups=mesh['row'=8,'colx'=8,'core'=2] {'row'}, dimensions={2} | all-to-all | bytes 1966080 | tf_op jit(solution)/shard_map/all_to_all | solution.py:44
  28.4 0.0 copy-start.4
  28.4 0.0 copy-start.6
  28.4 0.0 copy-start.5
  28.4 1.0 copy.27
  29.4 0.0 all-gather.2.cloned.1.call-update
  29.4 0.0 copy-start.1
  29.4 104.0 %all-gather.2.cloned.1.call-done = bf16[5120,3,256]{2,0,1:T(8,128)(2,1)} async-done(((bf16[640,3,256]{2,0,1:T(8,128)(2,1)}), bf16[5120,3,256]{2,0,1:T(8,128)(2,1)}) %all-gather.2.cloned.1.call-update) | async-done | bytes 7864336 | tf_op jit(solution)/shard_map/all_gather | solution.py:47
  133.4 1.4 collective-permute-start.7
  134.8 0.0 copy-done.2
  134.8 1.1 copy_bitcast_fusion.1
  135.9 3.5 %all-to-all-start = ((bf16[80,3,16,128]{3,0,1,2:T(8,128)(2,1)}), bf16[80,3,16,128]{3,0,1,2:T(8,128)(2,1)S(1)}, u32[]{:S(2)}, u32[]{:S(2)}) async-start(bf16[80,3,16,128]{3,0,1,2:T(8,128)(2,1)} %copy_bitcast_fusion.1), calls=%async_computation | async-start | bytes 1966080 | tf_op jit(solution)/shard_map/all_to_all | solution.py:49
  139.5 0.0 copy-done.4
  139.5 0.7 fusion.32
  140.1 0.0 copy-done.6
  140.1 0.0 copy-done.5
  140.2 1.9 fusion.30
  142.1 13.5 %all-to-all-done = bf16[80,3,16,128]{3,0,1,2:T(8,128)(2,1)S(1)} async-done(((bf16[80,3,16,128]{3,0,1,2:T(8,128)(2,1)}), bf16[80,3,16,128]{3,0,1,2:T(8,128)(2,1)S(1)}, u32[]{:S(2)}, u32[]{:S(2)}) %all-to-all-start) | async-done | bytes 983072 | tf_op jit(solution)/shard_map/all_to_all | solution.py:49
  155.6 0.1 copy.24
  155.7 1.3 collective-permute-start
  157.0 0.3 collective-permute-start.1
  157.2 0.0 copy-done.3
  157.3 0.6 dynamic_slice.37
  162.5 0.7 fusion.33
  172.2 0.8 dynamic_slice.48
  172.9 0.8 dynamic_slice.47
  173.7 0.0 copy-done
  173.7 0.7 gather_fusion.1
  174.4 0.7 gather_fusion.2
  179.5 0.0 copy-done.1
  179.5 0.7 gather_fusion.3
  180.2 0.1 broadcast_add_fusion
  180.3 1.7 broadcast_in_dim.51
  182.0 0.1 constant_dynamic-update-slice_fusion
  182.1 0.0 collective-permute-done
  182.2 1.3 collective-permute-start.2
  183.4 0.0 collective-permute-done.1
  183.4 0.3 collective-permute-start.3
  183.7 0.1 bitcast_dynamic-update-slice_fusion.6
  183.8 0.1 bitcast_dynamic-update-slice_fusion.5
  184.0 19.9 %collective-permute-done.2 = bf16[1280,3,128]{2,0,1:T(8,128)(2,1)S(1)} collective-permute-done((bf16[1280,3,128]{2,0,1:T(8,128)(2,1)S(1)}, bf16[1280,3,128]{2,0,1:T(8,128)(2,1)S(1)}, u32[]{:S(2)}, u32[]{:S(2)}) %collective-permute-start.2) | collective-permute-done | bytes 983072 | tf_op jit(solution)/shard_map/ppermute | solution.py:28
  203.8 1.2 collective-permute-start.4
  205.0 0.0 collective-permute-done.3
  205.0 0.3 collective-permute-start.5
  205.3 0.1 bitcast_dynamic-update-slice_fusion.4
  205.4 0.1 bitcast_dynamic-update-slice_fusion.3
  205.6 19.0 %collective-permute-done.4 = bf16[1280,3,128]{2,0,1:T(8,128)(2,1)S(1)} collective-permute-done((bf16[1280,3,128]{2,0,1:T(8,128)(2,1)S(1)}, bf16[1280,3,128]{2,0,1:T(8,128)(2,1)S(1)}, u32[]{:S(2)}, u32[]{:S(2)}) %collective-permute-start.4) | collective-permute-done | bytes 983072 | tf_op jit(solution)/shard_map/ppermute | solution.py:28
  224.6 1.2 collective-permute-start.6
  225.8 0.1 bitcast_dynamic-update-slice_fusion.2
  225.9 0.0 collective-permute-done.5
  225.9 0.1 bitcast_dynamic-update-slice_fusion.1
  226.1 18.7 %collective-permute-done.6 = bf16[1280,3,128]{2,0,1:T(8,128)(2,1)S(1)} collective-permute-done((bf16[1280,3,128]{2,0,1:T(8,128)(2,1)S(1)}, bf16[1280,3,128]{2,0,1:T(8,128)(2,1)S(1)}, u32[]{:S(2)}, u32[]{:S(2)}) %collective-permute-start.6) | collective-permute-done | bytes 983072 | tf_op jit(solution)/shard_map/ppermute | solution.py:28
  244.8 0.1 bitcast_dynamic-update-slice_fusion
  244.9 3.2 %constant_dynamic-slice_fusion.1 = (bf16[8,8,1,80,3,128]{5,3,2,1,4,0:T(8,128)(2,1)S(1)}, bf16[8,8,1,80,3,128]{5,3,2,1,4,0:T(8,128)(2,1)}) fusion(bf16[8,8,2,80,3,128]{5,3,2,1,4,0:T(8,128)(2,1)S(1)} %bitcast.111, s32[]{:T(128)S(6)} %select_n.160, s32[]{:T(128)S(6)} %select_n.162), kind=kLoop, calls=%fused_computation.40 | loop fusion | bytes 15728648 | tf_op jit(solution)/shard_map/jit(dynamic_index_in_dim)/dynamic_slice | solution.py:59
  248.2 0.0 collective-permute-done.7
  248.2 7.7 %fusion.15 = f32[3,128,3,256]{3,1,2,0:T(8,128)S(1)} fusion(bf16[8,8,80,3,256]{4,2,1,0,3:T(8,128)(2,1)} %bitcast.42, bf16[8,8,1,80,3,128]{5,3,2,1,4,0:T(8,128)(2,1)} %get-tuple-element.8), kind=kOutput, calls=%fused_computation.16 | convolution fusion | flops 3019898880 | bytes 12976128 | tf_op jit(solution)/shard_map/xrpia,rxpjb->ijab/dot_general | solution.py:61
  255.9 6.5 %fusion.25 = f32[3,3,256,128]{2,3,0,1:T(8,128)S(1)} fusion(f32[3,128,3,256]{3,1,2,0:T(8,128)S(1)} %fusion.15, bf16[8,8,80,3,256]{4,2,1,0,3:T(8,128)(2,1)} %bitcast.120, bf16[8,8,1,80,3,128]{5,3,2,1,4,0:T(8,128)(2,1)S(1)} %get-tuple-element.7), kind=kOutput, calls=%fused_computation.18 | convolution fusion | flops 3020193792 | bytes 14155776 | tf_op jit(solution)/shard_map/xrpia,rxpjb->ijab/dot_general | solution.py:56
  262.4 0.4 copy.31
  262.8 0.7 gather_fusion
  263.5 1.9 add_divide_fusion
  (6 shorter events, 0.0 us)
Async XLA Ops:
  6.5 167.2 %copy-start = (f32[300]{0:T(512)S(1)}, f32[300]{0:T(512)}, u32[]{:S(2)}) copy-start(f32[300]{0:T(512)} %param.10) | copy-start | bytes 3604
  6.5 128.3 %copy-start.2 = (bf16[80,3,2048]{2,0,1:T(8,128)(2,1)S(1)}, bf16[80,3,2048]{2,0,1:T(8,128)(2,1)}, u32[]{:S(2)}) copy-start(bf16[80,3,2048]{2,0,1:T(8,128)(2,1)} %param.9) | copy-start | bytes 2949124
  6.5 126.9 %all-gather.2.cloned.1.call-start = ((), (), s32[]{:S(2)}) async-start(), calls=%async_computation.2 | async-start | bytes 8847360 | tf_op jit(solution)/shard_map/all_gather | solution.py:47
  28.4 111.1 %copy-start.4 = (s32[3]{0:T(128)S(1)}, s32[3]{0:T(128)}, u32[]{:S(2)}) copy-start(s32[3]{0:T(128)} %param.12) | copy-start | bytes 40
  28.4 111.8 %copy-start.6 = (s32[16]{0:T(128)S(1)}, s32[16]{0:T(128)}, u32[]{:S(2)}) copy-start(s32[16]{0:T(128)} %param.14) | copy-start | bytes 196
  28.4 111.8 %copy-start.5 = (s32[16,2]{0,1:T(2,128)S(1)}, s32[16,2]{0,1:T(2,128)}, u32[]{:S(2)}) copy-start(s32[16,2]{0,1:T(2,128)} %param.13) | copy-start | bytes 388
  29.4 127.9 %copy-start.3 = (s32[8]{0:T(128)S(1)}, s32[8]{0:T(128)}, u32[]{:S(2)}) copy-start(s32[8]{0:T(128)} %constant.138.clone) | copy-start | bytes 100
  29.4 150.1 %copy-start.1 = (f32[4]{0:T(128)S(1)}, f32[4]{0:T(128)}, u32[]{:S(2)}) copy-start(f32[4]{0:T(128)} %param.15) | copy-start | bytes 52
  133.4 114.8 %collective-permute-start.7 = (bf16[5120,3,256]{2,0,1:T(8,128)(2,1)}, bf16[5120,3,256]{2,0,1:T(8,128)(2,1)}, u32[]{:S(2)}, u32[]{:S(2)}) collective-permute-start(bf16[5120,3,256]{2,0,1:T(8,128)(2,1)} %all-gather.2.cloned.1.call-done), channel_id=1, source_target_pairs={{0,1},{1,0},{2,3},{3,2},{4,5},{5,4},{6,7},{7,6},{8,9},{9,8},{10,11... | collective-permute-start | bytes 23592968 | tf_op jit(solution)/shard_map/ppermute | solution.py:48
  135.9 19.7 %all-to-all-start = ((bf16[80,3,16,128]{3,0,1,2:T(8,128)(2,1)}), bf16[80,3,16,128]{3,0,1,2:T(8,128)(2,1)S(1)}, u32[]{:S(2)}, u32[]{:S(2)}) async-start(bf16[80,3,16,128]{3,0,1,2:T(8,128)(2,1)} %copy_bitcast_fusion.1), calls=%async_computation | async-start | bytes 1966080 | tf_op jit(solution)/shard_map/all_to_all | solution.py:49
  155.7 26.4 %collective-permute-start = (bf16[1280,3,128]{2,0,1:T(8,128)(2,1)S(1)}, bf16[1280,3,128]{2,0,1:T(8,128)(2,1)S(1)}, u32[]{:S(2)}, u32[]{:S(2)}) collective-permute-start(bf16[1280,3,128]{2,0,1:T(8,128)(2,1)S(1)} %bitcast.114), channel_id=1, source_target_pairs={{0,16},{16,32},{32,48},{48,112},{112,96},{96,80},{80,64},{64,0},{1... | collective-permute-start | bytes 2949128 | tf_op jit(solution)/shard_map/ppermute | solution.py:28
  157.0 26.5 %collective-permute-start.1 = (bf16[1280,3,128]{2,0,1:T(8,128)(2,1)S(1)}, bf16[1280,3,128]{2,0,1:T(8,128)(2,1)S(1)}, u32[]{:S(2)}, u32[]{:S(2)}) collective-permute-start(bf16[1280,3,128]{2,0,1:T(8,128)(2,1)S(1)} %bitcast.115), channel_id=1, source_target_pairs={{0,64},{16,0},{32,16},{48,32},{112,48},{96,112},{80,96},{64,80},{1... | collective-permute-start | bytes 2949128 | tf_op jit(solution)/shard_map/ppermute | solution.py:31
  182.2 21.7 %collective-permute-start.2 = (bf16[1280,3,128]{2,0,1:T(8,128)(2,1)S(1)}, bf16[1280,3,128]{2,0,1:T(8,128)(2,1)S(1)}, u32[]{:S(2)}, u32[]{:S(2)}) collective-permute-start(bf16[1280,3,128]{2,0,1:T(8,128)(2,1)S(1)} %collective-permute-done), channel_id=1, source_target_pairs={{0,16},{16,32},{32,48},{48,112},{112,96},{96,80},{80,64},{64,0},{1... | collective-permute-start | bytes 2949128 | tf_op jit(solution)/shard_map/ppermute | solution.py:28
  183.4 21.6 %collective-permute-start.3 = (bf16[1280,3,128]{2,0,1:T(8,128)(2,1)S(1)}, bf16[1280,3,128]{2,0,1:T(8,128)(2,1)S(1)}, u32[]{:S(2)}, u32[]{:S(2)}) collective-permute-start(bf16[1280,3,128]{2,0,1:T(8,128)(2,1)S(1)} %collective-permute-done.1), channel_id=1, source_target_pairs={{0,64},{16,0},{32,16},{48,32},{112,48},{96,112},{80,96},{64,80},{1... | collective-permute-start | bytes 2949128 | tf_op jit(solution)/shard_map/ppermute | solution.py:31
  203.8 20.8 %collective-permute-start.4 = (bf16[1280,3,128]{2,0,1:T(8,128)(2,1)S(1)}, bf16[1280,3,128]{2,0,1:T(8,128)(2,1)S(1)}, u32[]{:S(2)}, u32[]{:S(2)}) collective-permute-start(bf16[1280,3,128]{2,0,1:T(8,128)(2,1)S(1)} %collective-permute-done.2), channel_id=1, source_target_pairs={{0,16},{16,32},{32,48},{48,112},{112,96},{96,80},{80,64},{64,0},{1... | collective-permute-start | bytes 2949128 | tf_op jit(solution)/shard_map/ppermute | solution.py:28
  205.0 20.9 %collective-permute-start.5 = (bf16[1280,3,128]{2,0,1:T(8,128)(2,1)S(1)}, bf16[1280,3,128]{2,0,1:T(8,128)(2,1)S(1)}, u32[]{:S(2)}, u32[]{:S(2)}) collective-permute-start(bf16[1280,3,128]{2,0,1:T(8,128)(2,1)S(1)} %collective-permute-done.3), channel_id=1, source_target_pairs={{0,64},{16,0},{32,16},{48,32},{112,48},{96,112},{80,96},{64,80},{1... | collective-permute-start | bytes 2949128 | tf_op jit(solution)/shard_map/ppermute | solution.py:31
  224.6 20.2 %collective-permute-start.6 = (bf16[1280,3,128]{2,0,1:T(8,128)(2,1)S(1)}, bf16[1280,3,128]{2,0,1:T(8,128)(2,1)S(1)}, u32[]{:S(2)}, u32[]{:S(2)}) collective-permute-start(bf16[1280,3,128]{2,0,1:T(8,128)(2,1)S(1)} %collective-permute-done.4), channel_id=1, source_target_pairs={{0,16},{16,32},{32,48},{48,112},{112,96},{96,80},{80,64},{64,0},{1... | collective-permute-start | bytes 2949128 | tf_op jit(solution)/shard_map/ppermute | solution.py:28
Sparse Core Ops, SparseCore 0:
  29.5 103.8 all-gather.1

commit v3 on v0

v3 whole, which is shorter than its diff:
```python
import jax
import jax.numpy as jnp
from jax import lax
from jax.sharding import Mesh, PartitionSpec as P


def y_ring_gather(shard, axis):
    n = lax.axis_size(axis)
    me = lax.axis_index(axis)
    right = [(k, (k + 1) % n) for k in range(n)]
    left = [(k, (k - 1) % n) for k in range(n)]
    out = jnp.zeros((n,) + shard.shape, shard.dtype)
    out = lax.dynamic_update_index_in_dim(out, shard, me, 0)
    go_right = go_left = shard
    steps = n // 2
    for step in range(1, steps + 1):
        if step < steps or n % 2 == 1:
            go_right = lax.ppermute(go_right, axis, right)
            go_left = lax.ppermute(go_left, axis, left)
            out = lax.dynamic_update_index_in_dim(out, go_right, (me - step) % n, 0)
            out = lax.dynamic_update_index_in_dim(out, go_left, (me + step) % n, 0)
        else:
            half = shard.shape[0] // 2
            from_left = lax.ppermute(go_right[:half], axis, right)
            from_right = lax.ppermute(go_left[half:], axis, left)
            far = jnp.concatenate([from_left, from_right], axis=0)
            out = lax.dynamic_update_index_in_dim(out, far, (me - step) % n, 0)
    return out


def shards(factors, occ_energy, vir_energy, slab_orbitals, pair_list, pair_state, state_shift):
    n_zl = lax.axis_size("zl")
    n_y = lax.axis_size("y")
    n_row = n_zl * n_y
    n_col = lax.axis_size("col")
    local_aux, nocc, nvir = factors.shape
    rows_a = nvir // n_row
    cols_b = nvir // n_col
    me_zl = lax.axis_index("zl")
    row_index = me_zl * n_y + lax.axis_index("y")
    spread_a = lax.all_to_all(
        factors.reshape(local_aux, nocc, n_row, rows_a), ("zl", "y"), split_axis=2, concat_axis=0, tiled=True
    ).reshape(n_row * local_aux, nocc, rows_a)
    block_a = lax.all_gather(spread_a, "col", axis=0, tiled=True)
    partner = lax.ppermute(factors, "zl", [(k, (k + 1) % n_zl) for k in range(n_zl)])
    pair = jnp.where(me_zl == 0, jnp.stack([factors, partner]), jnp.stack([partner, factors]))
    spread_b = lax.all_to_all(
        pair.reshape(n_zl * local_aux, nocc, n_col, cols_b), "col", split_axis=2, concat_axis=0, tiled=True
    ).reshape(n_col * n_zl * local_aux, nocc, cols_b)
    block_b = y_ring_gather(spread_b, "y")
    block_a = block_a.reshape(n_col, n_zl, n_y, local_aux, nocc, rows_a)
    block_b = block_b.reshape(n_y, n_col, n_zl, local_aux, nocc, cols_b)
    gram = jnp.einsum(
        "czypia,yczpjb->ijab",
        block_a,
        block_b,
        preferred_element_type=jnp.float32,
    ).reshape(nocc * nocc, rows_a, cols_b)
    first = pair_list[:, 0]
    second = pair_list[:, 1]
    kernel = jnp.take(gram, first * nocc + second, axis=0)
    vir_a = lax.dynamic_slice_in_dim(vir_energy, row_index * rows_a, rows_a)
    vir_b = lax.dynamic_slice_in_dim(vir_energy, lax.axis_index("col") * cols_b, cols_b)
    e_first = occ_energy[slab_orbitals[first]]
    e_second = occ_energy[slab_orbitals[second]]
    shift = state_shift[pair_state]
    denom = (
        (vir_a[None, :, None] + vir_b[None, None, :])
        - e_first[:, None, None]
        - e_second[:, None, None]
        + shift[:, None, None]
    )
    return -kernel / denom


def solution(mesh):
    n_row, n_col = mesh.devices.shape
    sub = Mesh(mesh.devices.reshape(2, n_row // 2, n_col), ("zl", "y", "col"))
    placed = (P(("zl", "y", "col"), None, None), P(), P(), P(), P(), P(), P())
    return jax.shard_map(
        shards, mesh=sub, in_specs=placed, out_specs=P(None, ("zl", "y"), "col"), check_vma=False
    )
```

time: 254 us -> 207 us (0.81)
  waiting for transfers between devices: 165 us -> 74 us
  blocking collectives: 50.5 us -> 71.4 us
  local copies, waits for them, and re-layouts: 8.74 us -> 23.4 us
  starting transfers between devices: 0.04 us -> 5.9 us
    all_gather x1, waiting for transfers between devices: 103 us -> 0.01 us  [shards(): block_a = lax.all_gather(spread_a, 'col', axis=0, tiled=True)]
    ppermute x0 -> x5, waiting for transfers between devices: none -> 74 us  [the longest x1 31.3 us: y_ring_gather(): go_right = lax.ppermute(go_right, axis, right)]
    all_gather x1 -> x0, waiting for transfers between devices: 61.6 us -> none  [shards(): block_b = lax.all_gather(spread_b, 'row', axis=0, tiled=True)]
    all_to_all x2, blocking collectives: 50.5 us -> 71.4 us  [the longest x1 50.8 us: shards(): lax.all_to_all(pair.reshape(n_zl * local_aux, nocc, n_col, cols_b), 'col'...]
    dynamic_update_slice x0 -> x3, local copies, waits for them, and re-layouts: none -> 7.34 us  [the longest x1 2.99 us: y_ring_gather(): out = lax.dynamic_update_index_in_dim(out, go_right, (me - step) % n, 0)]
    ppermute x0 -> x5, starting transfers between devices: none -> 5.9 us  [the longest x1 2.72 us: y_ring_gather(): from_right = lax.ppermute(go_left[half:], axis, left)]
    broadcast_in_dim x0 -> x1, local copies, waits for them, and re-layouts: none -> 4.5 us  [y_ring_gather(): out = jnp.zeros((n,) + shard.shape, shard.dtype)]
  transfers between devices with their start and end apart: 2 -> 6, of which waited for: 2 -> 4; matrix products, arithmetic and copies ran while one was open for 3% -> 12% of each run, Pallas kernels for 0% -> 0%
where the time goes in v3:
time: 207 us; the launch traced here: 206 us
  waiting for transfers between devices  74 us (36%)
  blocking collectives  71.4 us (34%)
  local copies, waits for them, and re-layouts  23.4 us (11%)
  between operations  13.6 us (7%)
  matrix products  11.8 us (6%)
  starting transfers between devices  5.9 us (3%)
  other arithmetic  5.73 us (3%)
    all_to_all x1, blocking collectives, shards(): lax.all_to_all(pair.reshape(n_zl * local_aux, nocc, n_col, cols_b), 'col'...  50.8 us
    ppermute x1, waiting for transfers between devices, y_ring_gather(): go_right = lax.ppermute(go_right, axis, right)  31.3 us
    ppermute x1, waiting for transfers between devices, shards(): lax.ppermute(factors, 'zl', [(k, (k + 1) % n_zl) for k in range(n_zl)])  28.3 us
    all_to_all x1, blocking collectives, shards(): lax.all_to_all(factors.reshape(local_aux, nocc, n_row, rows_a), ('zl', 'y...  20.6 us
    ppermute x1, waiting for transfers between devices, y_ring_gather(): from_left = lax.ppermute(go_right[:half], axis, right)  14.1 us
    dot_general x1, matrix products, shards(): jnp.einsum('czypia,yczpjb->ijab', block_a, block_b, preferred_element_typ...  11.8 us
    broadcast_in_dim x1, local copies, waits for them, and re-layouts, y_ring_gather(): out = jnp.zeros((n,) + shard.shape, shard.dtype)  4.5 us
  transfers between devices with their start and end apart: 6, of which 4 were waited for; matrix products, arithmetic and copies ran while one was open for 12% of the time, Pallas kernels for 0%

profile of v3, /device:TPU:1, one launch (start us, length us, event | category | flops | bytes accessed | tf_op | source)
XLA Modules:
  0.0 205.8 jit_solution(9490924230016394854)
XLA Ops:
  6.5 0.0 copy-start
  6.5 0.0 all-gather.2.cloned.1.call-start
  6.5 1.3 copy.38
  7.8 0.0 copy-start.2
  7.8 20.6 %all_to_all.30 = bf16[80,3,8,256]{3,0,1,2:T(8,128)(2,1)S(1)} all-to-all(bf16[80,3,8,256]{3,0,1,2:T(8,128)(2,1)S(1)} %bitcast.64), channel_id=1, replica_groups=mesh['zl'=2,'y'=4,'col'=16] {'zl','y'}, dimensions={2} | all-to-all | bytes 1966080 | tf_op jit(solution)/shard_map/all_to_all | solution.py:41
  28.4 1.0 copy.22
  29.5 0.0 all-gather.2.cloned.1.call-update
  29.5 0.0 copy-done.2
  29.5 0.4 collective-permute-start
  29.9 28.3 %collective-permute-done = bf16[80,3,2048]{2,0,1:T(8,128)(2,1)S(1)} collective-permute-done((bf16[80,3,2048]{2,0,1:T(8,128)(2,1)S(1)}, bf16[80,3,2048]{2,0,1:T(8,128)(2,1)S(1)}, u32[]{:S(2)}, u32[]{:S(2)}) %collective-permute-start) | collective-permute-done | bytes 983072 | tf_op jit(solution)/shard_map/ppermute | solution.py:45
  58.1 0.3 maximum_select_fusion
  58.5 0.2 copy.18
  58.7 0.6 copy.32
  59.3 0.5 copy.19
  59.8 50.8 %all_to_all.31 = bf16[160,3,16,128]{3,0,1,2:T(8,128)(2,1)S(1)} all-to-all(bf16[160,3,16,128]{3,0,1,2:T(8,128)(2,1)S(1)} %copy.19), channel_id=1, replica_groups=mesh['zl'=2,'y'=4,'col'=16] {'col'}, dimensions={2} | all-to-all | bytes 3932160 | tf_op jit(solution)/shard_map/all_to_all | solution.py:47
  110.6 0.0 copy-start.3
  110.6 0.0 copy-start.4
  110.6 0.0 copy-start.5
  110.6 0.0 copy-start.1
  110.6 0.2 copy.20
  110.8 0.3 collective-permute-start.1
  111.1 2.5 %collective-permute-start.2 = (bf16[2560,3,128]{2,0,1:T(8,128)(2,1)S(1)}, bf16[2560,3,128]{2,0,1:T(8,128)(2,1)}, u32[]{:S(2)}, u32[]{:S(2)}) collective-permute-start(bf16[2560,3,128]{2,0,1:T(8,128)(2,1)S(1)} %bitcast.59), channel_id=1, source_target_pairs={{0,48},{16,0},{32,16},{48,32},{1,49},{17,1},{33,17},{49,33},{2,50}... | collective-permute-start | bytes 5898248 | tf_op jit(solution)/shard_map/ppermute | solution.py:19
  113.5 0.8 dynamic_slice.6
  114.3 0.8 dynamic_slice.7
  115.1 0.0 copy-done.3
  115.1 0.7 fusion.8
  115.7 0.0 copy-done.4
  115.7 1.9 fusion.6
  117.6 0.0 copy-done
  117.7 0.7 gather_fusion.1
  118.3 0.7 gather_fusion.2
  119.0 0.0 copy-done.5
  119.0 0.0 copy-done.1
  119.0 0.7 gather_fusion.3
  119.7 0.1 broadcast_add_fusion
  119.8 4.5 %broadcast_in_dim.39 = bf16[4,2560,3,128]{3,1,2,0:T(8,128)(2,1)} broadcast(bf16[]{:T(256)} %constant.67.clone.1), dimensions={} | broadcast | bytes 7864322 | tf_op jit(solution)/shard_map/broadcast_in_dim | solution.py:12
  124.3 1.4 constant_dynamic-update-slice_fusion
  125.7 31.3 %collective-permute-done.1 = bf16[2560,3,128]{2,0,1:T(8,128)(2,1)} collective-permute-done((bf16[2560,3,128]{2,0,1:T(8,128)(2,1)S(1)}, bf16[2560,3,128]{2,0,1:T(8,128)(2,1)}, u32[]{:S(2)}, u32[]{:S(2)}) %collective-permute-start.1) | collective-permute-done | bytes 1966112 | tf_op jit(solution)/shard_map/ppermute | solution.py:18
  157.0 1.3 slice.32
  158.2 0.1 collective-permute-start.3
  158.3 0.0 collective-permute-done.2
  158.3 1.3 slice.33
  159.6 2.7 %collective-permute-start.4 = (bf16[1280,3,128]{2,0,1:T(8,128)(2,1)S(1)}, bf16[1280,3,128]{2,0,1:T(8,128)(2,1)S(1)}, u32[]{:S(2)}, u32[]{:S(2)}) collective-permute-start(bf16[1280,3,128]{2,0,1:T(8,128)(2,1)S(1)} %slice.33), channel_id=1, source_target_pairs={{0,48},{16,0},{32,16},{48,32},{1,49},{17,1},{33,17},{49,33},{2,50}... | collective-permute-start | bytes 2949128 | tf_op jit(solution)/shard_map/ppermute | solution.py:25
  162.3 3.0 %bitcast_dynamic-update-slice_fusion.1 = bf16[4,2560,3,128]{3,1,2,0:T(8,128)(2,1)} fusion(bf16[4,2560,3,128]{3,1,2,0:T(8,128)(2,1)} %constant_dynamic-update-slice_fusion, s32[]{:T(128)S(6)} %select_n.94, bf16[2560,3,128]{2,0,1:T(8,128)(2,1)} %collective-permute-done.1), kind=kLoop, calls=%fused_computation.11 | loop fusion | bytes 3932164 | tf_op jit(solution)/shard_map/jit(dynamic_update_index_in_dim)/dynamic_update_slice | solution.py:20
  165.3 3.0 %bitcast_dynamic-update-slice_fusion = bf16[4,2560,3,128]{3,1,2,0:T(8,128)(2,1)} fusion(bf16[4,2560,3,128]{3,1,2,0:T(8,128)(2,1)} %bitcast_dynamic-update-slice_fusion.1, s32[]{:T(128)S(6)} %select_n.96, bf16[2560,3,128]{2,0,1:T(8,128)(2,1)} %collective-permute-done.2), kind=kLoop, calls=%fused_computation.10 | loop fusion | bytes 3932164 | tf_op jit(solution)/shard_map/jit(dynamic_update_index_in_dim)/dynamic_update_slice | solution.py:21
  168.3 14.1 %collective-permute-done.3 = bf16[1280,3,128]{2,0,1:T(8,128)(2,1)S(1)} collective-permute-done((bf16[1280,3,128]{2,0,1:T(8,128)(2,1)S(1)}, bf16[1280,3,128]{2,0,1:T(8,128)(2,1)S(1)}, u32[]{:S(2)}, u32[]{:S(2)}) %collective-permute-start.3) | collective-permute-done | bytes 983072 | tf_op jit(solution)/shard_map/ppermute | solution.py:24
  182.4 0.3 collective-permute-done.4
  182.7 1.4 fusion.2
  184.2 0.0 all-gather.2.cloned.1.call-done
  184.2 11.8 %fusion.3 = f32[3,3,256,128]{2,3,1,0:T(8,128)S(1)} fusion(bf16[4,16,2,80,3,128,1]{5,3,2,1,4,6,0:T(8,128)(2,1)} %bitcast.14, bf16[16,2,4,80,3,256,1]{5,3,2,1,0,4,6:T(8,128)(2,1)} %bitcast.69), kind=kOutput, calls=%fused_computation.12 | convolution fusion | flops 6039797760 | bytes 24772608 | tf_op jit(solution)/shard_map/czypia,yczpjb->ijab/dot_general | solution.py:53
  195.9 0.4 copy.24
  196.3 0.7 gather_fusion
  197.0 1.9 add_divide_fusion
  (5 shorter events, 0.0 us)
Async XLA Ops:
  6.5 111.1 %copy-start = (f32[300]{0:T(512)S(1)}, f32[300]{0:T(512)}, u32[]{:S(2)}) copy-start(f32[300]{0:T(512)} %param.8) | copy-start | bytes 3604
  6.5 177.6 %all-gather.2.cloned.1.call-start = ((), (), s32[]{:S(2)}) async-start(), calls=%async_computation.2 | async-start | bytes 16711680 | tf_op jit(solution)/shard_map/all_gather | solution.py:44
  7.8 21.7 %copy-start.2 = (bf16[80,3,2048]{2,0,1:T(8,128)(2,1)S(1)}, bf16[80,3,2048]{2,0,1:T(8,128)(2,1)}, u32[]{:S(2)}) copy-start(bf16[80,3,2048]{2,0,1:T(8,128)(2,1)} %param.7) | copy-start | bytes 2949124
  29.5 28.6 %collective-permute-start = (bf16[80,3,2048]{2,0,1:T(8,128)(2,1)S(1)}, bf16[80,3,2048]{2,0,1:T(8,128)(2,1)S(1)}, u32[]{:S(2)}, u32[]{:S(2)}) collective-permute-start(bf16[80,3,2048]{2,0,1:T(8,128)(2,1)S(1)} %copy-done.2), channel_id=1, source_target_pairs={{0,64},{64,0},{1,65},{65,1},{2,66},{66,2},{3,67},{67,3},{4,68},{68... | collective-permute-start | bytes 2949128 | tf_op jit(solution)/shard_map/ppermute | solution.py:45
  110.6 4.4 %copy-start.3 = (s32[3]{0:T(128)S(1)}, s32[3]{0:T(128)}, u32[]{:S(2)}) copy-start(s32[3]{0:T(128)} %param.10) | copy-start | bytes 40
  110.6 5.1 %copy-start.4 = (s32[16,2]{0,1:T(2,128)S(1)}, s32[16,2]{0,1:T(2,128)}, u32[]{:S(2)}) copy-start(s32[16,2]{0,1:T(2,128)} %param.11) | copy-start | bytes 388
  110.6 8.4 %copy-start.5 = (s32[16]{0:T(128)S(1)}, s32[16]{0:T(128)}, u32[]{:S(2)}) copy-start(s32[16]{0:T(128)} %param.12) | copy-start | bytes 196
  110.6 8.4 %copy-start.1 = (f32[4]{0:T(128)S(1)}, f32[4]{0:T(128)}, u32[]{:S(2)}) copy-start(f32[4]{0:T(128)} %param.13) | copy-start | bytes 52
  110.8 46.2 %collective-permute-start.1 = (bf16[2560,3,128]{2,0,1:T(8,128)(2,1)S(1)}, bf16[2560,3,128]{2,0,1:T(8,128)(2,1)}, u32[]{:S(2)}, u32[]{:S(2)}) collective-permute-start(bf16[2560,3,128]{2,0,1:T(8,128)(2,1)S(1)} %bitcast.58), channel_id=1, source_target_pairs={{0,16},{16,32},{32,48},{48,0},{1,17},{17,33},{33,49},{49,1},{2,18}... | collective-permute-start | bytes 5898248 | tf_op jit(solution)/shard_map/ppermute | solution.py:18
  111.1 47.3 %collective-permute-start.2 = (bf16[2560,3,128]{2,0,1:T(8,128)(2,1)S(1)}, bf16[2560,3,128]{2,0,1:T(8,128)(2,1)}, u32[]{:S(2)}, u32[]{:S(2)}) collective-permute-start(bf16[2560,3,128]{2,0,1:T(8,128)(2,1)S(1)} %bitcast.59), channel_id=1, source_target_pairs={{0,48},{16,0},{32,16},{48,32},{1,49},{17,1},{33,17},{49,33},{2,50}... | collective-permute-start | bytes 5898248 | tf_op jit(solution)/shard_map/ppermute | solution.py:19
  158.2 24.2 %collective-permute-start.3 = (bf16[1280,3,128]{2,0,1:T(8,128)(2,1)S(1)}, bf16[1280,3,128]{2,0,1:T(8,128)(2,1)S(1)}, u32[]{:S(2)}, u32[]{:S(2)}) collective-permute-start(bf16[1280,3,128]{2,0,1:T(8,128)(2,1)S(1)} %slice.32), channel_id=1, source_target_pairs={{0,16},{16,32},{32,48},{48,0},{1,17},{17,33},{33,49},{49,1},{2,18}... | collective-permute-start | bytes 2949128 | tf_op jit(solution)/shard_map/ppermute | solution.py:24
  159.6 23.1 %collective-permute-start.4 = (bf16[1280,3,128]{2,0,1:T(8,128)(2,1)S(1)}, bf16[1280,3,128]{2,0,1:T(8,128)(2,1)S(1)}, u32[]{:S(2)}, u32[]{:S(2)}) collective-permute-start(bf16[1280,3,128]{2,0,1:T(8,128)(2,1)S(1)} %slice.33), channel_id=1, source_target_pairs={{0,48},{16,0},{32,16},{48,32},{1,49},{17,1},{33,17},{49,33},{2,50}... | collective-permute-start | bytes 2949128 | tf_op jit(solution)/shard_map/ppermute | solution.py:25
Sparse Core Ops, SparseCore 0:
  29.6 129.9 all-gather.1

commit v4 on v3

--- a/solution.py
+++ b/solution.py
@@ -28,30 +28,39 @@
     return out
 
 
+def swap_pair(part, axis):
+    n = lax.axis_size(axis)
+    other = lax.ppermute(part, axis, [(k, (k + 1) % n) for k in range(n)])
+    return jnp.where(lax.axis_index(axis) == 0, jnp.stack([part, other]), jnp.stack([other, part]))
+
+
 def shards(factors, occ_energy, vir_energy, slab_orbitals, pair_list, pair_state, state_shift):
     n_zl = lax.axis_size("zl")
     n_y = lax.axis_size("y")
+    n_x = lax.axis_size("x")
+    n_zh = lax.axis_size("zh")
+    n_core = lax.axis_size("core")
     n_row = n_zl * n_y
-    n_col = lax.axis_size("col")
+    n_col = n_x * n_zh * n_core
     local_aux, nocc, nvir = factors.shape
     rows_a = nvir // n_row
     cols_b = nvir // n_col
-    me_zl = lax.axis_index("zl")
-    row_index = me_zl * n_y + lax.axis_index("y")
+    row_index = lax.axis_index("zl") * n_y + lax.axis_index("y")
+    col_index = (lax.axis_index("x") * n_zh + lax.axis_index("zh")) * n_core + lax.axis_index("core")
     spread_a = lax.all_to_all(
         factors.reshape(local_aux, nocc, n_row, rows_a), ("zl", "y"), split_axis=2, concat_axis=0, tiled=True
-    ).reshape(n_row * local_aux, nocc, rows_a)
-    block_a = lax.all_gather(spread_a, "col", axis=0, tiled=True)
-    partner = lax.ppermute(factors, "zl", [(k, (k + 1) % n_zl) for k in range(n_zl)])
-    pair = jnp.where(me_zl == 0, jnp.stack([factors, partner]), jnp.stack([partner, factors]))
+    )
+    pair_a = swap_pair(spread_a.reshape(n_row * local_aux, nocc, rows_a), "zh")
+    block_a = lax.all_gather(pair_a, ("x", "core"), axis=0, tiled=True)
     spread_b = lax.all_to_all(
-        pair.reshape(n_zl * local_aux, nocc, n_col, cols_b), "col", split_axis=2, concat_axis=0, tiled=True
-    ).reshape(n_col * n_zl * local_aux, nocc, cols_b)
-    block_b = y_ring_gather(spread_b, "y")
-    block_a = block_a.reshape(n_col, n_zl, n_y, local_aux, nocc, rows_a)
-    block_b = block_b.reshape(n_y, n_col, n_zl, local_aux, nocc, cols_b)
+        factors.reshape(local_aux, nocc, n_col, cols_b), ("x", "zh", "core"), split_axis=2, concat_axis=0, tiled=True
+    )
+    pair_b = swap_pair(spread_b.reshape(n_col * local_aux, nocc, cols_b), "zl")
+    block_b = y_ring_gather(pair_b.reshape(n_zl * n_col * local_aux, nocc, cols_b), "y")
+    block_a = block_a.reshape(n_x, n_core, n_zh, n_zl, n_y, local_aux, nocc, rows_a)
+    block_b = block_b.reshape(n_y, n_zl, n_x, n_zh, n_core, local_aux, nocc, cols_b)
     gram = jnp.einsum(
-        "czypia,yczpjb->ijab",
+        "xchzypia,yzxhcpjb->ijab",
         block_a,
         block_b,
         preferred_element_type=jnp.float32,
@@ -60,7 +69,7 @@
     second = pair_list[:, 1]
     kernel = jnp.take(gram, first * nocc + second, axis=0)
     vir_a = lax.dynamic_slice_in_dim(vir_energy, row_index * rows_a, rows_a)
-    vir_b = lax.dynamic_slice_in_dim(vir_energy, lax.axis_index("col") * cols_b, cols_b)
+    vir_b = lax.dynamic_slice_in_dim(vir_energy, col_index * cols_b, cols_b)
     e_first = occ_energy[slab_orbitals[first]]
     e_second = occ_energy[slab_orbitals[second]]
     shift = state_shift[pair_state]
@@ -75,8 +84,8 @@
 
 def solution(mesh):
     n_row, n_col = mesh.devices.shape
-    sub = Mesh(mesh.devices.reshape(2, n_row // 2, n_col), ("zl", "y", "col"))
-    placed = (P(("zl", "y", "col"), None, None), P(), P(), P(), P(), P(), P())
+    sub = Mesh(mesh.devices.reshape(2, n_row // 2, n_col // 4, 2, 2), ("zl", "y", "x", "zh", "core"))
+    placed = (P(("zl", "y", "x", "zh", "core"), None, None), P(), P(), P(), P(), P(), P())
     return jax.shard_map(
-        shards, mesh=sub, in_specs=placed, out_specs=P(None, ("zl", "y"), "col"), check_vma=False
+        shards, mesh=sub, in_specs=placed, out_specs=P(None, ("zl", "y"), ("x", "zh", "core")), check_vma=False
     )

time: 207 us -> 205 us (level)
  blocking collectives: 71.4 us -> 52.2 us
  waiting for transfers between devices: 74 us -> 88.3 us
  starting transfers between devices: 5.9 us -> 9 us
  local copies, waits for them, and re-layouts: 23.4 us -> 21.3 us
    all_to_all x1, blocking collectives: 50.8 us -> 31.7 us  [shards(): lax.all_to_all(factors.reshape(local_aux, nocc, n_col, cols_b), ('x', 'zh...]
    ppermute x1 -> x2, waiting for transfers between devices: 28.3 us -> 43.2 us  [swap_pair(): other = lax.ppermute(part, axis, [(k, (k + 1) % n) for k in range(n)])]
    ppermute x1 -> x2, starting transfers between devices: 0.36 us -> 3.47 us  [swap_pair(): other = lax.ppermute(part, axis, [(k, (k + 1) % n) for k in range(n)])]
  transfers between devices with their start and end apart: 6 -> 7, of which waited for: 4 -> 5; matrix products, arithmetic and copies ran while one was open for 12% -> 11% of each run, Pallas kernels for 0% -> 0%
where the time goes in v4:
time: 205 us; the launch traced here: 204 us
  waiting for transfers between devices  88.3 us (43%)
  blocking collectives  52.2 us (25%)
  local copies, waits for them, and re-layouts  21.3 us (10%)
  between operations  13.6 us (7%)
  matrix products  11.8 us (6%)
  starting transfers between devices  9 us (4%)
  other arithmetic  7.4 us (4%)
    ppermute x2, waiting for transfers between devices, swap_pair(): other = lax.ppermute(part, axis, [(k, (k + 1) % n) for k in range(n)])  43.2 us
    all_to_all x1, blocking collectives, shards(): lax.all_to_all(factors.reshape(local_aux, nocc, n_col, cols_b), ('x', 'zh...  31.7 us
    ppermute x1, waiting for transfers between devices, y_ring_gather(): go_right = lax.ppermute(go_right, axis, right)  30.5 us
    all_to_all x1, blocking collectives, shards(): lax.all_to_all(factors.reshape(local_aux, nocc, n_row, rows_a), ('zl', 'y...  20.5 us
    ppermute x1, waiting for transfers between devices, y_ring_gather(): from_left = lax.ppermute(go_right[:half], axis, right)  14.3 us
    dot_general x1, matrix products, shards(): jnp.einsum('xchzypia,yzxhcpjb->ijab', block_a, block_b, preferred_element...  11.8 us
    broadcast_in_dim x1, local copies, waits for them, and re-layouts, y_ring_gather(): out = jnp.zeros((n,) + shard.shape, shard.dtype)  4.5 us
  transfers between devices with their start and end apart: 7, of which 5 were waited for; matrix products, arithmetic and copies ran while one was open for 11% of the time, Pallas kernels for 0%

profile of v4, /device:TPU:1, one launch (start us, length us, event | category | flops | bytes accessed | tf_op | source)
XLA Modules:
  0.0 203.7 jit_solution(7941266839609271732)
XLA Ops:
  6.5 0.0 copy-start
  6.5 0.0 all-gather.2.cloned.1.call-start
  6.5 1.3 copy.48
  7.8 20.5 %all_to_all.30 = bf16[80,3,8,256]{3,0,1,2:T(8,128)(2,1)S(1)} all-to-all(bf16[80,3,8,256]{3,0,1,2:T(8,128)(2,1)S(1)} %bitcast.63), channel_id=1, replica_groups=mesh['zl'=2,'y'=4,'x'=4,'zh'=2,'core'=2] {'zl','y'}, dimensions={2} | all-to-all | bytes 1966080 | tf_op jit(solution)/shard_map/all_to_all | solution.py:50
  28.3 0.1 copy.25
  28.4 3.4 %collective-permute-start.5 = (bf16[640,3,256]{2,0,1:T(8,128)(2,1)S(1)}, bf16[640,3,256]{2,0,1:T(8,128)(2,1)S(1)}, u32[]{:S(2)}, u32[]{:S(2)}) collective-permute-start(bf16[640,3,256]{2,0,1:T(8,128)(2,1)S(1)} %bitcast.64), channel_id=1, source_target_pairs={{0,2},{2,0},{1,3},{3,1},{4,6},{6,4},{5,7},{7,5},{8,10},{10,8},{9,1... | collective-permute-start | bytes 2949128 | tf_op jit(solution)/shard_map/ppermute | solution.py:33
  31.8 20.5 %collective-permute-done.5 = bf16[640,3,256]{2,0,1:T(8,128)(2,1)S(1)} collective-permute-done((bf16[640,3,256]{2,0,1:T(8,128)(2,1)S(1)}, bf16[640,3,256]{2,0,1:T(8,128)(2,1)S(1)}, u32[]{:S(2)}, u32[]{:S(2)}) %collective-permute-start.5) | collective-permute-done | bytes 983072 | tf_op jit(solution)/shard_map/ppermute | solution.py:33
  52.3 0.0 copy-start.2
  52.3 1.6 maximum_select_fusion.1
  53.8 0.0 all-gather.2.cloned.1.call-update
  53.9 0.0 copy-done.2
  53.9 0.2 copy_bitcast_fusion.1
  54.0 31.7 %all_to_all.31 = bf16[80,3,16,128]{3,0,1,2:T(8,128)(2,1)S(1)} all-to-all(bf16[80,3,16,128]{3,0,1,2:T(8,128)(2,1)S(1)} %copy_bitcast_fusion.1), channel_id=1, replica_groups=mesh['zl'=2,'y'=4,'x'=4,'zh'=2,'core'=2] {'x','zh','core'}, dimensions={2} | all-to-all | bytes 1966080 | tf_op jit(solution)/shard_map/all_to_all | solution.py:55
  85.7 0.1 copy.21
  85.8 0.1 collective-permute-start
  85.9 22.7 %collective-permute-done = bf16[1280,3,128]{2,0,1:T(8,128)(2,1)S(1)} collective-permute-done((bf16[1280,3,128]{2,0,1:T(8,128)(2,1)S(1)}, bf16[1280,3,128]{2,0,1:T(8,128)(2,1)S(1)}, u32[]{:S(2)}, u32[]{:S(2)}) %collective-permute-start) | collective-permute-done | bytes 983072 | tf_op jit(solution)/shard_map/ppermute | solution.py:33
  108.6 0.3 maximum_select_fusion
  108.9 0.0 copy-start.3
  109.0 0.0 copy-start.4
  109.0 0.0 copy-start.5
  109.0 0.0 copy-start.1
  109.0 0.1 copy.22
  109.1 0.1 collective-permute-start.1
  109.2 2.7 %collective-permute-start.2 = (bf16[2560,3,128]{2,0,1:T(8,128)(2,1)S(1)}, bf16[2560,3,128]{2,0,1:T(8,128)(2,1)}, u32[]{:S(2)}, u32[]{:S(2)}) collective-permute-start(bf16[2560,3,128]{2,0,1:T(8,128)(2,1)S(1)} %bitcast.60), channel_id=1, source_target_pairs={{0,48},{16,0},{32,16},{48,32},{1,49},{17,1},{33,17},{49,33},{2,50}... | collective-permute-start | bytes 5898248 | tf_op jit(solution)/shard_map/ppermute | solution.py:19
  111.9 0.8 dynamic_slice.6
  112.6 0.8 dynamic_slice.7
  113.4 0.0 copy-done.3
  113.4 0.6 fusion.11
  114.0 0.0 copy-done.4
  114.1 2.0 fusion.9
  116.1 0.0 copy-done
  116.1 0.7 gather_fusion.1
  116.7 0.7 gather_fusion.2
  117.4 0.0 copy-done.5
  117.4 0.0 copy-done.1
  117.5 0.7 gather_fusion.3
  118.1 0.1 broadcast_add_fusion
  118.3 4.5 %broadcast_in_dim.37 = bf16[4,2560,3,128]{3,1,2,0:T(8,128)(2,1)} broadcast(bf16[]{:T(256)} %constant.71.clone.1), dimensions={} | broadcast | bytes 7864322 | tf_op jit(solution)/shard_map/broadcast_in_dim | solution.py:12
  122.7 1.4 constant_dynamic-update-slice_fusion
  124.1 30.5 %collective-permute-done.1 = bf16[2560,3,128]{2,0,1:T(8,128)(2,1)} collective-permute-done((bf16[2560,3,128]{2,0,1:T(8,128)(2,1)S(1)}, bf16[2560,3,128]{2,0,1:T(8,128)(2,1)}, u32[]{:S(2)}, u32[]{:S(2)}) %collective-permute-start.1) | collective-permute-done | bytes 1966112 | tf_op jit(solution)/shard_map/ppermute | solution.py:18
  154.7 1.3 slice.32
  155.9 0.1 collective-permute-start.3
  156.0 0.0 collective-permute-done.2
  156.0 1.3 slice.33
  157.3 2.7 %collective-permute-start.4 = (bf16[1280,3,128]{2,0,1:T(8,128)(2,1)S(1)}, bf16[1280,3,128]{2,0,1:T(8,128)(2,1)S(1)}, u32[]{:S(2)}, u32[]{:S(2)}) collective-permute-start(bf16[1280,3,128]{2,0,1:T(8,128)(2,1)S(1)} %slice.33), channel_id=1, source_target_pairs={{0,48},{16,0},{32,16},{48,32},{1,49},{17,1},{33,17},{49,33},{2,50}... | collective-permute-start | bytes 2949128 | tf_op jit(solution)/shard_map/ppermute | solution.py:25
  160.0 3.0 %bitcast_dynamic-update-slice_fusion.1 = bf16[4,2560,3,128]{3,1,2,0:T(8,128)(2,1)} fusion(bf16[4,2560,3,128]{3,1,2,0:T(8,128)(2,1)} %constant_dynamic-update-slice_fusion, s32[]{:T(128)S(6)} %select_n.113, bf16[2560,3,128]{2,0,1:T(8,128)(2,1)} %collective-permute-done.1), kind=kLoop, calls=%fused_computation.13 | loop fusion | bytes 3932164 | tf_op jit(solution)/shard_map/jit(dynamic_update_index_in_dim)/dynamic_update_slice | solution.py:20
  163.0 3.0 %bitcast_dynamic-update-slice_fusion = bf16[4,2560,3,128]{3,1,2,0:T(8,128)(2,1)} fusion(bf16[4,2560,3,128]{3,1,2,0:T(8,128)(2,1)} %bitcast_dynamic-update-slice_fusion.1, s32[]{:T(128)S(6)} %select_n.115, bf16[2560,3,128]{2,0,1:T(8,128)(2,1)} %collective-permute-done.2), kind=kLoop, calls=%fused_computation.12 | loop fusion | bytes 3932164 | tf_op jit(solution)/shard_map/jit(dynamic_update_index_in_dim)/dynamic_update_slice | solution.py:21
  166.0 14.3 %collective-permute-done.3 = bf16[1280,3,128]{2,0,1:T(8,128)(2,1)S(1)} collective-permute-done((bf16[1280,3,128]{2,0,1:T(8,128)(2,1)S(1)}, bf16[1280,3,128]{2,0,1:T(8,128)(2,1)S(1)}, u32[]{:S(2)}, u32[]{:S(2)}) %collective-permute-start.3) | collective-permute-done | bytes 983072 | tf_op jit(solution)/shard_map/ppermute | solution.py:24
  180.2 0.3 collective-permute-done.4
  180.6 1.4 fusion.3
  182.0 0.0 all-gather.2.cloned.1.call-done
  182.0 11.8 %fusion.4 = f32[3,3,256,128]{2,3,0,1:T(8,128)S(1)} fusion(bf16[4,2,2,2,4,80,3,256,1]{7,5,4,3,6,2,1,0,8:T(8,128)(2,1)} %bitcast.71, bf16[4,2,4,2,2,80,3,128,1]{7,5,4,3,2,1,6,0,8:T(8,128)(2,1)} %bitcast.14), kind=kOutput, calls=%fused_computation.14 | convolution fusion | flops 6039797760 | bytes 24772608 | tf_op jit(solution)/shard_map/xchzypia,yzxhcpjb->ijab/dot_general | solution.py:62
  193.8 0.4 copy.28
  194.2 0.7 gather_fusion
  194.9 1.9 add_divide_fusion
  (5 shorter events, 0.0 us)
Async XLA Ops:
  6.5 109.5 %copy-start = (f32[300]{0:T(512)S(1)}, f32[300]{0:T(512)}, u32[]{:S(2)}) copy-start(f32[300]{0:T(512)} %param.8) | copy-start | bytes 3604
  6.5 175.5 %all-gather.2.cloned.1.call-start = ((), (), s32[]{:S(2)}) async-start(), calls=%async_computation.2 | async-start | bytes 17694720 | tf_op jit(solution)/shard_map/all_gather | solution.py:54
  28.4 23.9 %collective-permute-start.5 = (bf16[640,3,256]{2,0,1:T(8,128)(2,1)S(1)}, bf16[640,3,256]{2,0,1:T(8,128)(2,1)S(1)}, u32[]{:S(2)}, u32[]{:S(2)}) collective-permute-start(bf16[640,3,256]{2,0,1:T(8,128)(2,1)S(1)} %bitcast.64), channel_id=1, source_target_pairs={{0,2},{2,0},{1,3},{3,1},{4,6},{6,4},{5,7},{7,5},{8,10},{10,8},{9,1... | collective-permute-start | bytes 2949128 | tf_op jit(solution)/shard_map/ppermute | solution.py:33
  52.3 1.6 copy-start.2
  85.8 22.8 %collective-permute-start = (bf16[1280,3,128]{2,0,1:T(8,128)(2,1)S(1)}, bf16[1280,3,128]{2,0,1:T(8,128)(2,1)S(1)}, u32[]{:S(2)}, u32[]{:S(2)}) collective-permute-start(bf16[1280,3,128]{2,0,1:T(8,128)(2,1)S(1)} %bitcast.66), channel_id=1, source_target_pairs={{0,64},{64,0},{1,65},{65,1},{2,66},{66,2},{3,67},{67,3},{4,68},{68... | collective-permute-start | bytes 2949128 | tf_op jit(solution)/shard_map/ppermute | solution.py:33
  108.9 4.5 %copy-start.3 = (s32[3]{0:T(128)S(1)}, s32[3]{0:T(128)}, u32[]{:S(2)}) copy-start(s32[3]{0:T(128)} %param.10) | copy-start | bytes 40
  109.0 5.1 %copy-start.4 = (s32[16,2]{0,1:T(2,128)S(1)}, s32[16,2]{0,1:T(2,128)}, u32[]{:S(2)}) copy-start(s32[16,2]{0,1:T(2,128)} %param.11) | copy-start | bytes 388
  109.0 8.4 %copy-start.5 = (s32[16]{0:T(128)S(1)}, s32[16]{0:T(128)}, u32[]{:S(2)}) copy-start(s32[16]{0:T(128)} %param.12) | copy-start | bytes 196
  109.0 8.5 %copy-start.1 = (f32[4]{0:T(128)S(1)}, f32[4]{0:T(128)}, u32[]{:S(2)}) copy-start(f32[4]{0:T(128)} %param.13) | copy-start | bytes 52
  109.1 45.5 %collective-permute-start.1 = (bf16[2560,3,128]{2,0,1:T(8,128)(2,1)S(1)}, bf16[2560,3,128]{2,0,1:T(8,128)(2,1)}, u32[]{:S(2)}, u32[]{:S(2)}) collective-permute-start(bf16[2560,3,128]{2,0,1:T(8,128)(2,1)S(1)} %bitcast.59), channel_id=1, source_target_pairs={{0,16},{16,32},{32,48},{48,0},{1,17},{17,33},{33,49},{49,1},{2,18}... | collective-permute-start | bytes 5898248 | tf_op jit(solution)/shard_map/ppermute | solution.py:18
  109.2 46.8 %collective-permute-start.2 = (bf16[2560,3,128]{2,0,1:T(8,128)(2,1)S(1)}, bf16[2560,3,128]{2,0,1:T(8,128)(2,1)}, u32[]{:S(2)}, u32[]{:S(2)}) collective-permute-start(bf16[2560,3,128]{2,0,1:T(8,128)(2,1)S(1)} %bitcast.60), channel_id=1, source_target_pairs={{0,48},{16,0},{32,16},{48,32},{1,49},{17,1},{33,17},{49,33},{2,50}... | collective-permute-start | bytes 5898248 | tf_op jit(solution)/shard_map/ppermute | solution.py:19
  155.9 24.3 %collective-permute-start.3 = (bf16[1280,3,128]{2,0,1:T(8,128)(2,1)S(1)}, bf16[1280,3,128]{2,0,1:T(8,128)(2,1)S(1)}, u32[]{:S(2)}, u32[]{:S(2)}) collective-permute-start(bf16[1280,3,128]{2,0,1:T(8,128)(2,1)S(1)} %slice.32), channel_id=1, source_target_pairs={{0,16},{16,32},{32,48},{48,0},{1,17},{17,33},{33,49},{49,1},{2,18}... | collective-permute-start | bytes 2949128 | tf_op jit(solution)/shard_map/ppermute | solution.py:24
  157.3 23.3 %collective-permute-start.4 = (bf16[1280,3,128]{2,0,1:T(8,128)(2,1)S(1)}, bf16[1280,3,128]{2,0,1:T(8,128)(2,1)S(1)}, u32[]{:S(2)}, u32[]{:S(2)}) collective-permute-start(bf16[1280,3,128]{2,0,1:T(8,128)(2,1)S(1)} %slice.33), channel_id=1, source_target_pairs={{0,48},{16,0},{32,16},{48,32},{1,49},{17,1},{33,17},{49,33},{2,50}... | collective-permute-start | bytes 2949128 | tf_op jit(solution)/shard_map/ppermute | solution.py:25
Sparse Core Ops, SparseCore 0:
  54.0 89.0 all-gather.1

commit v5 on v4

--- a/solution.py
+++ b/solution.py
@@ -50,11 +50,15 @@
     spread_a = lax.all_to_all(
         factors.reshape(local_aux, nocc, n_row, rows_a), ("zl", "y"), split_axis=2, concat_axis=0, tiled=True
     )
-    pair_a = swap_pair(spread_a.reshape(n_row * local_aux, nocc, rows_a), "zh")
-    block_a = lax.all_gather(pair_a, ("x", "core"), axis=0, tiled=True)
+    spread_a = spread_a.reshape(n_row * local_aux, nocc, rows_a)
+    other_a = lax.ppermute(spread_a, "zh", [(k, (k + 1) % n_zh) for k in range(n_zh)])
     spread_b = lax.all_to_all(
         factors.reshape(local_aux, nocc, n_col, cols_b), ("x", "zh", "core"), split_axis=2, concat_axis=0, tiled=True
     )
+    other_a, spread_b = lax.optimization_barrier((other_a, spread_b))
+    first_zh = lax.axis_index("zh") == 0
+    pair_a = jnp.where(first_zh, jnp.stack([spread_a, other_a]), jnp.stack([other_a, spread_a]))
+    block_a = lax.all_gather(pair_a, ("x", "core"), axis=0, tiled=True)
     pair_b = swap_pair(spread_b.reshape(n_col * local_aux, nocc, cols_b), "zl")
     block_b = y_ring_gather(pair_b.reshape(n_zl * n_col * local_aux, nocc, cols_b), "y")
     block_a = block_a.reshape(n_x, n_core, n_zh, n_zl, n_y, local_aux, nocc, rows_a)

time: 205 us -> 187 us (0.912)
  blocking collectives: 52.2 us -> 20.6 us
  starting transfers between devices: 9 us -> 15.3 us
  waiting for transfers between devices: 88.3 us -> 91.8 us
    all_to_all x1 -> x0, blocking collectives: 31.7 us -> none  [shards(): lax.all_to_all(factors.reshape(local_aux, nocc, n_col, cols_b), ('x', 'zh...]
    all_to_all x0 -> x1, waiting for transfers between devices: none -> 25.2 us  [shards(): lax.all_to_all(factors.reshape(local_aux, nocc, n_col, cols_b), ('x', 'zh...]
    ppermute x2 -> x1, waiting for transfers between devices: 43.2 us -> 23.3 us  [swap_pair(): other = lax.ppermute(part, axis, [(k, (k + 1) % n) for k in range(n)])]
    all_to_all x0 -> x1, starting transfers between devices: none -> 6.23 us  [shards(): lax.all_to_all(factors.reshape(local_aux, nocc, n_col, cols_b), ('x', 'zh...]
    ppermute x2 -> x1, starting transfers between devices: 3.47 us -> 0.09 us  [swap_pair(): other = lax.ppermute(part, axis, [(k, (k + 1) % n) for k in range(n)])]
    ppermute x0 -> x1, starting transfers between devices: none -> 3.38 us  [shards(): lax.ppermute(spread_a, 'zh', [(k, (k + 1) % n_zh) for k in range(n_zh)])]
    select_n x0 -> x1, other arithmetic: none -> 3.18 us  [shards(): jnp.where(first_zh, jnp.stack([spread_a, other_a]), jnp.stack([other_a, s...]
  transfers between devices with their start and end apart: 7 -> 8, of which waited for: 5 -> 5; matrix products, arithmetic and copies ran while one was open for 11% -> 13% of each run, Pallas kernels for 0% -> 0%
where the time goes in v5:
time: 187 us; the launch traced here: 184 us
  waiting for transfers between devices  91.8 us (49%)
  local copies, waits for them, and re-layouts  22.2 us (12%)
  blocking collectives  20.6 us (11%)
  starting transfers between devices  15.3 us (8%)
  between operations  13.6 us (7%)
  matrix products  11.8 us (6%)
  other arithmetic  8.97 us (5%)
    ppermute x1, waiting for transfers between devices, y_ring_gather(): go_right = lax.ppermute(go_right, axis, right)  30 us
    all_to_all x1, waiting for transfers between devices, shards(): lax.all_to_all(factors.reshape(local_aux, nocc, n_col, cols_b), ('x', 'zh...  25.2 us
    ppermute x1, waiting for transfers between devices, swap_pair(): other = lax.ppermute(part, axis, [(k, (k + 1) % n) for k in range(n)])  23.3 us
    all_to_all x1, blocking collectives, shards(): lax.all_to_all(factors.reshape(local_aux, nocc, n_row, rows_a), ('zl', 'y...  20.6 us
    ppermute x1, waiting for transfers between devices, y_ring_gather(): from_left = lax.ppermute(go_right[:half], axis, right)  12.9 us
    dot_general x1, matrix products, shards(): jnp.einsum('xchzypia,yzxhcpjb->ijab', block_a, block_b, preferred_element...  11.8 us
    all_to_all x1, starting transfers between devices, shards(): lax.all_to_all(factors.reshape(local_aux, nocc, n_col, cols_b), ('x', 'zh...  6.23 us
    broadcast_in_dim x1, local copies, waits for them, and re-layouts, y_ring_gather(): out = jnp.zeros((n,) + shard.shape, shard.dtype)  4.49 us
  transfers between devices with their start and end apart: 8, of which 5 were waited for; matrix products, arithmetic and copies ran while one was open for 13% of the time, Pallas kernels for 0%

profile of v5, /device:TPU:1, one launch (start us, length us, event | category | flops | bytes accessed | tf_op | source)
XLA Modules:
  0.0 184.3 jit_solution(15730759580484253788)
XLA Ops:
  6.5 0.0 copy-start
  6.5 1.3 copy.47
  7.8 0.0 copy-start.2
  7.8 20.6 %all_to_all.33 = bf16[80,3,8,256]{3,0,1,2:T(8,128)(2,1)S(1)} all-to-all(bf16[80,3,8,256]{3,0,1,2:T(8,128)(2,1)S(1)} %bitcast.63), channel_id=1, replica_groups=mesh['zl'=2,'y'=4,'x'=4,'zh'=2,'core'=2] {'zl','y'}, dimensions={2} | all-to-all | bytes 1966080 | tf_op jit(solution)/shard_map/all_to_all | solution.py:50
  28.4 0.1 copy.20
  28.5 3.4 %collective-permute-start = (bf16[640,3,256]{2,0,1:T(8,128)(2,1)S(1)}, bf16[640,3,256]{2,0,1:T(8,128)(2,1)}, u32[]{:S(2)}, u32[]{:S(2)}) collective-permute-start(bf16[640,3,256]{2,0,1:T(8,128)(2,1)S(1)} %bitcast.64), channel_id=1, source_target_pairs={{0,2},{2,0},{1,3},{3,1},{4,6},{6,4},{5,7},{7,5},{8,10},{10,8},{9,1... | collective-permute-start | bytes 2949128 | tf_op jit(solution)/shard_map/ppermute | solution.py:54
  31.9 0.0 copy-done.2
  31.9 1.1 copy_bitcast_fusion
  33.0 6.2 %all-to-all-start.1 = ((bf16[80,3,16,128]{3,0,1,2:T(8,128)(2,1)}), bf16[80,3,16,128]{3,0,1,2:T(8,128)(2,1)S(1)}, u32[]{:S(2)}, u32[]{:S(2)}) async-start(bf16[80,3,16,128]{3,0,1,2:T(8,128)(2,1)} %copy_bitcast_fusion), calls=%async_computation.1 | async-start | bytes 1966080 | tf_op jit(solution)/shard_map/all_to_all | solution.py:55
  39.2 0.0 all-gather.2.cloned.1.call-start
  39.3 25.2 %all-to-all-done.1 = bf16[80,3,16,128]{3,0,1,2:T(8,128)(2,1)S(1)} async-done(((bf16[80,3,16,128]{3,0,1,2:T(8,128)(2,1)}), bf16[80,3,16,128]{3,0,1,2:T(8,128)(2,1)S(1)}, u32[]{:S(2)}, u32[]{:S(2)}) %all-to-all-start.1) | async-done | bytes 983072 | tf_op jit(solution)/shard_map/all_to_all | solution.py:55
  64.5 0.1 copy.22
  64.5 0.0 collective-permute-done
  64.5 3.2 %maximum_select_fusion.1 = bf16[2,640,3,256]{3,1,2,0:T(8,128)(2,1)} fusion(bf16[1,640,3,256]{3,1,2,0:T(8,128)(2,1)} %bitcast.19, bf16[1,640,3,256]{3,1,2,0:T(8,128)(2,1)S(1)} %bitcast.65, pred[]{:T(512)S(6)} %eq.11), kind=kLoop, calls=%fused_computation.11 | loop fusion | flops 2949120 | bytes 3932161 | tf_op jit(solution)/shard_map/jit(_where)/select_n | solution.py:60
  67.7 0.0 all-gather.2.cloned.1.call-update
  67.7 0.1 collective-permute-start.1
  67.8 23.3 %collective-permute-done.1 = bf16[1280,3,128]{2,0,1:T(8,128)(2,1)S(1)} collective-permute-done((bf16[1280,3,128]{2,0,1:T(8,128)(2,1)S(1)}, bf16[1280,3,128]{2,0,1:T(8,128)(2,1)S(1)}, u32[]{:S(2)}, u32[]{:S(2)}) %collective-permute-start.1) | collective-permute-done | bytes 983072 | tf_op jit(solution)/shard_map/ppermute | solution.py:33
  91.2 0.3 maximum_select_fusion
  91.5 0.0 copy-start.3
  91.5 0.0 copy-start.4
  91.5 0.0 copy-start.5
  91.5 0.0 copy-start.1
  91.6 0.1 copy.23
  91.7 0.3 collective-permute-start.2
  92.0 2.5 %collective-permute-start.3 = (bf16[2560,3,128]{2,0,1:T(8,128)(2,1)S(1)}, bf16[2560,3,128]{2,0,1:T(8,128)(2,1)}, u32[]{:S(2)}, u32[]{:S(2)}) collective-permute-start(bf16[2560,3,128]{2,0,1:T(8,128)(2,1)S(1)} %bitcast.60), channel_id=1, source_target_pairs={{0,48},{16,0},{32,16},{48,32},{1,49},{17,1},{33,17},{49,33},{2,50}... | collective-permute-start | bytes 5898248 | tf_op jit(solution)/shard_map/ppermute | solution.py:19
  94.4 0.8 dynamic_slice.6
  95.2 0.8 dynamic_slice.7
  96.0 0.0 copy-done.3
  96.0 0.6 fusion.11
  96.6 0.0 copy-done.4
  96.6 1.9 %fusion.9 = (s32[16]{0:T(128)S(1)}, s32[16]{0:T(128)S(1)}) fusion(s32[16,2]{0,1:T(2,128)S(1)} %copy-done.4, s32[]{:T(128)} %bitcast.28, s32[]{:T(128)} %bitcast.30, s32[]{:T(128)} %bitcast.29), kind=kLoop, calls=%fused_computation.34 | loop fusion | flops 320 | bytes 268 | tf_op jit(solution)/shard_map/select_n | solution.py:77
  98.6 0.0 copy-done
  98.6 0.7 gather_fusion.1
  99.2 0.7 gather_fusion.2
  99.9 0.0 copy-done.5
  100.0 0.0 copy-done.1
  100.0 0.7 gather_fusion.3
  100.7 0.1 broadcast_add_fusion
  100.8 4.5 %broadcast_in_dim.37 = bf16[4,2560,3,128]{3,1,2,0:T(8,128)(2,1)} broadcast(bf16[]{:T(256)} %constant.71.clone.1), dimensions={} | broadcast | bytes 7864322 | tf_op jit(solution)/shard_map/broadcast_in_dim | solution.py:12
  105.2 1.4 constant_dynamic-update-slice_fusion
  106.6 30.0 %collective-permute-done.2 = bf16[2560,3,128]{2,0,1:T(8,128)(2,1)} collective-permute-done((bf16[2560,3,128]{2,0,1:T(8,128)(2,1)S(1)}, bf16[2560,3,128]{2,0,1:T(8,128)(2,1)}, u32[]{:S(2)}, u32[]{:S(2)}) %collective-permute-start.2) | collective-permute-done | bytes 1966112 | tf_op jit(solution)/shard_map/ppermute | solution.py:18
  136.7 1.3 slice.32
  137.9 0.1 collective-permute-start.4
  138.0 0.0 collective-permute-done.3
  138.0 1.3 slice.33
  139.3 2.7 %collective-permute-start.5 = (bf16[1280,3,128]{2,0,1:T(8,128)(2,1)S(1)}, bf16[1280,3,128]{2,0,1:T(8,128)(2,1)S(1)}, u32[]{:S(2)}, u32[]{:S(2)}) collective-permute-start(bf16[1280,3,128]{2,0,1:T(8,128)(2,1)S(1)} %slice.33), channel_id=1, source_target_pairs={{0,48},{16,0},{32,16},{48,32},{1,49},{17,1},{33,17},{49,33},{2,50}... | collective-permute-start | bytes 2949128 | tf_op jit(solution)/shard_map/ppermute | solution.py:25
  142.0 3.0 %bitcast_dynamic-update-slice_fusion.1 = bf16[4,2560,3,128]{3,1,2,0:T(8,128)(2,1)} fusion(bf16[4,2560,3,128]{3,1,2,0:T(8,128)(2,1)} %constant_dynamic-update-slice_fusion, s32[]{:T(128)S(6)} %select_n.113, bf16[2560,3,128]{2,0,1:T(8,128)(2,1)} %collective-permute-done.2), kind=kLoop, calls=%fused_computation.13 | loop fusion | bytes 3932164 | tf_op jit(solution)/shard_map/jit(dynamic_update_index_in_dim)/dynamic_update_slice | solution.py:20
  145.0 2.9 %bitcast_dynamic-update-slice_fusion = bf16[4,2560,3,128]{3,1,2,0:T(8,128)(2,1)} fusion(bf16[4,2560,3,128]{3,1,2,0:T(8,128)(2,1)} %bitcast_dynamic-update-slice_fusion.1, s32[]{:T(128)S(6)} %select_n.115, bf16[2560,3,128]{2,0,1:T(8,128)(2,1)} %collective-permute-done.3), kind=kLoop, calls=%fused_computation.12 | loop fusion | bytes 3932164 | tf_op jit(solution)/shard_map/jit(dynamic_update_index_in_dim)/dynamic_update_slice | solution.py:21
  147.9 12.9 %collective-permute-done.4 = bf16[1280,3,128]{2,0,1:T(8,128)(2,1)S(1)} collective-permute-done((bf16[1280,3,128]{2,0,1:T(8,128)(2,1)S(1)}, bf16[1280,3,128]{2,0,1:T(8,128)(2,1)S(1)}, u32[]{:S(2)}, u32[]{:S(2)}) %collective-permute-start.4) | collective-permute-done | bytes 983072 | tf_op jit(solution)/shard_map/ppermute | solution.py:24
  160.9 0.3 collective-permute-done.5
  161.2 1.5 fusion.3
  162.6 0.0 all-gather.2.cloned.1.call-done
  162.6 11.8 %fusion.4 = f32[3,3,256,128]{2,3,0,1:T(8,128)S(1)} fusion(bf16[4,2,2,2,4,80,3,256,1]{7,5,4,3,6,2,1,0,8:T(8,128)(2,1)} %bitcast.70, bf16[4,2,4,2,2,80,3,128,1]{7,5,4,3,2,1,6,0,8:T(8,128)(2,1)} %bitcast.16), kind=kOutput, calls=%fused_computation.14 | convolution fusion | flops 6039797760 | bytes 24772608 | tf_op jit(solution)/shard_map/xchzypia,yzxhcpjb->ijab/dot_general | solution.py:66
  174.4 0.4 copy.27
  174.8 0.7 gather_fusion
  175.5 1.9 %add_divide_fusion = f32[16,256,128]{2,1,0:T(8,128)} fusion(f32[16,256,128]{2,1,0:T(8,128)S(1)} %gather_fusion, f32[16]{0:T(128)S(1)} %gather_fusion.3, f32[16]{0:T(128)S(1)} %gather_fusion.2, f32[16]{0:T(128)S(1)} %gather_fusion.1, f32[256,128]{1,0:T(8,128)S(1)} %broadcast_add_fusion, pred[16]{0:T(512)(128)(4,1)S(1)} %get-tuple-element.9), kind=kLoop, calls=%fused_computation.7 | loop fusion | flops 3145728 | bytes 4325584 | tf_op jit(solution)/shard_map/div | solution.py:86
  (5 shorter events, 0.0 us)
Async XLA Ops:
  6.5 92.0 %copy-start = (f32[300]{0:T(512)S(1)}, f32[300]{0:T(512)}, u32[]{:S(2)}) copy-start(f32[300]{0:T(512)} %param.8) | copy-start | bytes 3604
  7.8 24.1 %copy-start.2 = (bf16[80,3,2048]{2,0,1:T(8,128)(2,1)S(1)}, bf16[80,3,2048]{2,0,1:T(8,128)(2,1)}, u32[]{:S(2)}) copy-start(bf16[80,3,2048]{2,0,1:T(8,128)(2,1)} %param.7) | copy-start | bytes 2949124
  28.5 36.0 %collective-permute-start = (bf16[640,3,256]{2,0,1:T(8,128)(2,1)S(1)}, bf16[640,3,256]{2,0,1:T(8,128)(2,1)}, u32[]{:S(2)}, u32[]{:S(2)}) collective-permute-start(bf16[640,3,256]{2,0,1:T(8,128)(2,1)S(1)} %bitcast.64), channel_id=1, source_target_pairs={{0,2},{2,0},{1,3},{3,1},{4,6},{6,4},{5,7},{7,5},{8,10},{10,8},{9,1... | collective-permute-start | bytes 2949128 | tf_op jit(solution)/shard_map/ppermute | solution.py:54
  33.0 31.4 %all-to-all-start.1 = ((bf16[80,3,16,128]{3,0,1,2:T(8,128)(2,1)}), bf16[80,3,16,128]{3,0,1,2:T(8,128)(2,1)S(1)}, u32[]{:S(2)}, u32[]{:S(2)}) async-start(bf16[80,3,16,128]{3,0,1,2:T(8,128)(2,1)} %copy_bitcast_fusion), calls=%async_computation.1 | async-start | bytes 1966080 | tf_op jit(solution)/shard_map/all_to_all | solution.py:55
  39.2 123.4 %all-gather.2.cloned.1.call-start = ((), (), s32[]{:S(2)}) async-start(), calls=%async_computation.2 | async-start | bytes 17694720 | tf_op jit(solution)/shard_map/all_gather | solution.py:61
  67.7 23.4 %collective-permute-start.1 = (bf16[1280,3,128]{2,0,1:T(8,128)(2,1)S(1)}, bf16[1280,3,128]{2,0,1:T(8,128)(2,1)S(1)}, u32[]{:S(2)}, u32[]{:S(2)}) collective-permute-start(bf16[1280,3,128]{2,0,1:T(8,128)(2,1)S(1)} %bitcast.66), channel_id=1, source_target_pairs={{0,64},{64,0},{1,65},{65,1},{2,66},{66,2},{3,67},{67,3},{4,68},{68... | collective-permute-start | bytes 2949128 | tf_op jit(solution)/shard_map/ppermute | solution.py:33
  91.5 4.5 %copy-start.3 = (s32[3]{0:T(128)S(1)}, s32[3]{0:T(128)}, u32[]{:S(2)}) copy-start(s32[3]{0:T(128)} %param.10) | copy-start | bytes 40
  91.5 5.1 %copy-start.4 = (s32[16,2]{0,1:T(2,128)S(1)}, s32[16,2]{0,1:T(2,128)}, u32[]{:S(2)}) copy-start(s32[16,2]{0,1:T(2,128)} %param.11) | copy-start | bytes 388
  91.5 8.4 %copy-start.5 = (s32[16]{0:T(128)S(1)}, s32[16]{0:T(128)}, u32[]{:S(2)}) copy-start(s32[16]{0:T(128)} %param.12) | copy-start | bytes 196
  91.5 8.4 %copy-start.1 = (f32[4]{0:T(128)S(1)}, f32[4]{0:T(128)}, u32[]{:S(2)}) copy-start(f32[4]{0:T(128)} %param.13) | copy-start | bytes 52
  91.7 45.0 %collective-permute-start.2 = (bf16[2560,3,128]{2,0,1:T(8,128)(2,1)S(1)}, bf16[2560,3,128]{2,0,1:T(8,128)(2,1)}, u32[]{:S(2)}, u32[]{:S(2)}) collective-permute-start(bf16[2560,3,128]{2,0,1:T(8,128)(2,1)S(1)} %bitcast.59), channel_id=1, source_target_pairs={{0,16},{16,32},{32,48},{48,0},{1,17},{17,33},{33,49},{49,1},{2,18}... | collective-permute-start | bytes 5898248 | tf_op jit(solution)/shard_map/ppermute | solution.py:18
  92.0 46.0 %collective-permute-start.3 = (bf16[2560,3,128]{2,0,1:T(8,128)(2,1)S(1)}, bf16[2560,3,128]{2,0,1:T(8,128)(2,1)}, u32[]{:S(2)}, u32[]{:S(2)}) collective-permute-start(bf16[2560,3,128]{2,0,1:T(8,128)(2,1)S(1)} %bitcast.60), channel_id=1, source_target_pairs={{0,48},{16,0},{32,16},{48,32},{1,49},{17,1},{33,17},{49,33},{2,50}... | collective-permute-start | bytes 5898248 | tf_op jit(solution)/shard_map/ppermute | solution.py:19
  137.9 22.9 %collective-permute-start.4 = (bf16[1280,3,128]{2,0,1:T(8,128)(2,1)S(1)}, bf16[1280,3,128]{2,0,1:T(8,128)(2,1)S(1)}, u32[]{:S(2)}, u32[]{:S(2)}) collective-permute-start(bf16[1280,3,128]{2,0,1:T(8,128)(2,1)S(1)} %slice.32), channel_id=1, source_target_pairs={{0,16},{16,32},{32,48},{48,0},{1,17},{17,33},{33,49},{49,1},{2,18}... | collective-permute-start | bytes 2949128 | tf_op jit(solution)/shard_map/ppermute | solution.py:24
  139.3 21.9 %collective-permute-start.5 = (bf16[1280,3,128]{2,0,1:T(8,128)(2,1)S(1)}, bf16[1280,3,128]{2,0,1:T(8,128)(2,1)S(1)}, u32[]{:S(2)}, u32[]{:S(2)}) collective-permute-start(bf16[1280,3,128]{2,0,1:T(8,128)(2,1)S(1)} %slice.33), channel_id=1, source_target_pairs={{0,48},{16,0},{32,16},{48,32},{1,49},{17,1},{33,17},{49,33},{2,50}... | collective-permute-start | bytes 2949128 | tf_op jit(solution)/shard_map/ppermute | solution.py:25
Sparse Core Ops, SparseCore 0:
  67.9 80.2 all-gather.1

commit v6 on v5

--- a/solution.py
+++ b/solution.py
@@ -4,34 +4,33 @@
 from jax.sharding import Mesh, PartitionSpec as P
 
 
-def y_ring_gather(shard, axis):
+def ring_into(out, lead, shard, axis):
     n = lax.axis_size(axis)
     me = lax.axis_index(axis)
     right = [(k, (k + 1) % n) for k in range(n)]
     left = [(k, (k - 1) % n) for k in range(n)]
-    out = jnp.zeros((n,) + shard.shape, shard.dtype)
-    out = lax.dynamic_update_index_in_dim(out, shard, me, 0)
+    zeros = (0,) * shard.ndim
+
+    def put(buf, piece, index, offset=0):
+        start = (lead, index, offset) + zeros[1:]
+        return lax.dynamic_update_slice(buf, piece[None, None], start)
+
+    out = put(out, shard, me)
     go_right = go_left = shard
     steps = n // 2
     for step in range(1, steps + 1):
         if step < steps or n % 2 == 1:
             go_right = lax.ppermute(go_right, axis, right)
             go_left = lax.ppermute(go_left, axis, left)
-            out = lax.dynamic_update_index_in_dim(out, go_right, (me - step) % n, 0)
-            out = lax.dynamic_update_index_in_dim(out, go_left, (me + step) % n, 0)
+            out = put(out, go_right, (me - step) % n)
+            out = put(out, go_left, (me + step) % n)
         else:
             half = shard.shape[0] // 2
             from_left = lax.ppermute(go_right[:half], axis, right)
             from_right = lax.ppermute(go_left[half:], axis, left)
-            far = jnp.concatenate([from_left, from_right], axis=0)
-            out = lax.dynamic_update_index_in_dim(out, far, (me - step) % n, 0)
+            out = put(out, from_left, (me - step) % n)
+            out = put(out, from_right, (me - step) % n, half)
     return out
-
-
-def swap_pair(part, axis):
-    n = lax.axis_size(axis)
-    other = lax.ppermute(part, axis, [(k, (k + 1) % n) for k in range(n)])
-    return jnp.where(lax.axis_index(axis) == 0, jnp.stack([part, other]), jnp.stack([other, part]))
 
 
 def shards(factors, occ_energy, vir_energy, slab_orbitals, pair_list, pair_state, state_shift):
@@ -59,12 +58,16 @@
     first_zh = lax.axis_index("zh") == 0
     pair_a = jnp.where(first_zh, jnp.stack([spread_a, other_a]), jnp.stack([other_a, spread_a]))
     block_a = lax.all_gather(pair_a, ("x", "core"), axis=0, tiled=True)
-    pair_b = swap_pair(spread_b.reshape(n_col * local_aux, nocc, cols_b), "zl")
-    block_b = y_ring_gather(pair_b.reshape(n_zl * n_col * local_aux, nocc, cols_b), "y")
+    spread_b = spread_b.reshape(n_col * local_aux, nocc, cols_b)
+    other_b = lax.ppermute(spread_b, "zl", [(k, (k + 1) % n_zl) for k in range(n_zl)])
+    me_zl = lax.axis_index("zl")
+    block_b = jnp.zeros((n_zl, n_y) + spread_b.shape, spread_b.dtype)
+    block_b = ring_into(block_b, me_zl, spread_b, "y")
+    block_b = ring_into(block_b, (me_zl + 1) % n_zl, other_b, "y")
     block_a = block_a.reshape(n_x, n_core, n_zh, n_zl, n_y, local_aux, nocc, rows_a)
-    block_b = block_b.reshape(n_y, n_zl, n_x, n_zh, n_core, local_aux, nocc, cols_b)
+    block_b = block_b.reshape(n_zl, n_y, n_x, n_zh, n_core, local_aux, nocc, cols_b)
     gram = jnp.einsum(
-        "xchzypia,yzxhcpjb->ijab",
+        "xchzypia,zyxhcpjb->ijab",
         block_a,
         block_b,
         preferred_element_type=jnp.float32,

time: 187 us -> 170 us (0.909); the launches traced: 184 us -> 170 us
  waiting for transfers between devices: 91.8 us -> 71.3 us
  starting transfers between devices: 15.3 us -> 20.7 us
  local copies, waits for them, and re-layouts: 22.2 us -> 24.6 us
  other arithmetic: 8.97 us -> 7.08 us
    ppermute x5 -> x9, waiting for transfers between devices: 66.6 us -> 46.7 us  [the longest x2 33.2 us: ring_into(): go_right = lax.ppermute(go_right, axis, right)]
    ppermute x5 -> x9, starting transfers between devices: 5.63 us -> 11 us  [the longest x2 5.44 us: ring_into(): from_right = lax.ppermute(go_left[half:], axis, left)]
    slice x2 -> x4, local copies, waits for them, and re-layouts: 2.54 us -> 0.13 us  [the longest x2 0.07 us: ring_into(): from_right = lax.ppermute(go_left[half:], axis, left)]
    dynamic_update_slice x3 -> x10, local copies, waits for them, and re-layouts: 7.32 us -> 9.68 us  [put(): return lax.dynamic_update_slice(buf, piece[None, None], start)]
  transfers between devices with their start and end apart: 8 -> 12, of which waited for: 5 -> 6; matrix products, arithmetic and copies ran while one was open for 13% -> 14% of each run, Pallas kernels for 0% -> 0%
where the time goes in v6:
time: 170 us
  waiting for transfers between devices  71.3 us (42%)
  local copies, waits for them, and re-layouts  24.6 us (14%)
  starting transfers between devices  20.7 us (12%)
  blocking collectives  20.5 us (12%)
  between operations  13.7 us (8%)
  matrix products  11.8 us (7%)
  other arithmetic  7.08 us (4%)
    ppermute x2, waiting for transfers between devices, ring_into(): go_right = lax.ppermute(go_right, axis, right)  33.2 us
    all_to_all x1, waiting for transfers between devices, shards(): lax.all_to_all(factors.reshape(local_aux, nocc, n_col, cols_b), ('x', 'zh...  24 us
    all_to_all x1, blocking collectives, shards(): lax.all_to_all(factors.reshape(local_aux, nocc, n_row, rows_a), ('zl', 'y...  20.5 us
    ppermute x2, waiting for transfers between devices, ring_into(): from_left = lax.ppermute(go_right[:half], axis, right)  13.5 us
    dot_general x1, matrix products, shards(): jnp.einsum('xchzypia,zyxhcpjb->ijab', block_a, block_b, preferred_element...  11.8 us
    dynamic_update_slice x10, local copies, waits for them, and re-layouts, put(): return lax.dynamic_update_slice(buf, piece[None, None], start)  9.68 us
    all_to_all x1, starting transfers between devices, shards(): lax.all_to_all(factors.reshape(local_aux, nocc, n_col, cols_b), ('x', 'zh...  6.23 us
    broadcast_in_dim x1, local copies, waits for them, and re-layouts, shards(): block_b = jnp.zeros((n_zl, n_y) + spread_b.shape, spread_b.dtype)  5.83 us
  transfers between devices with their start and end apart: 12, of which 6 were waited for; matrix products, arithmetic and copies ran while one was open for 14% of the time, Pallas kernels for 0%

profile of v6, /device:TPU:1, one launch (start us, length us, event | category | flops | bytes accessed | tf_op | source)
XLA Modules:
  0.0 169.6 jit_solution(3050972872837032292)
XLA Ops:
  6.5 0.0 copy-start
  6.5 1.3 copy.43
  7.8 0.0 copy-start.2
  7.8 0.0 copy-start.3
  7.8 20.5 %all_to_all.33 = bf16[80,3,8,256]{3,0,1,2:T(8,128)(2,1)S(1)} all-to-all(bf16[80,3,8,256]{3,0,1,2:T(8,128)(2,1)S(1)} %bitcast.72), channel_id=1, replica_groups=mesh['zl'=2,'y'=4,'x'=4,'zh'=2,'core'=2] {'zl','y'}, dimensions={2} | all-to-all | bytes 1966080 | tf_op jit(solution)/shard_map/all_to_all | solution.py:49
  28.3 0.0 copy-start.4
  28.3 0.0 copy-start.1
  28.3 0.1 copy.18
  28.4 3.4 %collective-permute-start = (bf16[640,3,256]{2,0,1:T(8,128)(2,1)S(1)}, bf16[640,3,256]{2,0,1:T(8,128)(2,1)}, u32[]{:S(2)}, u32[]{:S(2)}) collective-permute-start(bf16[640,3,256]{2,0,1:T(8,128)(2,1)S(1)} %bitcast.73), channel_id=1, source_target_pairs={{0,2},{2,0},{1,3},{3,1},{4,6},{6,4},{5,7},{7,5},{8,10},{10,8},{9,1... | collective-permute-start | bytes 2949128 | tf_op jit(solution)/shard_map/ppermute | solution.py:53
  31.8 2.3 %copy_bitcast_fusion = bf16[80,3,16,128]{3,0,1,2:T(8,128)(2,1)} fusion(bf16[80,3,2048]{2,0,1:T(8,128)(2,1)} %param.7), kind=kLoop, calls=%fused_computation.10 | loop fusion | bytes 1966080 | tf_op jit(solution)/shard_map/reshape | solution.py:55
  34.1 6.2 %all-to-all-start.1 = ((bf16[80,3,16,128]{3,0,1,2:T(8,128)(2,1)}), bf16[80,3,16,128]{3,0,1,2:T(8,128)(2,1)S(1)}, u32[]{:S(2)}, u32[]{:S(2)}) async-start(bf16[80,3,16,128]{3,0,1,2:T(8,128)(2,1)} %copy_bitcast_fusion), calls=%async_computation.1 | async-start | bytes 1966080 | tf_op jit(solution)/shard_map/all_to_all | solution.py:54
  40.3 0.0 all-gather.2.cloned.1.call-start
  40.4 24.0 %all-to-all-done.1 = bf16[80,3,16,128]{3,0,1,2:T(8,128)(2,1)S(1)} async-done(((bf16[80,3,16,128]{3,0,1,2:T(8,128)(2,1)}), bf16[80,3,16,128]{3,0,1,2:T(8,128)(2,1)S(1)}, u32[]{:S(2)}, u32[]{:S(2)}) %all-to-all-start.1) | async-done | bytes 983072 | tf_op jit(solution)/shard_map/all_to_all | solution.py:54
  64.3 0.1 copy.20
  64.4 0.0 collective-permute-done
  64.4 3.1 %maximum_select_fusion = bf16[2,640,3,256]{3,1,2,0:T(8,128)(2,1)} fusion(bf16[1,640,3,256]{3,1,2,0:T(8,128)(2,1)} %bitcast.22, bf16[1,640,3,256]{3,1,2,0:T(8,128)(2,1)S(1)} %bitcast.74, pred[]{:T(512)S(6)} %eq.13), kind=kLoop, calls=%fused_computation.8 | loop fusion | flops 2949120 | bytes 3932161 | tf_op jit(solution)/shard_map/jit(_where)/select_n | solution.py:59
  67.6 0.0 all-gather.2.cloned.1.call-update
  67.7 0.8 dynamic_slice.6
  68.4 0.8 dynamic_slice.7
  69.2 0.0 copy-done.2
  69.2 0.7 fusion.10
  69.8 0.0 copy-done.3
  69.8 1.9 %fusion.8 = (s32[16]{0:T(128)S(1)}, s32[16]{0:T(128)S(1)}) fusion(s32[16,2]{0,1:T(2,128)S(1)} %copy-done.3, s32[]{:T(128)} %bitcast.31, s32[]{:T(128)} %bitcast.33, s32[]{:T(128)} %bitcast.32), kind=kLoop, calls=%fused_computation.38 | loop fusion | flops 320 | bytes 268 | tf_op jit(solution)/shard_map/select_n | solution.py:80
  71.7 0.0 copy-done
  71.8 0.7 gather_fusion.1
  72.4 0.7 gather_fusion.2
  73.1 0.0 copy-done.4
  73.1 0.0 copy-done.1
  73.1 0.7 gather_fusion.3
  73.8 0.3 collective-permute-start.1
  74.1 2.5 %collective-permute-start.2 = (bf16[1280,3,128]{2,0,1:T(8,128)(2,1)S(1)}, bf16[1280,3,128]{2,0,1:T(8,128)(2,1)S(1)}, u32[]{:S(2)}, u32[]{:S(2)}) collective-permute-start(bf16[1280,3,128]{2,0,1:T(8,128)(2,1)S(1)} %bitcast.68), channel_id=1, source_target_pairs={{0,48},{16,0},{32,16},{48,32},{1,49},{17,1},{33,17},{49,33},{2,50}... | collective-permute-start | bytes 2949128 | tf_op jit(solution)/shard_map/ppermute | solution.py:24
  76.5 0.0 collective-permute-start.5
  76.6 0.1 broadcast_add_fusion
  76.7 5.8 %broadcast_in_dim.53 = bf16[2,4,1280,3,128]{4,2,3,1,0:T(8,128)(2,1)} broadcast(bf16[]{:T(256)} %constant.79.clone.1), dimensions={} | broadcast | bytes 7864322 | tf_op jit(solution)/shard_map/broadcast_in_dim | solution.py:64
  82.5 1.0 bitcast_dynamic-update-slice_fusion.5
  83.5 14.9 %collective-permute-done.1 = bf16[1280,3,128]{2,0,1:T(8,128)(2,1)S(1)} collective-permute-done((bf16[1280,3,128]{2,0,1:T(8,128)(2,1)S(1)}, bf16[1280,3,128]{2,0,1:T(8,128)(2,1)S(1)}, u32[]{:S(2)}, u32[]{:S(2)}) %collective-permute-start.1) | collective-permute-done | bytes 983072 | tf_op jit(solution)/shard_map/ppermute | solution.py:23
  98.5 0.1 collective-permute-start.3
  98.6 0.0 collective-permute-done.2
  98.6 2.7 %collective-permute-start.4 = (bf16[640,3,128]{2,0,1:T(8,128)(2,1)S(1)}, bf16[640,3,128]{2,0,1:T(8,128)(2,1)S(1)}, u32[]{:S(2)}, u32[]{:S(2)}) collective-permute-start(bf16[640,3,128]{2,0,1:T(8,128)(2,1)S(1)} %slice.41), channel_id=1, source_target_pairs={{0,48},{16,0},{32,16},{48,32},{1,49},{17,1},{33,17},{49,33},{2,50}... | collective-permute-start | bytes 1474568 | tf_op jit(solution)/shard_map/ppermute | solution.py:30
  101.3 0.0 collective-permute-done.5
  101.3 0.0 collective-permute-start.6
  101.3 2.7 %collective-permute-start.7 = (bf16[1280,3,128]{2,0,1:T(8,128)(2,1)S(1)}, bf16[1280,3,128]{2,0,1:T(8,128)(2,1)S(1)}, u32[]{:S(2)}, u32[]{:S(2)}) collective-permute-start(bf16[1280,3,128]{2,0,1:T(8,128)(2,1)S(1)} %collective-permute-done.5), channel_id=1, source_target_pairs={{0,48},{16,0},{32,16},{48,32},{1,49},{17,1},{33,17},{49,33},{2,50}... | collective-permute-start | bytes 2949128 | tf_op jit(solution)/shard_map/ppermute | solution.py:24
  104.0 1.0 bitcast_dynamic-update-slice_fusion.4
  105.1 1.0 bitcast_dynamic-update-slice_fusion.3
  106.1 5.8 %collective-permute-done.3 = bf16[640,3,128]{2,0,1:T(8,128)(2,1)S(1)} collective-permute-done((bf16[640,3,128]{2,0,1:T(8,128)(2,1)S(1)}, bf16[640,3,128]{2,0,1:T(8,128)(2,1)S(1)}, u32[]{:S(2)}, u32[]{:S(2)}) %collective-permute-start.3) | collective-permute-done | bytes 491552 | tf_op jit(solution)/shard_map/ppermute | solution.py:29
  111.8 0.9 bitcast_dynamic-update-slice_fusion.9
  112.7 0.0 collective-permute-done.4
  112.7 0.9 bitcast_dynamic-update-slice_fusion.8
  113.6 1.0 bitcast_dynamic-update-slice_fusion.2
  114.6 18.3 %collective-permute-done.6 = bf16[1280,3,128]{2,0,1:T(8,128)(2,1)S(1)} collective-permute-done((bf16[1280,3,128]{2,0,1:T(8,128)(2,1)S(1)}, bf16[1280,3,128]{2,0,1:T(8,128)(2,1)S(1)}, u32[]{:S(2)}, u32[]{:S(2)}) %collective-permute-start.6) | collective-permute-done | bytes 983072 | tf_op jit(solution)/shard_map/ppermute | solution.py:23
  132.9 0.1 collective-permute-start.8
  133.0 0.0 collective-permute-done.7
  133.1 2.7 %collective-permute-start.9 = (bf16[640,3,128]{2,0,1:T(8,128)(2,1)S(1)}, bf16[640,3,128]{2,0,1:T(8,128)(2,1)S(1)}, u32[]{:S(2)}, u32[]{:S(2)}) collective-permute-start(bf16[640,3,128]{2,0,1:T(8,128)(2,1)S(1)} %slice.43), channel_id=1, source_target_pairs={{0,48},{16,0},{32,16},{48,32},{1,49},{17,1},{33,17},{49,33},{2,50}... | collective-permute-start | bytes 1474568 | tf_op jit(solution)/shard_map/ppermute | solution.py:30
  135.8 1.0 bitcast_dynamic-update-slice_fusion.1
  136.8 1.0 bitcast_dynamic-update-slice_fusion
  137.8 7.7 %collective-permute-done.8 = bf16[640,3,128]{2,0,1:T(8,128)(2,1)S(1)} collective-permute-done((bf16[640,3,128]{2,0,1:T(8,128)(2,1)S(1)}, bf16[640,3,128]{2,0,1:T(8,128)(2,1)S(1)}, u32[]{:S(2)}, u32[]{:S(2)}) %collective-permute-start.8) | collective-permute-done | bytes 491552 | tf_op jit(solution)/shard_map/ppermute | solution.py:29
  145.6 0.9 bitcast_dynamic-update-slice_fusion.7
  146.4 0.0 collective-permute-done.9
  146.4 0.9 bitcast_dynamic-update-slice_fusion.6
  147.3 0.6 all-gather.2.cloned.1.call-done
  148.0 11.8 %fusion.3 = f32[3,3,256,128]{2,3,0,1:T(8,128)S(1)} fusion(bf16[4,2,2,2,4,80,3,256,1]{7,5,4,3,6,2,1,0,8:T(8,128)(2,1)} %bitcast.76, bf16[2,4,4,2,2,80,3,128,1]{7,5,4,3,2,6,1,0,8:T(8,128)(2,1)} %bitcast.19), kind=kOutput, calls=%fused_computation.9 | convolution fusion | flops 6039797760 | bytes 24772608 | tf_op jit(solution)/shard_map/xchzypia,zyxhcpjb->ijab/dot_general | solution.py:69
  159.7 0.4 copy.23
  160.1 0.7 gather_fusion
  160.8 1.9 %add_divide_fusion = f32[16,256,128]{2,1,0:T(8,128)} fusion(f32[16,256,128]{2,1,0:T(8,128)S(1)} %gather_fusion, f32[16]{0:T(128)S(1)} %gather_fusion.3, f32[16]{0:T(128)S(1)} %gather_fusion.2, f32[16]{0:T(128)S(1)} %gather_fusion.1, f32[256,128]{1,0:T(8,128)S(1)} %broadcast_add_fusion, pred[16]{0:T(512)(128)(4,1)S(1)} %get-tuple-element.9), kind=kLoop, calls=%fused_computation.7 | loop fusion | flops 3145728 | bytes 4325584 | tf_op jit(solution)/shard_map/div | solution.py:89
  (9 shorter events, 0.2 us)
Async XLA Ops:
  6.5 65.2 %copy-start = (f32[300]{0:T(512)S(1)}, f32[300]{0:T(512)}, u32[]{:S(2)}) copy-start(f32[300]{0:T(512)} %param.8) | copy-start | bytes 3604
  7.8 61.4 %copy-start.2 = (s32[3]{0:T(128)S(1)}, s32[3]{0:T(128)}, u32[]{:S(2)}) copy-start(s32[3]{0:T(128)} %param.10) | copy-start | bytes 40
  7.8 62.0 %copy-start.3 = (s32[16,2]{0,1:T(2,128)S(1)}, s32[16,2]{0,1:T(2,128)}, u32[]{:S(2)}) copy-start(s32[16,2]{0,1:T(2,128)} %param.11) | copy-start | bytes 388
  28.3 44.8 %copy-start.4 = (s32[16]{0:T(128)S(1)}, s32[16]{0:T(128)}, u32[]{:S(2)}) copy-start(s32[16]{0:T(128)} %param.12) | copy-start | bytes 196
  28.3 44.8 %copy-start.1 = (f32[4]{0:T(128)S(1)}, f32[4]{0:T(128)}, u32[]{:S(2)}) copy-start(f32[4]{0:T(128)} %param.13) | copy-start | bytes 52
  28.4 36.0 %collective-permute-start = (bf16[640,3,256]{2,0,1:T(8,128)(2,1)S(1)}, bf16[640,3,256]{2,0,1:T(8,128)(2,1)}, u32[]{:S(2)}, u32[]{:S(2)}) collective-permute-start(bf16[640,3,256]{2,0,1:T(8,128)(2,1)S(1)} %bitcast.73), channel_id=1, source_target_pairs={{0,2},{2,0},{1,3},{3,1},{4,6},{6,4},{5,7},{7,5},{8,10},{10,8},{9,1... | collective-permute-start | bytes 2949128 | tf_op jit(solution)/shard_map/ppermute | solution.py:53
  34.1 30.2 %all-to-all-start.1 = ((bf16[80,3,16,128]{3,0,1,2:T(8,128)(2,1)}), bf16[80,3,16,128]{3,0,1,2:T(8,128)(2,1)S(1)}, u32[]{:S(2)}, u32[]{:S(2)}) async-start(bf16[80,3,16,128]{3,0,1,2:T(8,128)(2,1)} %copy_bitcast_fusion), calls=%async_computation.1 | async-start | bytes 1966080 | tf_op jit(solution)/shard_map/all_to_all | solution.py:54
  40.3 107.6 %all-gather.2.cloned.1.call-start = ((), (), s32[]{:S(2)}) async-start(), calls=%async_computation.2 | async-start | bytes 17694720 | tf_op jit(solution)/shard_map/all_gather | solution.py:60
  73.8 24.6 %collective-permute-start.1 = (bf16[1280,3,128]{2,0,1:T(8,128)(2,1)S(1)}, bf16[1280,3,128]{2,0,1:T(8,128)(2,1)S(1)}, u32[]{:S(2)}, u32[]{:S(2)}) collective-permute-start(bf16[1280,3,128]{2,0,1:T(8,128)(2,1)S(1)} %bitcast.67), channel_id=1, source_target_pairs={{0,16},{16,32},{32,48},{48,0},{1,17},{17,33},{33,49},{49,1},{2,18}... | collective-permute-start | bytes 2949128 | tf_op jit(solution)/shard_map/ppermute | solution.py:23
  74.1 24.5 %collective-permute-start.2 = (bf16[1280,3,128]{2,0,1:T(8,128)(2,1)S(1)}, bf16[1280,3,128]{2,0,1:T(8,128)(2,1)S(1)}, u32[]{:S(2)}, u32[]{:S(2)}) collective-permute-start(bf16[1280,3,128]{2,0,1:T(8,128)(2,1)S(1)} %bitcast.68), channel_id=1, source_target_pairs={{0,48},{16,0},{32,16},{48,32},{1,49},{17,1},{33,17},{49,33},{2,50}... | collective-permute-start | bytes 2949128 | tf_op jit(solution)/shard_map/ppermute | solution.py:24
  76.5 24.8 %collective-permute-start.5 = (bf16[1280,3,128]{2,0,1:T(8,128)(2,1)S(1)}, bf16[1280,3,128]{2,0,1:T(8,128)(2,1)S(1)}, u32[]{:S(2)}, u32[]{:S(2)}) collective-permute-start(bf16[1280,3,128]{2,0,1:T(8,128)(2,1)S(1)} %bitcast.69), channel_id=1, source_target_pairs={{0,64},{64,0},{1,65},{65,1},{2,66},{66,2},{3,67},{67,3},{4,68},{68... | collective-permute-start | bytes 2949128 | tf_op jit(solution)/shard_map/ppermute | solution.py:62
  98.5 13.4 %collective-permute-start.3 = (bf16[640,3,128]{2,0,1:T(8,128)(2,1)S(1)}, bf16[640,3,128]{2,0,1:T(8,128)(2,1)S(1)}, u32[]{:S(2)}, u32[]{:S(2)}) collective-permute-start(bf16[640,3,128]{2,0,1:T(8,128)(2,1)S(1)} %slice.40), channel_id=1, source_target_pairs={{0,16},{16,32},{32,48},{48,0},{1,17},{17,33},{33,49},{49,1},{2,18}... | collective-permute-start | bytes 1474568 | tf_op jit(solution)/shard_map/ppermute | solution.py:29
  98.6 14.1 %collective-permute-start.4 = (bf16[640,3,128]{2,0,1:T(8,128)(2,1)S(1)}, bf16[640,3,128]{2,0,1:T(8,128)(2,1)S(1)}, u32[]{:S(2)}, u32[]{:S(2)}) collective-permute-start(bf16[640,3,128]{2,0,1:T(8,128)(2,1)S(1)} %slice.41), channel_id=1, source_target_pairs={{0,48},{16,0},{32,16},{48,32},{1,49},{17,1},{33,17},{49,33},{2,50}... | collective-permute-start | bytes 1474568 | tf_op jit(solution)/shard_map/ppermute | solution.py:30
  101.3 31.6 %collective-permute-start.6 = (bf16[1280,3,128]{2,0,1:T(8,128)(2,1)S(1)}, bf16[1280,3,128]{2,0,1:T(8,128)(2,1)S(1)}, u32[]{:S(2)}, u32[]{:S(2)}) collective-permute-start(bf16[1280,3,128]{2,0,1:T(8,128)(2,1)S(1)} %collective-permute-done.5), channel_id=1, source_target_pairs={{0,16},{16,32},{32,48},{48,0},{1,17},{17,33},{33,49},{49,1},{2,18}... | collective-permute-start | bytes 2949128 | tf_op jit(solution)/shard_map/ppermute | solution.py:23
  101.3 31.7 %collective-permute-start.7 = (bf16[1280,3,128]{2,0,1:T(8,128)(2,1)S(1)}, bf16[1280,3,128]{2,0,1:T(8,128)(2,1)S(1)}, u32[]{:S(2)}, u32[]{:S(2)}) collective-permute-start(bf16[1280,3,128]{2,0,1:T(8,128)(2,1)S(1)} %collective-permute-done.5), channel_id=1, source_target_pairs={{0,48},{16,0},{32,16},{48,32},{1,49},{17,1},{33,17},{49,33},{2,50}... | collective-permute-start | bytes 2949128 | tf_op jit(solution)/shard_map/ppermute | solution.py:24
  132.9 12.6 %collective-permute-start.8 = (bf16[640,3,128]{2,0,1:T(8,128)(2,1)S(1)}, bf16[640,3,128]{2,0,1:T(8,128)(2,1)S(1)}, u32[]{:S(2)}, u32[]{:S(2)}) collective-permute-start(bf16[640,3,128]{2,0,1:T(8,128)(2,1)S(1)} %slice.42), channel_id=1, source_target_pairs={{0,16},{16,32},{32,48},{48,0},{1,17},{17,33},{33,49},{49,1},{2,18}... | collective-permute-start | bytes 1474568 | tf_op jit(solution)/shard_map/ppermute | solution.py:29
  133.1 13.4 %collective-permute-start.9 = (bf16[640,3,128]{2,0,1:T(8,128)(2,1)S(1)}, bf16[640,3,128]{2,0,1:T(8,128)(2,1)S(1)}, u32[]{:S(2)}, u32[]{:S(2)}) collective-permute-start(bf16[640,3,128]{2,0,1:T(8,128)(2,1)S(1)} %slice.43), channel_id=1, source_target_pairs={{0,48},{16,0},{32,16},{48,32},{1,49},{17,1},{33,17},{49,33},{2,50}... | collective-permute-start | bytes 1474568 | tf_op jit(solution)/shard_map/ppermute | solution.py:30
Sparse Core Ops, SparseCore 0:
  67.7 80.2 all-gather.1

commit v7 on v6

--- a/solution.py
+++ b/solution.py
@@ -33,6 +33,14 @@
     return out
 
 
+def permute_exchange(blocks, axes, me, n):
+    pieces = [lax.dynamic_index_in_dim(blocks, me, 2, keepdims=False)]
+    for shift in range(1, n):
+        send = lax.dynamic_index_in_dim(blocks, (me + shift) % n, 2, keepdims=False)
+        pieces.append(lax.ppermute(send, axes, [(k, (k + shift) % n) for k in range(n)]))
+    return jnp.take(jnp.stack(pieces), (me - jnp.arange(n)) % n, axis=0)
+
+
 def shards(factors, occ_energy, vir_energy, slab_orbitals, pair_list, pair_state, state_shift):
     n_zl = lax.axis_size("zl")
     n_y = lax.axis_size("y")
@@ -51,9 +59,7 @@
     )
     spread_a = spread_a.reshape(n_row * local_aux, nocc, rows_a)
     other_a = lax.ppermute(spread_a, "zh", [(k, (k + 1) % n_zh) for k in range(n_zh)])
-    spread_b = lax.all_to_all(
-        factors.reshape(local_aux, nocc, n_col, cols_b), ("x", "zh", "core"), split_axis=2, concat_axis=0, tiled=True
-    )
+    spread_b = permute_exchange(factors.reshape(local_aux, nocc, n_col, cols_b), ("x", "zh", "core"), col_index, n_col)
     other_a, spread_b = lax.optimization_barrier((other_a, spread_b))
     first_zh = lax.axis_index("zh") == 0
     pair_a = jnp.where(first_zh, jnp.stack([spread_a, other_a]), jnp.stack([other_a, spread_a]))

time: 170 us -> 187 us (1.10)
  starting transfers between devices: 20.7 us -> 51.7 us
  blocking collectives: 20.5 us -> 0 us
  local copies, waits for them, and re-layouts: 24.6 us -> 32.8 us
  waiting for transfers between devices: 71.3 us -> 68.6 us
    ppermute x0 -> x15, starting transfers between devices: none -> 34.1 us  [permute_exchange(): lax.ppermute(send, axes, [(k, (k + shift) % n) for k in range(n)])]
    all_to_all x1, waiting for transfers between devices: 24 us -> 0.01 us  [shards(): lax.all_to_all(factors.reshape(local_aux, nocc, n_row, rows_a), ('zl', 'y...]
    all_to_all x1 -> x0, blocking collectives: 20.5 us -> none  [shards(): lax.all_to_all(factors.reshape(local_aux, nocc, n_row, rows_a), ('zl', 'y...]
    ppermute x1, waiting for transfers between devices: 0.01 us -> 18.6 us  [shards(): lax.ppermute(spread_a, 'zh', [(k, (k + 1) % n_zh) for k in range(n_zh)])]
    all_gather x1, waiting for transfers between devices: 0.61 us -> 7.89 us  [shards(): block_a = lax.all_gather(pair_a, ('x', 'core'), axis=0, tiled=True)]
    unnamed x10 -> x43, local copies, waits for them, and re-layouts: 0.02 us -> 6.86 us
    ppermute x2, waiting for transfers between devices: 33.2 us -> 26.7 us  [ring_into(): go_right = lax.ppermute(go_right, axis, right)]
    ppermute x0 -> x15, waiting for transfers between devices: none -> 4.61 us  [permute_exchange(): lax.ppermute(send, axes, [(k, (k + shift) % n) for k in range(n)])]
  transfers between devices with their start and end apart: 12 -> 27, of which waited for: 6 -> 8; matrix products, arithmetic and copies ran while one was open for 14% -> 16% of each run, Pallas kernels for 0% -> 0%
where the time goes in v7:
time: 187 us; the launch traced here: 186 us
  waiting for transfers between devices  68.6 us (37%)
  starting transfers between devices  51.7 us (28%)
  local copies, waits for them, and re-layouts  32.8 us (18%)
  between operations  14 us (7%)
  matrix products  11.8 us (6%)
  other arithmetic  7.25 us (4%)
    ppermute x15, starting transfers between devices, permute_exchange(): lax.ppermute(send, axes, [(k, (k + shift) % n) for k in range(n)])  34.1 us
    ppermute x2, waiting for transfers between devices, ring_into(): go_right = lax.ppermute(go_right, axis, right)  26.7 us
    ppermute x1, waiting for transfers between devices, shards(): lax.ppermute(spread_a, 'zh', [(k, (k + 1) % n_zh) for k in range(n_zh)])  18.6 us
    dot_general x1, matrix products, shards(): jnp.einsum('xchzypia,zyxhcpjb->ijab', block_a, block_b, preferred_element...  11.8 us
    dynamic_update_slice x10, local copies, waits for them, and re-layouts, put(): return lax.dynamic_update_slice(buf, piece[None, None], start)  10.9 us
    ppermute x2, waiting for transfers between devices, ring_into(): from_left = lax.ppermute(go_right[:half], axis, right)  10.8 us
    all_gather x1, waiting for transfers between devices, shards(): block_a = lax.all_gather(pair_a, ('x', 'core'), axis=0, tiled=True)  7.89 us
    unnamed x43, local copies, waits for them, and re-layouts  6.86 us
  transfers between devices with their start and end apart: 27, of which 8 were waited for; matrix products, arithmetic and copies ran while one was open for 16% of the time, Pallas kernels for 0%

profile of v7, /device:TPU:1, one launch (start us, length us, event | category | flops | bytes accessed | tf_op | source)
XLA Modules:
  0.0 186.1 jit_solution(6458583925979104794)
XLA Ops:
  6.5 1.5 copy.51
  8.1 2.3 %constant_dynamic-slice_fusion = (bf16[80,3,1,128]{3,2,0,1:T(2,128)(2,1)S(1)}, bf16[80,3,1,128]{3,2,0,1:T(2,128)(2,1)S(1)}, bf16[80,3,1,128]{3,2,0,1:T(2,128)(2,...) fusion(bf16[80,3,16,128]{3,2,0,1:T(8,128)(2,1)S(1)} %bitcast.14, ...), kind=kLoop, calls=%fused_computation.55 | loop fusion | bytes 1966144 | tf_op jit(solution)/shard_map/jit(dynamic_index_in_dim)/dynamic_slice | solution.py:39
  10.4 0.6 copy.92
  11.0 5.0 %collective-permute-start.1 = (bf16[80,3,128]{2,0,1:T(8,128)(2,1)}, bf16[80,3,128]{2,0,1:T(8,128)(2,1)}, u32[]{:S(2)}, u32[]{:S(2)}) collective-permute-start(bf16[80,3,128]{2,0,1:T(8,128)(2,1)} %bitcast.139), channel_id=1, source_target_pairs={{0,1},{1,2},{2,3},{3,4},{4,5},{5,6},{6,7},{7,8},{8,9},{9,10},{10,1... | collective-permute-start | bytes 184328 | tf_op jit(solution)/shard_map/ppermute | solution.py:40
  16.0 0.6 copy.91
  16.7 0.3 collective-permute-start.2
  17.0 0.6 copy.90
  17.6 1.2 collective-permute-start.3
  18.8 0.6 copy.89
  19.4 1.2 collective-permute-start.4
  20.7 3.7 %collective-permute-start.5 = (bf16[80,3,128]{2,0,1:T(8,128)(2,1)S(1)}, bf16[80,3,128]{2,0,1:T(8,128)(2,1)S(1)}, u32[]{:S(2)}, u32[]{:S(2)}) collective-permute-start(bf16[80,3,128]{2,0,1:T(8,128)(2,1)S(1)} %bitcast.159), channel_id=1, source_target_pairs={{0,5},{1,6},{2,7},{3,8},{4,9},{5,10},{6,11},{7,12},{8,13},{9,14},{... | collective-permute-start | bytes 184328 | tf_op jit(solution)/shard_map/ppermute | solution.py:40
  24.3 1.0 copy.77
  25.3 4.8 %all-to-all-start = ((bf16[80,3,8,256]{3,0,1,2:T(8,128)(2,1)}), bf16[80,3,8,256]{3,0,1,2:T(8,128)(2,1)S(1)}, u32[]{:S(2)}, u32[]{:S(2)}) async-start(bf16[80,3,8,256]{3,0,1,2:T(8,128)(2,1)} %bitcast.124), calls=%async_computation | async-start | bytes 1966080 | tf_op jit(solution)/shard_map/all_to_all | solution.py:57
  30.5 4.3 %collective-permute-start.6 = (bf16[80,3,128]{2,0,1:T(8,128)(2,1)S(1)}, bf16[80,3,128]{2,0,1:T(8,128)(2,1)S(1)}, u32[]{:S(2)}, u32[]{:S(2)}) collective-permute-start(bf16[80,3,128]{2,0,1:T(8,128)(2,1)S(1)} %bitcast.160), channel_id=1, source_target_pairs={{0,6},{1,7},{2,8},{3,9},{4,10},{5,11},{6,12},{7,13},{8,14},{9,15},... | collective-permute-start | bytes 184328 | tf_op jit(solution)/shard_map/ppermute | solution.py:40
  34.8 0.8 bitcast_dynamic-update-slice_fusion.24
  35.8 0.8 bitcast_dynamic-update-slice_fusion.23
  36.6 2.5 %collective-permute-start.8 = (bf16[80,3,128]{2,0,1:T(8,128)(2,1)S(1)}, bf16[80,3,128]{2,0,1:T(8,128)(2,1)S(1)}, u32[]{:S(2)}, u32[]{:S(2)}) collective-permute-start(bf16[80,3,128]{2,0,1:T(8,128)(2,1)S(1)} %bitcast.157), channel_id=1, source_target_pairs={{0,8},{1,9},{2,10},{3,11},{4,12},{5,13},{6,14},{7,15},{8,0},{9,1},... | collective-permute-start | bytes 184328 | tf_op jit(solution)/shard_map/ppermute | solution.py:40
  39.1 0.8 bitcast_dynamic-update-slice_fusion.22
  40.0 6.0 %collective-permute-start.9 = (bf16[80,3,128]{2,0,1:T(8,128)(2,1)S(1)}, bf16[80,3,128]{2,0,1:T(8,128)(2,1)S(1)}, u32[]{:S(2)}, u32[]{:S(2)}) collective-permute-start(bf16[80,3,128]{2,0,1:T(8,128)(2,1)S(1)} %bitcast.156), channel_id=1, source_target_pairs={{0,9},{1,10},{2,11},{3,12},{4,13},{5,14},{6,15},{7,0},{8,1},{9,2},... | collective-permute-start | bytes 184328 | tf_op jit(solution)/shard_map/ppermute | solution.py:40
  46.0 0.6 collective-permute-start.10
  46.6 0.4 collective-permute-start.11
  47.0 0.6 collective-permute-start.12
  47.7 3.9 %collective-permute-start.13 = (bf16[80,3,128]{2,0,1:T(8,128)(2,1)S(1)}, bf16[80,3,128]{2,0,1:T(8,128)(2,1)S(1)}, u32[]{:S(2)}, u32[]{:S(2)}) collective-permute-start(bf16[80,3,128]{2,0,1:T(8,128)(2,1)S(1)} %bitcast.152), channel_id=1, source_target_pairs={{0,13},{1,14},{2,15},{3,0},{4,1},{5,2},{6,3},{7,4},{8,5},{9,6},{10... | collective-permute-start | bytes 184328 | tf_op jit(solution)/shard_map/ppermute | solution.py:40
  51.6 4.3 %collective-permute-start.14 = (bf16[80,3,128]{2,0,1:T(8,128)(2,1)S(1)}, bf16[80,3,128]{2,0,1:T(8,128)(2,1)S(1)}, u32[]{:S(2)}, u32[]{:S(2)}) collective-permute-start(bf16[80,3,128]{2,0,1:T(8,128)(2,1)S(1)} %bitcast.151), channel_id=1, source_target_pairs={{0,14},{1,15},{2,0},{3,1},{4,2},{5,3},{6,4},{7,5},{8,6},{9,7},{10,... | collective-permute-start | bytes 184328 | tf_op jit(solution)/shard_map/ppermute | solution.py:40
  56.2 1.0 collective-permute-start
  57.2 2.1 %collective-permute-done.14 = bf16[80,3,128]{2,0,1:T(8,128)(2,1)S(1)} collective-permute-done((bf16[80,3,128]{2,0,1:T(8,128)(2,1)S(1)}, bf16[80,3,128]{2,0,1:T(8,128)(2,1)S(1)}, u32[]{:S(2)}, u32[]{:S(2)}) %collective-permute-start.14) | collective-permute-done | bytes 61472 | tf_op jit(solution)/shard_map/ppermute | solution.py:40
  59.3 2.5 %collective-permute-done.15 = bf16[80,3,128]{2,0,1:T(8,128)(2,1)S(1)} collective-permute-done((bf16[80,3,128]{2,0,1:T(8,128)(2,1)S(1)}, bf16[80,3,128]{2,0,1:T(8,128)(2,1)S(1)}, u32[]{:S(2)}, u32[]{:S(2)}) %collective-permute-start.15) | collective-permute-done | bytes 61472 | tf_op jit(solution)/shard_map/ppermute | solution.py:40
  61.8 0.7 gather_fusion
  62.7 18.6 %collective-permute-done = bf16[640,3,256]{2,0,1:T(8,128)(2,1)} collective-permute-done((bf16[640,3,256]{2,0,1:T(8,128)(2,1)S(1)}, bf16[640,3,256]{2,0,1:T(8,128)(2,1)}, u32[]{:S(2)}, u32[]{:S(2)}) %collective-permute-start) | collective-permute-done | bytes 983072 | tf_op jit(solution)/shard_map/ppermute | solution.py:61
  81.3 3.2 %maximum_select_fusion = bf16[2,640,3,256]{3,1,2,0:T(8,128)(2,1)} fusion(bf16[1,640,3,256]{3,1,2,0:T(8,128)(2,1)} %bitcast.35, bf16[1,640,3,256]{3,1,2,0:T(8,128)(2,1)S(1)} %bitcast.149, pred[]{:T(512)S(6)} %eq.30), kind=kLoop, calls=%fused_computation.9 | loop fusion | flops 2949120 | bytes 3932161 | tf_op jit(solution)/shard_map/jit(_where)/select_n | solution.py:65
  84.5 0.6 fusion.13
  85.1 1.8 fusion.11
  87.0 1.5 collective-permute-start.16
  88.5 1.3 collective-permute-start.17
  89.8 0.7 collective-permute-start.20
  90.5 0.8 dynamic_slice.72
  91.3 0.8 dynamic_slice.71
  92.0 0.7 gather_fusion.2
  92.7 0.7 gather_fusion.3
  93.4 0.7 gather_fusion.4
  94.2 5.5 %broadcast_in_dim.63 = bf16[2,4,1280,3,128]{4,2,3,1,0:T(8,128)(2,1)} broadcast(bf16[]{:T(256)} %constant.211.clone.1), dimensions={} | broadcast | bytes 7864322 | tf_op jit(solution)/shard_map/broadcast_in_dim | solution.py:70
  99.7 1.0 constant_dynamic-update-slice_fusion
  100.7 9.6 %collective-permute-done.16 = bf16[1280,3,128]{2,0,1:T(8,128)(2,1)S(1)} collective-permute-done((bf16[1280,3,128]{2,0,1:T(8,128)(2,1)S(1)}, bf16[1280,3,128]{2,0,1:T(8,128)(2,1)S(1)}, u32[]{:S(2)}, u32[]{:S(2)}) %collective-permute-start.16) | collective-permute-done | bytes 983072 | tf_op jit(solution)/shard_map/ppermute | solution.py:23
  110.4 0.3 collective-permute-start.18
  110.7 2.5 %collective-permute-start.19 = (bf16[640,3,128]{2,0,1:T(8,128)(2,1)S(1)}, bf16[640,3,128]{2,0,1:T(8,128)(2,1)S(1)}, u32[]{:S(2)}, u32[]{:S(2)}) collective-permute-start(bf16[640,3,128]{2,0,1:T(8,128)(2,1)S(1)} %slice.43), channel_id=1, source_target_pairs={{0,48},{16,0},{32,16},{48,32},{1,49},{17,1},{33,17},{49,33},{2,50}... | collective-permute-start | bytes 1474568 | tf_op jit(solution)/shard_map/ppermute | solution.py:30
  113.2 2.7 %collective-permute-start.22 = (bf16[1280,3,128]{2,0,1:T(8,128)(2,1)}, bf16[1280,3,128]{2,0,1:T(8,128)(2,1)S(1)}, u32[]{:S(2)}, u32[]{:S(2)}) collective-permute-start(bf16[1280,3,128]{2,0,1:T(8,128)(2,1)} %collective-permute-done.20), channel_id=1, source_target_pairs={{0,48},{16,0},{32,16},{48,32},{1,49},{17,1},{33,17},{49,33},{2,50}... | collective-permute-start | bytes 2949128 | tf_op jit(solution)/shard_map/ppermute | solution.py:24
  115.9 1.0 bitcast_dynamic-update-slice_fusion.4
  117.0 1.0 bitcast_dynamic-update-slice_fusion.3
  118.0 4.4 %collective-permute-done.18 = bf16[640,3,128]{2,0,1:T(8,128)(2,1)S(1)} collective-permute-done((bf16[640,3,128]{2,0,1:T(8,128)(2,1)S(1)}, bf16[640,3,128]{2,0,1:T(8,128)(2,1)S(1)}, u32[]{:S(2)}, u32[]{:S(2)}) %collective-permute-start.18) | collective-permute-done | bytes 491552 | tf_op jit(solution)/shard_map/ppermute | solution.py:29
  122.4 0.9 bitcast_dynamic-update-slice_fusion.8
  123.3 0.9 bitcast_dynamic-update-slice_fusion.7
  124.2 2.2 %bitcast_dynamic-update-slice_fusion.2 = bf16[2,4,1280,3,128]{4,2,3,1,0:T(8,128)(2,1)} fusion(bf16[2,4,1280,3,128]{4,2,3,1,0:T(8,128)(2,1)} %bitcast_dynamic-update-slice_fusion.7, s32[]{:T(128)S(6)} %select_n.308, s32[]{:T(128)S(6)} %select_n.300, bf16[1280,3,128]{2,0,1:T(8,128)(2,1)} %collective-permute-done.20), kind=kLoop, calls=%fused_computation.14 | loop fusion | bytes 1966088 | tf_op jit(solution)/shard_map/dynamic_update_slice | solution.py:16
  126.4 17.1 %collective-permute-done.21 = bf16[1280,3,128]{2,0,1:T(8,128)(2,1)S(1)} collective-permute-done((bf16[1280,3,128]{2,0,1:T(8,128)(2,1)}, bf16[1280,3,128]{2,0,1:T(8,128)(2,1)S(1)}, u32[]{:S(2)}, u32[]{:S(2)}) %collective-permute-start.21) | collective-permute-done | bytes 983072 | tf_op jit(solution)/shard_map/ppermute | solution.py:23
  143.6 2.7 %collective-permute-start.24 = (bf16[640,3,128]{2,0,1:T(8,128)(2,1)S(1)}, bf16[640,3,128]{2,0,1:T(8,128)(2,1)S(1)}, u32[]{:S(2)}, u32[]{:S(2)}) collective-permute-start(bf16[640,3,128]{2,0,1:T(8,128)(2,1)S(1)} %slice.45), channel_id=1, source_target_pairs={{0,48},{16,0},{32,16},{48,32},{1,49},{17,1},{33,17},{49,33},{2,50}... | collective-permute-start | bytes 1474568 | tf_op jit(solution)/shard_map/ppermute | solution.py:30
  146.4 1.0 bitcast_dynamic-update-slice_fusion.1
  147.4 1.0 bitcast_dynamic-update-slice_fusion
  148.4 6.4 %collective-permute-done.23 = bf16[640,3,128]{2,0,1:T(8,128)(2,1)S(1)} collective-permute-done((bf16[640,3,128]{2,0,1:T(8,128)(2,1)S(1)}, bf16[640,3,128]{2,0,1:T(8,128)(2,1)S(1)}, u32[]{:S(2)}, u32[]{:S(2)}) %collective-permute-start.23) | collective-permute-done | bytes 491552 | tf_op jit(solution)/shard_map/ppermute | solution.py:29
  154.8 0.9 bitcast_dynamic-update-slice_fusion.6
  155.7 0.9 bitcast_dynamic-update-slice_fusion.5
  156.6 7.9 %all-gather.2.cloned.1.call-done = bf16[16,640,3,256]{3,1,2,0:T(8,128)(2,1)} async-done(((bf16[2,640,3,256]{3,1,2,0:T(8,128)(2,1)}), bf16[16,640,3,256]{3,1,2,0:T(8,128)(2,1)}) %all-gather.2.cloned.1.call-update) | async-done | bytes 15728656 | tf_op jit(solution)/shard_map/all_gather | solution.py:66
  164.5 11.8 %fusion.3 = f32[3,3,256,128]{2,3,0,1:T(8,128)S(1)} fusion(bf16[4,2,2,2,4,80,3,256,1]{7,5,4,3,6,2,1,0,8:T(8,128)(2,1)} %bitcast.162, bf16[2,4,4,2,2,80,3,128,1]{7,5,4,3,2,6,1,0,8:T(8,128)(2,1)} %bitcast.32), kind=kOutput, calls=%fused_computation.10 | convolution fusion | flops 6039797760 | bytes 24772608 | tf_op jit(solution)/shard_map/xchzypia,zyxhcpjb->ijab/dot_general | solution.py:75
  176.2 0.4 copy.26
  176.6 0.7 gather_fusion.1
  177.3 1.9 %add_divide_fusion = f32[16,256,128]{2,1,0:T(8,128)} fusion(f32[16,256,128]{2,1,0:T(8,128)S(1)} %gather_fusion.1, f32[16]{0:T(128)S(1)} %gather_fusion.4, f32[16]{0:T(128)S(1)} %gather_fusion.3, f32[16]{0:T(128)S(1)} %gather_fusion.2, f32[256,128]{1,0:T(8,128)S(1)} %broadcast_add_fusion, pred[16]{0:T(512)(128)(4,1)S(1)} %get-tuple-element.9), kind=kLoop, calls=%fused_computation.8 | loop fusion | flops 3145728 | bytes 4325584 | tf_op jit(solution)/shard_map/div | solution.py:95
  (77 shorter events, 1.2 us)
Async XLA Ops:
  6.5 85.5 %copy-start = (f32[300]{0:T(512)S(1)}, f32[300]{0:T(512)}, u32[]{:S(2)}) copy-start(f32[300]{0:T(512)} %param.8) | copy-start | bytes 3604
  6.5 17.8 %copy-start.2 = (bf16[80,3,2048]{2,0,1:T(8,128)(2,1)S(1)}, bf16[80,3,2048]{2,0,1:T(8,128)(2,1)}, u32[]{:S(2)}) copy-start(bf16[80,3,2048]{2,0,1:T(8,128)(2,1)} %param.7) | copy-start | bytes 2949124
  11.0 19.5 %collective-permute-start.1 = (bf16[80,3,128]{2,0,1:T(8,128)(2,1)}, bf16[80,3,128]{2,0,1:T(8,128)(2,1)}, u32[]{:S(2)}, u32[]{:S(2)}) collective-permute-start(bf16[80,3,128]{2,0,1:T(8,128)(2,1)} %bitcast.139), channel_id=1, source_target_pairs={{0,1},{1,2},{2,3},{3,4},{4,5},{5,6},{6,7},{7,8},{8,9},{9,10},{10,1... | collective-permute-start | bytes 184328 | tf_op jit(solution)/shard_map/ppermute | solution.py:40
  16.7 19.0 %collective-permute-start.2 = (bf16[80,3,128]{2,0,1:T(8,128)(2,1)}, bf16[80,3,128]{2,0,1:T(8,128)(2,1)}, u32[]{:S(2)}, u32[]{:S(2)}) collective-permute-start(bf16[80,3,128]{2,0,1:T(8,128)(2,1)} %bitcast.138), channel_id=1, source_target_pairs={{0,2},{1,3},{2,4},{3,5},{4,6},{5,7},{6,8},{7,9},{8,10},{9,11},{10,... | collective-permute-start | bytes 184328 | tf_op jit(solution)/shard_map/ppermute | solution.py:40
  17.6 19.0 %collective-permute-start.3 = (bf16[80,3,128]{2,0,1:T(8,128)(2,1)}, bf16[80,3,128]{2,0,1:T(8,128)(2,1)}, u32[]{:S(2)}, u32[]{:S(2)}) collective-permute-start(bf16[80,3,128]{2,0,1:T(8,128)(2,1)} %bitcast.137), channel_id=1, source_target_pairs={{0,3},{1,4},{2,5},{3,6},{4,7},{5,8},{6,9},{7,10},{8,11},{9,12},{10... | collective-permute-start | bytes 184328 | tf_op jit(solution)/shard_map/ppermute | solution.py:40
  19.4 20.5 %collective-permute-start.4 = (bf16[80,3,128]{2,0,1:T(8,128)(2,1)}, bf16[80,3,128]{2,0,1:T(8,128)(2,1)S(1)}, u32[]{:S(2)}, u32[]{:S(2)}) collective-permute-start(bf16[80,3,128]{2,0,1:T(8,128)(2,1)} %bitcast.136), channel_id=1, source_target_pairs={{0,4},{1,5},{2,6},{3,7},{4,8},{5,9},{6,10},{7,11},{8,12},{9,13},{1... | collective-permute-start | bytes 184328 | tf_op jit(solution)/shard_map/ppermute | solution.py:40
  20.7 25.3 %collective-permute-start.5 = (bf16[80,3,128]{2,0,1:T(8,128)(2,1)S(1)}, bf16[80,3,128]{2,0,1:T(8,128)(2,1)S(1)}, u32[]{:S(2)}, u32[]{:S(2)}) collective-permute-start(bf16[80,3,128]{2,0,1:T(8,128)(2,1)S(1)} %bitcast.159), channel_id=1, source_target_pairs={{0,5},{1,6},{2,7},{3,8},{4,9},{5,10},{6,11},{7,12},{8,13},{9,14},{... | collective-permute-start | bytes 184328 | tf_op jit(solution)/shard_map/ppermute | solution.py:40
  25.3 30.7 %all-to-all-start = ((bf16[80,3,8,256]{3,0,1,2:T(8,128)(2,1)}), bf16[80,3,8,256]{3,0,1,2:T(8,128)(2,1)S(1)}, u32[]{:S(2)}, u32[]{:S(2)}) async-start(bf16[80,3,8,256]{3,0,1,2:T(8,128)(2,1)} %bitcast.124), calls=%async_computation | async-start | bytes 1966080 | tf_op jit(solution)/shard_map/all_to_all | solution.py:57
  30.2 134.3 %all-gather.2.cloned.1.call-start = ((), (), s32[]{:S(2)}) async-start(), calls=%async_computation.1 | async-start | bytes 17694720 | tf_op jit(solution)/shard_map/all_gather | solution.py:66
  30.3 54.2 %copy-start.3 = (s32[3]{0:T(128)S(1)}, s32[3]{0:T(128)}, u32[]{:S(2)}) copy-start(s32[3]{0:T(128)} %param.10) | copy-start | bytes 40
  30.3 54.8 %copy-start.5 = (s32[16]{0:T(128)S(1)}, s32[16]{0:T(128)}, u32[]{:S(2)}) copy-start(s32[16]{0:T(128)} %param.12) | copy-start | bytes 196
  30.3 54.8 %copy-start.4 = (s32[16,2]{0,1:T(2,128)S(1)}, s32[16,2]{0,1:T(2,128)}, u32[]{:S(2)}) copy-start(s32[16,2]{0,1:T(2,128)} %param.11) | copy-start | bytes 388
  30.5 16.1 %collective-permute-start.6 = (bf16[80,3,128]{2,0,1:T(8,128)(2,1)S(1)}, bf16[80,3,128]{2,0,1:T(8,128)(2,1)S(1)}, u32[]{:S(2)}, u32[]{:S(2)}) collective-permute-start(bf16[80,3,128]{2,0,1:T(8,128)(2,1)S(1)} %bitcast.160), channel_id=1, source_target_pairs={{0,6},{1,7},{2,8},{3,9},{4,10},{5,11},{6,12},{7,13},{8,14},{9,15},... | collective-permute-start | bytes 184328 | tf_op jit(solution)/shard_map/ppermute | solution.py:40
  35.7 11.4 %collective-permute-start.7 = (bf16[80,3,128]{2,0,1:T(8,128)(2,1)S(1)}, bf16[80,3,128]{2,0,1:T(8,128)(2,1)S(1)}, u32[]{:S(2)}, u32[]{:S(2)}) collective-permute-start(bf16[80,3,128]{2,0,1:T(8,128)(2,1)S(1)} %bitcast.158), channel_id=1, source_target_pairs={{0,7},{1,8},{2,9},{3,10},{4,11},{5,12},{6,13},{7,14},{8,15},{9,0},... | collective-permute-start | bytes 184328 | tf_op jit(solution)/shard_map/ppermute | solution.py:40
  36.6 11.1 %collective-permute-start.8 = (bf16[80,3,128]{2,0,1:T(8,128)(2,1)S(1)}, bf16[80,3,128]{2,0,1:T(8,128)(2,1)S(1)}, u32[]{:S(2)}, u32[]{:S(2)}) collective-permute-start(bf16[80,3,128]{2,0,1:T(8,128)(2,1)S(1)} %bitcast.157), channel_id=1, source_target_pairs={{0,8},{1,9},{2,10},{3,11},{4,12},{5,13},{6,14},{7,15},{8,0},{9,1},... | collective-permute-start | bytes 184328 | tf_op jit(solution)/shard_map/ppermute | solution.py:40
  40.0 11.6 %collective-permute-start.9 = (bf16[80,3,128]{2,0,1:T(8,128)(2,1)S(1)}, bf16[80,3,128]{2,0,1:T(8,128)(2,1)S(1)}, u32[]{:S(2)}, u32[]{:S(2)}) collective-permute-start(bf16[80,3,128]{2,0,1:T(8,128)(2,1)S(1)} %bitcast.156), channel_id=1, source_target_pairs={{0,9},{1,10},{2,11},{3,12},{4,13},{5,14},{6,15},{7,0},{8,1},{9,2},... | collective-permute-start | bytes 184328 | tf_op jit(solution)/shard_map/ppermute | solution.py:40
  46.0 9.9 %collective-permute-start.10 = (bf16[80,3,128]{2,0,1:T(8,128)(2,1)S(1)}, bf16[80,3,128]{2,0,1:T(8,128)(2,1)S(1)}, u32[]{:S(2)}, u32[]{:S(2)}) collective-permute-start(bf16[80,3,128]{2,0,1:T(8,128)(2,1)S(1)} %bitcast.155), channel_id=1, source_target_pairs={{0,10},{1,11},{2,12},{3,13},{4,14},{5,15},{6,0},{7,1},{8,2},{9,3},... | collective-permute-start | bytes 184328 | tf_op jit(solution)/shard_map/ppermute | solution.py:40
  46.6 9.4 %collective-permute-start.11 = (bf16[80,3,128]{2,0,1:T(8,128)(2,1)S(1)}, bf16[80,3,128]{2,0,1:T(8,128)(2,1)S(1)}, u32[]{:S(2)}, u32[]{:S(2)}) collective-permute-start(bf16[80,3,128]{2,0,1:T(8,128)(2,1)S(1)} %bitcast.154), channel_id=1, source_target_pairs={{0,11},{1,12},{2,13},{3,14},{4,15},{5,0},{6,1},{7,2},{8,3},{9,4},{... | collective-permute-start | bytes 184328 | tf_op jit(solution)/shard_map/ppermute | solution.py:40
  47.0 10.1 %collective-permute-start.12 = (bf16[80,3,128]{2,0,1:T(8,128)(2,1)S(1)}, bf16[80,3,128]{2,0,1:T(8,128)(2,1)S(1)}, u32[]{:S(2)}, u32[]{:S(2)}) collective-permute-start(bf16[80,3,128]{2,0,1:T(8,128)(2,1)S(1)} %bitcast.153), channel_id=1, source_target_pairs={{0,12},{1,13},{2,14},{3,15},{4,0},{5,1},{6,2},{7,3},{8,4},{9,5},{1... | collective-permute-start | bytes 184328 | tf_op jit(solution)/shard_map/ppermute | solution.py:40
  47.7 9.5 %collective-permute-start.13 = (bf16[80,3,128]{2,0,1:T(8,128)(2,1)S(1)}, bf16[80,3,128]{2,0,1:T(8,128)(2,1)S(1)}, u32[]{:S(2)}, u32[]{:S(2)}) collective-permute-start(bf16[80,3,128]{2,0,1:T(8,128)(2,1)S(1)} %bitcast.152), channel_id=1, source_target_pairs={{0,13},{1,14},{2,15},{3,0},{4,1},{5,2},{6,3},{7,4},{8,5},{9,6},{10... | collective-permute-start | bytes 184328 | tf_op jit(solution)/shard_map/ppermute | solution.py:40
  51.6 7.7 %collective-permute-start.14 = (bf16[80,3,128]{2,0,1:T(8,128)(2,1)S(1)}, bf16[80,3,128]{2,0,1:T(8,128)(2,1)S(1)}, u32[]{:S(2)}, u32[]{:S(2)}) collective-permute-start(bf16[80,3,128]{2,0,1:T(8,128)(2,1)S(1)} %bitcast.151), channel_id=1, source_target_pairs={{0,14},{1,15},{2,0},{3,1},{4,2},{5,3},{6,4},{7,5},{8,6},{9,7},{10,... | collective-permute-start | bytes 184328 | tf_op jit(solution)/shard_map/ppermute | solution.py:40
  55.9 5.9 %collective-permute-start.15 = (bf16[80,3,128]{2,0,1:T(8,128)(2,1)S(1)}, bf16[80,3,128]{2,0,1:T(8,128)(2,1)S(1)}, u32[]{:S(2)}, u32[]{:S(2)}) collective-permute-start(bf16[80,3,128]{2,0,1:T(8,128)(2,1)S(1)} %bitcast.150), channel_id=1, source_target_pairs={{0,15},{1,0},{2,1},{3,2},{4,3},{5,4},{6,5},{7,6},{8,7},{9,8},{10,9... | collective-permute-start | bytes 184328 | tf_op jit(solution)/shard_map/ppermute | solution.py:40
  56.0 37.3 %copy-start.1 = (f32[4]{0:T(128)S(1)}, f32[4]{0:T(128)}, u32[]{:S(2)}) copy-start(f32[4]{0:T(128)} %param.13) | copy-start | bytes 52
  56.2 25.1 %collective-permute-start = (bf16[640,3,256]{2,0,1:T(8,128)(2,1)S(1)}, bf16[640,3,256]{2,0,1:T(8,128)(2,1)}, u32[]{:S(2)}, u32[]{:S(2)}) collective-permute-start(bf16[640,3,256]{2,0,1:T(8,128)(2,1)S(1)} %bitcast.148), channel_id=1, source_target_pairs={{0,2},{2,0},{1,3},{3,1},{4,6},{6,4},{5,7},{7,5},{8,10},{10,8},{9,1... | collective-permute-start | bytes 2949128 | tf_op jit(solution)/shard_map/ppermute | solution.py:61
  87.0 23.3 %collective-permute-start.16 = (bf16[1280,3,128]{2,0,1:T(8,128)(2,1)S(1)}, bf16[1280,3,128]{2,0,1:T(8,128)(2,1)S(1)}, u32[]{:S(2)}, u32[]{:S(2)}) collective-permute-start(bf16[1280,3,128]{2,0,1:T(8,128)(2,1)S(1)} %bitcast.142), channel_id=1, source_target_pairs={{0,16},{16,32},{32,48},{48,0},{1,17},{17,33},{33,49},{49,1},{2,18}... | collective-permute-start | bytes 2949128 | tf_op jit(solution)/shard_map/ppermute | solution.py:23
  88.5 22.1 %collective-permute-start.17 = (bf16[1280,3,128]{2,0,1:T(8,128)(2,1)S(1)}, bf16[1280,3,128]{2,0,1:T(8,128)(2,1)S(1)}, u32[]{:S(2)}, u32[]{:S(2)}) collective-permute-start(bf16[1280,3,128]{2,0,1:T(8,128)(2,1)S(1)} %bitcast.143), channel_id=1, source_target_pairs={{0,48},{16,0},{32,16},{48,32},{1,49},{17,1},{33,17},{49,33},{2,50}... | collective-permute-start | bytes 2949128 | tf_op jit(solution)/shard_map/ppermute | solution.py:24
  89.8 23.4 %collective-permute-start.20 = (bf16[1280,3,128]{2,0,1:T(8,128)(2,1)S(1)}, bf16[1280,3,128]{2,0,1:T(8,128)(2,1)}, u32[]{:S(2)}, u32[]{:S(2)}) collective-permute-start(bf16[1280,3,128]{2,0,1:T(8,128)(2,1)S(1)} %bitcast.144), channel_id=1, source_target_pairs={{0,64},{64,0},{1,65},{65,1},{2,66},{66,2},{3,67},{67,3},{4,68},{68... | collective-permute-start | bytes 2949128 | tf_op jit(solution)/shard_map/ppermute | solution.py:68
  110.4 12.0 %collective-permute-start.18 = (bf16[640,3,128]{2,0,1:T(8,128)(2,1)S(1)}, bf16[640,3,128]{2,0,1:T(8,128)(2,1)S(1)}, u32[]{:S(2)}, u32[]{:S(2)}) collective-permute-start(bf16[640,3,128]{2,0,1:T(8,128)(2,1)S(1)} %slice.42), channel_id=1, source_target_pairs={{0,16},{16,32},{32,48},{48,0},{1,17},{17,33},{33,49},{49,1},{2,18}... | collective-permute-start | bytes 1474568 | tf_op jit(solution)/shard_map/ppermute | solution.py:29
  110.7 12.6 %collective-permute-start.19 = (bf16[640,3,128]{2,0,1:T(8,128)(2,1)S(1)}, bf16[640,3,128]{2,0,1:T(8,128)(2,1)S(1)}, u32[]{:S(2)}, u32[]{:S(2)}) collective-permute-start(bf16[640,3,128]{2,0,1:T(8,128)(2,1)S(1)} %slice.43), channel_id=1, source_target_pairs={{0,48},{16,0},{32,16},{48,32},{1,49},{17,1},{33,17},{49,33},{2,50}... | collective-permute-start | bytes 1474568 | tf_op jit(solution)/shard_map/ppermute | solution.py:30
  113.2 30.2 %collective-permute-start.21 = (bf16[1280,3,128]{2,0,1:T(8,128)(2,1)}, bf16[1280,3,128]{2,0,1:T(8,128)(2,1)S(1)}, u32[]{:S(2)}, u32[]{:S(2)}) collective-permute-start(bf16[1280,3,128]{2,0,1:T(8,128)(2,1)} %collective-permute-done.20), channel_id=1, source_target_pairs={{0,16},{16,32},{32,48},{48,0},{1,17},{17,33},{33,49},{49,1},{2,18}... | collective-permute-start | bytes 2949128 | tf_op jit(solution)/shard_map/ppermute | solution.py:23
  113.2 30.4 %collective-permute-start.22 = (bf16[1280,3,128]{2,0,1:T(8,128)(2,1)}, bf16[1280,3,128]{2,0,1:T(8,128)(2,1)S(1)}, u32[]{:S(2)}, u32[]{:S(2)}) collective-permute-start(bf16[1280,3,128]{2,0,1:T(8,128)(2,1)} %collective-permute-done.20), channel_id=1, source_target_pairs={{0,48},{16,0},{32,16},{48,32},{1,49},{17,1},{33,17},{49,33},{2,50}... | collective-permute-start | bytes 2949128 | tf_op jit(solution)/shard_map/ppermute | solution.py:24
  143.5 11.3 %collective-permute-start.23 = (bf16[640,3,128]{2,0,1:T(8,128)(2,1)S(1)}, bf16[640,3,128]{2,0,1:T(8,128)(2,1)S(1)}, u32[]{:S(2)}, u32[]{:S(2)}) collective-permute-start(bf16[640,3,128]{2,0,1:T(8,128)(2,1)S(1)} %slice.44), channel_id=1, source_target_pairs={{0,16},{16,32},{32,48},{48,0},{1,17},{17,33},{33,49},{49,1},{2,18}... | collective-permute-start | bytes 1474568 | tf_op jit(solution)/shard_map/ppermute | solution.py:29
  143.6 12.1 %collective-permute-start.24 = (bf16[640,3,128]{2,0,1:T(8,128)(2,1)S(1)}, bf16[640,3,128]{2,0,1:T(8,128)(2,1)S(1)}, u32[]{:S(2)}, u32[]{:S(2)}) collective-permute-start(bf16[640,3,128]{2,0,1:T(8,128)(2,1)S(1)} %slice.45), channel_id=1, source_target_pairs={{0,48},{16,0},{32,16},{48,32},{1,49},{17,1},{33,17},{49,33},{2,50}... | collective-permute-start | bytes 1474568 | tf_op jit(solution)/shard_map/ppermute | solution.py:30
Sparse Core Ops, SparseCore 0:
  84.6 79.8 all-gather.1

commit v8 on v6

--- a/solution.py
+++ b/solution.py
@@ -4,7 +4,7 @@
 from jax.sharding import Mesh, PartitionSpec as P
 
 
-def ring_into(out, lead, shard, axis):
+def ring_into(out, lead, shard, axis, mirror=None):
     n = lax.axis_size(axis)
     me = lax.axis_index(axis)
     right = [(k, (k + 1) % n) for k in range(n)]
@@ -13,7 +13,13 @@
 
     def put(buf, piece, index, offset=0):
         start = (lead, index, offset) + zeros[1:]
-        return lax.dynamic_update_slice(buf, piece[None, None], start)
+        buf = lax.dynamic_update_slice(buf, piece[None, None], start)
+        if mirror is not None:
+            mirror_axis, mirror_lead = mirror
+            m = lax.axis_size(mirror_axis)
+            twin = lax.ppermute(piece, mirror_axis, [(k, (k + 1) % m) for k in range(m)])
+            buf = lax.dynamic_update_slice(buf, twin[None, None], (mirror_lead, index, offset) + zeros[1:])
+        return buf
 
     out = put(out, shard, me)
     go_right = go_left = shard
@@ -57,17 +63,19 @@
     other_a, spread_b = lax.optimization_barrier((other_a, spread_b))
     first_zh = lax.axis_index("zh") == 0
     pair_a = jnp.where(first_zh, jnp.stack([spread_a, other_a]), jnp.stack([other_a, spread_a]))
-    block_a = lax.all_gather(pair_a, ("x", "core"), axis=0, tiled=True)
+    me_core = lax.axis_index("core")
+    block_a = jnp.zeros((n_core, n_x) + pair_a.shape, pair_a.dtype)
+    block_a = ring_into(block_a, me_core, pair_a, "x", mirror=("core", (me_core + 1) % n_core))
     spread_b = spread_b.reshape(n_col * local_aux, nocc, cols_b)
     other_b = lax.ppermute(spread_b, "zl", [(k, (k + 1) % n_zl) for k in range(n_zl)])
     me_zl = lax.axis_index("zl")
     block_b = jnp.zeros((n_zl, n_y) + spread_b.shape, spread_b.dtype)
     block_b = ring_into(block_b, me_zl, spread_b, "y")
     block_b = ring_into(block_b, (me_zl + 1) % n_zl, other_b, "y")
-    block_a = block_a.reshape(n_x, n_core, n_zh, n_zl, n_y, local_aux, nocc, rows_a)
+    block_a = block_a.reshape(n_core, n_x, n_zh, n_zl, n_y, local_aux, nocc, rows_a)
     block_b = block_b.reshape(n_zl, n_y, n_x, n_zh, n_core, local_aux, nocc, cols_b)
     gram = jnp.einsum(
-        "xchzypia,zyxhcpjb->ijab",
+        "cxhzypia,zyxhcpjb->ijab",
         block_a,
         block_b,
         preferred_element_type=jnp.float32,

time: 170 us -> 187 us (1.10)
  local copies, waits for them, and re-layouts: 24.6 us -> 53.7 us
  blocking collectives: 20.5 us -> 0 us
  starting transfers between devices: 20.7 us -> 37.9 us
  between operations: 13.7 us -> 0.24 us
  other arithmetic: 7.08 us -> 9.54 us
    all_to_all x1 -> x0, blocking collectives: 20.5 us -> none  [shards(): lax.all_to_all(factors.reshape(local_aux, nocc, n_row, rows_a), ('zl', 'y...]
    ppermute x2 -> x3, waiting for transfers between devices: 33.2 us -> 14.1 us  [ring_into(): go_right = lax.ppermute(go_right, axis, right)]
    ppermute x1, waiting for transfers between devices: 0.01 us -> 18.2 us  [shards(): lax.ppermute(spread_a, 'zh', [(k, (k + 1) % n_zh) for k in range(n_zh)])]
    dynamic_update_slice x10 -> x19, local copies, waits for them, and re-layouts: 9.68 us -> 27.3 us  [the longest x14 20.9 us: put(): buf = lax.dynamic_update_slice(buf, piece[None, None], start)]
    all_to_all x1, waiting for transfers between devices: 24 us -> 9.02 us  [shards(): lax.all_to_all(factors.reshape(local_aux, nocc, n_col, cols_b), ('x', 'zh...]
    all_to_all x0 -> x1, waiting for transfers between devices: none -> 12.1 us  [shards(): lax.all_to_all(factors.reshape(local_aux, nocc, n_row, rows_a), ('zl', 'y...]
    ppermute x2 -> x3, waiting for transfers between devices: 0.01 us -> 8.06 us  [ring_into(): from_right = lax.ppermute(go_left[half:], axis, left)]
    ppermute x0 -> x5, starting transfers between devices: none -> 7.68 us  [put(): lax.ppermute(piece, mirror_axis, [(k, (k + 1) % m) for k in range(m)])]
  transfers between devices with their start and end apart: 12 -> 21, of which waited for: 6 -> 8; matrix products, arithmetic and copies ran while one was open for 14% -> 31% of each run, Pallas kernels for 0% -> 0%
where the time goes in v8:
time: 187 us; the launch traced here: 186 us
  waiting for transfers between devices  72.8 us (39%)
  local copies, waits for them, and re-layouts  53.7 us (29%)
  starting transfers between devices  37.9 us (20%)
  matrix products  11.8 us (6%)
  other arithmetic  9.54 us (5%)
    dynamic_update_slice x14, local copies, waits for them, and re-layouts, put(): buf = lax.dynamic_update_slice(buf, piece[None, None], start)  20.9 us
    ppermute x1, waiting for transfers between devices, shards(): lax.ppermute(spread_a, 'zh', [(k, (k + 1) % n_zh) for k in range(n_zh)])  18.2 us
    ppermute x3, waiting for transfers between devices, ring_into(): go_right = lax.ppermute(go_right, axis, right)  14.1 us
    all_to_all x1, waiting for transfers between devices, shards(): lax.all_to_all(factors.reshape(local_aux, nocc, n_row, rows_a), ('zl', 'y...  12.1 us
    dot_general x1, matrix products, shards(): jnp.einsum('cxhzypia,zyxhcpjb->ijab', block_a, block_b, preferred_element...  11.8 us
    ppermute x3, waiting for transfers between devices, ring_into(): from_left = lax.ppermute(go_right[:half], axis, right)  11.4 us
    all_to_all x1, waiting for transfers between devices, shards(): lax.all_to_all(factors.reshape(local_aux, nocc, n_col, cols_b), ('x', 'zh...  9.02 us
    all_to_all x1, starting transfers between devices, shards(): lax.all_to_all(factors.reshape(local_aux, nocc, n_col, cols_b), ('x', 'zh...  8.12 us
  transfers between devices with their start and end apart: 21, of which 8 were waited for; matrix products, arithmetic and copies ran while one was open for 31% of the time, Pallas kernels for 0%

profile of v8, /device:TPU:1, one launch (start us, length us, event | category | flops | bytes accessed | tf_op | source)
XLA Modules:
  0.0 186.0 jit_solution(5453514723561238455)
XLA Ops:
  0.0 2.2 %copy.44 = bf16[3,10,8,8,256]{4,3,1,0,2:T(8,128)(2,1)} copy(bf16[3,10,8,8,256]{4,3,2,1,0:T(8,128)(2,1)} %bitcast.91) | data formatting | bytes 1966080 | tf_op jit(solution)/shard_map/reshape | solution.py:56
  2.3 6.4 %all-to-all-start = ((bf16[80,3,8,256]{3,0,1,2:T(8,128)(2,1)}), bf16[80,3,8,256]{3,0,1,2:T(8,128)(2,1)S(1)}, u32[]{:S(2)}, u32[]{:S(2)}) async-start(bf16[80,3,8,256]{3,0,1,2:T(8,128)(2,1)} %bitcast.86), calls=%async_computation | async-start | bytes 1966080 | tf_op jit(solution)/shard_map/all_to_all | solution.py:55
  8.6 0.8 and_bitcast_fusion
  9.4 2.3 %copy_bitcast_fusion = bf16[80,3,16,128]{3,0,1,2:T(8,128)(2,1)} fusion(bf16[80,3,2048]{2,0,1:T(8,128)(2,1)} %param.7), kind=kLoop, calls=%fused_computation.17 | loop fusion | bytes 1966080 | tf_op jit(solution)/shard_map/reshape | solution.py:61
  11.7 12.1 %all-to-all-done = bf16[80,3,8,256]{3,0,1,2:T(8,128)(2,1)S(1)} async-done(((bf16[80,3,8,256]{3,0,1,2:T(8,128)(2,1)}), bf16[80,3,8,256]{3,0,1,2:T(8,128)(2,1)S(1)}, u32[]{:S(2)}, u32[]{:S(2)}) %all-to-all-start) | async-done | bytes 983072 | tf_op jit(solution)/shard_map/all_to_all | solution.py:55
  23.8 8.1 %all-to-all-start.1 = ((bf16[80,3,16,128]{3,0,1,2:T(8,128)(2,1)}), bf16[80,3,16,128]{3,0,1,2:T(8,128)(2,1)S(1)}, u32[]{:S(2)}, u32[]{:S(2)}) async-start(bf16[80,3,16,128]{3,0,1,2:T(8,128)(2,1)} %copy_bitcast_fusion), calls=%async_computation.1 | async-start | bytes 1966080 | tf_op jit(solution)/shard_map/all_to_all | solution.py:60
  32.0 2.9 %collective-permute-start = (bf16[640,3,256]{2,0,1:T(8,128)(2,1)S(1)}, bf16[640,3,256]{2,0,1:T(8,128)(2,1)S(1)}, u32[]{:S(2)}, u32[]{:S(2)}) collective-permute-start(bf16[640,3,256]{2,0,1:T(8,128)(2,1)S(1)} %bitcast.88), channel_id=1, source_target_pairs={{0,2},{2,0},{1,3},{3,1},{4,6},{6,4},{5,7},{7,5},{8,10},{10,8},{9,1... | collective-permute-start | bytes 2949128 | tf_op jit(solution)/shard_map/ppermute | solution.py:59
  34.9 0.8 dynamic_slice.7
  35.7 0.8 dynamic_slice.6
  36.5 0.6 fusion.11
  37.0 1.8 fusion.9
  38.9 0.1 broadcast_add_fusion
  39.0 9.0 %all-to-all-done.1 = bf16[80,3,16,128]{3,0,1,2:T(8,128)(2,1)S(1)} async-done(((bf16[80,3,16,128]{3,0,1,2:T(8,128)(2,1)}), bf16[80,3,16,128]{3,0,1,2:T(8,128)(2,1)S(1)}, u32[]{:S(2)}, u32[]{:S(2)}) %all-to-all-start.1) | async-done | bytes 983072 | tf_op jit(solution)/shard_map/all_to_all | solution.py:60
  48.1 1.0 copy.21
  49.1 18.2 %collective-permute-done = bf16[640,3,256]{2,0,1:T(8,128)(2,1)S(1)} collective-permute-done((bf16[640,3,256]{2,0,1:T(8,128)(2,1)S(1)}, bf16[640,3,256]{2,0,1:T(8,128)(2,1)S(1)}, u32[]{:S(2)}, u32[]{:S(2)}) %collective-permute-start) | collective-permute-done | bytes 983072 | tf_op jit(solution)/shard_map/ppermute | solution.py:59
  67.2 0.6 collective-permute-start.1
  67.8 2.1 %collective-permute-start.2 = (bf16[1280,3,128]{2,0,1:T(8,128)(2,1)}, bf16[1280,3,128]{2,0,1:T(8,128)(2,1)}, u32[]{:S(2)}, u32[]{:S(2)}) collective-permute-start(bf16[1280,3,128]{2,0,1:T(8,128)(2,1)} %bitcast.8), channel_id=1, source_target_pairs={{0,48},{16,0},{32,16},{48,32},{1,49},{17,1},{33,17},{49,33},{2,50}... | collective-permute-start | bytes 2949128 | tf_op jit(solution)/shard_map/ppermute | solution.py:30
  69.9 0.7 gather_fusion.1
  70.6 0.7 gather_fusion.2
  71.3 0.7 gather_fusion.3
  72.0 1.6 maximum_select_fusion.1
  73.5 1.2 collective-permute-start.11
  74.7 1.7 collective-permute-start.13
  76.5 7.3 %broadcast_in_dim.94 = bf16[2,4,2,640,3,256]{5,3,4,2,1,0:T(8,128)(2,1)} broadcast(bf16[]{:T(256)} %constant.100.clone.1), dimensions={} | broadcast | bytes 15728642 | tf_op jit(solution)/shard_map/broadcast_in_dim | solution.py:67
  83.8 3.3 %fusion.3 = bf16[2,4,2,640,3,256]{5,3,4,2,1,0:T(8,128)(2,1)} fusion(bf16[2,4,2,640,3,256]{5,3,4,2,1,0:T(8,128)(2,1)} %broadcast_in_dim.94, s32[]{:T(128)S(6)} %select_n.191, s32[]{:T(128)S(6)} %select_n.192, bf16[1,1,1,640,3,256]{5,3,4,2,1,0:T(8,128)(2,1)} %bitcast.93, bf16[1,1,1,640,3,256]{5,3,4,2,1,0:T(8,128)(2,1)S(1)} %bitcast.90, pred[]{:T(512)S(6)} %eq.18), kind=kLoop, calls=%fused_computation.9 | loop fusion | flops 8847360 | bytes 3932169 | tf_op jit(solution)/shard_map/dynamic_update_slice | solution.py:16
  87.1 4.8 %broadcast_in_dim.84 = bf16[2,4,1280,3,128]{4,2,3,1,0:T(8,128)(2,1)} broadcast(bf16[]{:T(256)} %constant.100.clone.1), dimensions={} | broadcast | bytes 7864322 | tf_op jit(solution)/shard_map/broadcast_in_dim | solution.py:72
  91.9 2.2 %bitcast_dynamic-update-slice_fusion.14 = bf16[2,4,1280,3,128]{4,2,3,1,0:T(8,128)(2,1)} fusion(bf16[2,4,1280,3,128]{4,2,3,1,0:T(8,128)(2,1)} %broadcast_in_dim.84, s32[]{:T(128)S(6)} %select_n.179, s32[]{:T(128)S(6)} %select_n.180, bf16[1280,3,1,128]{3,0,1,2:T(8,128)(2,1)} %bitcast.6), kind=kLoop, calls=%fused_computation.28 | loop fusion | bytes 1966088 | tf_op jit(solution)/shard_map/dynamic_update_slice | solution.py:16
  94.1 1.1 slice.48
  95.3 1.1 slice.49
  96.3 2.7 %collective-permute-start.4 = (bf16[640,3,128]{2,0,1:T(8,128)(2,1)S(1)}, bf16[640,3,128]{2,0,1:T(8,128)(2,1)S(1)}, u32[]{:S(2)}, u32[]{:S(2)}) collective-permute-start(bf16[640,3,128]{2,0,1:T(8,128)(2,1)S(1)} %slice.49), channel_id=1, source_target_pairs={{0,48},{16,0},{32,16},{48,32},{1,49},{17,1},{33,17},{49,33},{2,50}... | collective-permute-start | bytes 1474568 | tf_op jit(solution)/shard_map/ppermute | solution.py:36
  99.0 2.2 %bitcast_dynamic-update-slice_fusion.13 = bf16[2,4,1280,3,128]{4,2,3,1,0:T(8,128)(2,1)} fusion(bf16[2,4,1280,3,128]{4,2,3,1,0:T(8,128)(2,1)} %bitcast_dynamic-update-slice_fusion.14, s32[]{:T(128)S(6)} %select_n.179, s32[]{:T(128)S(6)} %select_n.182, bf16[1280,3,128]{2,0,1:T(8,128)(2,1)} %collective-permute-done.1), kind=kLoop, calls=%fused_computation.27 | loop fusion | bytes 1966088 | tf_op jit(solution)/shard_map/dynamic_update_slice | solution.py:16
  101.3 2.2 %bitcast_dynamic-update-slice_fusion.12 = bf16[2,4,1280,3,128]{4,2,3,1,0:T(8,128)(2,1)} fusion(bf16[2,4,1280,3,128]{4,2,3,1,0:T(8,128)(2,1)} %bitcast_dynamic-update-slice_fusion.13, s32[]{:T(128)S(6)} %select_n.179, s32[]{:T(128)S(6)} %select_n.184, bf16[1280,3,128]{2,0,1:T(8,128)(2,1)} %collective-permute-done.2), kind=kLoop, calls=%fused_computation.26 | loop fusion | bytes 1966088 | tf_op jit(solution)/shard_map/dynamic_update_slice | solution.py:16
  103.5 2.4 %collective-permute-start.10 = (bf16[2,640,3,256]{3,1,2,0:T(8,128)(2,1)}, bf16[2,640,3,256]{3,1,2,0:T(8,128)(2,1)S(1)}, u32[]{:S(2)}, u32[]{:S(2)}) collective-permute-start(bf16[2,640,3,256]{3,1,2,0:T(8,128)(2,1)} %maximum_select_fusion.1), channel_id=1, source_target_pairs={{0,1},{1,0},{2,3},{3,2},{4,5},{5,4},{6,7},{7,6},{8,9},{9,8},{10,11... | collective-permute-start | bytes 5898248 | tf_op jit(solution)/shard_map/ppermute | solution.py:20
  105.9 1.7 collective-permute-done.3
  107.5 0.9 bitcast_dynamic-update-slice_fusion.18
  108.4 2.7 %collective-permute-start.7 = (bf16[1280,3,128]{2,0,1:T(8,128)(2,1)}, bf16[1280,3,128]{2,0,1:T(8,128)(2,1)S(1)}, u32[]{:S(2)}, u32[]{:S(2)}) collective-permute-start(bf16[1280,3,128]{2,0,1:T(8,128)(2,1)} %collective-permute-done.5), channel_id=1, source_target_pairs={{0,48},{16,0},{32,16},{48,32},{1,49},{17,1},{33,17},{49,33},{2,50}... | collective-permute-start | bytes 2949128 | tf_op jit(solution)/shard_map/ppermute | solution.py:30
  111.1 0.9 bitcast_dynamic-update-slice_fusion.17
  112.0 2.2 %bitcast_dynamic-update-slice_fusion.11 = bf16[2,4,1280,3,128]{4,2,3,1,0:T(8,128)(2,1)} fusion(bf16[2,4,1280,3,128]{4,2,3,1,0:T(8,128)(2,1)} %bitcast_dynamic-update-slice_fusion.17, s32[]{:T(128)S(6)} %select_n.188, s32[]{:T(128)S(6)} %select_n.180, bf16[1280,3,128]{2,0,1:T(8,128)(2,1)} %collective-permute-done.5), kind=kLoop, calls=%fused_computation.25 | loop fusion | bytes 1966088 | tf_op jit(solution)/shard_map/dynamic_update_slice | solution.py:16
  114.2 4.2 %collective-permute-done.11 = bf16[2,640,3,256]{3,1,2,0:T(8,128)(2,1)} collective-permute-done((bf16[2,640,3,256]{3,1,2,0:T(8,128)(2,1)}, bf16[2,640,3,256]{3,1,2,0:T(8,128)(2,1)}, u32[]{:S(2)}, u32[]{:S(2)}) %collective-permute-start.11) | collective-permute-done | bytes 1966112 | tf_op jit(solution)/shard_map/ppermute | solution.py:29
  118.4 1.3 slice.52
  119.7 9.9 %collective-permute-done.6 = bf16[1280,3,128]{2,0,1:T(8,128)(2,1)S(1)} collective-permute-done((bf16[1280,3,128]{2,0,1:T(8,128)(2,1)}, bf16[1280,3,128]{2,0,1:T(8,128)(2,1)S(1)}, u32[]{:S(2)}, u32[]{:S(2)}) %collective-permute-start.6) | collective-permute-done | bytes 983072 | tf_op jit(solution)/shard_map/ppermute | solution.py:29
  129.7 3.4 %collective-permute-start.12 = (bf16[2,640,3,256]{3,1,2,0:T(8,128)(2,1)}, bf16[2,640,3,256]{3,1,2,0:T(8,128)(2,1)S(1)}, u32[]{:S(2)}, u32[]{:S(2)}) collective-permute-start(bf16[2,640,3,256]{3,1,2,0:T(8,128)(2,1)} %collective-permute-done.11), channel_id=1, source_target_pairs={{0,1},{1,0},{2,3},{3,2},{4,5},{5,4},{6,7},{7,6},{8,9},{9,8},{10,11... | collective-permute-start | bytes 5898248 | tf_op jit(solution)/shard_map/ppermute | solution.py:20
  133.1 1.0 bitcast_dynamic-update-slice_fusion.10
  134.2 0.1 collective-permute-start.14
  134.3 1.0 bitcast_dynamic-update-slice_fusion.9
  135.4 1.6 collective-permute-start.17
  137.0 1.4 bitcast_dynamic-update-slice_fusion.4
  138.5 9.7 %collective-permute-done.8 = bf16[640,3,128]{2,0,1:T(8,128)(2,1)S(1)} collective-permute-done((bf16[640,3,128]{2,0,1:T(8,128)(2,1)S(1)}, bf16[640,3,128]{2,0,1:T(8,128)(2,1)S(1)}, u32[]{:S(2)}, u32[]{:S(2)}) %collective-permute-start.8) | collective-permute-done | bytes 491552 | tf_op jit(solution)/shard_map/ppermute | solution.py:35
  148.2 3.0 %bitcast_dynamic-update-slice_fusion.3 = bf16[2,4,2,640,3,256]{5,3,4,2,1,0:T(8,128)(2,1)} fusion(bf16[2,4,2,640,3,256]{5,3,4,2,1,0:T(8,128)(2,1)} %bitcast_dynamic-update-slice_fusion.4, s32[]{:T(128)S(6)} %select_n.191, s32[]{:T(128)S(6)} %select_n.198, bf16[2,640,3,256]{3,1,2,0:T(8,128)(2,1)} %collective-permute-done.11), kind=kLoop, calls=%fused_computation.14 | loop fusion | bytes 3932168 | tf_op jit(solution)/shard_map/dynamic_update_slice | solution.py:16
  151.1 0.9 bitcast_dynamic-update-slice_fusion.16
  152.0 8.1 %collective-permute-done.9 = bf16[640,3,128]{2,0,1:T(8,128)(2,1)S(1)} collective-permute-done((bf16[640,3,128]{2,0,1:T(8,128)(2,1)S(1)}, bf16[640,3,128]{2,0,1:T(8,128)(2,1)S(1)}, u32[]{:S(2)}, u32[]{:S(2)}) %collective-permute-start.9) | collective-permute-done | bytes 491552 | tf_op jit(solution)/shard_map/ppermute | solution.py:36
  160.1 0.9 bitcast_dynamic-update-slice_fusion.15
  161.0 1.7 collective-permute-start.16
  162.8 1.4 bitcast_dynamic-update-slice_fusion.2
  164.2 1.4 bitcast_dynamic-update-slice_fusion.1
  165.6 1.4 bitcast_dynamic-update-slice_fusion
  167.0 1.0 bitcast_dynamic-update-slice_fusion.8
  168.1 1.0 bitcast_dynamic-update-slice_fusion.7
  169.1 1.0 bitcast_dynamic-update-slice_fusion.6
  170.1 1.0 bitcast_dynamic-update-slice_fusion.5
  171.2 11.8 %fusion.4 = f32[3,3,256,128]{2,3,0,1:T(8,128)S(1)} fusion(bf16[2,4,2,2,4,80,3,256,1]{7,5,4,3,6,2,1,0,8:T(8,128)(2,1)} %bitcast.37, bf16[2,4,4,2,2,80,3,128,1]{7,5,4,3,2,6,1,0,8:T(8,128)(2,1)} %bitcast.19), kind=kOutput, calls=%fused_computation.16 | convolution fusion | flops 6039797760 | bytes 24772608 | tf_op jit(solution)/shard_map/cxhzypia,zyxhcpjb->ijab/dot_general | solution.py:77
  182.9 0.4 copy.24
  183.3 0.7 gather_fusion
  184.0 1.9 %add_divide_fusion = f32[16,256,128]{2,1,0:T(8,128)} fusion(f32[16,256,128]{2,1,0:T(8,128)S(1)} %gather_fusion, f32[16]{0:T(128)S(1)} %gather_fusion.3, f32[16]{0:T(128)S(1)} %gather_fusion.2, f32[16]{0:T(128)S(1)} %gather_fusion.1, f32[256,128]{1,0:T(8,128)S(1)} %broadcast_add_fusion, pred[16]{0:T(512)(128)(4,1)S(1)} %get-tuple-element.9), kind=kLoop, calls=%fused_computation.7 | loop fusion | flops 3145728 | bytes 4325584 | tf_op jit(solution)/shard_map/div | solution.py:97
  (40 shorter events, 0.5 us)
Async XLA Ops:
  0.0 69.9 %copy-start = (f32[300]{0:T(512)S(1)}, f32[300]{0:T(512)}, u32[]{:S(2)}) copy-start(f32[300]{0:T(512)} %param.8) | copy-start | bytes 3604
  0.0 37.0 %copy-start.4 = (s32[16,2]{0,1:T(2,128)S(1)}, s32[16,2]{0,1:T(2,128)}, u32[]{:S(2)}) copy-start(s32[16,2]{0,1:T(2,128)} %param.11) | copy-start | bytes 388
  0.0 36.4 %copy-start.3 = (s32[3]{0:T(128)S(1)}, s32[3]{0:T(128)}, u32[]{:S(2)}) copy-start(s32[3]{0:T(128)} %param.10) | copy-start | bytes 40
  0.0 38.9 %copy-start.5 = (s32[16]{0:T(128)S(1)}, s32[16]{0:T(128)}, u32[]{:S(2)}) copy-start(s32[16]{0:T(128)} %param.12) | copy-start | bytes 196
  0.0 71.3 %copy-start.1 = (f32[4]{0:T(128)S(1)}, f32[4]{0:T(128)}, u32[]{:S(2)}) copy-start(f32[4]{0:T(128)} %param.13) | copy-start | bytes 52
  2.3 21.5 %all-to-all-start = ((bf16[80,3,8,256]{3,0,1,2:T(8,128)(2,1)}), bf16[80,3,8,256]{3,0,1,2:T(8,128)(2,1)S(1)}, u32[]{:S(2)}, u32[]{:S(2)}) async-start(bf16[80,3,8,256]{3,0,1,2:T(8,128)(2,1)} %bitcast.86), calls=%async_computation | async-start | bytes 1966080 | tf_op jit(solution)/shard_map/all_to_all | solution.py:55
  23.8 24.3 %all-to-all-start.1 = ((bf16[80,3,16,128]{3,0,1,2:T(8,128)(2,1)}), bf16[80,3,16,128]{3,0,1,2:T(8,128)(2,1)S(1)}, u32[]{:S(2)}, u32[]{:S(2)}) async-start(bf16[80,3,16,128]{3,0,1,2:T(8,128)(2,1)} %copy_bitcast_fusion), calls=%async_computation.1 | async-start | bytes 1966080 | tf_op jit(solution)/shard_map/all_to_all | solution.py:60
  32.0 35.2 %collective-permute-start = (bf16[640,3,256]{2,0,1:T(8,128)(2,1)S(1)}, bf16[640,3,256]{2,0,1:T(8,128)(2,1)S(1)}, u32[]{:S(2)}, u32[]{:S(2)}) collective-permute-start(bf16[640,3,256]{2,0,1:T(8,128)(2,1)S(1)} %bitcast.88), channel_id=1, source_target_pairs={{0,2},{2,0},{1,3},{3,1},{4,6},{6,4},{5,7},{7,5},{8,10},{10,8},{9,1... | collective-permute-start | bytes 2949128 | tf_op jit(solution)/shard_map/ppermute | solution.py:59
  67.2 6.3 %copy-start.2 = (bf16[640,3,256]{2,0,1:T(8,128)(2,1)}, bf16[640,3,256]{2,0,1:T(8,128)(2,1)S(1)}, u32[]{:S(2)}) copy-start(bf16[640,3,256]{2,0,1:T(8,128)(2,1)S(1)} %collective-permute-done) | copy-start | bytes 2949124
  67.2 26.9 %collective-permute-start.1 = (bf16[1280,3,128]{2,0,1:T(8,128)(2,1)}, bf16[1280,3,128]{2,0,1:T(8,128)(2,1)}, u32[]{:S(2)}, u32[]{:S(2)}) collective-permute-start(bf16[1280,3,128]{2,0,1:T(8,128)(2,1)} %bitcast.8), channel_id=1, source_target_pairs={{0,16},{16,32},{32,48},{48,0},{1,17},{17,33},{33,49},{49,1},{2,18}... | collective-permute-start | bytes 2949128 | tf_op jit(solution)/shard_map/ppermute | solution.py:29
  67.8 27.4 %collective-permute-start.2 = (bf16[1280,3,128]{2,0,1:T(8,128)(2,1)}, bf16[1280,3,128]{2,0,1:T(8,128)(2,1)}, u32[]{:S(2)}, u32[]{:S(2)}) collective-permute-start(bf16[1280,3,128]{2,0,1:T(8,128)(2,1)} %bitcast.8), channel_id=1, source_target_pairs={{0,48},{16,0},{32,16},{48,32},{1,49},{17,1},{33,17},{49,33},{2,50}... | collective-permute-start | bytes 2949128 | tf_op jit(solution)/shard_map/ppermute | solution.py:30
  73.5 44.9 %collective-permute-start.11 = (bf16[2,640,3,256]{3,1,2,0:T(8,128)(2,1)}, bf16[2,640,3,256]{3,1,2,0:T(8,128)(2,1)}, u32[]{:S(2)}, u32[]{:S(2)}) collective-permute-start(bf16[2,640,3,256]{3,1,2,0:T(8,128)(2,1)} %maximum_select_fusion.1), channel_id=1, source_target_pairs={{0,4},{4,8},{8,12},{12,0},{1,5},{5,9},{9,13},{13,1},{2,6},{6,10},{... | collective-permute-start | bytes 5898248 | tf_op jit(solution)/shard_map/ppermute | solution.py:29
  74.7 59.5 %collective-permute-start.13 = (bf16[2,640,3,256]{3,1,2,0:T(8,128)(2,1)}, bf16[2,640,3,256]{3,1,2,0:T(8,128)(2,1)S(1)}, u32[]{:S(2)}, u32[]{:S(2)}) collective-permute-start(bf16[2,640,3,256]{3,1,2,0:T(8,128)(2,1)} %maximum_select_fusion.1), channel_id=1, source_target_pairs={{0,12},{4,0},{8,4},{12,8},{1,13},{5,1},{9,5},{13,9},{2,14},{6,2},{... | collective-permute-start | bytes 5898248 | tf_op jit(solution)/shard_map/ppermute | solution.py:30
  76.5 27.0 %collective-permute-start.5 = (bf16[1280,3,128]{2,0,1:T(8,128)(2,1)}, bf16[1280,3,128]{2,0,1:T(8,128)(2,1)}, u32[]{:S(2)}, u32[]{:S(2)}) collective-permute-start(bf16[1280,3,128]{2,0,1:T(8,128)(2,1)} %bitcast.8), channel_id=1, source_target_pairs={{0,64},{64,0},{1,65},{65,1},{2,66},{66,2},{3,67},{67,3},{4,68},{68... | collective-permute-start | bytes 2949128 | tf_op jit(solution)/shard_map/ppermute | solution.py:70
  95.2 12.4 %collective-permute-start.3 = (bf16[640,3,128]{2,0,1:T(8,128)(2,1)S(1)}, bf16[640,3,128]{2,0,1:T(8,128)(2,1)S(1)}, u32[]{:S(2)}, u32[]{:S(2)}) collective-permute-start(bf16[640,3,128]{2,0,1:T(8,128)(2,1)S(1)} %slice.48), channel_id=1, source_target_pairs={{0,16},{16,32},{32,48},{48,0},{1,17},{17,33},{33,49},{49,1},{2,18}... | collective-permute-start | bytes 1474568 | tf_op jit(solution)/shard_map/ppermute | solution.py:35
  96.3 12.1 %collective-permute-start.4 = (bf16[640,3,128]{2,0,1:T(8,128)(2,1)S(1)}, bf16[640,3,128]{2,0,1:T(8,128)(2,1)S(1)}, u32[]{:S(2)}, u32[]{:S(2)}) collective-permute-start(bf16[640,3,128]{2,0,1:T(8,128)(2,1)S(1)} %slice.49), channel_id=1, source_target_pairs={{0,48},{16,0},{32,16},{48,32},{1,49},{17,1},{33,17},{49,33},{2,50}... | collective-permute-start | bytes 1474568 | tf_op jit(solution)/shard_map/ppermute | solution.py:36
  103.5 31.9 %collective-permute-start.10 = (bf16[2,640,3,256]{3,1,2,0:T(8,128)(2,1)}, bf16[2,640,3,256]{3,1,2,0:T(8,128)(2,1)S(1)}, u32[]{:S(2)}, u32[]{:S(2)}) collective-permute-start(bf16[2,640,3,256]{3,1,2,0:T(8,128)(2,1)} %maximum_select_fusion.1), channel_id=1, source_target_pairs={{0,1},{1,0},{2,3},{3,2},{4,5},{5,4},{6,7},{7,6},{8,9},{9,8},{10,11... | collective-permute-start | bytes 5898248 | tf_op jit(solution)/shard_map/ppermute | solution.py:20
  107.5 22.2 %collective-permute-start.6 = (bf16[1280,3,128]{2,0,1:T(8,128)(2,1)}, bf16[1280,3,128]{2,0,1:T(8,128)(2,1)S(1)}, u32[]{:S(2)}, u32[]{:S(2)}) collective-permute-start(bf16[1280,3,128]{2,0,1:T(8,128)(2,1)} %collective-permute-done.5), channel_id=1, source_target_pairs={{0,16},{16,32},{32,48},{48,0},{1,17},{17,33},{33,49},{49,1},{2,18}... | collective-permute-start | bytes 2949128 | tf_op jit(solution)/shard_map/ppermute | solution.py:29
  108.4 25.8 %collective-permute-start.7 = (bf16[1280,3,128]{2,0,1:T(8,128)(2,1)}, bf16[1280,3,128]{2,0,1:T(8,128)(2,1)S(1)}, u32[]{:S(2)}, u32[]{:S(2)}) collective-permute-start(bf16[1280,3,128]{2,0,1:T(8,128)(2,1)} %collective-permute-done.5), channel_id=1, source_target_pairs={{0,48},{16,0},{32,16},{48,32},{1,49},{17,1},{33,17},{49,33},{2,50}... | collective-permute-start | bytes 2949128 | tf_op jit(solution)/shard_map/ppermute | solution.py:30
  119.7 41.3 %collective-permute-start.15 = (bf16[1,640,3,256]{3,1,2,0:T(8,128)(2,1)S(1)}, bf16[1,640,3,256]{3,1,2,0:T(8,128)(2,1)S(1)}, u32[]{:S(2)}, u32[]{:S(2)}) collective-permute-start(bf16[1,640,3,256]{3,1,2,0:T(8,128)(2,1)S(1)} %slice.52), channel_id=1, source_target_pairs={{0,4},{4,8},{8,12},{12,0},{1,5},{5,9},{9,13},{13,1},{2,6},{6,10},{... | collective-permute-start | bytes 2949128 | tf_op jit(solution)/shard_map/ppermute | solution.py:35
  129.7 33.1 %collective-permute-start.12 = (bf16[2,640,3,256]{3,1,2,0:T(8,128)(2,1)}, bf16[2,640,3,256]{3,1,2,0:T(8,128)(2,1)S(1)}, u32[]{:S(2)}, u32[]{:S(2)}) collective-permute-start(bf16[2,640,3,256]{3,1,2,0:T(8,128)(2,1)} %collective-permute-done.11), channel_id=1, source_target_pairs={{0,1},{1,0},{2,3},{3,2},{4,5},{5,4},{6,7},{7,6},{8,9},{9,8},{10,11... | collective-permute-start | bytes 5898248 | tf_op jit(solution)/shard_map/ppermute | solution.py:20
  134.2 14.0 %collective-permute-start.8 = (bf16[640,3,128]{2,0,1:T(8,128)(2,1)S(1)}, bf16[640,3,128]{2,0,1:T(8,128)(2,1)S(1)}, u32[]{:S(2)}, u32[]{:S(2)}) collective-permute-start(bf16[640,3,128]{2,0,1:T(8,128)(2,1)S(1)} %slice.50), channel_id=1, source_target_pairs={{0,16},{16,32},{32,48},{48,0},{1,17},{17,33},{33,49},{49,1},{2,18}... | collective-permute-start | bytes 1474568 | tf_op jit(solution)/shard_map/ppermute | solution.py:35
  134.2 31.4 %collective-permute-start.14 = (bf16[2,640,3,256]{3,1,2,0:T(8,128)(2,1)S(1)}, bf16[2,640,3,256]{3,1,2,0:T(8,128)(2,1)S(1)}, u32[]{:S(2)}, u32[]{:S(2)}) collective-permute-start(bf16[2,640,3,256]{3,1,2,0:T(8,128)(2,1)S(1)} %collective-permute-done.13), channel_id=1, source_target_pairs={{0,1},{1,0},{2,3},{3,2},{4,5},{5,4},{6,7},{7,6},{8,9},{9,8},{10,11... | collective-permute-start | bytes 5898248 | tf_op jit(solution)/shard_map/ppermute | solution.py:20
  135.4 27.3 %collective-permute-start.17 = (bf16[1,640,3,256]{3,1,2,0:T(8,128)(2,1)S(1)}, bf16[1,640,3,256]{3,1,2,0:T(8,128)(2,1)S(1)}, u32[]{:S(2)}, u32[]{:S(2)}) collective-permute-start(bf16[1,640,3,256]{3,1,2,0:T(8,128)(2,1)S(1)} %slice.53), channel_id=1, source_target_pairs={{0,12},{4,0},{8,4},{12,8},{1,13},{5,1},{9,5},{13,9},{2,14},{6,2},{... | collective-permute-start | bytes 2949128 | tf_op jit(solution)/shard_map/ppermute | solution.py:36
  148.2 11.9 %collective-permute-start.9 = (bf16[640,3,128]{2,0,1:T(8,128)(2,1)S(1)}, bf16[640,3,128]{2,0,1:T(8,128)(2,1)S(1)}, u32[]{:S(2)}, u32[]{:S(2)}) collective-permute-start(bf16[640,3,128]{2,0,1:T(8,128)(2,1)S(1)} %slice.51), channel_id=1, source_target_pairs={{0,48},{16,0},{32,16},{48,32},{1,49},{17,1},{33,17},{49,33},{2,50}... | collective-permute-start | bytes 1474568 | tf_op jit(solution)/shard_map/ppermute | solution.py:36
  161.0 7.1 %collective-permute-start.16 = (bf16[1,640,3,256]{3,1,2,0:T(8,128)(2,1)S(1)}, bf16[1,640,3,256]{3,1,2,0:T(8,128)(2,1)S(1)}, u32[]{:S(2)}, u32[]{:S(2)}) collective-permute-start(bf16[1,640,3,256]{3,1,2,0:T(8,128)(2,1)S(1)} %collective-permute-done.15), channel_id=1, source_target_pairs={{0,1},{1,0},{2,3},{3,2},{4,5},{5,4},{6,7},{7,6},{8,9},{9,8},{10,11... | collective-permute-start | bytes 2949128 | tf_op jit(solution)/shard_map/ppermute | solution.py:20
  162.7 7.4 %collective-permute-start.18 = (bf16[1,640,3,256]{3,1,2,0:T(8,128)(2,1)S(1)}, bf16[1,640,3,256]{3,1,2,0:T(8,128)(2,1)S(1)}, u32[]{:S(2)}, u32[]{:S(2)}) collective-permute-start(bf16[1,640,3,256]{3,1,2,0:T(8,128)(2,1)S(1)} %collective-permute-done.17), channel_id=1, source_target_pairs={{0,1},{1,0},{2,3},{3,2},{4,5},{5,4},{6,7},{7,6},{8,9},{9,8},{10,11... | collective-permute-start | bytes 2949128 | tf_op jit(solution)/shard_map/ppermute | solution.py:20

commit v9 on v6

--- a/solution.py
+++ b/solution.py
@@ -46,32 +46,38 @@
     cols_b = nvir // n_col
     row_index = lax.axis_index("zl") * n_y + lax.axis_index("y")
     col_index = (lax.axis_index("x") * n_zh + lax.axis_index("zh")) * n_core + lax.axis_index("core")
-    spread_a = lax.all_to_all(
-        factors.reshape(local_aux, nocc, n_row, rows_a), ("zl", "y"), split_axis=2, concat_axis=0, tiled=True
-    )
-    spread_a = spread_a.reshape(n_row * local_aux, nocc, rows_a)
-    other_a = lax.ppermute(spread_a, "zh", [(k, (k + 1) % n_zh) for k in range(n_zh)])
-    spread_b = lax.all_to_all(
-        factors.reshape(local_aux, nocc, n_col, cols_b), ("x", "zh", "core"), split_axis=2, concat_axis=0, tiled=True
-    )
-    other_a, spread_b = lax.optimization_barrier((other_a, spread_b))
-    first_zh = lax.axis_index("zh") == 0
-    pair_a = jnp.where(first_zh, jnp.stack([spread_a, other_a]), jnp.stack([other_a, spread_a]))
-    block_a = lax.all_gather(pair_a, ("x", "core"), axis=0, tiled=True)
-    spread_b = spread_b.reshape(n_col * local_aux, nocc, cols_b)
-    other_b = lax.ppermute(spread_b, "zl", [(k, (k + 1) % n_zl) for k in range(n_zl)])
-    me_zl = lax.axis_index("zl")
-    block_b = jnp.zeros((n_zl, n_y) + spread_b.shape, spread_b.dtype)
-    block_b = ring_into(block_b, me_zl, spread_b, "y")
-    block_b = ring_into(block_b, (me_zl + 1) % n_zl, other_b, "y")
-    block_a = block_a.reshape(n_x, n_core, n_zh, n_zl, n_y, local_aux, nocc, rows_a)
-    block_b = block_b.reshape(n_zl, n_y, n_x, n_zh, n_core, local_aux, nocc, cols_b)
-    gram = jnp.einsum(
-        "xchzypia,zyxhcpjb->ijab",
-        block_a,
-        block_b,
-        preferred_element_type=jnp.float32,
-    ).reshape(nocc * nocc, rows_a, cols_b)
+    n_chunks = 2
+    chunk = local_aux // n_chunks
+    gram = None
+    for c in range(n_chunks):
+        part = lax.slice_in_dim(factors, c * chunk, (c + 1) * chunk, axis=0)
+        spread_a = lax.all_to_all(
+            part.reshape(chunk, nocc, n_row, rows_a), ("zl", "y"), split_axis=2, concat_axis=0, tiled=True
+        )
+        spread_a = spread_a.reshape(n_row * chunk, nocc, rows_a)
+        other_a = lax.ppermute(spread_a, "zh", [(k, (k + 1) % n_zh) for k in range(n_zh)])
+        spread_b = lax.all_to_all(
+            part.reshape(chunk, nocc, n_col, cols_b), ("x", "zh", "core"), split_axis=2, concat_axis=0, tiled=True
+        )
+        other_a, spread_b = lax.optimization_barrier((other_a, spread_b))
+        first_zh = lax.axis_index("zh") == 0
+        pair_a = jnp.where(first_zh, jnp.stack([spread_a, other_a]), jnp.stack([other_a, spread_a]))
+        block_a = lax.all_gather(pair_a, ("x", "core"), axis=0, tiled=True)
+        spread_b = spread_b.reshape(n_col * chunk, nocc, cols_b)
+        other_b = lax.ppermute(spread_b, "zl", [(k, (k + 1) % n_zl) for k in range(n_zl)])
+        me_zl = lax.axis_index("zl")
+        block_b = jnp.zeros((n_zl, n_y) + spread_b.shape, spread_b.dtype)
+        block_b = ring_into(block_b, me_zl, spread_b, "y")
+        block_b = ring_into(block_b, (me_zl + 1) % n_zl, other_b, "y")
+        block_a = block_a.reshape(n_x, n_core, n_zh, n_zl, n_y, chunk, nocc, rows_a)
+        block_b = block_b.reshape(n_zl, n_y, n_x, n_zh, n_core, chunk, nocc, cols_b)
+        piece = jnp.einsum(
+            "xchzypia,zyxhcpjb->ijab",
+            block_a,
+            block_b,
+            preferred_element_type=jnp.float32,
+        ).reshape(nocc * nocc, rows_a, cols_b)
+        gram = piece if gram is None else gram + piece
     first = pair_list[:, 0]
     second = pair_list[:, 1]
     kernel = jnp.take(gram, first * nocc + second, axis=0)

time: 170 us -> 182 us (1.071)
  waiting for transfers between devices: 71.3 us -> 39.5 us
  blocking collectives: 20.5 us -> 47.5 us
  starting transfers between devices: 20.7 us -> 29.2 us
  local copies, waits for them, and re-layouts: 24.6 us -> 29.3 us
  matrix products: 11.8 us -> 15.4 us
    all_to_all x1 -> x3, blocking collectives: 20.5 us -> 47.5 us  [the longest x2 26.3 us: shards(): lax.all_to_all(part.reshape(chunk, nocc, n_row, rows_a), ('zl', 'y'), spl...]
    all_to_all x1, waiting for transfers between devices: 24 us -> 10.9 us  [shards(): lax.all_to_all(part.reshape(chunk, nocc, n_col, cols_b), ('x', 'zh', 'cor...]
    ppermute x2 -> x4, waiting for transfers between devices: 33.2 us -> 22.5 us  [ring_into(): go_right = lax.ppermute(go_right, axis, right)]
    ppermute x2 -> x4, waiting for transfers between devices: 13.5 us -> 3.4 us  [ring_into(): from_left = lax.ppermute(go_right[:half], axis, right)]
    dynamic_update_slice x10 -> x20, local copies, waits for them, and re-layouts: 9.68 us -> 15.9 us  [put(): return lax.dynamic_update_slice(buf, piece[None, None], start)]
    broadcast_in_dim x1 -> x0, local copies, waits for them, and re-layouts: 5.83 us -> none  [shards(): block_b = jnp.zeros((n_zl, n_y) + spread_b.shape, spread_b.dtype)]
    another operation x0 -> x2, local copies, waits for them, and re-layouts: none -> 5.48 us
    ppermute x2 -> x4, starting transfers between devices: 5.15 us -> 10.1 us  [ring_into(): go_left = lax.ppermute(go_left, axis, left)]
  transfers between devices with their start and end apart: 12 -> 23, of which waited for: 6 -> 10; matrix products, arithmetic and copies ran while one was open for 14% -> 21% of each run, Pallas kernels for 0% -> 0%
where the time goes in v9:
time: 182 us; the launch traced here: 181 us
  blocking collectives  47.5 us (26%)
  waiting for transfers between devices  39.5 us (22%)
  local copies, waits for them, and re-layouts  29.3 us (16%)
  starting transfers between devices  29.2 us (16%)
  matrix products  15.4 us (8%)
  between operations  13.8 us (8%)
  other arithmetic  6.15 us (3%)
    all_to_all x2, blocking collectives, shards(): lax.all_to_all(part.reshape(chunk, nocc, n_row, rows_a), ('zl', 'y'), spl...  26.3 us
    ppermute x4, waiting for transfers between devices, ring_into(): go_right = lax.ppermute(go_right, axis, right)  22.5 us
    all_to_all x1, blocking collectives, shards(): lax.all_to_all(part.reshape(chunk, nocc, n_col, cols_b), ('x', 'zh', 'cor...  21.1 us
    dynamic_update_slice x20, local copies, waits for them, and re-layouts, put(): return lax.dynamic_update_slice(buf, piece[None, None], start)  15.9 us
    dot_general x2, matrix products, shards(): jnp.einsum('xchzypia,zyxhcpjb->ijab', block_a, block_b, preferred_element...  15.4 us
    all_to_all x1, waiting for transfers between devices, shards(): lax.all_to_all(part.reshape(chunk, nocc, n_col, cols_b), ('x', 'zh', 'cor...  10.9 us
    ppermute x4, starting transfers between devices, ring_into(): go_left = lax.ppermute(go_left, axis, left)  10.1 us
    all_to_all x1, starting transfers between devices, shards(): lax.all_to_all(part.reshape(chunk, nocc, n_col, cols_b), ('x', 'zh', 'cor...  6.31 us
  transfers between devices with their start and end apart: 23, of which 10 were waited for; matrix products, arithmetic and copies ran while one was open for 21% of the time, Pallas kernels for 0%

profile of v9, /device:TPU:1, one launch (start us, length us, event | category | flops | bytes accessed | tf_op | source)
XLA Modules:
  0.0 180.8 jit_solution(13211661255176621854)
XLA Ops:
  6.5 1.4 slice_bitcast_fusion.1
  8.0 15.1 %all_to_all.66 = bf16[40,3,8,256]{3,0,1,2:T(8,128)(2,1)S(1)} all-to-all(bf16[40,3,8,256]{3,0,1,2:T(8,128)(2,1)S(1)} %bitcast.138), channel_id=1, replica_groups=mesh['zl'=2,'y'=4,'x'=4,'zh'=2,'core'=2] {'zl','y'}, dimensions={2} | all-to-all | bytes 983040 | tf_op jit(solution)/shard_map/all_to_all | solution.py:54
  23.1 3.4 %collective-permute-start.10 = (bf16[320,3,256]{2,0,1:T(8,128)(2,1)S(1)}, bf16[320,3,256]{2,0,1:T(8,128)(2,1)S(1)}, u32[]{:S(2)}, u32[]{:S(2)}) collective-permute-start(bf16[320,3,256]{2,0,1:T(8,128)(2,1)S(1)} %bitcast.133), channel_id=1, source_target_pairs={{0,2},{2,0},{1,3},{3,1},{4,6},{6,4},{5,7},{7,5},{8,10},{10,8},{9,1... | collective-permute-start | bytes 1474568 | tf_op jit(solution)/shard_map/ppermute | solution.py:58
  26.5 0.9 copy.83
  27.4 6.3 %all-to-all-start.3 = ((bf16[40,3,16,128]{3,0,1,2:T(8,128)(2,1)}), bf16[40,3,16,128]{3,0,1,2:T(8,128)(2,1)S(1)}, u32[]{:S(2)}, u32[]{:S(2)}) async-start(bf16[40,3,16,128]{3,0,1,2:T(8,128)(2,1)} %bitcast.119), calls=%async_computation.3 | async-start | bytes 983040 | tf_op jit(solution)/shard_map/all_to_all | solution.py:59
  33.8 10.9 %all-to-all-done.3 = bf16[40,3,16,128]{3,0,1,2:T(8,128)(2,1)S(1)} async-done(((bf16[40,3,16,128]{3,0,1,2:T(8,128)(2,1)}), bf16[40,3,16,128]{3,0,1,2:T(8,128)(2,1)S(1)}, u32[]{:S(2)}, u32[]{:S(2)}) %all-to-all-start.3) | async-done | bytes 491552 | tf_op jit(solution)/shard_map/all_to_all | solution.py:59
  44.7 1.1 maximum_select_fusion.1
  45.9 11.2 %all_to_all.67 = bf16[40,3,8,256]{3,0,1,2:T(8,128)(2,1)S(1)} all-to-all(bf16[40,3,8,256]{3,0,1,2:T(8,128)(2,1)S(1)} %bitcast.139), channel_id=1, replica_groups=mesh['zl'=2,'y'=4,'x'=4,'zh'=2,'core'=2] {'zl','y'}, dimensions={2} | all-to-all | bytes 983040 | tf_op jit(solution)/shard_map/all_to_all | solution.py:54
  57.2 1.4 collective-permute-start
  58.7 21.1 %all_to_all.68 = bf16[40,3,16,128]{3,0,1,2:T(8,128)(2,1)S(1)} all-to-all(bf16[40,3,16,128]{3,0,1,2:T(8,128)(2,1)S(1)} %bitcast.140), channel_id=1, replica_groups=mesh['zl'=2,'y'=4,'x'=4,'zh'=2,'core'=2] {'x','zh','core'}, dimensions={2} | all-to-all | bytes 983040 | tf_op jit(solution)/shard_map/all_to_all | solution.py:59
  79.9 1.1 maximum_select_fusion
  81.1 0.8 dynamic_slice.6
  81.9 0.8 dynamic_slice.7
  82.6 0.7 fusion.28
  83.3 1.9 %fusion.26 = (s32[16]{0:T(128)S(1)}, s32[16]{0:T(128)S(1)}) fusion(s32[16,2]{0,1:T(2,128)S(1)} %copy-done.3, s32[]{:T(128)} %bitcast.58, s32[]{:T(128)} %bitcast.60, s32[]{:T(128)} %bitcast.59), kind=kLoop, calls=%fused_computation.57 | loop fusion | flops 320 | bytes 268 | tf_op jit(solution)/shard_map/select_n | solution.py:86
  85.2 0.7 gather_fusion.1
  85.9 0.7 gather_fusion.2
  86.6 0.7 gather_fusion.3
  87.4 0.6 collective-permute-start.1
  88.0 2.1 %collective-permute-start.2 = (bf16[640,3,128]{2,0,1:T(8,128)(2,1)S(1)}, bf16[640,3,128]{2,0,1:T(8,128)(2,1)S(1)}, u32[]{:S(2)}, u32[]{:S(2)}) collective-permute-start(bf16[640,3,128]{2,0,1:T(8,128)(2,1)S(1)} %bitcast.129), channel_id=1, source_target_pairs={{0,48},{16,0},{32,16},{48,32},{1,49},{17,1},{33,17},{49,33},{2,50}... | collective-permute-start | bytes 1474568 | tf_op jit(solution)/shard_map/ppermute | solution.py:24
  90.4 2.7 %collective-permute-start.12 = (bf16[640,3,128]{2,0,1:T(8,128)(2,1)S(1)}, bf16[640,3,128]{2,0,1:T(8,128)(2,1)S(1)}, u32[]{:S(2)}, u32[]{:S(2)}) collective-permute-start(bf16[640,3,128]{2,0,1:T(8,128)(2,1)S(1)} %bitcast.125), channel_id=1, source_target_pairs={{0,48},{16,0},{32,16},{48,32},{1,49},{17,1},{33,17},{49,33},{2,50}... | collective-permute-start | bytes 1474568 | tf_op jit(solution)/shard_map/ppermute | solution.py:24
  93.1 2.8 %broadcast.94.clone.1 = bf16[2,4,640,3,128]{4,2,3,1,0:T(8,128)(2,1)} broadcast(bf16[]{:T(256)} %constant.97.clone.1), dimensions={} | broadcast | bytes 3932162 | tf_op jit(solution)/shard_map/broadcast.17
  95.8 0.8 bitcast_dynamic-update-slice_fusion.11
  96.6 2.7 %broadcast.94.clone = bf16[2,4,640,3,128]{4,2,3,1,0:T(8,128)(2,1)} broadcast(bf16[]{:T(256)} %constant.97.clone.1), dimensions={} | broadcast | bytes 3932162 | tf_op jit(solution)/shard_map/broadcast.17
  99.4 0.8 bitcast_dynamic-update-slice_fusion.5
  100.2 1.1 collective-permute-done.1
  101.3 0.3 collective-permute-start.15
  101.8 0.8 bitcast_dynamic-update-slice_fusion.10
  102.6 0.8 bitcast_dynamic-update-slice_fusion.9
  103.4 8.4 %collective-permute-done.11 = bf16[640,3,128]{2,0,1:T(8,128)(2,1)S(1)} collective-permute-done((bf16[640,3,128]{2,0,1:T(8,128)(2,1)S(1)}, bf16[640,3,128]{2,0,1:T(8,128)(2,1)S(1)}, u32[]{:S(2)}, u32[]{:S(2)}) %collective-permute-start.11) | collective-permute-done | bytes 491552 | tf_op jit(solution)/shard_map/ppermute | solution.py:23
  111.9 0.8 bitcast_dynamic-update-slice_fusion.4
  112.7 1.5 collective-permute-start.13
  114.3 0.8 bitcast_dynamic-update-slice_fusion.3
  115.1 1.3 collective-permute-start.14
  116.4 0.8 collective-permute-done.3
  117.2 0.8 bitcast_dynamic-update-slice_fusion.19
  118.0 2.7 %collective-permute-start.7 = (bf16[640,3,128]{2,0,1:T(8,128)(2,1)S(1)}, bf16[640,3,128]{2,0,1:T(8,128)(2,1)S(1)}, u32[]{:S(2)}, u32[]{:S(2)}) collective-permute-start(bf16[640,3,128]{2,0,1:T(8,128)(2,1)S(1)} %collective-permute-done.5), channel_id=1, source_target_pairs={{0,48},{16,0},{32,16},{48,32},{1,49},{17,1},{33,17},{49,33},{2,50}... | collective-permute-start | bytes 1474568 | tf_op jit(solution)/shard_map/ppermute | solution.py:24
  120.7 0.8 bitcast_dynamic-update-slice_fusion.18
  121.4 0.8 bitcast_dynamic-update-slice_fusion.8
  122.3 2.6 %collective-permute-start.17 = (bf16[640,3,128]{2,0,1:T(8,128)(2,1)S(1)}, bf16[640,3,128]{2,0,1:T(8,128)(2,1)S(1)}, u32[]{:S(2)}, u32[]{:S(2)}) collective-permute-start(bf16[640,3,128]{2,0,1:T(8,128)(2,1)S(1)} %collective-permute-done.15), channel_id=1, source_target_pairs={{0,48},{16,0},{32,16},{48,32},{1,49},{17,1},{33,17},{49,33},{2,50}... | collective-permute-start | bytes 1474568 | tf_op jit(solution)/shard_map/ppermute | solution.py:24
  124.9 0.7 bitcast_dynamic-update-slice_fusion.15
  125.6 0.8 bitcast_dynamic-update-slice_fusion.14
  126.4 0.8 bitcast_dynamic-update-slice_fusion.2
  127.2 5.3 %collective-permute-done.6 = bf16[640,3,128]{2,0,1:T(8,128)(2,1)S(1)} collective-permute-done((bf16[640,3,128]{2,0,1:T(8,128)(2,1)S(1)}, bf16[640,3,128]{2,0,1:T(8,128)(2,1)S(1)}, u32[]{:S(2)}, u32[]{:S(2)}) %collective-permute-start.6) | collective-permute-done | bytes 491552 | tf_op jit(solution)/shard_map/ppermute | solution.py:23
  132.7 1.1 collective-permute-done.7
  133.8 1.7 collective-permute-start.9
  135.5 7.6 %collective-permute-done.16 = bf16[640,3,128]{2,0,1:T(8,128)(2,1)S(1)} collective-permute-done((bf16[640,3,128]{2,0,1:T(8,128)(2,1)S(1)}, bf16[640,3,128]{2,0,1:T(8,128)(2,1)S(1)}, u32[]{:S(2)}, u32[]{:S(2)}) %collective-permute-start.16) | collective-permute-done | bytes 491552 | tf_op jit(solution)/shard_map/ppermute | solution.py:23
  143.2 1.1 collective-permute-done.17
  144.3 1.9 %collective-permute-start.19 = (bf16[320,3,128]{2,0,1:T(8,128)(2,1)S(1)}, bf16[320,3,128]{2,0,1:T(8,128)(2,1)S(1)}, u32[]{:S(2)}, u32[]{:S(2)}) collective-permute-start(bf16[320,3,128]{2,0,1:T(8,128)(2,1)S(1)} %slice.71), channel_id=1, source_target_pairs={{0,48},{16,0},{32,16},{48,32},{1,49},{17,1},{33,17},{49,33},{2,50}... | collective-permute-start | bytes 737288 | tf_op jit(solution)/shard_map/ppermute | solution.py:30
  146.2 0.8 bitcast_dynamic-update-slice_fusion.7
  147.0 0.8 bitcast_dynamic-update-slice_fusion.6
  147.8 0.8 bitcast_dynamic-update-slice_fusion.1
  148.6 0.8 bitcast_dynamic-update-slice_fusion
  149.5 0.8 bitcast_dynamic-update-slice_fusion.17
  150.2 0.8 bitcast_dynamic-update-slice_fusion.16
  151.0 2.6 %collective-permute-done.18 = bf16[320,3,128]{2,0,1:T(8,128)(2,1)S(1)} collective-permute-done((bf16[320,3,128]{2,0,1:T(8,128)(2,1)S(1)}, bf16[320,3,128]{2,0,1:T(8,128)(2,1)S(1)}, u32[]{:S(2)}, u32[]{:S(2)}) %collective-permute-start.18) | collective-permute-done | bytes 245792 | tf_op jit(solution)/shard_map/ppermute | solution.py:29
  153.5 0.8 bitcast_dynamic-update-slice_fusion.13
  154.3 0.4 collective-permute-done.19
  154.7 0.8 bitcast_dynamic-update-slice_fusion.12
  155.5 7.7 %fusion.11 = f32[3,128,3,256]{3,1,2,0:T(8,128)S(1)} fusion(bf16[4,2,2,2,4,40,3,256,1]{7,5,4,3,6,2,1,0,8:T(8,128)(2,1)} %bitcast.144, bf16[2,4,4,2,2,40,3,128,1]{7,5,4,3,2,6,1,0,8:T(8,128)(2,1)} %bitcast.46), kind=kOutput, calls=%fused_computation.12 | convolution fusion | flops 3019898880 | bytes 12976128 | tf_op jit(solution)/shard_map/xchzypia,zyxhcpjb->ijab/dot_general | solution.py:74
  163.2 7.7 %fusion.21 = f32[3,3,256,128]{2,3,0,1:T(8,128)S(1)} fusion(f32[3,128,3,256]{3,1,2,0:T(8,128)S(1)} %fusion.11, bf16[4,2,2,2,4,40,3,256,1]{7,5,4,3,6,2,1,0,8:T(8,128)(2,1)} %bitcast.145, bf16[2,4,4,2,2,40,3,128,1]{7,5,4,3,2,6,1,0,8:T(8,128)(2,1)} %bitcast.19), kind=kOutput, calls=%fused_computation.14 | convolution fusion | flops 3020193792 | bytes 14155776 | tf_op jit(solution)/shard_map/xchzypia,zyxhcpjb->ijab/dot_general | solution.py:74
  170.9 0.4 copy.36
  171.3 0.7 gather_fusion
  172.0 1.9 %add_divide_fusion = f32[16,256,128]{2,1,0:T(8,128)} fusion(f32[16,256,128]{2,1,0:T(8,128)S(1)} %gather_fusion, f32[16]{0:T(128)S(1)} %gather_fusion.3, f32[16]{0:T(128)S(1)} %gather_fusion.2, f32[16]{0:T(128)S(1)} %gather_fusion.1, f32[256,128]{1,0:T(8,128)S(1)} %broadcast_add_fusion, pred[16]{0:T(512)(128)(4,1)S(1)} %get-tuple-element.13), kind=kLoop, calls=%fused_computation.10 | loop fusion | flops 3145728 | bytes 4325584 | tf_op jit(solution)/shard_map/div | solution.py:95
  (56 shorter events, 1.3 us)
Async XLA Ops:
  6.5 78.6 %copy-start = (f32[300]{0:T(512)S(1)}, f32[300]{0:T(512)}, u32[]{:S(2)}) copy-start(f32[300]{0:T(512)} %param.8) | copy-start | bytes 3604
  23.1 21.6 %collective-permute-start.10 = (bf16[320,3,256]{2,0,1:T(8,128)(2,1)S(1)}, bf16[320,3,256]{2,0,1:T(8,128)(2,1)S(1)}, u32[]{:S(2)}, u32[]{:S(2)}) collective-permute-start(bf16[320,3,256]{2,0,1:T(8,128)(2,1)S(1)} %bitcast.133), channel_id=1, source_target_pairs={{0,2},{2,0},{1,3},{3,1},{4,6},{6,4},{5,7},{7,5},{8,10},{10,8},{9,1... | collective-permute-start | bytes 1474568 | tf_op jit(solution)/shard_map/ppermute | solution.py:58
  27.4 17.3 %all-to-all-start.3 = ((bf16[40,3,16,128]{3,0,1,2:T(8,128)(2,1)}), bf16[40,3,16,128]{3,0,1,2:T(8,128)(2,1)S(1)}, u32[]{:S(2)}, u32[]{:S(2)}) async-start(bf16[40,3,16,128]{3,0,1,2:T(8,128)(2,1)} %bitcast.119), calls=%async_computation.3 | async-start | bytes 983040 | tf_op jit(solution)/shard_map/all_to_all | solution.py:59
  33.7 121.8 %all-gather.5.cloned.1.call-start = ((), (), s32[]{:S(2)}) async-start(), calls=%async_computation.5 | async-start | bytes 8847360 | tf_op jit(solution)/shard_map/all_gather | solution.py:65
  45.8 117.4 %all-gather.3.cloned.1.call-start = ((), (), s32[]{:S(2)}) async-start(), calls=%async_computation.4 | async-start | bytes 8847360 | tf_op jit(solution)/shard_map/all_gather | solution.py:65
  45.9 36.7 %copy-start.2 = (s32[3]{0:T(128)S(1)}, s32[3]{0:T(128)}, u32[]{:S(2)}) copy-start(s32[3]{0:T(128)} %param.10) | copy-start | bytes 40
  45.9 37.4 %copy-start.3 = (s32[16,2]{0,1:T(2,128)S(1)}, s32[16,2]{0,1:T(2,128)}, u32[]{:S(2)}) copy-start(s32[16,2]{0,1:T(2,128)} %param.11) | copy-start | bytes 388
  57.1 29.4 %copy-start.4 = (s32[16]{0:T(128)S(1)}, s32[16]{0:T(128)}, u32[]{:S(2)}) copy-start(s32[16]{0:T(128)} %param.12) | copy-start | bytes 196
  57.1 29.4 %copy-start.1 = (f32[4]{0:T(128)S(1)}, f32[4]{0:T(128)}, u32[]{:S(2)}) copy-start(f32[4]{0:T(128)} %param.13) | copy-start | bytes 52
  57.2 22.7 %collective-permute-start = (bf16[320,3,256]{2,0,1:T(8,128)(2,1)S(1)}, bf16[320,3,256]{2,0,1:T(8,128)(2,1)S(1)}, u32[]{:S(2)}, u32[]{:S(2)}) collective-permute-start(bf16[320,3,256]{2,0,1:T(8,128)(2,1)S(1)} %bitcast.135), channel_id=1, source_target_pairs={{0,2},{2,0},{1,3},{3,1},{4,6},{6,4},{5,7},{7,5},{8,10},{10,8},{9,1... | collective-permute-start | bytes 1474568 | tf_op jit(solution)/shard_map/ppermute | solution.py:58
  87.4 14.0 %collective-permute-start.1 = (bf16[640,3,128]{2,0,1:T(8,128)(2,1)S(1)}, bf16[640,3,128]{2,0,1:T(8,128)(2,1)S(1)}, u32[]{:S(2)}, u32[]{:S(2)}) collective-permute-start(bf16[640,3,128]{2,0,1:T(8,128)(2,1)S(1)} %bitcast.128), channel_id=1, source_target_pairs={{0,16},{16,32},{32,48},{48,0},{1,17},{17,33},{33,49},{49,1},{2,18}... | collective-permute-start | bytes 1474568 | tf_op jit(solution)/shard_map/ppermute | solution.py:23
  88.0 13.6 %collective-permute-start.2 = (bf16[640,3,128]{2,0,1:T(8,128)(2,1)S(1)}, bf16[640,3,128]{2,0,1:T(8,128)(2,1)S(1)}, u32[]{:S(2)}, u32[]{:S(2)}) collective-permute-start(bf16[640,3,128]{2,0,1:T(8,128)(2,1)S(1)} %bitcast.129), channel_id=1, source_target_pairs={{0,48},{16,0},{32,16},{48,32},{1,49},{17,1},{33,17},{49,33},{2,50}... | collective-permute-start | bytes 1474568 | tf_op jit(solution)/shard_map/ppermute | solution.py:24
  90.1 25.0 %collective-permute-start.5 = (bf16[640,3,128]{2,0,1:T(8,128)(2,1)S(1)}, bf16[640,3,128]{2,0,1:T(8,128)(2,1)S(1)}, u32[]{:S(2)}, u32[]{:S(2)}) collective-permute-start(bf16[640,3,128]{2,0,1:T(8,128)(2,1)S(1)} %bitcast.130), channel_id=1, source_target_pairs={{0,64},{64,0},{1,65},{65,1},{2,66},{66,2},{3,67},{67,3},{4,68},{68... | collective-permute-start | bytes 1474568 | tf_op jit(solution)/shard_map/ppermute | solution.py:67
  90.4 21.4 %collective-permute-start.11 = (bf16[640,3,128]{2,0,1:T(8,128)(2,1)S(1)}, bf16[640,3,128]{2,0,1:T(8,128)(2,1)S(1)}, u32[]{:S(2)}, u32[]{:S(2)}) collective-permute-start(bf16[640,3,128]{2,0,1:T(8,128)(2,1)S(1)} %bitcast.124), channel_id=1, source_target_pairs={{0,16},{16,32},{32,48},{48,0},{1,17},{17,33},{33,49},{49,1},{2,18}... | collective-permute-start | bytes 1474568 | tf_op jit(solution)/shard_map/ppermute | solution.py:23
  90.4 22.3 %collective-permute-start.12 = (bf16[640,3,128]{2,0,1:T(8,128)(2,1)S(1)}, bf16[640,3,128]{2,0,1:T(8,128)(2,1)S(1)}, u32[]{:S(2)}, u32[]{:S(2)}) collective-permute-start(bf16[640,3,128]{2,0,1:T(8,128)(2,1)S(1)} %bitcast.125), channel_id=1, source_target_pairs={{0,48},{16,0},{32,16},{48,32},{1,49},{17,1},{33,17},{49,33},{2,50}... | collective-permute-start | bytes 1474568 | tf_op jit(solution)/shard_map/ppermute | solution.py:24
  101.3 16.7 %collective-permute-start.15 = (bf16[640,3,128]{2,0,1:T(8,128)(2,1)S(1)}, bf16[640,3,128]{2,0,1:T(8,128)(2,1)S(1)}, u32[]{:S(2)}, u32[]{:S(2)}) collective-permute-start(bf16[640,3,128]{2,0,1:T(8,128)(2,1)S(1)} %bitcast.127), channel_id=1, source_target_pairs={{0,64},{64,0},{1,65},{65,1},{2,66},{66,2},{3,67},{67,3},{4,68},{68... | collective-permute-start | bytes 1474568 | tf_op jit(solution)/shard_map/ppermute | solution.py:67
  101.7 15.6 %collective-permute-start.3 = (bf16[320,3,128]{2,0,1:T(8,128)(2,1)S(1)}, bf16[320,3,128]{2,0,1:T(8,128)(2,1)S(1)}, u32[]{:S(2)}, u32[]{:S(2)}) collective-permute-start(bf16[320,3,128]{2,0,1:T(8,128)(2,1)S(1)} %slice.64), channel_id=1, source_target_pairs={{0,16},{16,32},{32,48},{48,0},{1,17},{17,33},{33,49},{49,1},{2,18}... | collective-permute-start | bytes 737288 | tf_op jit(solution)/shard_map/ppermute | solution.py:29
  111.9 8.8 %collective-permute-start.4 = (bf16[320,3,128]{2,0,1:T(8,128)(2,1)S(1)}, bf16[320,3,128]{2,0,1:T(8,128)(2,1)S(1)}, u32[]{:S(2)}, u32[]{:S(2)}) collective-permute-start(bf16[320,3,128]{2,0,1:T(8,128)(2,1)S(1)} %slice.65), channel_id=1, source_target_pairs={{0,48},{16,0},{32,16},{48,32},{1,49},{17,1},{33,17},{49,33},{2,50}... | collective-permute-start | bytes 737288 | tf_op jit(solution)/shard_map/ppermute | solution.py:30
  112.7 9.5 %collective-permute-start.13 = (bf16[320,3,128]{2,0,1:T(8,128)(2,1)S(1)}, bf16[320,3,128]{2,0,1:T(8,128)(2,1)S(1)}, u32[]{:S(2)}, u32[]{:S(2)}) collective-permute-start(bf16[320,3,128]{2,0,1:T(8,128)(2,1)S(1)} %slice.68), channel_id=1, source_target_pairs={{0,16},{16,32},{32,48},{48,0},{1,17},{17,33},{33,49},{49,1},{2,18}... | collective-permute-start | bytes 737288 | tf_op jit(solution)/shard_map/ppermute | solution.py:29
  115.1 10.6 %collective-permute-start.14 = (bf16[320,3,128]{2,0,1:T(8,128)(2,1)S(1)}, bf16[320,3,128]{2,0,1:T(8,128)(2,1)S(1)}, u32[]{:S(2)}, u32[]{:S(2)}) collective-permute-start(bf16[320,3,128]{2,0,1:T(8,128)(2,1)S(1)} %slice.69), channel_id=1, source_target_pairs={{0,48},{16,0},{32,16},{48,32},{1,49},{17,1},{33,17},{49,33},{2,50}... | collective-permute-start | bytes 737288 | tf_op jit(solution)/shard_map/ppermute | solution.py:30
  117.2 15.4 %collective-permute-start.6 = (bf16[640,3,128]{2,0,1:T(8,128)(2,1)S(1)}, bf16[640,3,128]{2,0,1:T(8,128)(2,1)S(1)}, u32[]{:S(2)}, u32[]{:S(2)}) collective-permute-start(bf16[640,3,128]{2,0,1:T(8,128)(2,1)S(1)} %collective-permute-done.5), channel_id=1, source_target_pairs={{0,16},{16,32},{32,48},{48,0},{1,17},{17,33},{33,49},{49,1},{2,18}... | collective-permute-start | bytes 1474568 | tf_op jit(solution)/shard_map/ppermute | solution.py:23
  118.0 15.8 %collective-permute-start.7 = (bf16[640,3,128]{2,0,1:T(8,128)(2,1)S(1)}, bf16[640,3,128]{2,0,1:T(8,128)(2,1)S(1)}, u32[]{:S(2)}, u32[]{:S(2)}) collective-permute-start(bf16[640,3,128]{2,0,1:T(8,128)(2,1)S(1)} %collective-permute-done.5), channel_id=1, source_target_pairs={{0,48},{16,0},{32,16},{48,32},{1,49},{17,1},{33,17},{49,33},{2,50}... | collective-permute-start | bytes 1474568 | tf_op jit(solution)/shard_map/ppermute | solution.py:24
  120.7 22.5 %collective-permute-start.16 = (bf16[640,3,128]{2,0,1:T(8,128)(2,1)S(1)}, bf16[640,3,128]{2,0,1:T(8,128)(2,1)S(1)}, u32[]{:S(2)}, u32[]{:S(2)}) collective-permute-start(bf16[640,3,128]{2,0,1:T(8,128)(2,1)S(1)} %collective-permute-done.15), channel_id=1, source_target_pairs={{0,16},{16,32},{32,48},{48,0},{1,17},{17,33},{33,49},{49,1},{2,18}... | collective-permute-start | bytes 1474568 | tf_op jit(solution)/shard_map/ppermute | solution.py:23
  122.3 22.0 %collective-permute-start.17 = (bf16[640,3,128]{2,0,1:T(8,128)(2,1)S(1)}, bf16[640,3,128]{2,0,1:T(8,128)(2,1)S(1)}, u32[]{:S(2)}, u32[]{:S(2)}) collective-permute-start(bf16[640,3,128]{2,0,1:T(8,128)(2,1)S(1)} %collective-permute-done.15), channel_id=1, source_target_pairs={{0,48},{16,0},{32,16},{48,32},{1,49},{17,1},{33,17},{49,33},{2,50}... | collective-permute-start | bytes 1474568 | tf_op jit(solution)/shard_map/ppermute | solution.py:24
  132.6 16.8 %collective-permute-start.8 = (bf16[320,3,128]{2,0,1:T(8,128)(2,1)S(1)}, bf16[320,3,128]{2,0,1:T(8,128)(2,1)S(1)}, u32[]{:S(2)}, u32[]{:S(2)}) collective-permute-start(bf16[320,3,128]{2,0,1:T(8,128)(2,1)S(1)} %slice.66), channel_id=1, source_target_pairs={{0,16},{16,32},{32,48},{48,0},{1,17},{17,33},{33,49},{49,1},{2,18}... | collective-permute-start | bytes 737288 | tf_op jit(solution)/shard_map/ppermute | solution.py:29
  133.8 16.4 %collective-permute-start.9 = (bf16[320,3,128]{2,0,1:T(8,128)(2,1)S(1)}, bf16[320,3,128]{2,0,1:T(8,128)(2,1)S(1)}, u32[]{:S(2)}, u32[]{:S(2)}) collective-permute-start(bf16[320,3,128]{2,0,1:T(8,128)(2,1)S(1)} %slice.67), channel_id=1, source_target_pairs={{0,48},{16,0},{32,16},{48,32},{1,49},{17,1},{33,17},{49,33},{2,50}... | collective-permute-start | bytes 737288 | tf_op jit(solution)/shard_map/ppermute | solution.py:30
  143.1 10.4 %collective-permute-start.18 = (bf16[320,3,128]{2,0,1:T(8,128)(2,1)S(1)}, bf16[320,3,128]{2,0,1:T(8,128)(2,1)S(1)}, u32[]{:S(2)}, u32[]{:S(2)}) collective-permute-start(bf16[320,3,128]{2,0,1:T(8,128)(2,1)S(1)} %slice.70), channel_id=1, source_target_pairs={{0,16},{16,32},{32,48},{48,0},{1,17},{17,33},{33,49},{49,1},{2,18}... | collective-permute-start | bytes 737288 | tf_op jit(solution)/shard_map/ppermute | solution.py:29
  144.3 10.4 %collective-permute-start.19 = (bf16[320,3,128]{2,0,1:T(8,128)(2,1)S(1)}, bf16[320,3,128]{2,0,1:T(8,128)(2,1)S(1)}, u32[]{:S(2)}, u32[]{:S(2)}) collective-permute-start(bf16[320,3,128]{2,0,1:T(8,128)(2,1)S(1)} %slice.71), channel_id=1, source_target_pairs={{0,48},{16,0},{32,16},{48,32},{1,49},{17,1},{33,17},{49,33},{2,50}... | collective-permute-start | bytes 737288 | tf_op jit(solution)/shard_map/ppermute | solution.py:30
Sparse Core Ops, SparseCore 0:
  45.9 51.0 all-gather.4
  98.7 47.5 all-gather.2

commit v10 on v6

--- a/solution.py
+++ b/solution.py
@@ -50,24 +50,20 @@
         factors.reshape(local_aux, nocc, n_row, rows_a), ("zl", "y"), split_axis=2, concat_axis=0, tiled=True
     )
     spread_a = spread_a.reshape(n_row * local_aux, nocc, rows_a)
-    other_a = lax.ppermute(spread_a, "zh", [(k, (k + 1) % n_zh) for k in range(n_zh)])
+    block_a = lax.all_gather(spread_a, ("x", "zh", "core"), axis=0, tiled=True)
     spread_b = lax.all_to_all(
         factors.reshape(local_aux, nocc, n_col, cols_b), ("x", "zh", "core"), split_axis=2, concat_axis=0, tiled=True
     )
-    other_a, spread_b = lax.optimization_barrier((other_a, spread_b))
-    first_zh = lax.axis_index("zh") == 0
-    pair_a = jnp.where(first_zh, jnp.stack([spread_a, other_a]), jnp.stack([other_a, spread_a]))
-    block_a = lax.all_gather(pair_a, ("x", "core"), axis=0, tiled=True)
     spread_b = spread_b.reshape(n_col * local_aux, nocc, cols_b)
     other_b = lax.ppermute(spread_b, "zl", [(k, (k + 1) % n_zl) for k in range(n_zl)])
     me_zl = lax.axis_index("zl")
     block_b = jnp.zeros((n_zl, n_y) + spread_b.shape, spread_b.dtype)
     block_b = ring_into(block_b, me_zl, spread_b, "y")
     block_b = ring_into(block_b, (me_zl + 1) % n_zl, other_b, "y")
-    block_a = block_a.reshape(n_x, n_core, n_zh, n_zl, n_y, local_aux, nocc, rows_a)
+    block_a = block_a.reshape(n_x, n_zh, n_core, n_zl, n_y, local_aux, nocc, rows_a)
     block_b = block_b.reshape(n_zl, n_y, n_x, n_zh, n_core, local_aux, nocc, cols_b)
     gram = jnp.einsum(
-        "xchzypia,zyxhcpjb->ijab",
+        "xhczypia,zyxhcpjb->ijab",
         block_a,
         block_b,
         preferred_element_type=jnp.float32,

time: 170 us -> 173 us (1.018)
  waiting for transfers between devices: 71.3 us -> 75.5 us
  other arithmetic: 7.08 us -> 3.87 us
    ppermute x1, waiting for transfers between devices: 0.01 us -> 8.94 us  [shards(): lax.ppermute(spread_b, 'zl', [(k, (k + 1) % n_zl) for k in range(n_zl)])]
    all_gather x1, waiting for transfers between devices: 0.61 us -> 8.86 us  [shards(): block_a = lax.all_gather(spread_a, ('x', 'zh', 'core'), axis=0, tiled=True)]
    ppermute x2, waiting for transfers between devices: 33.2 us -> 27.1 us  [ring_into(): go_right = lax.ppermute(go_right, axis, right)]
    ppermute x2, waiting for transfers between devices: 13.5 us -> 9.23 us  [ring_into(): from_left = lax.ppermute(go_right[:half], axis, right)]
    ppermute x1 -> x0, starting transfers between devices: 3.38 us -> none  [shards(): lax.ppermute(spread_a, 'zh', [(k, (k + 1) % n_zh) for k in range(n_zh)])]
    select_n x1 -> x0, other arithmetic: 3.13 us -> none  [shards(): jnp.where(first_zh, jnp.stack([spread_a, other_a]), jnp.stack([other_a, s...]
    all_to_all x1, starting transfers between devices: 6.23 us -> 8.97 us  [shards(): lax.all_to_all(factors.reshape(local_aux, nocc, n_col, cols_b), ('x', 'zh...]
    all_to_all x1, waiting for transfers between devices: 24 us -> 21.4 us  [shards(): lax.all_to_all(factors.reshape(local_aux, nocc, n_col, cols_b), ('x', 'zh...]
  transfers between devices with their start and end apart: 12 -> 11, of which waited for: 6 -> 6; matrix products, arithmetic and copies ran while one was open for 14% -> 14% of each run, Pallas kernels for 0% -> 0%
where the time goes in v10:
time: 173 us; the launch traced here: 171 us
  waiting for transfers between devices  75.5 us (44%)
  local copies, waits for them, and re-layouts  25.8 us (15%)
  blocking collectives  20.5 us (12%)
  starting transfers between devices  20.4 us (12%)
  between operations  13.7 us (8%)
  matrix products  11.8 us (7%)
  other arithmetic  3.87 us (2%)
    ppermute x2, waiting for transfers between devices, ring_into(): go_right = lax.ppermute(go_right, axis, right)  27.1 us
    all_to_all x1, waiting for transfers between devices, shards(): lax.all_to_all(factors.reshape(local_aux, nocc, n_col, cols_b), ('x', 'zh...  21.4 us
    all_to_all x1, blocking collectives, shards(): lax.all_to_all(factors.reshape(local_aux, nocc, n_row, rows_a), ('zl', 'y...  20.5 us
    dot_general x1, matrix products, shards(): jnp.einsum('xhczypia,zyxhcpjb->ijab', block_a, block_b, preferred_element...  11.8 us
    dynamic_update_slice x10, local copies, waits for them, and re-layouts, put(): return lax.dynamic_update_slice(buf, piece[None, None], start)  10.9 us
    ppermute x2, waiting for transfers between devices, ring_into(): from_left = lax.ppermute(go_right[:half], axis, right)  9.23 us
    all_to_all x1, starting transfers between devices, shards(): lax.all_to_all(factors.reshape(local_aux, nocc, n_col, cols_b), ('x', 'zh...  8.97 us
    ppermute x1, waiting for transfers between devices, shards(): lax.ppermute(spread_b, 'zl', [(k, (k + 1) % n_zl) for k in range(n_zl)])  8.94 us
  transfers between devices with their start and end apart: 11, of which 6 were waited for; matrix products, arithmetic and copies ran while one was open for 14% of the time, Pallas kernels for 0%

profile of v10, /device:TPU:1, one launch (start us, length us, event | category | flops | bytes accessed | tf_op | source)
XLA Modules:
  0.0 171.4 jit_solution(10007506090423585819)
XLA Ops:
  6.5 0.0 copy-start
  6.5 0.0 copy-start.2
  6.5 0.0 copy-start.4
  6.5 0.0 copy-start.3
  6.5 0.0 copy-start.1
  6.5 0.0 all-gather.2.cloned.1.call-start
  6.6 1.3 copy.43
  7.9 20.5 %all_to_all.30 = bf16[80,3,8,256]{3,0,1,2:T(8,128)(2,1)S(1)} all-to-all(bf16[80,3,8,256]{3,0,1,2:T(8,128)(2,1)S(1)} %bitcast.69), channel_id=1, replica_groups=mesh['zl'=2,'y'=4,'x'=4,'zh'=2,'core'=2] {'zl','y'}, dimensions={2} | all-to-all | bytes 1966080 | tf_op jit(solution)/shard_map/all_to_all | solution.py:49
  28.3 1.0 copy.20
  29.4 0.0 all-gather.2.cloned.1.call-update
  29.4 2.3 %copy_bitcast_fusion.1 = bf16[80,3,16,128]{3,0,1,2:T(8,128)(2,1)} fusion(bf16[80,3,2048]{2,0,1:T(8,128)(2,1)} %param.7), kind=kLoop, calls=%fused_computation.10 | loop fusion | bytes 1966080 | tf_op jit(solution)/shard_map/reshape | solution.py:55
  31.7 9.0 %all-to-all-start = ((bf16[80,3,16,128]{3,0,1,2:T(8,128)(2,1)}), bf16[80,3,16,128]{3,0,1,2:T(8,128)(2,1)S(1)}, u32[]{:S(2)}, u32[]{:S(2)}) async-start(bf16[80,3,16,128]{3,0,1,2:T(8,128)(2,1)} %copy_bitcast_fusion.1), calls=%async_computation | async-start | bytes 1966080 | tf_op jit(solution)/shard_map/all_to_all | solution.py:54
  40.7 0.0 copy-done.2
  40.7 0.7 fusion.10
  41.4 0.0 copy-done.4
  41.4 0.0 copy-done.3
  41.4 1.8 %fusion.8 = (s32[16]{0:T(128)S(1)}, s32[16]{0:T(128)S(1)}) fusion(s32[16,2]{0,1:T(2,128)S(1)} %copy-done.3, s32[]{:T(128)} %bitcast.28, s32[]{:T(128)} %bitcast.30, s32[]{:T(128)} %bitcast.29), kind=kLoop, calls=%fused_computation.37 | loop fusion | flops 320 | bytes 268 | tf_op jit(solution)/shard_map/select_n | solution.py:76
  43.2 21.4 %all-to-all-done = bf16[80,3,16,128]{3,0,1,2:T(8,128)(2,1)S(1)} async-done(((bf16[80,3,16,128]{3,0,1,2:T(8,128)(2,1)}), bf16[80,3,16,128]{3,0,1,2:T(8,128)(2,1)S(1)}, u32[]{:S(2)}, u32[]{:S(2)}) %all-to-all-start) | async-done | bytes 983072 | tf_op jit(solution)/shard_map/all_to_all | solution.py:54
  64.5 0.1 copy.18
  64.6 0.3 collective-permute-start
  64.9 2.5 %collective-permute-start.1 = (bf16[1280,3,128]{2,0,1:T(8,128)(2,1)S(1)}, bf16[1280,3,128]{2,0,1:T(8,128)(2,1)S(1)}, u32[]{:S(2)}, u32[]{:S(2)}) collective-permute-start(bf16[1280,3,128]{2,0,1:T(8,128)(2,1)S(1)} %bitcast.64), channel_id=1, source_target_pairs={{0,48},{16,0},{32,16},{48,32},{1,49},{17,1},{33,17},{49,33},{2,50}... | collective-permute-start | bytes 2949128 | tf_op jit(solution)/shard_map/ppermute | solution.py:24
  67.4 0.0 collective-permute-start.4
  67.4 0.8 dynamic_slice.6
  68.2 0.8 dynamic_slice.7
  69.0 0.0 copy-done
  69.0 0.7 gather_fusion.1
  69.6 0.7 gather_fusion.2
  70.3 0.0 copy-done.1
  70.3 0.7 gather_fusion.3
  71.0 0.1 broadcast_add_fusion
  71.1 4.8 %broadcast_in_dim.53 = bf16[2,4,1280,3,128]{4,2,3,1,0:T(8,128)(2,1)} broadcast(bf16[]{:T(256)} %constant.79.clone.1), dimensions={} | broadcast | bytes 7864322 | tf_op jit(solution)/shard_map/broadcast_in_dim | solution.py:60
  76.0 1.0 constant_dynamic-update-slice_fusion
  77.0 11.6 %collective-permute-done = bf16[1280,3,128]{2,0,1:T(8,128)(2,1)S(1)} collective-permute-done((bf16[1280,3,128]{2,0,1:T(8,128)(2,1)S(1)}, bf16[1280,3,128]{2,0,1:T(8,128)(2,1)S(1)}, u32[]{:S(2)}, u32[]{:S(2)}) %collective-permute-start) | collective-permute-done | bytes 983072 | tf_op jit(solution)/shard_map/ppermute | solution.py:23
  88.6 0.1 collective-permute-start.2
  88.7 0.0 collective-permute-done.1
  88.7 2.9 %collective-permute-start.3 = (bf16[640,3,128]{2,0,1:T(8,128)(2,1)S(1)}, bf16[640,3,128]{2,0,1:T(8,128)(2,1)S(1)}, u32[]{:S(2)}, u32[]{:S(2)}) collective-permute-start(bf16[640,3,128]{2,0,1:T(8,128)(2,1)S(1)} %slice.41), channel_id=1, source_target_pairs={{0,48},{16,0},{32,16},{48,32},{1,49},{17,1},{33,17},{49,33},{2,50}... | collective-permute-start | bytes 1474568 | tf_op jit(solution)/shard_map/ppermute | solution.py:30
  91.6 8.9 %collective-permute-done.4 = bf16[1280,3,128]{2,0,1:T(8,128)(2,1)} collective-permute-done((bf16[1280,3,128]{2,0,1:T(8,128)(2,1)S(1)}, bf16[1280,3,128]{2,0,1:T(8,128)(2,1)}, u32[]{:S(2)}, u32[]{:S(2)}) %collective-permute-start.4) | collective-permute-done | bytes 983072 | tf_op jit(solution)/shard_map/ppermute | solution.py:58
  100.6 0.0 collective-permute-start.5
  100.6 2.7 %collective-permute-start.6 = (bf16[1280,3,128]{2,0,1:T(8,128)(2,1)}, bf16[1280,3,128]{2,0,1:T(8,128)(2,1)S(1)}, u32[]{:S(2)}, u32[]{:S(2)}) collective-permute-start(bf16[1280,3,128]{2,0,1:T(8,128)(2,1)} %collective-permute-done.4), channel_id=1, source_target_pairs={{0,48},{16,0},{32,16},{48,32},{1,49},{17,1},{33,17},{49,33},{2,50}... | collective-permute-start | bytes 2949128 | tf_op jit(solution)/shard_map/ppermute | solution.py:24
  103.3 1.0 bitcast_dynamic-update-slice_fusion.4
  104.3 1.0 bitcast_dynamic-update-slice_fusion.3
  105.3 0.0 collective-permute-done.2
  105.3 0.9 bitcast_dynamic-update-slice_fusion.8
  106.2 0.0 collective-permute-done.3
  106.2 0.9 bitcast_dynamic-update-slice_fusion.7
  107.1 2.2 %bitcast_dynamic-update-slice_fusion.2 = bf16[2,4,1280,3,128]{4,2,3,1,0:T(8,128)(2,1)} fusion(bf16[2,4,1280,3,128]{4,2,3,1,0:T(8,128)(2,1)} %bitcast_dynamic-update-slice_fusion.7, s32[]{:T(128)S(6)} %select_n.119, s32[]{:T(128)S(6)} %select_n.111, bf16[1280,3,128]{2,0,1:T(8,128)(2,1)} %collective-permute-done.4), kind=kLoop, calls=%fused_computation.13 | loop fusion | bytes 1966088 | tf_op jit(solution)/shard_map/dynamic_update_slice | solution.py:16
  109.3 15.5 %collective-permute-done.5 = bf16[1280,3,128]{2,0,1:T(8,128)(2,1)S(1)} collective-permute-done((bf16[1280,3,128]{2,0,1:T(8,128)(2,1)}, bf16[1280,3,128]{2,0,1:T(8,128)(2,1)S(1)}, u32[]{:S(2)}, u32[]{:S(2)}) %collective-permute-start.5) | collective-permute-done | bytes 983072 | tf_op jit(solution)/shard_map/ppermute | solution.py:23
  124.9 0.1 collective-permute-start.7
  124.9 0.0 collective-permute-done.6
  125.0 2.9 %collective-permute-start.8 = (bf16[640,3,128]{2,0,1:T(8,128)(2,1)S(1)}, bf16[640,3,128]{2,0,1:T(8,128)(2,1)S(1)}, u32[]{:S(2)}, u32[]{:S(2)}) collective-permute-start(bf16[640,3,128]{2,0,1:T(8,128)(2,1)S(1)} %slice.43), channel_id=1, source_target_pairs={{0,48},{16,0},{32,16},{48,32},{1,49},{17,1},{33,17},{49,33},{2,50}... | collective-permute-start | bytes 1474568 | tf_op jit(solution)/shard_map/ppermute | solution.py:30
  127.9 1.0 bitcast_dynamic-update-slice_fusion.1
  128.9 1.0 bitcast_dynamic-update-slice_fusion
  129.9 9.2 %collective-permute-done.7 = bf16[640,3,128]{2,0,1:T(8,128)(2,1)S(1)} collective-permute-done((bf16[640,3,128]{2,0,1:T(8,128)(2,1)S(1)}, bf16[640,3,128]{2,0,1:T(8,128)(2,1)S(1)}, u32[]{:S(2)}, u32[]{:S(2)}) %collective-permute-start.7) | collective-permute-done | bytes 491552 | tf_op jit(solution)/shard_map/ppermute | solution.py:29
  139.2 0.9 bitcast_dynamic-update-slice_fusion.6
  140.1 0.0 collective-permute-done.8
  140.1 0.9 bitcast_dynamic-update-slice_fusion.5
  141.0 8.9 %all-gather.2.cloned.1.call-done = bf16[10240,3,256]{2,0,1:T(8,128)(2,1)} async-done(((bf16[640,3,256]{2,0,1:T(8,128)(2,1)}), bf16[10240,3,256]{2,0,1:T(8,128)(2,1)}) %all-gather.2.cloned.1.call-update) | async-done | bytes 15728656 | tf_op jit(solution)/shard_map/all_gather | solution.py:53
  149.8 11.8 %fusion.3 = f32[3,3,256,128]{2,3,0,1:T(8,128)S(1)} fusion(bf16[4,2,2,2,4,80,3,256,1]{7,5,4,3,2,1,0,6,8:T(8,128)(2,1)} %bitcast.71, bf16[2,4,4,2,2,80,3,128,1]{7,5,4,3,2,6,1,0,8:T(8,128)(2,1)} %bitcast.17), kind=kOutput, calls=%fused_computation.8 | convolution fusion | flops 6039797760 | bytes 24772608 | tf_op jit(solution)/shard_map/xhczypia,zyxhcpjb->ijab/dot_general | solution.py:65
  161.6 0.4 copy.23
  162.0 0.7 gather_fusion
  162.7 1.9 %add_divide_fusion = f32[16,256,128]{2,1,0:T(8,128)} fusion(f32[16,256,128]{2,1,0:T(8,128)S(1)} %gather_fusion, f32[16]{0:T(128)S(1)} %gather_fusion.3, f32[16]{0:T(128)S(1)} %gather_fusion.2, f32[16]{0:T(128)S(1)} %gather_fusion.1, f32[256,128]{1,0:T(8,128)S(1)} %broadcast_add_fusion, pred[16]{0:T(512)(128)(4,1)S(1)} %get-tuple-element.5), kind=kLoop, calls=%fused_computation.7 | loop fusion | flops 3145728 | bytes 4325584 | tf_op jit(solution)/shard_map/div | solution.py:85
  (9 shorter events, 0.2 us)
Async XLA Ops:
  6.5 62.4 %copy-start = (f32[300]{0:T(512)S(1)}, f32[300]{0:T(512)}, u32[]{:S(2)}) copy-start(f32[300]{0:T(512)} %param.8) | copy-start | bytes 3604
  6.5 34.2 %copy-start.2 = (s32[3]{0:T(128)S(1)}, s32[3]{0:T(128)}, u32[]{:S(2)}) copy-start(s32[3]{0:T(128)} %param.10) | copy-start | bytes 40
  6.5 34.8 %copy-start.4 = (s32[16]{0:T(128)S(1)}, s32[16]{0:T(128)}, u32[]{:S(2)}) copy-start(s32[16]{0:T(128)} %param.12) | copy-start | bytes 196
  6.5 34.8 %copy-start.3 = (s32[16,2]{0,1:T(2,128)S(1)}, s32[16,2]{0,1:T(2,128)}, u32[]{:S(2)}) copy-start(s32[16,2]{0,1:T(2,128)} %param.11) | copy-start | bytes 388
  6.5 63.8 %copy-start.1 = (f32[4]{0:T(128)S(1)}, f32[4]{0:T(128)}, u32[]{:S(2)}) copy-start(f32[4]{0:T(128)} %param.13) | copy-start | bytes 52
  6.5 143.3 %all-gather.2.cloned.1.call-start = ((), (), s32[]{:S(2)}) async-start(), calls=%async_computation.2 | async-start | bytes 16711680 | tf_op jit(solution)/shard_map/all_gather | solution.py:53
  31.7 32.8 %all-to-all-start = ((bf16[80,3,16,128]{3,0,1,2:T(8,128)(2,1)}), bf16[80,3,16,128]{3,0,1,2:T(8,128)(2,1)S(1)}, u32[]{:S(2)}, u32[]{:S(2)}) async-start(bf16[80,3,16,128]{3,0,1,2:T(8,128)(2,1)} %copy_bitcast_fusion.1), calls=%async_computation | async-start | bytes 1966080 | tf_op jit(solution)/shard_map/all_to_all | solution.py:54
  64.6 24.0 %collective-permute-start = (bf16[1280,3,128]{2,0,1:T(8,128)(2,1)S(1)}, bf16[1280,3,128]{2,0,1:T(8,128)(2,1)S(1)}, u32[]{:S(2)}, u32[]{:S(2)}) collective-permute-start(bf16[1280,3,128]{2,0,1:T(8,128)(2,1)S(1)} %bitcast.63), channel_id=1, source_target_pairs={{0,16},{16,32},{32,48},{48,0},{1,17},{17,33},{33,49},{49,1},{2,18}... | collective-permute-start | bytes 2949128 | tf_op jit(solution)/shard_map/ppermute | solution.py:23
  64.9 23.8 %collective-permute-start.1 = (bf16[1280,3,128]{2,0,1:T(8,128)(2,1)S(1)}, bf16[1280,3,128]{2,0,1:T(8,128)(2,1)S(1)}, u32[]{:S(2)}, u32[]{:S(2)}) collective-permute-start(bf16[1280,3,128]{2,0,1:T(8,128)(2,1)S(1)} %bitcast.64), channel_id=1, source_target_pairs={{0,48},{16,0},{32,16},{48,32},{1,49},{17,1},{33,17},{49,33},{2,50}... | collective-permute-start | bytes 2949128 | tf_op jit(solution)/shard_map/ppermute | solution.py:24
  67.4 33.2 %collective-permute-start.4 = (bf16[1280,3,128]{2,0,1:T(8,128)(2,1)S(1)}, bf16[1280,3,128]{2,0,1:T(8,128)(2,1)}, u32[]{:S(2)}, u32[]{:S(2)}) collective-permute-start(bf16[1280,3,128]{2,0,1:T(8,128)(2,1)S(1)} %bitcast.65), channel_id=1, source_target_pairs={{0,64},{64,0},{1,65},{65,1},{2,66},{66,2},{3,67},{67,3},{4,68},{68... | collective-permute-start | bytes 2949128 | tf_op jit(solution)/shard_map/ppermute | solution.py:58
  88.6 16.7 %collective-permute-start.2 = (bf16[640,3,128]{2,0,1:T(8,128)(2,1)S(1)}, bf16[640,3,128]{2,0,1:T(8,128)(2,1)S(1)}, u32[]{:S(2)}, u32[]{:S(2)}) collective-permute-start(bf16[640,3,128]{2,0,1:T(8,128)(2,1)S(1)} %slice.40), channel_id=1, source_target_pairs={{0,16},{16,32},{32,48},{48,0},{1,17},{17,33},{33,49},{49,1},{2,18}... | collective-permute-start | bytes 1474568 | tf_op jit(solution)/shard_map/ppermute | solution.py:29
  88.7 17.5 %collective-permute-start.3 = (bf16[640,3,128]{2,0,1:T(8,128)(2,1)S(1)}, bf16[640,3,128]{2,0,1:T(8,128)(2,1)S(1)}, u32[]{:S(2)}, u32[]{:S(2)}) collective-permute-start(bf16[640,3,128]{2,0,1:T(8,128)(2,1)S(1)} %slice.41), channel_id=1, source_target_pairs={{0,48},{16,0},{32,16},{48,32},{1,49},{17,1},{33,17},{49,33},{2,50}... | collective-permute-start | bytes 1474568 | tf_op jit(solution)/shard_map/ppermute | solution.py:30
  100.6 24.2 %collective-permute-start.5 = (bf16[1280,3,128]{2,0,1:T(8,128)(2,1)}, bf16[1280,3,128]{2,0,1:T(8,128)(2,1)S(1)}, u32[]{:S(2)}, u32[]{:S(2)}) collective-permute-start(bf16[1280,3,128]{2,0,1:T(8,128)(2,1)} %collective-permute-done.4), channel_id=1, source_target_pairs={{0,16},{16,32},{32,48},{48,0},{1,17},{17,33},{33,49},{49,1},{2,18}... | collective-permute-start | bytes 2949128 | tf_op jit(solution)/shard_map/ppermute | solution.py:23
  100.6 24.4 %collective-permute-start.6 = (bf16[1280,3,128]{2,0,1:T(8,128)(2,1)}, bf16[1280,3,128]{2,0,1:T(8,128)(2,1)S(1)}, u32[]{:S(2)}, u32[]{:S(2)}) collective-permute-start(bf16[1280,3,128]{2,0,1:T(8,128)(2,1)} %collective-permute-done.4), channel_id=1, source_target_pairs={{0,48},{16,0},{32,16},{48,32},{1,49},{17,1},{33,17},{49,33},{2,50}... | collective-permute-start | bytes 2949128 | tf_op jit(solution)/shard_map/ppermute | solution.py:24
  124.9 14.3 %collective-permute-start.7 = (bf16[640,3,128]{2,0,1:T(8,128)(2,1)S(1)}, bf16[640,3,128]{2,0,1:T(8,128)(2,1)S(1)}, u32[]{:S(2)}, u32[]{:S(2)}) collective-permute-start(bf16[640,3,128]{2,0,1:T(8,128)(2,1)S(1)} %slice.42), channel_id=1, source_target_pairs={{0,16},{16,32},{32,48},{48,0},{1,17},{17,33},{33,49},{49,1},{2,18}... | collective-permute-start | bytes 1474568 | tf_op jit(solution)/shard_map/ppermute | solution.py:29
  125.0 15.1 %collective-permute-start.8 = (bf16[640,3,128]{2,0,1:T(8,128)(2,1)S(1)}, bf16[640,3,128]{2,0,1:T(8,128)(2,1)S(1)}, u32[]{:S(2)}, u32[]{:S(2)}) collective-permute-start(bf16[640,3,128]{2,0,1:T(8,128)(2,1)S(1)} %slice.43), channel_id=1, source_target_pairs={{0,48},{16,0},{32,16},{48,32},{1,49},{17,1},{33,17},{49,33},{2,50}... | collective-permute-start | bytes 1474568 | tf_op jit(solution)/shard_map/ppermute | solution.py:30
Sparse Core Ops, SparseCore 0:
  29.5 120.2 all-gather.1

commit v11 on v10

--- a/solution.py
+++ b/solution.py
@@ -50,7 +50,6 @@
         factors.reshape(local_aux, nocc, n_row, rows_a), ("zl", "y"), split_axis=2, concat_axis=0, tiled=True
     )
     spread_a = spread_a.reshape(n_row * local_aux, nocc, rows_a)
-    block_a = lax.all_gather(spread_a, ("x", "zh", "core"), axis=0, tiled=True)
     spread_b = lax.all_to_all(
         factors.reshape(local_aux, nocc, n_col, cols_b), ("x", "zh", "core"), split_axis=2, concat_axis=0, tiled=True
     )
@@ -60,14 +59,18 @@
     block_b = jnp.zeros((n_zl, n_y) + spread_b.shape, spread_b.dtype)
     block_b = ring_into(block_b, me_zl, spread_b, "y")
     block_b = ring_into(block_b, (me_zl + 1) % n_zl, other_b, "y")
-    block_a = block_a.reshape(n_x, n_zh, n_core, n_zl, n_y, local_aux, nocc, rows_a)
     block_b = block_b.reshape(n_zl, n_y, n_x, n_zh, n_core, local_aux, nocc, cols_b)
-    gram = jnp.einsum(
-        "xhczypia,zyxhcpjb->ijab",
-        block_a,
-        block_b,
-        preferred_element_type=jnp.float32,
-    ).reshape(nocc * nocc, rows_a, cols_b)
+    n_half = 2
+    width = rows_a // n_half
+    grams = []
+    for h in range(n_half):
+        part = lax.slice_in_dim(spread_a, h * width, (h + 1) * width, axis=2)
+        block_a = lax.all_gather(part, ("x", "zh", "core"), axis=0, tiled=True)
+        block_a = block_a.reshape(n_x, n_zh, n_core, n_zl, n_y, local_aux, nocc, width)
+        grams.append(
+            jnp.einsum("xhczypia,zyxhcpjb->ijab", block_a, block_b, preferred_element_type=jnp.float32)
+        )
+    gram = jnp.concatenate(grams, axis=2).reshape(nocc * nocc, rows_a, cols_b)
     first = pair_list[:, 0]
     second = pair_list[:, 1]
     kernel = jnp.take(gram, first * nocc + second, axis=0)

time: 173 us -> 210 us (1.21)
  waiting for transfers between devices: 75.5 us -> 107 us
  matrix products: 11.8 us -> 19.9 us
    all_gather x1 -> x2, waiting for transfers between devices: 8.86 us -> 54.7 us  [shards(): block_a = lax.all_gather(part, ('x', 'zh', 'core'), axis=0, tiled=True)]
    ppermute x2, waiting for transfers between devices: 27.1 us -> 16.7 us  [ring_into(): go_right = lax.ppermute(go_right, axis, right)]
    dot_general x1 -> x2, matrix products: 11.8 us -> 19.9 us  [shards(): jnp.einsum('xhczypia,zyxhcpjb->ijab', block_a, block_b, preferred_element...]
    all_to_all x1, waiting for transfers between devices: 21.4 us -> 17.2 us  [shards(): lax.all_to_all(factors.reshape(local_aux, nocc, n_col, cols_b), ('x', 'zh...]
  transfers between devices with their start and end apart: 11 -> 12, of which waited for: 6 -> 6; matrix products, arithmetic and copies ran while one was open for 14% -> 16% of each run, Pallas kernels for 0% -> 0%
where the time goes in v11:
time: 210 us
  waiting for transfers between devices  107 us (51%)
  local copies, waits for them, and re-layouts  24.6 us (12%)
  blocking collectives  20.5 us (10%)
  starting transfers between devices  20.2 us (10%)
  matrix products  19.9 us (9%)
  between operations  13.7 us (7%)
  other arithmetic  4.09 us (2%)
    all_gather x2, waiting for transfers between devices, shards(): block_a = lax.all_gather(part, ('x', 'zh', 'core'), axis=0, tiled=True)  54.7 us
    all_to_all x1, blocking collectives, shards(): lax.all_to_all(factors.reshape(local_aux, nocc, n_row, rows_a), ('zl', 'y...  20.5 us
    dot_general x2, matrix products, shards(): jnp.einsum('xhczypia,zyxhcpjb->ijab', block_a, block_b, preferred_element...  19.9 us
    all_to_all x1, waiting for transfers between devices, shards(): lax.all_to_all(factors.reshape(local_aux, nocc, n_col, cols_b), ('x', 'zh...  17.2 us
    ppermute x2, waiting for transfers between devices, ring_into(): go_right = lax.ppermute(go_right, axis, right)  16.7 us
    dynamic_update_slice x10, local copies, waits for them, and re-layouts, put(): return lax.dynamic_update_slice(buf, piece[None, None], start)  10.9 us
    ppermute x2, waiting for transfers between devices, ring_into(): from_left = lax.ppermute(go_right[:half], axis, right)  9.44 us
    all_to_all x1, starting transfers between devices, shards(): lax.all_to_all(factors.reshape(local_aux, nocc, n_col, cols_b), ('x', 'zh...  8.97 us
  transfers between devices with their start and end apart: 12, of which 6 were waited for; matrix products, arithmetic and copies ran while one was open for 16% of the time, Pallas kernels for 0%

profile of v11, /device:TPU:1, one launch (start us, length us, event | category | flops | bytes accessed | tf_op | source)
XLA Modules:
  0.0 209.7 jit_solution(4795299200144627238)
XLA Ops:
  6.5 0.0 copy-start
  6.5 0.0 all-gather.3.cloned.1.call-start
  6.6 0.0 copy-start.1
  6.6 1.3 copy.64
  7.9 20.5 %all_to_all.30 = bf16[80,3,8,256]{3,0,1,2:T(8,128)(2,1)S(1)} all-to-all(bf16[80,3,8,256]{3,0,1,2:T(8,128)(2,1)S(1)} %bitcast.79), channel_id=1, replica_groups=mesh['zl'=2,'y'=4,'x'=4,'zh'=2,'core'=2] {'zl','y'}, dimensions={2} | all-to-all | bytes 1966080 | tf_op jit(solution)/shard_map/all_to_all | solution.py:49
  28.4 0.1 copy.24
  28.5 1.2 fusion.18
  29.7 0.0 all-gather.3.cloned.1.call-update
  29.7 0.0 all-gather.5.cloned.1.call-start
  29.8 0.7 all-gather.5.cloned.1.call-update
  30.5 0.0 copy-done.2
  30.5 1.1 copy_bitcast_fusion.1
  31.6 9.0 %all-to-all-start = ((bf16[80,3,16,128]{3,0,1,2:T(8,128)(2,1)}), bf16[80,3,16,128]{3,0,1,2:T(8,128)(2,1)S(1)}, u32[]{:S(2)}, u32[]{:S(2)}) async-start(bf16[80,3,16,128]{3,0,1,2:T(8,128)(2,1)} %copy_bitcast_fusion.1), calls=%async_computation | async-start | bytes 1966080 | tf_op jit(solution)/shard_map/all_to_all | solution.py:53
  40.5 0.0 copy-done.3
  40.5 0.6 fusion.19
  41.2 0.0 copy-done.5
  41.2 0.0 copy-done.4
  41.2 1.9 fusion.16
  43.1 17.2 %all-to-all-done = bf16[80,3,16,128]{3,0,1,2:T(8,128)(2,1)S(1)} async-done(((bf16[80,3,16,128]{3,0,1,2:T(8,128)(2,1)}), bf16[80,3,16,128]{3,0,1,2:T(8,128)(2,1)S(1)}, u32[]{:S(2)}, u32[]{:S(2)}) %all-to-all-start) | async-done | bytes 983072 | tf_op jit(solution)/shard_map/all_to_all | solution.py:53
  60.3 0.1 copy.22
  60.4 0.7 collective-permute-start
  61.1 2.1 collective-permute-start.1
  63.1 0.0 collective-permute-start.4
  63.2 0.8 dynamic_slice.6
  64.0 0.8 dynamic_slice.7
  64.7 0.0 copy-done
  64.8 0.7 gather_fusion.1
  65.4 0.7 gather_fusion.2
  66.1 0.0 copy-done.1
  66.1 0.7 gather_fusion.3
  66.8 0.1 broadcast_add_fusion
  66.9 4.8 %broadcast_in_dim.53 = bf16[2,4,1280,3,128]{4,2,3,1,0:T(8,128)(2,1)} broadcast(bf16[]{:T(256)} %constant.79.clone.1), dimensions={} | broadcast | bytes 7864322 | tf_op jit(solution)/shard_map/broadcast_in_dim | solution.py:59
  71.7 1.0 constant_dynamic-update-slice_fusion
  72.7 10.3 %collective-permute-done = bf16[1280,3,128]{2,0,1:T(8,128)(2,1)S(1)} collective-permute-done((bf16[1280,3,128]{2,0,1:T(8,128)(2,1)S(1)}, bf16[1280,3,128]{2,0,1:T(8,128)(2,1)S(1)}, u32[]{:S(2)}, u32[]{:S(2)}) %collective-permute-start) | collective-permute-done | bytes 983072 | tf_op jit(solution)/shard_map/ppermute | solution.py:23
  83.1 0.1 collective-permute-start.2
  83.2 0.0 collective-permute-done.1
  83.2 2.7 %collective-permute-start.3 = (bf16[640,3,128]{2,0,1:T(8,128)(2,1)S(1)}, bf16[640,3,128]{2,0,1:T(8,128)(2,1)S(1)}, u32[]{:S(2)}, u32[]{:S(2)}) collective-permute-start(bf16[640,3,128]{2,0,1:T(8,128)(2,1)S(1)} %slice.49), channel_id=1, source_target_pairs={{0,48},{16,0},{32,16},{48,32},{1,49},{17,1},{33,17},{49,33},{2,50}... | collective-permute-start | bytes 1474568 | tf_op jit(solution)/shard_map/ppermute | solution.py:30
  85.9 8.0 %collective-permute-done.4 = bf16[1280,3,128]{2,0,1:T(8,128)(2,1)} collective-permute-done((bf16[1280,3,128]{2,0,1:T(8,128)(2,1)S(1)}, bf16[1280,3,128]{2,0,1:T(8,128)(2,1)}, u32[]{:S(2)}, u32[]{:S(2)}) %collective-permute-start.4) | collective-permute-done | bytes 983072 | tf_op jit(solution)/shard_map/ppermute | solution.py:57
  93.9 0.0 collective-permute-start.5
  93.9 2.7 %collective-permute-start.6 = (bf16[1280,3,128]{2,0,1:T(8,128)(2,1)}, bf16[1280,3,128]{2,0,1:T(8,128)(2,1)S(1)}, u32[]{:S(2)}, u32[]{:S(2)}) collective-permute-start(bf16[1280,3,128]{2,0,1:T(8,128)(2,1)} %collective-permute-done.4), channel_id=1, source_target_pairs={{0,48},{16,0},{32,16},{48,32},{1,49},{17,1},{33,17},{49,33},{2,50}... | collective-permute-start | bytes 2949128 | tf_op jit(solution)/shard_map/ppermute | solution.py:24
  96.6 1.0 bitcast_dynamic-update-slice_fusion.4
  97.6 1.0 bitcast_dynamic-update-slice_fusion.3
  98.6 0.0 collective-permute-done.2
  98.6 0.9 bitcast_dynamic-update-slice_fusion.8
  99.6 0.0 collective-permute-done.3
  99.6 0.9 bitcast_dynamic-update-slice_fusion.7
  100.4 2.2 %bitcast_dynamic-update-slice_fusion.2 = bf16[2,4,1280,3,128]{4,2,3,1,0:T(8,128)(2,1)} fusion(bf16[2,4,1280,3,128]{4,2,3,1,0:T(8,128)(2,1)} %bitcast_dynamic-update-slice_fusion.7, s32[]{:T(128)S(6)} %select_n.119, s32[]{:T(128)S(6)} %select_n.111, bf16[1280,3,128]{2,0,1:T(8,128)(2,1)} %collective-permute-done.4), kind=kLoop, calls=%fused_computation.18 | loop fusion | bytes 1966088 | tf_op jit(solution)/shard_map/dynamic_update_slice | solution.py:16
  102.7 6.4 %collective-permute-done.5 = bf16[1280,3,128]{2,0,1:T(8,128)(2,1)S(1)} collective-permute-done((bf16[1280,3,128]{2,0,1:T(8,128)(2,1)}, bf16[1280,3,128]{2,0,1:T(8,128)(2,1)S(1)}, u32[]{:S(2)}, u32[]{:S(2)}) %collective-permute-start.5) | collective-permute-done | bytes 983072 | tf_op jit(solution)/shard_map/ppermute | solution.py:23
  109.1 0.1 collective-permute-start.7
  109.2 0.0 collective-permute-done.6
  109.3 2.9 %collective-permute-start.8 = (bf16[640,3,128]{2,0,1:T(8,128)(2,1)S(1)}, bf16[640,3,128]{2,0,1:T(8,128)(2,1)S(1)}, u32[]{:S(2)}, u32[]{:S(2)}) collective-permute-start(bf16[640,3,128]{2,0,1:T(8,128)(2,1)S(1)} %slice.51), channel_id=1, source_target_pairs={{0,48},{16,0},{32,16},{48,32},{1,49},{17,1},{33,17},{49,33},{2,50}... | collective-permute-start | bytes 1474568 | tf_op jit(solution)/shard_map/ppermute | solution.py:30
  112.2 1.0 bitcast_dynamic-update-slice_fusion.1
  113.2 1.0 bitcast_dynamic-update-slice_fusion
  114.2 9.4 %collective-permute-done.7 = bf16[640,3,128]{2,0,1:T(8,128)(2,1)S(1)} collective-permute-done((bf16[640,3,128]{2,0,1:T(8,128)(2,1)S(1)}, bf16[640,3,128]{2,0,1:T(8,128)(2,1)S(1)}, u32[]{:S(2)}, u32[]{:S(2)}) %collective-permute-start.7) | collective-permute-done | bytes 491552 | tf_op jit(solution)/shard_map/ppermute | solution.py:29
  123.6 0.9 bitcast_dynamic-update-slice_fusion.6
  124.5 0.0 collective-permute-done.8
  124.5 0.9 bitcast_dynamic-update-slice_fusion.5
  125.5 10.2 %fusion.6 = f32[3,3,128,128]{3,2,0,1:T(8,128)S(1)} fusion(bf16[4,2,2,2,4,80,3,128,1]{7,5,4,3,2,1,0,6,8:T(8,128)(2,1)} %bitcast.81, bf16[2,4,4,2,2,80,3,128,1]{7,5,4,3,2,6,1,0,8:T(8,128)(2,1)} %bitcast.17), kind=kOutput, calls=%fused_computation.11 | convolution fusion | flops 3019898880 | bytes 16318464 | tf_op jit(solution)/shard_map/xhczypia,zyxhcpjb->ijab/dot_general | solution.py:71
  135.7 54.7 %all-gather.5.cloned.1.call-done = bf16[10240,3,128]{2,0,1:T(8,128)(2,1)} async-done(((bf16[640,3,128]{2,0,1:T(8,128)(2,1)}), bf16[10240,3,128]{2,0,1:T(8,128)(2,1)}) %all-gather.5.cloned.1.call-update) | async-done | bytes 7864336 | tf_op jit(solution)/shard_map/all_gather | solution.py:68
  190.4 9.7 %fusion.11 = f32[3,3,128,128]{3,2,0,1:T(8,128)S(1)} fusion(bf16[4,2,2,2,4,80,3,128,1]{7,5,4,3,2,1,0,6,8:T(8,128)(2,1)} %bitcast.82, bf16[2,4,4,2,2,80,3,128,1]{7,5,4,3,2,6,1,0,8:T(8,128)(2,1)} %bitcast.17), kind=kOutput, calls=%fused_computation.12 | convolution fusion | flops 3019898880 | bytes 16318464 | tf_op jit(solution)/shard_map/xhczypia,zyxhcpjb->ijab/dot_general | solution.py:71
  200.1 0.1 pad_maximum_fusion
  200.2 0.1 copy.29
  200.3 0.7 gather_fusion
  201.0 1.9 add_divide_fusion
  (14 shorter events, 0.2 us)
Async XLA Ops:
  6.5 58.2 %copy-start = (f32[300]{0:T(512)S(1)}, f32[300]{0:T(512)}, u32[]{:S(2)}) copy-start(f32[300]{0:T(512)} %param.8) | copy-start | bytes 3604
  6.5 23.9 %copy-start.2 = (bf16[80,3,2048]{2,0,1:T(8,128)(2,1)S(1)}, bf16[80,3,2048]{2,0,1:T(8,128)(2,1)}, u32[]{:S(2)}) copy-start(bf16[80,3,2048]{2,0,1:T(8,128)(2,1)} %param.7) | copy-start | bytes 2949124
  6.5 34.0 %copy-start.3 = (s32[3]{0:T(128)S(1)}, s32[3]{0:T(128)}, u32[]{:S(2)}) copy-start(s32[3]{0:T(128)} %param.10) | copy-start | bytes 40
  6.5 34.6 %copy-start.5 = (s32[16]{0:T(128)S(1)}, s32[16]{0:T(128)}, u32[]{:S(2)}) copy-start(s32[16]{0:T(128)} %param.12) | copy-start | bytes 196
  6.5 34.6 %copy-start.4 = (s32[16,2]{0,1:T(2,128)S(1)}, s32[16,2]{0,1:T(2,128)}, u32[]{:S(2)}) copy-start(s32[16,2]{0,1:T(2,128)} %param.11) | copy-start | bytes 388
  6.5 118.9 %all-gather.3.cloned.1.call-start = ((), (), s32[]{:S(2)}) async-start(), calls=%async_computation.2 | async-start | bytes 8355840 | tf_op jit(solution)/shard_map/all_gather | solution.py:68
  6.6 59.5 %copy-start.1 = (f32[4]{0:T(128)S(1)}, f32[4]{0:T(128)}, u32[]{:S(2)}) copy-start(f32[4]{0:T(128)} %param.13) | copy-start | bytes 52
  29.7 160.7 %all-gather.5.cloned.1.call-start = ((), (), s32[]{:S(2)}) async-start(), calls=%async_computation.3 | async-start | bytes 8355840 | tf_op jit(solution)/shard_map/all_gather | solution.py:68
  31.6 28.7 %all-to-all-start = ((bf16[80,3,16,128]{3,0,1,2:T(8,128)(2,1)}), bf16[80,3,16,128]{3,0,1,2:T(8,128)(2,1)S(1)}, u32[]{:S(2)}, u32[]{:S(2)}) async-start(bf16[80,3,16,128]{3,0,1,2:T(8,128)(2,1)} %copy_bitcast_fusion.1), calls=%async_computation | async-start | bytes 1966080 | tf_op jit(solution)/shard_map/all_to_all | solution.py:53
  60.4 22.7 %collective-permute-start = (bf16[1280,3,128]{2,0,1:T(8,128)(2,1)S(1)}, bf16[1280,3,128]{2,0,1:T(8,128)(2,1)S(1)}, u32[]{:S(2)}, u32[]{:S(2)}) collective-permute-start(bf16[1280,3,128]{2,0,1:T(8,128)(2,1)S(1)} %bitcast.73), channel_id=1, source_target_pairs={{0,16},{16,32},{32,48},{48,0},{1,17},{17,33},{33,49},{49,1},{2,18}... | collective-permute-start | bytes 2949128 | tf_op jit(solution)/shard_map/ppermute | solution.py:23
  61.1 22.1 %collective-permute-start.1 = (bf16[1280,3,128]{2,0,1:T(8,128)(2,1)S(1)}, bf16[1280,3,128]{2,0,1:T(8,128)(2,1)S(1)}, u32[]{:S(2)}, u32[]{:S(2)}) collective-permute-start(bf16[1280,3,128]{2,0,1:T(8,128)(2,1)S(1)} %bitcast.74), channel_id=1, source_target_pairs={{0,48},{16,0},{32,16},{48,32},{1,49},{17,1},{33,17},{49,33},{2,50}... | collective-permute-start | bytes 2949128 | tf_op jit(solution)/shard_map/ppermute | solution.py:24
  63.1 30.8 %collective-permute-start.4 = (bf16[1280,3,128]{2,0,1:T(8,128)(2,1)S(1)}, bf16[1280,3,128]{2,0,1:T(8,128)(2,1)}, u32[]{:S(2)}, u32[]{:S(2)}) collective-permute-start(bf16[1280,3,128]{2,0,1:T(8,128)(2,1)S(1)} %bitcast.75), channel_id=1, source_target_pairs={{0,64},{64,0},{1,65},{65,1},{2,66},{66,2},{3,67},{67,3},{4,68},{68... | collective-permute-start | bytes 2949128 | tf_op jit(solution)/shard_map/ppermute | solution.py:57
  83.1 15.6 %collective-permute-start.2 = (bf16[640,3,128]{2,0,1:T(8,128)(2,1)S(1)}, bf16[640,3,128]{2,0,1:T(8,128)(2,1)S(1)}, u32[]{:S(2)}, u32[]{:S(2)}) collective-permute-start(bf16[640,3,128]{2,0,1:T(8,128)(2,1)S(1)} %slice.48), channel_id=1, source_target_pairs={{0,16},{16,32},{32,48},{48,0},{1,17},{17,33},{33,49},{49,1},{2,18}... | collective-permute-start | bytes 1474568 | tf_op jit(solution)/shard_map/ppermute | solution.py:29
  83.2 16.3 %collective-permute-start.3 = (bf16[640,3,128]{2,0,1:T(8,128)(2,1)S(1)}, bf16[640,3,128]{2,0,1:T(8,128)(2,1)S(1)}, u32[]{:S(2)}, u32[]{:S(2)}) collective-permute-start(bf16[640,3,128]{2,0,1:T(8,128)(2,1)S(1)} %slice.49), channel_id=1, source_target_pairs={{0,48},{16,0},{32,16},{48,32},{1,49},{17,1},{33,17},{49,33},{2,50}... | collective-permute-start | bytes 1474568 | tf_op jit(solution)/shard_map/ppermute | solution.py:30
  93.9 15.2 %collective-permute-start.5 = (bf16[1280,3,128]{2,0,1:T(8,128)(2,1)}, bf16[1280,3,128]{2,0,1:T(8,128)(2,1)S(1)}, u32[]{:S(2)}, u32[]{:S(2)}) collective-permute-start(bf16[1280,3,128]{2,0,1:T(8,128)(2,1)} %collective-permute-done.4), channel_id=1, source_target_pairs={{0,16},{16,32},{32,48},{48,0},{1,17},{17,33},{33,49},{49,1},{2,18}... | collective-permute-start | bytes 2949128 | tf_op jit(solution)/shard_map/ppermute | solution.py:23
  93.9 15.3 %collective-permute-start.6 = (bf16[1280,3,128]{2,0,1:T(8,128)(2,1)}, bf16[1280,3,128]{2,0,1:T(8,128)(2,1)S(1)}, u32[]{:S(2)}, u32[]{:S(2)}) collective-permute-start(bf16[1280,3,128]{2,0,1:T(8,128)(2,1)} %collective-permute-done.4), channel_id=1, source_target_pairs={{0,48},{16,0},{32,16},{48,32},{1,49},{17,1},{33,17},{49,33},{2,50}... | collective-permute-start | bytes 2949128 | tf_op jit(solution)/shard_map/ppermute | solution.py:24
  109.1 14.5 %collective-permute-start.7 = (bf16[640,3,128]{2,0,1:T(8,128)(2,1)S(1)}, bf16[640,3,128]{2,0,1:T(8,128)(2,1)S(1)}, u32[]{:S(2)}, u32[]{:S(2)}) collective-permute-start(bf16[640,3,128]{2,0,1:T(8,128)(2,1)S(1)} %slice.50), channel_id=1, source_target_pairs={{0,16},{16,32},{32,48},{48,0},{1,17},{17,33},{33,49},{49,1},{2,18}... | collective-permute-start | bytes 1474568 | tf_op jit(solution)/shard_map/ppermute | solution.py:29
  109.3 15.3 %collective-permute-start.8 = (bf16[640,3,128]{2,0,1:T(8,128)(2,1)S(1)}, bf16[640,3,128]{2,0,1:T(8,128)(2,1)S(1)}, u32[]{:S(2)}, u32[]{:S(2)}) collective-permute-start(bf16[640,3,128]{2,0,1:T(8,128)(2,1)S(1)} %slice.51), channel_id=1, source_target_pairs={{0,48},{16,0},{32,16},{48,32},{1,49},{17,1},{33,17},{49,33},{2,50}... | collective-permute-start | bytes 1474568 | tf_op jit(solution)/shard_map/ppermute | solution.py:30
Sparse Core Ops, SparseCore 0:
  29.8 89.4 all-gather.2
  121.8 68.5 all-gather.4

commit v12 on v6

--- a/solution.py
+++ b/solution.py
@@ -50,13 +50,11 @@
         factors.reshape(local_aux, nocc, n_row, rows_a), ("zl", "y"), split_axis=2, concat_axis=0, tiled=True
     )
     spread_a = spread_a.reshape(n_row * local_aux, nocc, rows_a)
-    other_a = lax.ppermute(spread_a, "zh", [(k, (k + 1) % n_zh) for k in range(n_zh)])
+    pair_a = lax.all_gather(spread_a, "zh", axis=0, tiled=False)
     spread_b = lax.all_to_all(
         factors.reshape(local_aux, nocc, n_col, cols_b), ("x", "zh", "core"), split_axis=2, concat_axis=0, tiled=True
     )
-    other_a, spread_b = lax.optimization_barrier((other_a, spread_b))
-    first_zh = lax.axis_index("zh") == 0
-    pair_a = jnp.where(first_zh, jnp.stack([spread_a, other_a]), jnp.stack([other_a, spread_a]))
+    pair_a, spread_b = lax.optimization_barrier((pair_a, spread_b))
     block_a = lax.all_gather(pair_a, ("x", "core"), axis=0, tiled=True)
     spread_b = spread_b.reshape(n_col * local_aux, nocc, cols_b)
     other_b = lax.ppermute(spread_b, "zl", [(k, (k + 1) % n_zl) for k in range(n_zl)])

time: 170 us -> 177 us (1.041)
  blocking collectives: 20.5 us -> 45.5 us
  starting transfers between devices: 20.7 us -> 11.1 us
  waiting for transfers between devices: 71.3 us -> 66.4 us
  other arithmetic: 7.08 us -> 3.91 us
    all_to_all x0 -> x1, blocking collectives: none -> 25.1 us  [shards(): lax.all_to_all(factors.reshape(local_aux, nocc, n_col, cols_b), ('x', 'zh...]
    all_to_all x1 -> x0, waiting for transfers between devices: 24 us -> none  [shards(): lax.all_to_all(factors.reshape(local_aux, nocc, n_col, cols_b), ('x', 'zh...]
    all_gather x0 -> x1, waiting for transfers between devices: none -> 19.6 us  [shards(): pair_a = lax.all_gather(spread_a, 'zh', axis=0, tiled=False)]
    all_to_all x1 -> x0, starting transfers between devices: 6.23 us -> none  [shards(): lax.all_to_all(factors.reshape(local_aux, nocc, n_col, cols_b), ('x', 'zh...]
    ppermute x1 -> x0, starting transfers between devices: 3.38 us -> none  [shards(): lax.ppermute(spread_a, 'zh', [(k, (k + 1) % n_zh) for k in range(n_zh)])]
    select_n x1 -> x0, other arithmetic: 3.13 us -> none  [shards(): jnp.where(first_zh, jnp.stack([spread_a, other_a]), jnp.stack([other_a, s...]
  transfers between devices with their start and end apart: 12 -> 11, of which waited for: 6 -> 6; matrix products, arithmetic and copies ran while one was open for 14% -> 13% of each run, Pallas kernels for 0% -> 0%
where the time goes in v12:
time: 177 us
  waiting for transfers between devices  66.4 us (38%)
  blocking collectives  45.5 us (26%)
  local copies, waits for them, and re-layouts  24.3 us (14%)
  between operations  13.7 us (8%)
  matrix products  11.8 us (7%)
  starting transfers between devices  11.1 us (6%)
  other arithmetic  3.91 us (2%)
    ppermute x2, waiting for transfers between devices, ring_into(): go_right = lax.ppermute(go_right, axis, right)  33 us
    all_to_all x1, blocking collectives, shards(): lax.all_to_all(factors.reshape(local_aux, nocc, n_col, cols_b), ('x', 'zh...  25.1 us
    all_to_all x1, blocking collectives, shards(): lax.all_to_all(factors.reshape(local_aux, nocc, n_row, rows_a), ('zl', 'y...  20.5 us
    all_gather x1, waiting for transfers between devices, shards(): pair_a = lax.all_gather(spread_a, 'zh', axis=0, tiled=False)  19.6 us
    ppermute x2, waiting for transfers between devices, ring_into(): from_left = lax.ppermute(go_right[:half], axis, right)  12.5 us
    dot_general x1, matrix products, shards(): jnp.einsum('xchzypia,zyxhcpjb->ijab', block_a, block_b, preferred_element...  11.8 us
    dynamic_update_slice x10, local copies, waits for them, and re-layouts, put(): return lax.dynamic_update_slice(buf, piece[None, None], start)  9.68 us
    broadcast_in_dim x1, local copies, waits for them, and re-layouts, shards(): block_b = jnp.zeros((n_zl, n_y) + spread_b.shape, spread_b.dtype)  5.54 us
  transfers between devices with their start and end apart: 11, of which 6 were waited for; matrix products, arithmetic and copies ran while one was open for 13% of the time, Pallas kernels for 0%

profile of v12, /device:TPU:1, one launch (start us, length us, event | category | flops | bytes accessed | tf_op | source)
XLA Modules:
  0.0 176.6 jit_solution(7023317602498881961)
XLA Ops:
  6.5 0.0 copy-start
  6.5 0.0 copy-start.2
  6.5 0.0 copy-start.3
  6.5 0.0 all-gather.3.cloned.1.call-start
  6.5 0.0 copy-start.4
  6.6 0.0 copy-start.1
  6.6 1.3 copy.42
  7.9 20.5 %all_to_all.33 = bf16[80,3,8,256]{3,0,1,2:T(8,128)(2,1)S(1)} all-to-all(bf16[80,3,8,256]{3,0,1,2:T(8,128)(2,1)S(1)} %bitcast.70), channel_id=1, replica_groups=mesh['zl'=2,'y'=4,'x'=4,'zh'=2,'core'=2] {'zl','y'}, dimensions={2} | all-to-all | bytes 1966080 | tf_op jit(solution)/shard_map/all_to_all | solution.py:49
  28.3 1.0 copy.17
  29.4 0.0 all-gather.3.cloned.1.call-update
  29.4 0.0 all-gather.5.cloned.1.call-start
  29.4 1.4 copy_bitcast_fusion
  30.8 25.1 %all_to_all.34 = bf16[80,3,16,128]{3,0,1,2:T(8,128)(2,1)S(1)} all-to-all(bf16[80,3,16,128]{3,0,1,2:T(8,128)(2,1)S(1)} %copy_bitcast_fusion), channel_id=1, replica_groups=mesh['zl'=2,'y'=4,'x'=4,'zh'=2,'core'=2] {'x','zh','core'}, dimensions={2} | all-to-all | bytes 1966080 | tf_op jit(solution)/shard_map/all_to_all | solution.py:54
  55.9 0.1 copy.19
  55.9 19.6 %all-gather.3.cloned.1.call-done = bf16[2,640,3,256]{3,1,2,0:T(8,128)(2,1)} async-done(((bf16[1,640,3,256]{3,1,2,0:T(8,128)(2,1)}), bf16[2,640,3,256]{3,1,2,0:T(8,128)(2,1)}) %all-gather.3.cloned.1.call-update) | async-done | bytes 1966096 | tf_op jit(solution)/shard_map/all_gather | solution.py:53
  75.6 0.0 all-gather.5.cloned.1.call-update
  75.7 0.8 dynamic_slice.6
  76.4 0.8 dynamic_slice.7
  77.2 0.0 copy-done.2
  77.2 0.6 fusion.10
  77.8 0.0 copy-done.3
  77.8 1.8 %fusion.8 = (s32[16]{0:T(128)S(1)}, s32[16]{0:T(128)S(1)}) fusion(s32[16,2]{0,1:T(2,128)S(1)} %copy-done.3, s32[]{:T(128)} %bitcast.27, s32[]{:T(128)} %bitcast.29, s32[]{:T(128)} %bitcast.28), kind=kLoop, calls=%fused_computation.37 | loop fusion | flops 320 | bytes 268 | tf_op jit(solution)/shard_map/select_n | solution.py:78
  79.6 0.0 copy-done
  79.7 0.7 gather_fusion.1
  80.3 0.7 gather_fusion.2
  81.0 0.0 copy-done.4
  81.0 0.0 copy-done.1
  81.0 0.7 gather_fusion.3
  81.7 0.8 collective-permute-start
  82.5 2.0 %collective-permute-start.1 = (bf16[1280,3,128]{2,0,1:T(8,128)(2,1)S(1)}, bf16[1280,3,128]{2,0,1:T(8,128)(2,1)S(1)}, u32[]{:S(2)}, u32[]{:S(2)}) collective-permute-start(bf16[1280,3,128]{2,0,1:T(8,128)(2,1)S(1)} %bitcast.65), channel_id=1, source_target_pairs={{0,48},{16,0},{32,16},{48,32},{1,49},{17,1},{33,17},{49,33},{2,50}... | collective-permute-start | bytes 2949128 | tf_op jit(solution)/shard_map/ppermute | solution.py:24
  84.4 0.0 collective-permute-start.4
  84.5 0.1 broadcast_add_fusion
  84.6 5.5 %broadcast_in_dim.53 = bf16[2,4,1280,3,128]{4,2,3,1,0:T(8,128)(2,1)} broadcast(bf16[]{:T(256)} %constant.79.clone.1), dimensions={} | broadcast | bytes 7864322 | tf_op jit(solution)/shard_map/broadcast_in_dim | solution.py:62
  90.1 1.0 bitcast_dynamic-update-slice_fusion.5
  91.1 14.7 %collective-permute-done = bf16[1280,3,128]{2,0,1:T(8,128)(2,1)S(1)} collective-permute-done((bf16[1280,3,128]{2,0,1:T(8,128)(2,1)S(1)}, bf16[1280,3,128]{2,0,1:T(8,128)(2,1)S(1)}, u32[]{:S(2)}, u32[]{:S(2)}) %collective-permute-start) | collective-permute-done | bytes 983072 | tf_op jit(solution)/shard_map/ppermute | solution.py:23
  105.9 0.1 collective-permute-start.2
  106.0 0.0 collective-permute-done.1
  106.0 2.7 %collective-permute-start.3 = (bf16[640,3,128]{2,0,1:T(8,128)(2,1)S(1)}, bf16[640,3,128]{2,0,1:T(8,128)(2,1)S(1)}, u32[]{:S(2)}, u32[]{:S(2)}) collective-permute-start(bf16[640,3,128]{2,0,1:T(8,128)(2,1)S(1)} %slice.41), channel_id=1, source_target_pairs={{0,48},{16,0},{32,16},{48,32},{1,49},{17,1},{33,17},{49,33},{2,50}... | collective-permute-start | bytes 1474568 | tf_op jit(solution)/shard_map/ppermute | solution.py:30
  108.8 0.0 collective-permute-done.4
  108.8 0.0 collective-permute-start.5
  108.8 2.7 %collective-permute-start.6 = (bf16[1280,3,128]{2,0,1:T(8,128)(2,1)S(1)}, bf16[1280,3,128]{2,0,1:T(8,128)(2,1)S(1)}, u32[]{:S(2)}, u32[]{:S(2)}) collective-permute-start(bf16[1280,3,128]{2,0,1:T(8,128)(2,1)S(1)} %collective-permute-done.4), channel_id=1, source_target_pairs={{0,48},{16,0},{32,16},{48,32},{1,49},{17,1},{33,17},{49,33},{2,50}... | collective-permute-start | bytes 2949128 | tf_op jit(solution)/shard_map/ppermute | solution.py:24
  111.4 1.0 bitcast_dynamic-update-slice_fusion.4
  112.5 1.0 bitcast_dynamic-update-slice_fusion.3
  113.5 5.3 %collective-permute-done.2 = bf16[640,3,128]{2,0,1:T(8,128)(2,1)S(1)} collective-permute-done((bf16[640,3,128]{2,0,1:T(8,128)(2,1)S(1)}, bf16[640,3,128]{2,0,1:T(8,128)(2,1)S(1)}, u32[]{:S(2)}, u32[]{:S(2)}) %collective-permute-start.2) | collective-permute-done | bytes 491552 | tf_op jit(solution)/shard_map/ppermute | solution.py:29
  118.8 0.9 bitcast_dynamic-update-slice_fusion.9
  119.7 0.0 collective-permute-done.3
  119.7 0.9 bitcast_dynamic-update-slice_fusion.8
  120.5 1.0 bitcast_dynamic-update-slice_fusion.2
  121.6 18.3 %collective-permute-done.5 = bf16[1280,3,128]{2,0,1:T(8,128)(2,1)S(1)} collective-permute-done((bf16[1280,3,128]{2,0,1:T(8,128)(2,1)S(1)}, bf16[1280,3,128]{2,0,1:T(8,128)(2,1)S(1)}, u32[]{:S(2)}, u32[]{:S(2)}) %collective-permute-start.5) | collective-permute-done | bytes 983072 | tf_op jit(solution)/shard_map/ppermute | solution.py:23
  139.9 0.1 collective-permute-start.7
  140.0 0.0 collective-permute-done.6
  140.0 2.7 %collective-permute-start.8 = (bf16[640,3,128]{2,0,1:T(8,128)(2,1)S(1)}, bf16[640,3,128]{2,0,1:T(8,128)(2,1)S(1)}, u32[]{:S(2)}, u32[]{:S(2)}) collective-permute-start(bf16[640,3,128]{2,0,1:T(8,128)(2,1)S(1)} %slice.43), channel_id=1, source_target_pairs={{0,48},{16,0},{32,16},{48,32},{1,49},{17,1},{33,17},{49,33},{2,50}... | collective-permute-start | bytes 1474568 | tf_op jit(solution)/shard_map/ppermute | solution.py:30
  142.7 1.0 bitcast_dynamic-update-slice_fusion.1
  143.7 1.0 bitcast_dynamic-update-slice_fusion
  144.8 7.2 %collective-permute-done.7 = bf16[640,3,128]{2,0,1:T(8,128)(2,1)S(1)} collective-permute-done((bf16[640,3,128]{2,0,1:T(8,128)(2,1)S(1)}, bf16[640,3,128]{2,0,1:T(8,128)(2,1)S(1)}, u32[]{:S(2)}, u32[]{:S(2)}) %collective-permute-start.7) | collective-permute-done | bytes 491552 | tf_op jit(solution)/shard_map/ppermute | solution.py:29
  152.0 0.9 bitcast_dynamic-update-slice_fusion.7
  152.9 0.0 collective-permute-done.8
  152.9 0.9 bitcast_dynamic-update-slice_fusion.6
  153.8 1.2 all-gather.5.cloned.1.call-done
  155.0 11.8 %fusion.3 = f32[3,3,256,128]{2,3,0,1:T(8,128)S(1)} fusion(bf16[4,2,2,2,4,80,3,256,1]{7,5,4,3,6,2,1,0,8:T(8,128)(2,1)} %bitcast.72, bf16[2,4,4,2,2,80,3,128,1]{7,5,4,3,2,6,1,0,8:T(8,128)(2,1)} %bitcast.19), kind=kOutput, calls=%fused_computation.8 | convolution fusion | flops 6039797760 | bytes 24772608 | tf_op jit(solution)/shard_map/xchzypia,zyxhcpjb->ijab/dot_general | solution.py:67
  166.8 0.4 copy.22
  167.1 0.7 gather_fusion
  167.8 1.9 %add_divide_fusion = f32[16,256,128]{2,1,0:T(8,128)} fusion(f32[16,256,128]{2,1,0:T(8,128)S(1)} %gather_fusion, f32[16]{0:T(128)S(1)} %gather_fusion.3, f32[16]{0:T(128)S(1)} %gather_fusion.2, f32[16]{0:T(128)S(1)} %gather_fusion.1, f32[256,128]{1,0:T(8,128)S(1)} %broadcast_add_fusion, pred[16]{0:T(512)(128)(4,1)S(1)} %get-tuple-element.9), kind=kLoop, calls=%fused_computation.7 | loop fusion | flops 3145728 | bytes 4325584 | tf_op jit(solution)/shard_map/div | solution.py:87
  (9 shorter events, 0.2 us)
Async XLA Ops:
  6.5 73.1 %copy-start = (f32[300]{0:T(512)S(1)}, f32[300]{0:T(512)}, u32[]{:S(2)}) copy-start(f32[300]{0:T(512)} %param.8) | copy-start | bytes 3604
  6.5 70.7 %copy-start.2 = (s32[3]{0:T(128)S(1)}, s32[3]{0:T(128)}, u32[]{:S(2)}) copy-start(s32[3]{0:T(128)} %param.10) | copy-start | bytes 40
  6.5 71.2 %copy-start.3 = (s32[16,2]{0,1:T(2,128)S(1)}, s32[16,2]{0,1:T(2,128)}, u32[]{:S(2)}) copy-start(s32[16,2]{0,1:T(2,128)} %param.11) | copy-start | bytes 388
  6.5 69.0 %all-gather.3.cloned.1.call-start = ((), (), s32[]{:S(2)}) async-start(), calls=%async_computation.2 | async-start | bytes 2949120 | tf_op jit(solution)/shard_map/all_gather | solution.py:53
  6.5 74.5 %copy-start.4 = (s32[16]{0:T(128)S(1)}, s32[16]{0:T(128)}, u32[]{:S(2)}) copy-start(s32[16]{0:T(128)} %param.12) | copy-start | bytes 196
  6.6 74.5 %copy-start.1 = (f32[4]{0:T(128)S(1)}, f32[4]{0:T(128)}, u32[]{:S(2)}) copy-start(f32[4]{0:T(128)} %param.13) | copy-start | bytes 52
  29.4 125.6 %all-gather.5.cloned.1.call-start = ((), (), s32[]{:S(2)}) async-start(), calls=%async_computation.3 | async-start | bytes 17694720 | tf_op jit(solution)/shard_map/all_gather | solution.py:58
  81.7 24.2 %collective-permute-start = (bf16[1280,3,128]{2,0,1:T(8,128)(2,1)S(1)}, bf16[1280,3,128]{2,0,1:T(8,128)(2,1)S(1)}, u32[]{:S(2)}, u32[]{:S(2)}) collective-permute-start(bf16[1280,3,128]{2,0,1:T(8,128)(2,1)S(1)} %bitcast.64), channel_id=1, source_target_pairs={{0,16},{16,32},{32,48},{48,0},{1,17},{17,33},{33,49},{49,1},{2,18}... | collective-permute-start | bytes 2949128 | tf_op jit(solution)/shard_map/ppermute | solution.py:23
  82.5 23.5 %collective-permute-start.1 = (bf16[1280,3,128]{2,0,1:T(8,128)(2,1)S(1)}, bf16[1280,3,128]{2,0,1:T(8,128)(2,1)S(1)}, u32[]{:S(2)}, u32[]{:S(2)}) collective-permute-start(bf16[1280,3,128]{2,0,1:T(8,128)(2,1)S(1)} %bitcast.65), channel_id=1, source_target_pairs={{0,48},{16,0},{32,16},{48,32},{1,49},{17,1},{33,17},{49,33},{2,50}... | collective-permute-start | bytes 2949128 | tf_op jit(solution)/shard_map/ppermute | solution.py:24
  84.4 24.3 %collective-permute-start.4 = (bf16[1280,3,128]{2,0,1:T(8,128)(2,1)S(1)}, bf16[1280,3,128]{2,0,1:T(8,128)(2,1)S(1)}, u32[]{:S(2)}, u32[]{:S(2)}) collective-permute-start(bf16[1280,3,128]{2,0,1:T(8,128)(2,1)S(1)} %bitcast.66), channel_id=1, source_target_pairs={{0,64},{64,0},{1,65},{65,1},{2,66},{66,2},{3,67},{67,3},{4,68},{68... | collective-permute-start | bytes 2949128 | tf_op jit(solution)/shard_map/ppermute | solution.py:60
  105.9 12.9 %collective-permute-start.2 = (bf16[640,3,128]{2,0,1:T(8,128)(2,1)S(1)}, bf16[640,3,128]{2,0,1:T(8,128)(2,1)S(1)}, u32[]{:S(2)}, u32[]{:S(2)}) collective-permute-start(bf16[640,3,128]{2,0,1:T(8,128)(2,1)S(1)} %slice.40), channel_id=1, source_target_pairs={{0,16},{16,32},{32,48},{48,0},{1,17},{17,33},{33,49},{49,1},{2,18}... | collective-permute-start | bytes 1474568 | tf_op jit(solution)/shard_map/ppermute | solution.py:29
  106.0 13.6 %collective-permute-start.3 = (bf16[640,3,128]{2,0,1:T(8,128)(2,1)S(1)}, bf16[640,3,128]{2,0,1:T(8,128)(2,1)S(1)}, u32[]{:S(2)}, u32[]{:S(2)}) collective-permute-start(bf16[640,3,128]{2,0,1:T(8,128)(2,1)S(1)} %slice.41), channel_id=1, source_target_pairs={{0,48},{16,0},{32,16},{48,32},{1,49},{17,1},{33,17},{49,33},{2,50}... | collective-permute-start | bytes 1474568 | tf_op jit(solution)/shard_map/ppermute | solution.py:30
  108.8 31.1 %collective-permute-start.5 = (bf16[1280,3,128]{2,0,1:T(8,128)(2,1)S(1)}, bf16[1280,3,128]{2,0,1:T(8,128)(2,1)S(1)}, u32[]{:S(2)}, u32[]{:S(2)}) collective-permute-start(bf16[1280,3,128]{2,0,1:T(8,128)(2,1)S(1)} %collective-permute-done.4), channel_id=1, source_target_pairs={{0,16},{16,32},{32,48},{48,0},{1,17},{17,33},{33,49},{49,1},{2,18}... | collective-permute-start | bytes 2949128 | tf_op jit(solution)/shard_map/ppermute | solution.py:23
  108.8 31.2 %collective-permute-start.6 = (bf16[1280,3,128]{2,0,1:T(8,128)(2,1)S(1)}, bf16[1280,3,128]{2,0,1:T(8,128)(2,1)S(1)}, u32[]{:S(2)}, u32[]{:S(2)}) collective-permute-start(bf16[1280,3,128]{2,0,1:T(8,128)(2,1)S(1)} %collective-permute-done.4), channel_id=1, source_target_pairs={{0,48},{16,0},{32,16},{48,32},{1,49},{17,1},{33,17},{49,33},{2,50}... | collective-permute-start | bytes 2949128 | tf_op jit(solution)/shard_map/ppermute | solution.py:24
  139.9 12.1 %collective-permute-start.7 = (bf16[640,3,128]{2,0,1:T(8,128)(2,1)S(1)}, bf16[640,3,128]{2,0,1:T(8,128)(2,1)S(1)}, u32[]{:S(2)}, u32[]{:S(2)}) collective-permute-start(bf16[640,3,128]{2,0,1:T(8,128)(2,1)S(1)} %slice.42), channel_id=1, source_target_pairs={{0,16},{16,32},{32,48},{48,0},{1,17},{17,33},{33,49},{49,1},{2,18}... | collective-permute-start | bytes 1474568 | tf_op jit(solution)/shard_map/ppermute | solution.py:29
  140.0 12.9 %collective-permute-start.8 = (bf16[640,3,128]{2,0,1:T(8,128)(2,1)S(1)}, bf16[640,3,128]{2,0,1:T(8,128)(2,1)S(1)}, u32[]{:S(2)}, u32[]{:S(2)}) collective-permute-start(bf16[640,3,128]{2,0,1:T(8,128)(2,1)S(1)} %slice.43), channel_id=1, source_target_pairs={{0,48},{16,0},{32,16},{48,32},{1,49},{17,1},{33,17},{49,33},{2,50}... | collective-permute-start | bytes 1474568 | tf_op jit(solution)/shard_map/ppermute | solution.py:30
Sparse Core Ops, SparseCore 0:
  29.5 46.0 all-gather.2
  77.3 77.6 all-gather.4

commit v13 on v6

--- a/solution.py
+++ b/solution.py
@@ -51,10 +51,16 @@
     )
     spread_a = spread_a.reshape(n_row * local_aux, nocc, rows_a)
     other_a = lax.ppermute(spread_a, "zh", [(k, (k + 1) % n_zh) for k in range(n_zh)])
-    spread_b = lax.all_to_all(
-        factors.reshape(local_aux, nocc, n_col, cols_b), ("x", "zh", "core"), split_axis=2, concat_axis=0, tiled=True
+    by_chip = lax.all_to_all(
+        factors.reshape(local_aux, nocc, n_x * n_zh, n_core, cols_b), ("x", "zh"), split_axis=2, concat_axis=0, tiled=True
     )
-    other_a, spread_b = lax.optimization_barrier((other_a, spread_b))
+    other_a, by_chip = lax.optimization_barrier((other_a, by_chip))
+    me_core = lax.axis_index("core")
+    by_chip = by_chip.reshape(n_x * n_zh * local_aux, nocc, n_core, cols_b)
+    keep = lax.dynamic_index_in_dim(by_chip, me_core, 2, keepdims=False)
+    give = lax.dynamic_index_in_dim(by_chip, (me_core + 1) % n_core, 2, keepdims=False)
+    got = lax.ppermute(give, "core", [(k, (k + 1) % n_core) for k in range(n_core)])
+    spread_b = jnp.where(me_core == 0, jnp.stack([keep, got]), jnp.stack([got, keep]))
     first_zh = lax.axis_index("zh") == 0
     pair_a = jnp.where(first_zh, jnp.stack([spread_a, other_a]), jnp.stack([other_a, spread_a]))
     block_a = lax.all_gather(pair_a, ("x", "core"), axis=0, tiled=True)
@@ -65,9 +71,9 @@
     block_b = ring_into(block_b, me_zl, spread_b, "y")
     block_b = ring_into(block_b, (me_zl + 1) % n_zl, other_b, "y")
     block_a = block_a.reshape(n_x, n_core, n_zh, n_zl, n_y, local_aux, nocc, rows_a)
-    block_b = block_b.reshape(n_zl, n_y, n_x, n_zh, n_core, local_aux, nocc, cols_b)
+    block_b = block_b.reshape(n_zl, n_y, n_core, n_x, n_zh, local_aux, nocc, cols_b)
     gram = jnp.einsum(
-        "xchzypia,zyxhcpjb->ijab",
+        "xchzypia,zycxhpjb->ijab",
         block_a,
         block_b,
         preferred_element_type=jnp.float32,

time: 170 us -> 170 us (level)
  waiting for transfers between devices: 71.3 us -> 67.3 us
  local copies, waits for them, and re-layouts: 24.6 us -> 28 us
    ppermute x2, waiting for transfers between devices: 33.2 us -> 28.7 us  [ring_into(): go_right = lax.ppermute(go_right, axis, right)]
    reshape x1 -> x2, local copies, waits for them, and re-layouts: 2.31 us -> 4.54 us  [shards(): factors.reshape(local_aux, nocc, n_x * n_zh, n_core, cols_b)]
    all_gather x1, waiting for transfers between devices: 0.61 us -> 2.81 us  [shards(): block_a = lax.all_gather(pair_a, ('x', 'core'), axis=0, tiled=True)]
    ppermute x0 -> x1, starting transfers between devices: none -> 2.19 us  [shards(): lax.ppermute(give, 'core', [(k, (k + 1) % n_core) for k in range(n_core)])]
    all_to_all x1, starting transfers between devices: 6.23 us -> 4.15 us  [shards(): lax.all_to_all(factors.reshape(local_aux, nocc, n_x * n_zh, n_core, cols_...]
  transfers between devices with their start and end apart: 12 -> 13, of which waited for: 6 -> 6; matrix products, arithmetic and copies ran while one was open for 14% -> 16% of each run, Pallas kernels for 0% -> 0%
where the time goes in v13:
time: 170 us
  waiting for transfers between devices  67.3 us (40%)
  local copies, waits for them, and re-layouts  28 us (16%)
  starting transfers between devices  20.9 us (12%)
  blocking collectives  20.5 us (12%)
  between operations  13.8 us (8%)
  matrix products  11.8 us (7%)
  other arithmetic  7.4 us (4%)
    ppermute x2, waiting for transfers between devices, ring_into(): go_right = lax.ppermute(go_right, axis, right)  28.7 us
    all_to_all x1, waiting for transfers between devices, shards(): lax.all_to_all(factors.reshape(local_aux, nocc, n_x * n_zh, n_core, cols_...  22.4 us
    all_to_all x1, blocking collectives, shards(): lax.all_to_all(factors.reshape(local_aux, nocc, n_row, rows_a), ('zl', 'y...  20.5 us
    ppermute x2, waiting for transfers between devices, ring_into(): from_left = lax.ppermute(go_right[:half], axis, right)  13.4 us
    dot_general x1, matrix products, shards(): jnp.einsum('xchzypia,zycxhpjb->ijab', block_a, block_b, preferred_element...  11.8 us
    dynamic_update_slice x10, local copies, waits for them, and re-layouts, put(): return lax.dynamic_update_slice(buf, piece[None, None], start)  10.9 us
    ppermute x2, starting transfers between devices, ring_into(): from_right = lax.ppermute(go_left[half:], axis, left)  5.62 us
    broadcast_in_dim x1, local copies, waits for them, and re-layouts, shards(): block_b = jnp.zeros((n_zl, n_y) + spread_b.shape, spread_b.dtype)  5.48 us
  transfers between devices with their start and end apart: 13, of which 6 were waited for; matrix products, arithmetic and copies ran while one was open for 16% of the time, Pallas kernels for 0%

profile of v13, /device:TPU:1, one launch (start us, length us, event | category | flops | bytes accessed | tf_op | source)
XLA Modules:
  0.0 169.7 jit_solution(929178936702780012)
XLA Ops:
  6.5 0.0 copy-start
  6.5 1.3 copy.51
  7.8 20.5 %all_to_all.33 = bf16[80,3,8,256]{3,0,1,2:T(8,128)(2,1)S(1)} all-to-all(bf16[80,3,8,256]{3,0,1,2:T(8,128)(2,1)S(1)} %bitcast.79), channel_id=1, replica_groups=mesh['zl'=2,'y'=4,'x'=4,'zh'=2,'core'=2] {'zl','y'}, dimensions={2} | all-to-all | bytes 1966080 | tf_op jit(solution)/shard_map/all_to_all | solution.py:49
  28.3 0.1 copy.24
  28.4 0.0 copy-start.2
  28.4 0.0 copy-start.4
  28.4 0.0 copy-start.3
  28.4 3.4 %collective-permute-start = (bf16[640,3,256]{2,0,1:T(8,128)(2,1)S(1)}, bf16[640,3,256]{2,0,1:T(8,128)(2,1)}, u32[]{:S(2)}, u32[]{:S(2)}) collective-permute-start(bf16[640,3,256]{2,0,1:T(8,128)(2,1)S(1)} %bitcast.80), channel_id=1, source_target_pairs={{0,2},{2,0},{1,3},{3,1},{4,6},{6,4},{5,7},{7,5},{8,10},{10,8},{9,1... | collective-permute-start | bytes 2949128 | tf_op jit(solution)/shard_map/ppermute | solution.py:53
  31.8 2.9 %reshape.117 = bf16[80,3,8,2,128]{4,3,2,0,1:T(2,128)(2,1)S(1)} reshape(bf16[80,3,2048]{2,0,1:T(8,128)(2,1)} %param.7) | data formatting | bytes 1966080 | tf_op jit(solution)/shard_map/reshape | solution.py:55
  34.7 1.6 copy.25
  36.3 4.2 %all-to-all-start.1 = ((bf16[80,3,8,2,128]{4,3,0,1,2:T(2,128)(2,1)}), bf16[80,3,8,2,128]{4,3,0,1,2:T(2,128)(2,1)S(1)}, u32[]{:S(2)}, u32[]{:S(2)}) async-start(bf16[80,3,8,2,128]{4,3,0,1,2:T(2,128)(2,1)} %copy.25), calls=%async_computation.1 | async-start | bytes 1966080 | tf_op jit(solution)/shard_map/all_to_all | solution.py:54
  40.5 0.0 all-gather.2.cloned.1.call-start
  40.5 22.4 %all-to-all-done.1 = bf16[80,3,8,2,128]{4,3,0,1,2:T(2,128)(2,1)S(1)} async-done(((bf16[80,3,8,2,128]{4,3,0,1,2:T(2,128)(2,1)}), bf16[80,3,8,2,128]{4,3,0,1,2:T(2,128)(2,1)S(1)}, u32[]{:S(2)}, u32[]{:S(2)}) %all-to-all-start.1) | async-done | bytes 983072 | tf_op jit(solution)/shard_map/all_to_all | solution.py:54
  62.9 0.1 copy.26
  63.1 0.0 collective-permute-done
  63.1 3.1 %maximum_select_fusion = bf16[2,640,3,256]{3,1,2,0:T(8,128)(2,1)} fusion(bf16[1,640,3,256]{3,1,2,0:T(8,128)(2,1)} %bitcast.27, bf16[1,640,3,256]{3,1,2,0:T(8,128)(2,1)S(1)} %bitcast.81, pred[]{:T(512)S(6)} %eq.18), kind=kLoop, calls=%fused_computation.8 | loop fusion | flops 2949120 | bytes 3932161 | tf_op jit(solution)/shard_map/jit(_where)/select_n | solution.py:65
  66.2 0.0 all-gather.2.cloned.1.call-update
  66.2 0.2 dynamic-slice_bitcast_fusion.2
  66.5 2.2 %collective-permute-start.1 = (bf16[640,3,128]{2,0,1:T(8,128)(2,1)S(1)}, bf16[640,3,128]{2,0,1:T(8,128)(2,1)S(1)}, u32[]{:S(2)}, u32[]{:S(2)}) collective-permute-start(bf16[640,3,128]{2,0,1:T(8,128)(2,1)S(1)} %get-tuple-element.13), channel_id=1, source_target_pairs={{0,1},{1,0},{2,3},{3,2},{4,5},{5,4},{6,7},{7,6},{8,9},{9,8},{10,11... | collective-permute-start | bytes 1474568 | tf_op jit(solution)/shard_map/ppermute | solution.py:62
  68.6 0.0 copy-done.2
  68.6 0.7 fusion.10
  69.3 1.9 %fusion.8 = (s32[16]{0:T(128)S(1)}, s32[16]{0:T(128)S(1)}) fusion(s32[16,2]{0,1:T(2,128)S(1)} %copy-done.3, s32[]{:T(128)} %bitcast.36, s32[]{:T(128)} %bitcast.38, s32[]{:T(128)} %bitcast.37), kind=kLoop, calls=%fused_computation.42 | loop fusion | flops 320 | bytes 268 | tf_op jit(solution)/shard_map/select_n | solution.py:86
  71.3 0.0 collective-permute-done.1
  71.3 0.3 maximum_select_fusion.1
  71.5 0.3 collective-permute-start.2
  71.8 2.5 %collective-permute-start.3 = (bf16[1280,3,128]{2,0,1:T(8,128)(2,1)S(1)}, bf16[1280,3,128]{2,0,1:T(8,128)(2,1)S(1)}, u32[]{:S(2)}, u32[]{:S(2)}) collective-permute-start(bf16[1280,3,128]{2,0,1:T(8,128)(2,1)S(1)} %bitcast.74), channel_id=1, source_target_pairs={{0,48},{16,0},{32,16},{48,32},{1,49},{17,1},{33,17},{49,33},{2,50}... | collective-permute-start | bytes 2949128 | tf_op jit(solution)/shard_map/ppermute | solution.py:24
  74.3 0.0 collective-permute-start.6
  74.4 0.8 dynamic_slice.16
  75.2 0.8 dynamic_slice.15
  75.9 0.7 gather_fusion.1
  76.6 0.7 gather_fusion.2
  77.3 0.7 gather_fusion.3
  78.0 0.1 broadcast_add_fusion
  78.1 5.5 %broadcast_in_dim.53 = bf16[2,4,1280,3,128]{4,2,3,1,0:T(8,128)(2,1)} broadcast(bf16[]{:T(256)} %constant.91.clone.1), dimensions={} | broadcast | bytes 7864322 | tf_op jit(solution)/shard_map/broadcast_in_dim | solution.py:70
  83.6 1.0 constant_dynamic-update-slice_fusion
  84.6 11.6 %collective-permute-done.2 = bf16[1280,3,128]{2,0,1:T(8,128)(2,1)S(1)} collective-permute-done((bf16[1280,3,128]{2,0,1:T(8,128)(2,1)S(1)}, bf16[1280,3,128]{2,0,1:T(8,128)(2,1)S(1)}, u32[]{:S(2)}, u32[]{:S(2)}) %collective-permute-start.2) | collective-permute-done | bytes 983072 | tf_op jit(solution)/shard_map/ppermute | solution.py:23
  96.3 0.1 collective-permute-start.4
  96.3 0.0 collective-permute-done.3
  96.4 2.7 %collective-permute-start.5 = (bf16[640,3,128]{2,0,1:T(8,128)(2,1)S(1)}, bf16[640,3,128]{2,0,1:T(8,128)(2,1)S(1)}, u32[]{:S(2)}, u32[]{:S(2)}) collective-permute-start(bf16[640,3,128]{2,0,1:T(8,128)(2,1)S(1)} %slice.41), channel_id=1, source_target_pairs={{0,48},{16,0},{32,16},{48,32},{1,49},{17,1},{33,17},{49,33},{2,50}... | collective-permute-start | bytes 1474568 | tf_op jit(solution)/shard_map/ppermute | solution.py:30
  99.1 0.0 collective-permute-done.6
  99.1 0.0 collective-permute-start.7
  99.1 2.7 %collective-permute-start.8 = (bf16[1280,3,128]{2,0,1:T(8,128)(2,1)}, bf16[1280,3,128]{2,0,1:T(8,128)(2,1)S(1)}, u32[]{:S(2)}, u32[]{:S(2)}) collective-permute-start(bf16[1280,3,128]{2,0,1:T(8,128)(2,1)} %collective-permute-done.6), channel_id=1, source_target_pairs={{0,48},{16,0},{32,16},{48,32},{1,49},{17,1},{33,17},{49,33},{2,50}... | collective-permute-start | bytes 2949128 | tf_op jit(solution)/shard_map/ppermute | solution.py:24
  101.8 1.0 bitcast_dynamic-update-slice_fusion.4
  102.8 1.0 bitcast_dynamic-update-slice_fusion.3
  103.8 5.8 %collective-permute-done.4 = bf16[640,3,128]{2,0,1:T(8,128)(2,1)S(1)} collective-permute-done((bf16[640,3,128]{2,0,1:T(8,128)(2,1)S(1)}, bf16[640,3,128]{2,0,1:T(8,128)(2,1)S(1)}, u32[]{:S(2)}, u32[]{:S(2)}) %collective-permute-start.4) | collective-permute-done | bytes 491552 | tf_op jit(solution)/shard_map/ppermute | solution.py:29
  109.7 0.9 bitcast_dynamic-update-slice_fusion.8
  110.5 0.0 collective-permute-done.5
  110.5 0.9 bitcast_dynamic-update-slice_fusion.7
  111.4 2.2 %bitcast_dynamic-update-slice_fusion.2 = bf16[2,4,1280,3,128]{4,2,3,1,0:T(8,128)(2,1)} fusion(bf16[2,4,1280,3,128]{4,2,3,1,0:T(8,128)(2,1)} %bitcast_dynamic-update-slice_fusion.7, s32[]{:T(128)S(6)} %select_n.167, s32[]{:T(128)S(6)} %select_n.158, bf16[1280,3,128]{2,0,1:T(8,128)(2,1)} %collective-permute-done.6), kind=kLoop, calls=%fused_computation.15 | loop fusion | bytes 1966088 | tf_op jit(solution)/shard_map/dynamic_update_slice | solution.py:16
  113.6 17.1 %collective-permute-done.7 = bf16[1280,3,128]{2,0,1:T(8,128)(2,1)S(1)} collective-permute-done((bf16[1280,3,128]{2,0,1:T(8,128)(2,1)}, bf16[1280,3,128]{2,0,1:T(8,128)(2,1)S(1)}, u32[]{:S(2)}, u32[]{:S(2)}) %collective-permute-start.7) | collective-permute-done | bytes 983072 | tf_op jit(solution)/shard_map/ppermute | solution.py:23
  130.8 0.1 collective-permute-start.9
  130.8 0.0 collective-permute-done.8
  130.9 2.9 %collective-permute-start.10 = (bf16[640,3,128]{2,0,1:T(8,128)(2,1)S(1)}, bf16[640,3,128]{2,0,1:T(8,128)(2,1)S(1)}, u32[]{:S(2)}, u32[]{:S(2)}) collective-permute-start(bf16[640,3,128]{2,0,1:T(8,128)(2,1)S(1)} %slice.43), channel_id=1, source_target_pairs={{0,48},{16,0},{32,16},{48,32},{1,49},{17,1},{33,17},{49,33},{2,50}... | collective-permute-start | bytes 1474568 | tf_op jit(solution)/shard_map/ppermute | solution.py:30
  133.8 1.0 bitcast_dynamic-update-slice_fusion.1
  134.8 1.0 bitcast_dynamic-update-slice_fusion
  135.8 7.6 %collective-permute-done.9 = bf16[640,3,128]{2,0,1:T(8,128)(2,1)S(1)} collective-permute-done((bf16[640,3,128]{2,0,1:T(8,128)(2,1)S(1)}, bf16[640,3,128]{2,0,1:T(8,128)(2,1)S(1)}, u32[]{:S(2)}, u32[]{:S(2)}) %collective-permute-start.9) | collective-permute-done | bytes 491552 | tf_op jit(solution)/shard_map/ppermute | solution.py:29
  143.4 0.9 bitcast_dynamic-update-slice_fusion.6
  144.3 0.0 collective-permute-done.10
  144.3 0.9 bitcast_dynamic-update-slice_fusion.5
  145.2 2.8 %all-gather.2.cloned.1.call-done = bf16[16,640,3,256]{3,1,2,0:T(8,128)(2,1)} async-done(((bf16[2,640,3,256]{3,1,2,0:T(8,128)(2,1)}), bf16[16,640,3,256]{3,1,2,0:T(8,128)(2,1)}) %all-gather.2.cloned.1.call-update) | async-done | bytes 15728656 | tf_op jit(solution)/shard_map/all_gather | solution.py:66
  148.0 11.8 %fusion.3 = f32[3,3,256,128]{2,3,0,1:T(8,128)S(1)} fusion(bf16[4,2,2,2,4,80,3,256,1]{7,5,4,3,6,2,1,0,8:T(8,128)(2,1)} %bitcast.85, bf16[2,4,2,4,2,80,3,128,1]{7,5,4,3,2,6,1,0,8:T(8,128)(2,1)} %bitcast.24), kind=kOutput, calls=%fused_computation.9 | convolution fusion | flops 6039797760 | bytes 24772608 | tf_op jit(solution)/shard_map/xchzypia,zycxhpjb->ijab/dot_general | solution.py:75
  159.8 0.4 copy.32
  160.2 0.7 gather_fusion
  160.9 1.9 %add_divide_fusion = f32[16,256,128]{2,1,0:T(8,128)} fusion(f32[16,256,128]{2,1,0:T(8,128)S(1)} %gather_fusion, f32[16]{0:T(128)S(1)} %gather_fusion.3, f32[16]{0:T(128)S(1)} %gather_fusion.2, f32[16]{0:T(128)S(1)} %gather_fusion.1, f32[256,128]{1,0:T(8,128)S(1)} %broadcast_add_fusion, pred[16]{0:T(512)(128)(4,1)S(1)} %get-tuple-element.9), kind=kLoop, calls=%fused_computation.7 | loop fusion | flops 3145728 | bytes 4325584 | tf_op jit(solution)/shard_map/div | solution.py:95
  (14 shorter events, 0.2 us)
Async XLA Ops:
  6.5 69.4 %copy-start = (f32[300]{0:T(512)S(1)}, f32[300]{0:T(512)}, u32[]{:S(2)}) copy-start(f32[300]{0:T(512)} %param.8) | copy-start | bytes 3604
  28.4 40.3 %copy-start.2 = (s32[3]{0:T(128)S(1)}, s32[3]{0:T(128)}, u32[]{:S(2)}) copy-start(s32[3]{0:T(128)} %param.10) | copy-start | bytes 40
  28.4 40.9 %copy-start.4 = (s32[16]{0:T(128)S(1)}, s32[16]{0:T(128)}, u32[]{:S(2)}) copy-start(s32[16]{0:T(128)} %param.12) | copy-start | bytes 196
  28.4 40.9 %copy-start.3 = (s32[16,2]{0,1:T(2,128)S(1)}, s32[16,2]{0,1:T(2,128)}, u32[]{:S(2)}) copy-start(s32[16,2]{0,1:T(2,128)} %param.11) | copy-start | bytes 388
  28.4 34.7 %collective-permute-start = (bf16[640,3,256]{2,0,1:T(8,128)(2,1)S(1)}, bf16[640,3,256]{2,0,1:T(8,128)(2,1)}, u32[]{:S(2)}, u32[]{:S(2)}) collective-permute-start(bf16[640,3,256]{2,0,1:T(8,128)(2,1)S(1)} %bitcast.80), channel_id=1, source_target_pairs={{0,2},{2,0},{1,3},{3,1},{4,6},{6,4},{5,7},{7,5},{8,10},{10,8},{9,1... | collective-permute-start | bytes 2949128 | tf_op jit(solution)/shard_map/ppermute | solution.py:53
  36.3 40.9 %copy-start.1 = (f32[4]{0:T(128)S(1)}, f32[4]{0:T(128)}, u32[]{:S(2)}) copy-start(f32[4]{0:T(128)} %param.13) | copy-start | bytes 52
  36.3 26.6 %all-to-all-start.1 = ((bf16[80,3,8,2,128]{4,3,0,1,2:T(2,128)(2,1)}), bf16[80,3,8,2,128]{4,3,0,1,2:T(2,128)(2,1)S(1)}, u32[]{:S(2)}, u32[]{:S(2)}) async-start(bf16[80,3,8,2,128]{4,3,0,1,2:T(2,128)(2,1)} %copy.25), calls=%async_computation.1 | async-start | bytes 1966080 | tf_op jit(solution)/shard_map/all_to_all | solution.py:54
  40.5 107.5 %all-gather.2.cloned.1.call-start = ((), (), s32[]{:S(2)}) async-start(), calls=%async_computation.2 | async-start | bytes 17694720 | tf_op jit(solution)/shard_map/all_gather | solution.py:66
  66.5 4.8 %collective-permute-start.1 = (bf16[640,3,128]{2,0,1:T(8,128)(2,1)S(1)}, bf16[640,3,128]{2,0,1:T(8,128)(2,1)S(1)}, u32[]{:S(2)}, u32[]{:S(2)}) collective-permute-start(bf16[640,3,128]{2,0,1:T(8,128)(2,1)S(1)} %get-tuple-element.13), channel_id=1, source_target_pairs={{0,1},{1,0},{2,3},{3,2},{4,5},{5,4},{6,7},{7,6},{8,9},{9,8},{10,11... | collective-permute-start | bytes 1474568 | tf_op jit(solution)/shard_map/ppermute | solution.py:62
  71.5 24.7 %collective-permute-start.2 = (bf16[1280,3,128]{2,0,1:T(8,128)(2,1)S(1)}, bf16[1280,3,128]{2,0,1:T(8,128)(2,1)S(1)}, u32[]{:S(2)}, u32[]{:S(2)}) collective-permute-start(bf16[1280,3,128]{2,0,1:T(8,128)(2,1)S(1)} %bitcast.73), channel_id=1, source_target_pairs={{0,16},{16,32},{32,48},{48,0},{1,17},{17,33},{33,49},{49,1},{2,18}... | collective-permute-start | bytes 2949128 | tf_op jit(solution)/shard_map/ppermute | solution.py:23
  71.8 24.5 %collective-permute-start.3 = (bf16[1280,3,128]{2,0,1:T(8,128)(2,1)S(1)}, bf16[1280,3,128]{2,0,1:T(8,128)(2,1)S(1)}, u32[]{:S(2)}, u32[]{:S(2)}) collective-permute-start(bf16[1280,3,128]{2,0,1:T(8,128)(2,1)S(1)} %bitcast.74), channel_id=1, source_target_pairs={{0,48},{16,0},{32,16},{48,32},{1,49},{17,1},{33,17},{49,33},{2,50}... | collective-permute-start | bytes 2949128 | tf_op jit(solution)/shard_map/ppermute | solution.py:24
  74.3 24.8 %collective-permute-start.6 = (bf16[1280,3,128]{2,0,1:T(8,128)(2,1)S(1)}, bf16[1280,3,128]{2,0,1:T(8,128)(2,1)}, u32[]{:S(2)}, u32[]{:S(2)}) collective-permute-start(bf16[1280,3,128]{2,0,1:T(8,128)(2,1)S(1)} %bitcast.75), channel_id=1, source_target_pairs={{0,64},{64,0},{1,65},{65,1},{2,66},{66,2},{3,67},{67,3},{4,68},{68... | collective-permute-start | bytes 2949128 | tf_op jit(solution)/shard_map/ppermute | solution.py:68
  96.3 13.4 %collective-permute-start.4 = (bf16[640,3,128]{2,0,1:T(8,128)(2,1)S(1)}, bf16[640,3,128]{2,0,1:T(8,128)(2,1)S(1)}, u32[]{:S(2)}, u32[]{:S(2)}) collective-permute-start(bf16[640,3,128]{2,0,1:T(8,128)(2,1)S(1)} %slice.40), channel_id=1, source_target_pairs={{0,16},{16,32},{32,48},{48,0},{1,17},{17,33},{33,49},{49,1},{2,18}... | collective-permute-start | bytes 1474568 | tf_op jit(solution)/shard_map/ppermute | solution.py:29
  96.4 14.2 %collective-permute-start.5 = (bf16[640,3,128]{2,0,1:T(8,128)(2,1)S(1)}, bf16[640,3,128]{2,0,1:T(8,128)(2,1)S(1)}, u32[]{:S(2)}, u32[]{:S(2)}) collective-permute-start(bf16[640,3,128]{2,0,1:T(8,128)(2,1)S(1)} %slice.41), channel_id=1, source_target_pairs={{0,48},{16,0},{32,16},{48,32},{1,49},{17,1},{33,17},{49,33},{2,50}... | collective-permute-start | bytes 1474568 | tf_op jit(solution)/shard_map/ppermute | solution.py:30
  99.1 31.6 %collective-permute-start.7 = (bf16[1280,3,128]{2,0,1:T(8,128)(2,1)}, bf16[1280,3,128]{2,0,1:T(8,128)(2,1)S(1)}, u32[]{:S(2)}, u32[]{:S(2)}) collective-permute-start(bf16[1280,3,128]{2,0,1:T(8,128)(2,1)} %collective-permute-done.6), channel_id=1, source_target_pairs={{0,16},{16,32},{32,48},{48,0},{1,17},{17,33},{33,49},{49,1},{2,18}... | collective-permute-start | bytes 2949128 | tf_op jit(solution)/shard_map/ppermute | solution.py:23
  99.1 31.7 %collective-permute-start.8 = (bf16[1280,3,128]{2,0,1:T(8,128)(2,1)}, bf16[1280,3,128]{2,0,1:T(8,128)(2,1)S(1)}, u32[]{:S(2)}, u32[]{:S(2)}) collective-permute-start(bf16[1280,3,128]{2,0,1:T(8,128)(2,1)} %collective-permute-done.6), channel_id=1, source_target_pairs={{0,48},{16,0},{32,16},{48,32},{1,49},{17,1},{33,17},{49,33},{2,50}... | collective-permute-start | bytes 2949128 | tf_op jit(solution)/shard_map/ppermute | solution.py:24
  130.8 12.6 %collective-permute-start.9 = (bf16[640,3,128]{2,0,1:T(8,128)(2,1)S(1)}, bf16[640,3,128]{2,0,1:T(8,128)(2,1)S(1)}, u32[]{:S(2)}, u32[]{:S(2)}) collective-permute-start(bf16[640,3,128]{2,0,1:T(8,128)(2,1)S(1)} %slice.42), channel_id=1, source_target_pairs={{0,16},{16,32},{32,48},{48,0},{1,17},{17,33},{33,49},{49,1},{2,18}... | collective-permute-start | bytes 1474568 | tf_op jit(solution)/shard_map/ppermute | solution.py:29
  130.9 13.4 %collective-permute-start.10 = (bf16[640,3,128]{2,0,1:T(8,128)(2,1)S(1)}, bf16[640,3,128]{2,0,1:T(8,128)(2,1)S(1)}, u32[]{:S(2)}, u32[]{:S(2)}) collective-permute-start(bf16[640,3,128]{2,0,1:T(8,128)(2,1)S(1)} %slice.43), channel_id=1, source_target_pairs={{0,48},{16,0},{32,16},{48,32},{1,49},{17,1},{33,17},{49,33},{2,50}... | collective-permute-start | bytes 1474568 | tf_op jit(solution)/shard_map/ppermute | solution.py:30
Sparse Core Ops, SparseCore 0:
  66.4 81.6 all-gather.1

commit v14 on v13

--- a/solution.py
+++ b/solution.py
@@ -54,15 +54,16 @@
     by_chip = lax.all_to_all(
         factors.reshape(local_aux, nocc, n_x * n_zh, n_core, cols_b), ("x", "zh"), split_axis=2, concat_axis=0, tiled=True
     )
-    other_a, by_chip = lax.optimization_barrier((other_a, by_chip))
+    twice_a = jnp.stack([spread_a, spread_a])
+    other_a, by_chip, twice_a = lax.optimization_barrier((other_a, by_chip, twice_a))
     me_core = lax.axis_index("core")
     by_chip = by_chip.reshape(n_x * n_zh * local_aux, nocc, n_core, cols_b)
     keep = lax.dynamic_index_in_dim(by_chip, me_core, 2, keepdims=False)
     give = lax.dynamic_index_in_dim(by_chip, (me_core + 1) % n_core, 2, keepdims=False)
     got = lax.ppermute(give, "core", [(k, (k + 1) % n_core) for k in range(n_core)])
     spread_b = jnp.where(me_core == 0, jnp.stack([keep, got]), jnp.stack([got, keep]))
-    first_zh = lax.axis_index("zh") == 0
-    pair_a = jnp.where(first_zh, jnp.stack([spread_a, other_a]), jnp.stack([other_a, spread_a]))
+    other_slot = (lax.axis_index("zh") + 1) % n_zh
+    pair_a = lax.dynamic_update_index_in_dim(twice_a, other_a, other_slot, 0)
     block_a = lax.all_gather(pair_a, ("x", "core"), axis=0, tiled=True)
     spread_b = spread_b.reshape(n_col * local_aux, nocc, cols_b)
     other_b = lax.ppermute(spread_b, "zl", [(k, (k + 1) % n_zl) for k in range(n_zl)])

time: 170 us -> 176 us (1.035)
  blocking collectives: 20.5 us -> 0 us
  waiting for transfers between devices: 67.3 us -> 82.2 us
  starting transfers between devices: 20.9 us -> 29.6 us
  local copies, waits for them, and re-layouts: 28 us -> 32 us
    all_to_all x1 -> x0, blocking collectives: 20.5 us -> none  [shards(): lax.all_to_all(factors.reshape(local_aux, nocc, n_row, rows_a), ('zl', 'y...]
    ppermute x1, waiting for transfers between devices: 0.01 us -> 17.7 us  [shards(): lax.ppermute(spread_a, 'zh', [(k, (k + 1) % n_zh) for k in range(n_zh)])]
    all_to_all x1, waiting for transfers between devices: 22.4 us -> 11 us  [shards(): lax.all_to_all(factors.reshape(local_aux, nocc, n_x * n_zh, n_core, cols_...]
    all_to_all x0 -> x1, waiting for transfers between devices: none -> 10.6 us  [shards(): lax.all_to_all(factors.reshape(local_aux, nocc, n_row, rows_a), ('zl', 'y...]
    all_to_all x0 -> x1, starting transfers between devices: none -> 6.36 us  [shards(): lax.all_to_all(factors.reshape(local_aux, nocc, n_row, rows_a), ('zl', 'y...]
    select_n x1 -> x0, other arithmetic: 3.13 us -> none  [shards(): jnp.where(first_zh, jnp.stack([spread_a, other_a]), jnp.stack([other_a, s...]
    all_to_all x1, starting transfers between devices: 4.15 us -> 7.04 us  [shards(): lax.all_to_all(factors.reshape(local_aux, nocc, n_x * n_zh, n_core, cols_...]
    all_gather x1, waiting for transfers between devices: 2.81 us -> 0.29 us  [shards(): block_a = lax.all_gather(pair_a, ('x', 'core'), axis=0, tiled=True)]
  transfers between devices with their start and end apart: 13 -> 14, of which waited for: 6 -> 8; matrix products, arithmetic and copies ran while one was open for 16% -> 17% of each run, Pallas kernels for 0% -> 0%
where the time goes in v14:
time: 176 us; the launch traced here: 175 us
  waiting for transfers between devices  82.2 us (47%)
  local copies, waits for them, and re-layouts  32 us (18%)
  starting transfers between devices  29.6 us (17%)
  between operations  13.7 us (8%)
  matrix products  11.8 us (7%)
  other arithmetic  5.97 us (3%)
    ppermute x2, waiting for transfers between devices, ring_into(): go_right = lax.ppermute(go_right, axis, right)  29.3 us
    ppermute x1, waiting for transfers between devices, shards(): lax.ppermute(spread_a, 'zh', [(k, (k + 1) % n_zh) for k in range(n_zh)])  17.7 us
    ppermute x2, waiting for transfers between devices, ring_into(): from_left = lax.ppermute(go_right[:half], axis, right)  13.3 us
    dot_general x1, matrix products, shards(): jnp.einsum('xchzypia,zycxhpjb->ijab', block_a, block_b, preferred_element...  11.8 us
    dynamic_update_slice x10, local copies, waits for them, and re-layouts, put(): return lax.dynamic_update_slice(buf, piece[None, None], start)  11.1 us
    all_to_all x1, waiting for transfers between devices, shards(): lax.all_to_all(factors.reshape(local_aux, nocc, n_x * n_zh, n_core, cols_...  11 us
    all_to_all x1, waiting for transfers between devices, shards(): lax.all_to_all(factors.reshape(local_aux, nocc, n_row, rows_a), ('zl', 'y...  10.6 us
    all_to_all x1, starting transfers between devices, shards(): lax.all_to_all(factors.reshape(local_aux, nocc, n_x * n_zh, n_core, cols_...  7.04 us
  transfers between devices with their start and end apart: 14, of which 8 were waited for; matrix products, arithmetic and copies ran while one was open for 17% of the time, Pallas kernels for 0%

profile of v14, /device:TPU:1, one launch (start us, length us, event | category | flops | bytes accessed | tf_op | source)
XLA Modules:
  0.0 175.2 jit_solution(13170316118552499680)
XLA Ops:
  6.5 2.2 %copy.51 = bf16[3,10,8,8,256]{4,3,1,0,2:T(8,128)(2,1)} copy(bf16[3,10,8,8,256]{4,3,2,1,0:T(8,128)(2,1)} %bitcast.78) | data formatting | bytes 1966080 | tf_op jit(solution)/shard_map/reshape | solution.py:50
  8.8 6.4 %all-to-all-start = ((bf16[80,3,8,256]{3,0,1,2:T(8,128)(2,1)}), bf16[80,3,8,256]{3,0,1,2:T(8,128)(2,1)S(1)}, u32[]{:S(2)}, u32[]{:S(2)}) async-start(bf16[80,3,8,256]{3,0,1,2:T(8,128)(2,1)} %bitcast.72), calls=%async_computation | async-start | bytes 1966080 | tf_op jit(solution)/shard_map/all_to_all | solution.py:49
  15.1 2.9 %reshape.117 = bf16[80,3,8,2,128]{4,3,2,0,1:T(2,128)(2,1)S(1)} reshape(bf16[80,3,2048]{2,0,1:T(8,128)(2,1)} %param.7) | data formatting | bytes 1966080 | tf_op jit(solution)/shard_map/reshape | solution.py:55
  18.0 1.6 copy.25
  19.7 10.6 %all-to-all-done = bf16[80,3,8,256]{3,0,1,2:T(8,128)(2,1)S(1)} async-done(((bf16[80,3,8,256]{3,0,1,2:T(8,128)(2,1)}), bf16[80,3,8,256]{3,0,1,2:T(8,128)(2,1)S(1)}, u32[]{:S(2)}, u32[]{:S(2)}) %all-to-all-start) | async-done | bytes 983072 | tf_op jit(solution)/shard_map/all_to_all | solution.py:49
  30.3 7.0 %all-to-all-start.1 = ((bf16[80,3,8,2,128]{4,3,0,1,2:T(2,128)(2,1)}), bf16[80,3,8,2,128]{4,3,0,1,2:T(2,128)(2,1)S(1)}, u32[]{:S(2)}, u32[]{:S(2)}) async-start(bf16[80,3,8,2,128]{4,3,0,1,2:T(2,128)(2,1)} %copy.25), calls=%async_computation.1 | async-start | bytes 1966080 | tf_op jit(solution)/shard_map/all_to_all | solution.py:54
  37.3 0.0 all-gather.2.cloned.1.call-start
  37.4 1.0 copy.24
  38.4 2.9 %collective-permute-start = (bf16[640,3,256]{2,0,1:T(8,128)(2,1)}, bf16[640,3,256]{2,0,1:T(8,128)(2,1)}, u32[]{:S(2)}, u32[]{:S(2)}) collective-permute-start(bf16[640,3,256]{2,0,1:T(8,128)(2,1)} %bitcast.3), channel_id=1, source_target_pairs={{0,2},{2,0},{1,3},{3,1},{4,6},{6,4},{5,7},{7,5},{8,10},{10,8},{9,1... | collective-permute-start | bytes 2949128 | tf_op jit(solution)/shard_map/ppermute | solution.py:53
  41.3 11.0 %all-to-all-done.1 = bf16[80,3,8,2,128]{4,3,0,1,2:T(2,128)(2,1)S(1)} async-done(((bf16[80,3,8,2,128]{4,3,0,1,2:T(2,128)(2,1)}), bf16[80,3,8,2,128]{4,3,0,1,2:T(2,128)(2,1)S(1)}, u32[]{:S(2)}, u32[]{:S(2)}) %all-to-all-start.1) | async-done | bytes 983072 | tf_op jit(solution)/shard_map/all_to_all | solution.py:54
  52.3 0.1 copy.26
  52.5 1.8 %pad_maximum_fusion = bf16[2,640,3,256]{3,1,2,0:T(8,128)(2,1)S(1)} fusion(bf16[1,640,3,256]{3,1,2,0:T(8,128)(2,1)} %bitcast.8), kind=kLoop, calls=%fused_computation.8 | loop fusion | flops 983040 | bytes 2949120 | tf_op jit(solution)/shard_map/stack | solution.py:57
  54.2 17.7 %collective-permute-done = bf16[640,3,256]{2,0,1:T(8,128)(2,1)} collective-permute-done((bf16[640,3,256]{2,0,1:T(8,128)(2,1)}, bf16[640,3,256]{2,0,1:T(8,128)(2,1)}, u32[]{:S(2)}, u32[]{:S(2)}) %collective-permute-start) | collective-permute-done | bytes 983072 | tf_op jit(solution)/shard_map/ppermute | solution.py:53
  71.9 1.3 bitcast_dynamic-update-slice_fusion
  73.2 0.0 copy-start.2
  73.2 1.3 copy-done.2
  74.5 0.0 all-gather.2.cloned.1.call-update
  74.5 0.2 dynamic-slice_bitcast_fusion.2
  74.7 2.0 %collective-permute-start.1 = (bf16[640,3,128]{2,0,1:T(8,128)(2,1)S(1)}, bf16[640,3,128]{2,0,1:T(8,128)(2,1)S(1)}, u32[]{:S(2)}, u32[]{:S(2)}) collective-permute-start(bf16[640,3,128]{2,0,1:T(8,128)(2,1)S(1)} %get-tuple-element.15), channel_id=1, source_target_pairs={{0,1},{1,0},{2,3},{3,2},{4,5},{5,4},{6,7},{7,6},{8,9},{9,8},{10,11... | collective-permute-start | bytes 1474568 | tf_op jit(solution)/shard_map/ppermute | solution.py:63
  76.7 0.7 fusion.10
  77.4 1.9 %fusion.8 = (s32[16]{0:T(128)S(1)}, s32[16]{0:T(128)S(1)}) fusion(s32[16,2]{0,1:T(2,128)S(1)} %copy-done.4, s32[]{:T(128)} %bitcast.35, s32[]{:T(128)} %bitcast.37, s32[]{:T(128)} %bitcast.36), kind=kLoop, calls=%fused_computation.43 | loop fusion | flops 320 | bytes 268 | tf_op jit(solution)/shard_map/select_n | solution.py:87
  79.3 0.0 collective-permute-done.1
  79.3 0.3 maximum_select_fusion
  79.6 0.1 collective-permute-start.2
  79.6 2.7 %collective-permute-start.3 = (bf16[1280,3,128]{2,0,1:T(8,128)(2,1)S(1)}, bf16[1280,3,128]{2,0,1:T(8,128)(2,1)S(1)}, u32[]{:S(2)}, u32[]{:S(2)}) collective-permute-start(bf16[1280,3,128]{2,0,1:T(8,128)(2,1)S(1)} %bitcast.75), channel_id=1, source_target_pairs={{0,48},{16,0},{32,16},{48,32},{1,49},{17,1},{33,17},{49,33},{2,50}... | collective-permute-start | bytes 2949128 | tf_op jit(solution)/shard_map/ppermute | solution.py:24
  82.3 0.0 collective-permute-start.6
  82.4 0.8 dynamic_slice.16
  83.2 0.8 dynamic_slice.15
  84.0 0.7 gather_fusion.1
  84.6 0.7 gather_fusion.2
  85.3 0.0 copy-done.1
  85.3 0.7 gather_fusion.3
  86.0 0.1 broadcast_add_fusion
  86.1 4.8 %broadcast_in_dim.57 = bf16[2,4,1280,3,128]{4,2,3,1,0:T(8,128)(2,1)} broadcast(bf16[]{:T(256)} %constant.99.clone.1), dimensions={} | broadcast | bytes 7864322 | tf_op jit(solution)/shard_map/broadcast_in_dim | solution.py:71
  90.9 1.0 constant_dynamic-update-slice_fusion
  91.9 12.3 %collective-permute-done.2 = bf16[1280,3,128]{2,0,1:T(8,128)(2,1)S(1)} collective-permute-done((bf16[1280,3,128]{2,0,1:T(8,128)(2,1)S(1)}, bf16[1280,3,128]{2,0,1:T(8,128)(2,1)S(1)}, u32[]{:S(2)}, u32[]{:S(2)}) %collective-permute-start.2) | collective-permute-done | bytes 983072 | tf_op jit(solution)/shard_map/ppermute | solution.py:23
  104.3 0.1 collective-permute-start.4
  104.4 0.0 collective-permute-done.3
  104.4 2.7 %collective-permute-start.5 = (bf16[640,3,128]{2,0,1:T(8,128)(2,1)S(1)}, bf16[640,3,128]{2,0,1:T(8,128)(2,1)S(1)}, u32[]{:S(2)}, u32[]{:S(2)}) collective-permute-start(bf16[640,3,128]{2,0,1:T(8,128)(2,1)S(1)} %slice.41), channel_id=1, source_target_pairs={{0,48},{16,0},{32,16},{48,32},{1,49},{17,1},{33,17},{49,33},{2,50}... | collective-permute-start | bytes 1474568 | tf_op jit(solution)/shard_map/ppermute | solution.py:30
  107.1 0.0 collective-permute-done.6
  107.1 0.0 collective-permute-start.7
  107.1 2.7 %collective-permute-start.8 = (bf16[1280,3,128]{2,0,1:T(8,128)(2,1)}, bf16[1280,3,128]{2,0,1:T(8,128)(2,1)S(1)}, u32[]{:S(2)}, u32[]{:S(2)}) collective-permute-start(bf16[1280,3,128]{2,0,1:T(8,128)(2,1)} %collective-permute-done.6), channel_id=1, source_target_pairs={{0,48},{16,0},{32,16},{48,32},{1,49},{17,1},{33,17},{49,33},{2,50}... | collective-permute-start | bytes 2949128 | tf_op jit(solution)/shard_map/ppermute | solution.py:24
  109.8 1.0 bitcast_dynamic-update-slice_fusion.5
  110.8 1.0 bitcast_dynamic-update-slice_fusion.4
  111.9 5.8 %collective-permute-done.4 = bf16[640,3,128]{2,0,1:T(8,128)(2,1)S(1)} collective-permute-done((bf16[640,3,128]{2,0,1:T(8,128)(2,1)S(1)}, bf16[640,3,128]{2,0,1:T(8,128)(2,1)S(1)}, u32[]{:S(2)}, u32[]{:S(2)}) %collective-permute-start.4) | collective-permute-done | bytes 491552 | tf_op jit(solution)/shard_map/ppermute | solution.py:29
  117.7 0.9 bitcast_dynamic-update-slice_fusion.9
  118.6 0.0 collective-permute-done.5
  118.6 0.9 bitcast_dynamic-update-slice_fusion.8
  119.5 2.3 %bitcast_dynamic-update-slice_fusion.3 = bf16[2,4,1280,3,128]{4,2,3,1,0:T(8,128)(2,1)} fusion(bf16[2,4,1280,3,128]{4,2,3,1,0:T(8,128)(2,1)} %bitcast_dynamic-update-slice_fusion.8, s32[]{:T(128)S(6)} %select_n.167, s32[]{:T(128)S(6)} %select_n.158, bf16[1280,3,128]{2,0,1:T(8,128)(2,1)} %collective-permute-done.6), kind=kLoop, calls=%fused_computation.16 | loop fusion | bytes 1966088 | tf_op jit(solution)/shard_map/dynamic_update_slice | solution.py:16
  121.8 17.0 %collective-permute-done.7 = bf16[1280,3,128]{2,0,1:T(8,128)(2,1)S(1)} collective-permute-done((bf16[1280,3,128]{2,0,1:T(8,128)(2,1)}, bf16[1280,3,128]{2,0,1:T(8,128)(2,1)S(1)}, u32[]{:S(2)}, u32[]{:S(2)}) %collective-permute-start.7) | collective-permute-done | bytes 983072 | tf_op jit(solution)/shard_map/ppermute | solution.py:23
  138.8 0.1 collective-permute-start.9
  138.9 0.0 collective-permute-done.8
  138.9 2.9 %collective-permute-start.10 = (bf16[640,3,128]{2,0,1:T(8,128)(2,1)S(1)}, bf16[640,3,128]{2,0,1:T(8,128)(2,1)S(1)}, u32[]{:S(2)}, u32[]{:S(2)}) collective-permute-start(bf16[640,3,128]{2,0,1:T(8,128)(2,1)S(1)} %slice.43), channel_id=1, source_target_pairs={{0,48},{16,0},{32,16},{48,32},{1,49},{17,1},{33,17},{49,33},{2,50}... | collective-permute-start | bytes 1474568 | tf_op jit(solution)/shard_map/ppermute | solution.py:30
  141.8 1.0 bitcast_dynamic-update-slice_fusion.2
  142.9 1.0 bitcast_dynamic-update-slice_fusion.1
  143.9 7.5 %collective-permute-done.9 = bf16[640,3,128]{2,0,1:T(8,128)(2,1)S(1)} collective-permute-done((bf16[640,3,128]{2,0,1:T(8,128)(2,1)S(1)}, bf16[640,3,128]{2,0,1:T(8,128)(2,1)S(1)}, u32[]{:S(2)}, u32[]{:S(2)}) %collective-permute-start.9) | collective-permute-done | bytes 491552 | tf_op jit(solution)/shard_map/ppermute | solution.py:29
  151.4 0.9 bitcast_dynamic-update-slice_fusion.7
  152.3 0.0 collective-permute-done.10
  152.3 1.0 bitcast_dynamic-update-slice_fusion.6
  153.3 0.3 all-gather.2.cloned.1.call-done
  153.6 11.8 %fusion.3 = f32[3,3,256,128]{2,3,0,1:T(8,128)S(1)} fusion(bf16[4,2,2,2,4,80,3,256,1]{7,5,4,3,6,2,1,0,8:T(8,128)(2,1)} %bitcast.83, bf16[2,4,2,4,2,80,3,128,1]{7,5,4,3,2,6,1,0,8:T(8,128)(2,1)} %bitcast.26), kind=kOutput, calls=%fused_computation.9 | convolution fusion | flops 6039797760 | bytes 24772608 | tf_op jit(solution)/shard_map/xchzypia,zycxhpjb->ijab/dot_general | solution.py:76
  165.3 0.4 copy.32
  165.7 0.7 gather_fusion
  166.4 1.9 %add_divide_fusion = f32[16,256,128]{2,1,0:T(8,128)} fusion(f32[16,256,128]{2,1,0:T(8,128)S(1)} %gather_fusion, f32[16]{0:T(128)S(1)} %gather_fusion.3, f32[16]{0:T(128)S(1)} %gather_fusion.2, f32[16]{0:T(128)S(1)} %gather_fusion.1, f32[256,128]{1,0:T(8,128)S(1)} %broadcast_add_fusion, pred[16]{0:T(512)(128)(4,1)S(1)} %get-tuple-element.11), kind=kLoop, calls=%fused_computation.7 | loop fusion | flops 3145728 | bytes 4325584 | tf_op jit(solution)/shard_map/div | solution.py:96
  (18 shorter events, 0.2 us)
Async XLA Ops:
  6.5 77.4 %copy-start = (f32[300]{0:T(512)S(1)}, f32[300]{0:T(512)}, u32[]{:S(2)}) copy-start(f32[300]{0:T(512)} %param.8) | copy-start | bytes 3604
  8.8 21.5 %all-to-all-start = ((bf16[80,3,8,256]{3,0,1,2:T(8,128)(2,1)}), bf16[80,3,8,256]{3,0,1,2:T(8,128)(2,1)S(1)}, u32[]{:S(2)}, u32[]{:S(2)}) async-start(bf16[80,3,8,256]{3,0,1,2:T(8,128)(2,1)} %bitcast.72), calls=%async_computation | async-start | bytes 1966080 | tf_op jit(solution)/shard_map/all_to_all | solution.py:49
  19.7 57.0 %copy-start.3 = (s32[3]{0:T(128)S(1)}, s32[3]{0:T(128)}, u32[]{:S(2)}) copy-start(s32[3]{0:T(128)} %param.10) | copy-start | bytes 40
  19.7 57.7 %copy-start.5 = (s32[16]{0:T(128)S(1)}, s32[16]{0:T(128)}, u32[]{:S(2)}) copy-start(s32[16]{0:T(128)} %param.12) | copy-start | bytes 196
  19.7 57.7 %copy-start.4 = (s32[16,2]{0,1:T(2,128)S(1)}, s32[16,2]{0,1:T(2,128)}, u32[]{:S(2)}) copy-start(s32[16,2]{0,1:T(2,128)} %param.11) | copy-start | bytes 388
  30.3 22.1 %all-to-all-start.1 = ((bf16[80,3,8,2,128]{4,3,0,1,2:T(2,128)(2,1)}), bf16[80,3,8,2,128]{4,3,0,1,2:T(2,128)(2,1)S(1)}, u32[]{:S(2)}, u32[]{:S(2)}) async-start(bf16[80,3,8,2,128]{4,3,0,1,2:T(2,128)(2,1)} %copy.25), calls=%async_computation.1 | async-start | bytes 1966080 | tf_op jit(solution)/shard_map/all_to_all | solution.py:54
  37.3 116.2 %all-gather.2.cloned.1.call-start = ((), (), s32[]{:S(2)}) async-start(), calls=%async_computation.2 | async-start | bytes 17694720 | tf_op jit(solution)/shard_map/all_gather | solution.py:67
  38.4 46.9 %copy-start.1 = (f32[4]{0:T(128)S(1)}, f32[4]{0:T(128)}, u32[]{:S(2)}) copy-start(f32[4]{0:T(128)} %param.13) | copy-start | bytes 52
  38.4 33.5 %collective-permute-start = (bf16[640,3,256]{2,0,1:T(8,128)(2,1)}, bf16[640,3,256]{2,0,1:T(8,128)(2,1)}, u32[]{:S(2)}, u32[]{:S(2)}) collective-permute-start(bf16[640,3,256]{2,0,1:T(8,128)(2,1)} %bitcast.3), channel_id=1, source_target_pairs={{0,2},{2,0},{1,3},{3,1},{4,6},{6,4},{5,7},{7,5},{8,10},{10,8},{9,1... | collective-permute-start | bytes 2949128 | tf_op jit(solution)/shard_map/ppermute | solution.py:53
  73.2 1.3 copy-start.2
  74.7 4.6 %collective-permute-start.1 = (bf16[640,3,128]{2,0,1:T(8,128)(2,1)S(1)}, bf16[640,3,128]{2,0,1:T(8,128)(2,1)S(1)}, u32[]{:S(2)}, u32[]{:S(2)}) collective-permute-start(bf16[640,3,128]{2,0,1:T(8,128)(2,1)S(1)} %get-tuple-element.15), channel_id=1, source_target_pairs={{0,1},{1,0},{2,3},{3,2},{4,5},{5,4},{6,7},{7,6},{8,9},{9,8},{10,11... | collective-permute-start | bytes 1474568 | tf_op jit(solution)/shard_map/ppermute | solution.py:63
  79.6 24.7 %collective-permute-start.2 = (bf16[1280,3,128]{2,0,1:T(8,128)(2,1)S(1)}, bf16[1280,3,128]{2,0,1:T(8,128)(2,1)S(1)}, u32[]{:S(2)}, u32[]{:S(2)}) collective-permute-start(bf16[1280,3,128]{2,0,1:T(8,128)(2,1)S(1)} %bitcast.74), channel_id=1, source_target_pairs={{0,16},{16,32},{32,48},{48,0},{1,17},{17,33},{33,49},{49,1},{2,18}... | collective-permute-start | bytes 2949128 | tf_op jit(solution)/shard_map/ppermute | solution.py:23
  79.6 24.7 %collective-permute-start.3 = (bf16[1280,3,128]{2,0,1:T(8,128)(2,1)S(1)}, bf16[1280,3,128]{2,0,1:T(8,128)(2,1)S(1)}, u32[]{:S(2)}, u32[]{:S(2)}) collective-permute-start(bf16[1280,3,128]{2,0,1:T(8,128)(2,1)S(1)} %bitcast.75), channel_id=1, source_target_pairs={{0,48},{16,0},{32,16},{48,32},{1,49},{17,1},{33,17},{49,33},{2,50}... | collective-permute-start | bytes 2949128 | tf_op jit(solution)/shard_map/ppermute | solution.py:24
  82.3 24.8 %collective-permute-start.6 = (bf16[1280,3,128]{2,0,1:T(8,128)(2,1)S(1)}, bf16[1280,3,128]{2,0,1:T(8,128)(2,1)}, u32[]{:S(2)}, u32[]{:S(2)}) collective-permute-start(bf16[1280,3,128]{2,0,1:T(8,128)(2,1)S(1)} %bitcast.76), channel_id=1, source_target_pairs={{0,64},{64,0},{1,65},{65,1},{2,66},{66,2},{3,67},{67,3},{4,68},{68... | collective-permute-start | bytes 2949128 | tf_op jit(solution)/shard_map/ppermute | solution.py:69
  104.3 13.4 %collective-permute-start.4 = (bf16[640,3,128]{2,0,1:T(8,128)(2,1)S(1)}, bf16[640,3,128]{2,0,1:T(8,128)(2,1)S(1)}, u32[]{:S(2)}, u32[]{:S(2)}) collective-permute-start(bf16[640,3,128]{2,0,1:T(8,128)(2,1)S(1)} %slice.40), channel_id=1, source_target_pairs={{0,16},{16,32},{32,48},{48,0},{1,17},{17,33},{33,49},{49,1},{2,18}... | collective-permute-start | bytes 1474568 | tf_op jit(solution)/shard_map/ppermute | solution.py:29
  104.4 14.2 %collective-permute-start.5 = (bf16[640,3,128]{2,0,1:T(8,128)(2,1)S(1)}, bf16[640,3,128]{2,0,1:T(8,128)(2,1)S(1)}, u32[]{:S(2)}, u32[]{:S(2)}) collective-permute-start(bf16[640,3,128]{2,0,1:T(8,128)(2,1)S(1)} %slice.41), channel_id=1, source_target_pairs={{0,48},{16,0},{32,16},{48,32},{1,49},{17,1},{33,17},{49,33},{2,50}... | collective-permute-start | bytes 1474568 | tf_op jit(solution)/shard_map/ppermute | solution.py:30
  107.1 31.6 %collective-permute-start.7 = (bf16[1280,3,128]{2,0,1:T(8,128)(2,1)}, bf16[1280,3,128]{2,0,1:T(8,128)(2,1)S(1)}, u32[]{:S(2)}, u32[]{:S(2)}) collective-permute-start(bf16[1280,3,128]{2,0,1:T(8,128)(2,1)} %collective-permute-done.6), channel_id=1, source_target_pairs={{0,16},{16,32},{32,48},{48,0},{1,17},{17,33},{33,49},{49,1},{2,18}... | collective-permute-start | bytes 2949128 | tf_op jit(solution)/shard_map/ppermute | solution.py:23
  107.1 31.7 %collective-permute-start.8 = (bf16[1280,3,128]{2,0,1:T(8,128)(2,1)}, bf16[1280,3,128]{2,0,1:T(8,128)(2,1)S(1)}, u32[]{:S(2)}, u32[]{:S(2)}) collective-permute-start(bf16[1280,3,128]{2,0,1:T(8,128)(2,1)} %collective-permute-done.6), channel_id=1, source_target_pairs={{0,48},{16,0},{32,16},{48,32},{1,49},{17,1},{33,17},{49,33},{2,50}... | collective-permute-start | bytes 2949128 | tf_op jit(solution)/shard_map/ppermute | solution.py:24
  138.8 12.6 %collective-permute-start.9 = (bf16[640,3,128]{2,0,1:T(8,128)(2,1)S(1)}, bf16[640,3,128]{2,0,1:T(8,128)(2,1)S(1)}, u32[]{:S(2)}, u32[]{:S(2)}) collective-permute-start(bf16[640,3,128]{2,0,1:T(8,128)(2,1)S(1)} %slice.42), channel_id=1, source_target_pairs={{0,16},{16,32},{32,48},{48,0},{1,17},{17,33},{33,49},{49,1},{2,18}... | collective-permute-start | bytes 1474568 | tf_op jit(solution)/shard_map/ppermute | solution.py:29
  138.9 13.4 %collective-permute-start.10 = (bf16[640,3,128]{2,0,1:T(8,128)(2,1)S(1)}, bf16[640,3,128]{2,0,1:T(8,128)(2,1)S(1)}, u32[]{:S(2)}, u32[]{:S(2)}) collective-permute-start(bf16[640,3,128]{2,0,1:T(8,128)(2,1)S(1)} %slice.43), channel_id=1, source_target_pairs={{0,48},{16,0},{32,16},{48,32},{1,49},{17,1},{33,17},{49,33},{2,50}... | collective-permute-start | bytes 1474568 | tf_op jit(solution)/shard_map/ppermute | solution.py:30
Sparse Core Ops, SparseCore 0:
  74.6 78.9 all-gather.1

commit v15 on v13

--- a/solution.py
+++ b/solution.py
@@ -46,14 +46,10 @@
     cols_b = nvir // n_col
     row_index = lax.axis_index("zl") * n_y + lax.axis_index("y")
     col_index = (lax.axis_index("x") * n_zh + lax.axis_index("zh")) * n_core + lax.axis_index("core")
-    spread_a = lax.all_to_all(
-        factors.reshape(local_aux, nocc, n_row, rows_a), ("zl", "y"), split_axis=2, concat_axis=0, tiled=True
-    )
+    spread_a = lax.all_to_all(factors, ("zl", "y"), split_axis=2, concat_axis=0, tiled=True)
     spread_a = spread_a.reshape(n_row * local_aux, nocc, rows_a)
     other_a = lax.ppermute(spread_a, "zh", [(k, (k + 1) % n_zh) for k in range(n_zh)])
-    by_chip = lax.all_to_all(
-        factors.reshape(local_aux, nocc, n_x * n_zh, n_core, cols_b), ("x", "zh"), split_axis=2, concat_axis=0, tiled=True
-    )
+    by_chip = lax.all_to_all(factors, ("x", "zh"), split_axis=2, concat_axis=0, tiled=True)
     other_a, by_chip = lax.optimization_barrier((other_a, by_chip))
     me_core = lax.axis_index("core")
     by_chip = by_chip.reshape(n_x * n_zh * local_aux, nocc, n_core, cols_b)

time: 170 us -> 189 us (1.11)
  local copies, waits for them, and re-layouts: 28 us -> 45.4 us
    unnamed x10 -> x15, local copies, waits for them, and re-layouts: 0.03 us -> 17.8 us
    reshape x3 -> x0, local copies, waits for them, and re-layouts: 5.81 us -> none  [the longest x2 4.54 us: shards(): factors.reshape(local_aux, nocc, n_x * n_zh, n_core, cols_b)]
    all_to_all x2, local copies, waits for them, and re-layouts: 0.2 us -> 5.08 us  [the longest x1 3.96 us: shards(): lax.all_to_all(factors, ('zl', 'y'), split_axis=2, concat_axis=0, tiled=T...]
  transfers between devices with their start and end apart: 13 -> 13, of which waited for: 6 -> 6; matrix products, arithmetic and copies ran while one was open for 16% -> 17% of each run, Pallas kernels for 0% -> 0%
where the time goes in v15:
time: 189 us; the launch traced here: 188 us
  waiting for transfers between devices  68 us (36%)
  local copies, waits for them, and re-layouts  45.4 us (24%)
  blocking collectives  20.7 us (11%)
  starting transfers between devices  20.7 us (11%)
  between operations  13.8 us (7%)
  matrix products  11.8 us (6%)
  other arithmetic  7.97 us (4%)
    ppermute x2, waiting for transfers between devices, ring_into(): go_right = lax.ppermute(go_right, axis, right)  29.4 us
    all_to_all x1, waiting for transfers between devices, shards(): lax.all_to_all(factors, ('x', 'zh'), split_axis=2, concat_axis=0, tiled=T...  23.6 us
    all_to_all x1, blocking collectives, shards(): lax.all_to_all(factors, ('zl', 'y'), split_axis=2, concat_axis=0, tiled=T...  20.7 us
    unnamed x15, local copies, waits for them, and re-layouts  17.8 us
    ppermute x2, waiting for transfers between devices, ring_into(): from_left = lax.ppermute(go_right[:half], axis, right)  13.4 us
    dot_general x1, matrix products, shards(): jnp.einsum('xchzypia,zycxhpjb->ijab', block_a, block_b, preferred_element...  11.8 us
    dynamic_update_slice x10, local copies, waits for them, and re-layouts, put(): return lax.dynamic_update_slice(buf, piece[None, None], start)  10.9 us
    ppermute x2, starting transfers between devices, ring_into(): from_right = lax.ppermute(go_left[half:], axis, left)  5.62 us
  transfers between devices with their start and end apart: 13, of which 6 were waited for; matrix products, arithmetic and copies ran while one was open for 17% of the time, Pallas kernels for 0%

profile of v15, /device:TPU:1, one launch (start us, length us, event | category | flops | bytes accessed | tf_op | source)
XLA Modules:
  0.0 188.3 jit_solution(6720754215467054860)
XLA Ops:
  6.5 2.9 %copy.33 = bf16[80,3,2048]{0,1,2:T(4,128)(2,1)S(1)} copy(bf16[80,3,2048]{2,0,1:T(8,128)(2,1)} %param.7) | data formatting | bytes 1966080 | tf_op args[0]
  9.4 3.7 %reshape.187 = bf16[8,2,30720]{2,1,0:T(2,128)(2,1)} reshape(bf16[2048,3,80]{2,1,0:T(4,128)(2,1)S(1)} %bitcast.65) | data formatting | bytes 1966080
  13.1 20.7 %all_to_all.36 = bf16[8,2,30720]{2,1,0:T(2,128)(2,1)S(1)} all-to-all(bf16[8,2,30720]{2,1,0:T(2,128)(2,1)} %reshape.187), channel_id=1, replica_groups=mesh['zl'=2,'y'=4,'x'=4,'zh'=2,'core'=2] {'zl','y'}, dimensions={0} | all-to-all | bytes 1966080 | tf_op jit(solution)/shard_map/all_to_all | solution.py:49
  33.8 4.1 %reshape.188 = bf16[2048,3,80]{2,1,0:T(4,128)(2,1)} reshape(bf16[8,2,30720]{2,1,0:T(2,128)(2,1)S(1)} %all_to_all.36) | data formatting | bytes 1966080
  38.0 4.0 %copy.52 = bf16[80,3,8,256]{3,0,2,1:T(8,128)(2,1)} copy(bf16[80,3,8,256]{0,1,3,2:T(4,128)(2,1)} %bitcast.68) | data formatting | bytes 1966080 | tf_op jit(solution)/shard_map/all_to_all | solution.py:49
  41.9 3.3 %collective-permute-start = (bf16[640,3,256]{2,0,1:T(8,128)(2,1)}, bf16[640,3,256]{2,0,1:T(8,128)(2,1)}, u32[]{:S(2)}, u32[]{:S(2)}) collective-permute-start(bf16[640,3,256]{2,0,1:T(8,128)(2,1)} %bitcast.4), channel_id=1, source_target_pairs={{0,2},{2,0},{1,3},{3,1},{4,6},{6,4},{5,7},{7,5},{8,10},{10,8},{9,1... | collective-permute-start | bytes 2949128 | tf_op jit(solution)/shard_map/ppermute | solution.py:51
  45.2 3.7 %reshape.189 = bf16[8,2,30720]{2,1,0:T(2,128)(2,1)} reshape(bf16[2048,3,80]{2,1,0:T(4,128)(2,1)S(1)} %bitcast.66) | data formatting | bytes 1966080
  48.9 4.0 %all-to-all-start.1 = ((bf16[8,2,30720]{2,1,0:T(2,128)(2,1)}), bf16[8,2,30720]{2,1,0:T(2,128)(2,1)S(1)}, u32[]{:S(2)}, u32[]{:S(2)}) async-start(bf16[8,2,30720]{2,1,0:T(2,128)(2,1)} %reshape.189), calls=%async_computation.1 | async-start | bytes 1966080 | tf_op jit(solution)/shard_map/all_to_all | solution.py:52
  52.9 0.0 all-gather.2.cloned.1.call-start
  53.0 0.0 copy-start.2
  53.0 0.0 copy-start.4
  53.0 0.0 copy-start.3
  53.0 23.6 %all-to-all-done.1 = bf16[8,2,30720]{2,1,0:T(2,128)(2,1)S(1)} async-done(((bf16[8,2,30720]{2,1,0:T(2,128)(2,1)}), bf16[8,2,30720]{2,1,0:T(2,128)(2,1)S(1)}, u32[]{:S(2)}, u32[]{:S(2)}) %all-to-all-start.1) | async-done | bytes 983072 | tf_op jit(solution)/shard_map/all_to_all | solution.py:52
  76.6 3.4 %reshape.190 = bf16[2048,3,80]{2,1,0:T(4,128)(2,1)S(1)} reshape(bf16[8,2,30720]{2,1,0:T(2,128)(2,1)S(1)} %all-to-all-done.1) | data formatting | bytes 1966080
  79.9 1.1 copy.54
  81.0 0.0 collective-permute-done
  81.1 0.0 copy-start.1
  81.1 3.8 %maximum_select_fusion = bf16[2,640,3,256]{3,1,2,0:T(8,128)(2,1)} fusion(bf16[1,640,3,256]{3,1,2,0:T(8,128)(2,1)} %bitcast.28, bf16[1,640,3,256]{3,1,2,0:T(8,128)(2,1)} %bitcast.27, pred[]{:T(512)S(6)} %eq.18), kind=kLoop, calls=%fused_computation.8 | loop fusion | flops 2949120 | bytes 3932161 | tf_op jit(solution)/shard_map/jit(_where)/select_n | solution.py:61
  84.9 0.0 all-gather.2.cloned.1.call-update
  84.9 0.7 copy.39
  85.6 0.1 constant_dynamic-slice_fusion.1
  85.7 0.3 copy.41
  86.0 2.2 %collective-permute-start.1 = (bf16[640,3,128]{2,0,1:T(8,128)(2,1)S(1)}, bf16[640,3,128]{2,0,1:T(8,128)(2,1)S(1)}, u32[]{:S(2)}, u32[]{:S(2)}) collective-permute-start(bf16[640,3,128]{2,0,1:T(8,128)(2,1)S(1)} %bitcast.77), channel_id=1, source_target_pairs={{0,1},{1,0},{2,3},{3,2},{4,5},{5,4},{6,7},{7,6},{8,9},{9,8},{10,11... | collective-permute-start | bytes 1474568 | tf_op jit(solution)/shard_map/ppermute | solution.py:58
  88.2 0.7 fusion.10
  88.9 1.9 %fusion.8 = (s32[16]{0:T(128)S(1)}, s32[16]{0:T(128)S(1)}) fusion(s32[16,2]{0,1:T(2,128)S(1)} %copy-done.3, s32[]{:T(128)} %bitcast.37, s32[]{:T(128)} %bitcast.39, s32[]{:T(128)} %bitcast.38), kind=kLoop, calls=%fused_computation.39 | loop fusion | flops 320 | bytes 268 | tf_op jit(solution)/shard_map/select_n | solution.py:82
  90.8 0.3 copy.40
  91.1 0.2 maximum_select_fusion.1
  91.3 0.1 copy.42
  91.4 0.3 collective-permute-start.2
  91.6 2.5 %collective-permute-start.3 = (bf16[1280,3,128]{2,0,1:T(8,128)(2,1)S(1)}, bf16[1280,3,128]{2,0,1:T(8,128)(2,1)S(1)}, u32[]{:S(2)}, u32[]{:S(2)}) collective-permute-start(bf16[1280,3,128]{2,0,1:T(8,128)(2,1)S(1)} %bitcast.71), channel_id=1, source_target_pairs={{0,48},{16,0},{32,16},{48,32},{1,49},{17,1},{33,17},{49,33},{2,50}... | collective-permute-start | bytes 2949128 | tf_op jit(solution)/shard_map/ppermute | solution.py:24
  94.1 0.0 collective-permute-start.6
  94.2 0.8 dynamic_slice.16
  95.0 0.8 dynamic_slice.15
  95.7 0.7 gather_fusion.1
  96.4 0.7 gather_fusion.2
  97.1 0.7 gather_fusion.3
  97.8 0.1 broadcast_add_fusion
  97.9 4.8 %broadcast_in_dim.53 = bf16[2,4,1280,3,128]{4,2,3,1,0:T(8,128)(2,1)} broadcast(bf16[]{:T(256)} %constant.89.clone.1), dimensions={} | broadcast | bytes 7864322 | tf_op jit(solution)/shard_map/broadcast_in_dim | solution.py:66
  102.7 1.0 constant_dynamic-update-slice_fusion
  103.8 12.3 %collective-permute-done.2 = bf16[1280,3,128]{2,0,1:T(8,128)(2,1)S(1)} collective-permute-done((bf16[1280,3,128]{2,0,1:T(8,128)(2,1)S(1)}, bf16[1280,3,128]{2,0,1:T(8,128)(2,1)S(1)}, u32[]{:S(2)}, u32[]{:S(2)}) %collective-permute-start.2) | collective-permute-done | bytes 983072 | tf_op jit(solution)/shard_map/ppermute | solution.py:23
  116.1 0.1 collective-permute-start.4
  116.2 0.0 collective-permute-done.3
  116.2 2.7 %collective-permute-start.5 = (bf16[640,3,128]{2,0,1:T(8,128)(2,1)S(1)}, bf16[640,3,128]{2,0,1:T(8,128)(2,1)S(1)}, u32[]{:S(2)}, u32[]{:S(2)}) collective-permute-start(bf16[640,3,128]{2,0,1:T(8,128)(2,1)S(1)} %slice.41), channel_id=1, source_target_pairs={{0,48},{16,0},{32,16},{48,32},{1,49},{17,1},{33,17},{49,33},{2,50}... | collective-permute-start | bytes 1474568 | tf_op jit(solution)/shard_map/ppermute | solution.py:30
  118.9 2.7 %collective-permute-start.8 = (bf16[1280,3,128]{2,0,1:T(8,128)(2,1)}, bf16[1280,3,128]{2,0,1:T(8,128)(2,1)S(1)}, u32[]{:S(2)}, u32[]{:S(2)}) collective-permute-start(bf16[1280,3,128]{2,0,1:T(8,128)(2,1)} %collective-permute-done.6), channel_id=1, source_target_pairs={{0,48},{16,0},{32,16},{48,32},{1,49},{17,1},{33,17},{49,33},{2,50}... | collective-permute-start | bytes 2949128 | tf_op jit(solution)/shard_map/ppermute | solution.py:24
  121.6 1.0 bitcast_dynamic-update-slice_fusion.4
  122.6 1.0 bitcast_dynamic-update-slice_fusion.3
  123.7 5.8 %collective-permute-done.4 = bf16[640,3,128]{2,0,1:T(8,128)(2,1)S(1)} collective-permute-done((bf16[640,3,128]{2,0,1:T(8,128)(2,1)S(1)}, bf16[640,3,128]{2,0,1:T(8,128)(2,1)S(1)}, u32[]{:S(2)}, u32[]{:S(2)}) %collective-permute-start.4) | collective-permute-done | bytes 491552 | tf_op jit(solution)/shard_map/ppermute | solution.py:29
  129.5 0.9 bitcast_dynamic-update-slice_fusion.8
  130.4 0.9 bitcast_dynamic-update-slice_fusion.7
  131.2 2.2 %bitcast_dynamic-update-slice_fusion.2 = bf16[2,4,1280,3,128]{4,2,3,1,0:T(8,128)(2,1)} fusion(bf16[2,4,1280,3,128]{4,2,3,1,0:T(8,128)(2,1)} %bitcast_dynamic-update-slice_fusion.7, s32[]{:T(128)S(6)} %select_n.167, s32[]{:T(128)S(6)} %select_n.158, bf16[1280,3,128]{2,0,1:T(8,128)(2,1)} %collective-permute-done.6), kind=kLoop, calls=%fused_computation.13 | loop fusion | bytes 1966088 | tf_op jit(solution)/shard_map/dynamic_update_slice | solution.py:16
  133.4 17.1 %collective-permute-done.7 = bf16[1280,3,128]{2,0,1:T(8,128)(2,1)S(1)} collective-permute-done((bf16[1280,3,128]{2,0,1:T(8,128)(2,1)}, bf16[1280,3,128]{2,0,1:T(8,128)(2,1)S(1)}, u32[]{:S(2)}, u32[]{:S(2)}) %collective-permute-start.7) | collective-permute-done | bytes 983072 | tf_op jit(solution)/shard_map/ppermute | solution.py:23
  150.6 0.1 collective-permute-start.9
  150.7 0.0 collective-permute-done.8
  150.7 2.9 %collective-permute-start.10 = (bf16[640,3,128]{2,0,1:T(8,128)(2,1)S(1)}, bf16[640,3,128]{2,0,1:T(8,128)(2,1)S(1)}, u32[]{:S(2)}, u32[]{:S(2)}) collective-permute-start(bf16[640,3,128]{2,0,1:T(8,128)(2,1)S(1)} %slice.43), channel_id=1, source_target_pairs={{0,48},{16,0},{32,16},{48,32},{1,49},{17,1},{33,17},{49,33},{2,50}... | collective-permute-start | bytes 1474568 | tf_op jit(solution)/shard_map/ppermute | solution.py:30
  153.6 1.0 bitcast_dynamic-update-slice_fusion.1
  154.6 1.0 bitcast_dynamic-update-slice_fusion
  155.6 7.6 %collective-permute-done.9 = bf16[640,3,128]{2,0,1:T(8,128)(2,1)S(1)} collective-permute-done((bf16[640,3,128]{2,0,1:T(8,128)(2,1)S(1)}, bf16[640,3,128]{2,0,1:T(8,128)(2,1)S(1)}, u32[]{:S(2)}, u32[]{:S(2)}) %collective-permute-start.9) | collective-permute-done | bytes 491552 | tf_op jit(solution)/shard_map/ppermute | solution.py:29
  163.2 0.9 bitcast_dynamic-update-slice_fusion.6
  164.1 0.9 bitcast_dynamic-update-slice_fusion.5
  165.0 1.7 all-gather.2.cloned.1.call-done
  166.7 11.8 %fusion.3 = f32[3,3,256,128]{2,3,0,1:T(8,128)S(1)} fusion(bf16[4,2,2,2,4,80,3,256,1]{7,5,4,3,6,2,1,0,8:T(8,128)(2,1)} %bitcast.80, bf16[2,4,2,4,2,80,3,128,1]{7,5,4,3,2,6,1,0,8:T(8,128)(2,1)} %bitcast.25), kind=kOutput, calls=%fused_computation.9 | convolution fusion | flops 6039797760 | bytes 24772608 | tf_op jit(solution)/shard_map/xchzypia,zycxhpjb->ijab/dot_general | solution.py:71
  178.5 0.4 copy.47
  178.8 0.7 gather_fusion
  179.5 1.9 %add_divide_fusion = f32[16,256,128]{2,1,0:T(8,128)} fusion(f32[16,256,128]{2,1,0:T(8,128)S(1)} %gather_fusion, f32[16]{0:T(128)S(1)} %gather_fusion.3, f32[16]{0:T(128)S(1)} %gather_fusion.2, f32[16]{0:T(128)S(1)} %gather_fusion.1, f32[256,128]{1,0:T(8,128)S(1)} %broadcast_add_fusion, pred[16]{0:T(512)(128)(4,1)S(1)} %get-tuple-element.9), kind=kLoop, calls=%fused_computation.7 | loop fusion | flops 3145728 | bytes 4325584 | tf_op jit(solution)/shard_map/div | solution.py:91
  (20 shorter events, 0.2 us)
Async XLA Ops:
  6.5 89.2 %copy-start = (f32[300]{0:T(512)S(1)}, f32[300]{0:T(512)}, u32[]{:S(2)}) copy-start(f32[300]{0:T(512)} %param.8) | copy-start | bytes 3604
  41.9 39.1 %collective-permute-start = (bf16[640,3,256]{2,0,1:T(8,128)(2,1)}, bf16[640,3,256]{2,0,1:T(8,128)(2,1)}, u32[]{:S(2)}, u32[]{:S(2)}) collective-permute-start(bf16[640,3,256]{2,0,1:T(8,128)(2,1)} %bitcast.4), channel_id=1, source_target_pairs={{0,2},{2,0},{1,3},{3,1},{4,6},{6,4},{5,7},{7,5},{8,10},{10,8},{9,1... | collective-permute-start | bytes 2949128 | tf_op jit(solution)/shard_map/ppermute | solution.py:51
  48.9 27.7 %all-to-all-start.1 = ((bf16[8,2,30720]{2,1,0:T(2,128)(2,1)}), bf16[8,2,30720]{2,1,0:T(2,128)(2,1)S(1)}, u32[]{:S(2)}, u32[]{:S(2)}) async-start(bf16[8,2,30720]{2,1,0:T(2,128)(2,1)} %reshape.189), calls=%async_computation.1 | async-start | bytes 1966080 | tf_op jit(solution)/shard_map/all_to_all | solution.py:52
  52.9 113.8 %all-gather.2.cloned.1.call-start = ((), (), s32[]{:S(2)}) async-start(), calls=%async_computation.2 | async-start | bytes 17694720 | tf_op jit(solution)/shard_map/all_gather | solution.py:62
  53.0 35.2 %copy-start.2 = (s32[3]{0:T(128)S(1)}, s32[3]{0:T(128)}, u32[]{:S(2)}) copy-start(s32[3]{0:T(128)} %param.10) | copy-start | bytes 40
  53.0 35.9 %copy-start.4 = (s32[16]{0:T(128)S(1)}, s32[16]{0:T(128)}, u32[]{:S(2)}) copy-start(s32[16]{0:T(128)} %param.12) | copy-start | bytes 196
  53.0 35.9 %copy-start.3 = (s32[16,2]{0,1:T(2,128)S(1)}, s32[16,2]{0,1:T(2,128)}, u32[]{:S(2)}) copy-start(s32[16,2]{0,1:T(2,128)} %param.11) | copy-start | bytes 388
  81.1 16.1 %copy-start.1 = (f32[4]{0:T(128)S(1)}, f32[4]{0:T(128)}, u32[]{:S(2)}) copy-start(f32[4]{0:T(128)} %param.13) | copy-start | bytes 52
  86.0 5.1 %collective-permute-start.1 = (bf16[640,3,128]{2,0,1:T(8,128)(2,1)S(1)}, bf16[640,3,128]{2,0,1:T(8,128)(2,1)S(1)}, u32[]{:S(2)}, u32[]{:S(2)}) collective-permute-start(bf16[640,3,128]{2,0,1:T(8,128)(2,1)S(1)} %bitcast.77), channel_id=1, source_target_pairs={{0,1},{1,0},{2,3},{3,2},{4,5},{5,4},{6,7},{7,6},{8,9},{9,8},{10,11... | collective-permute-start | bytes 1474568 | tf_op jit(solution)/shard_map/ppermute | solution.py:58
  91.4 24.7 %collective-permute-start.2 = (bf16[1280,3,128]{2,0,1:T(8,128)(2,1)S(1)}, bf16[1280,3,128]{2,0,1:T(8,128)(2,1)S(1)}, u32[]{:S(2)}, u32[]{:S(2)}) collective-permute-start(bf16[1280,3,128]{2,0,1:T(8,128)(2,1)S(1)} %bitcast.70), channel_id=1, source_target_pairs={{0,16},{16,32},{32,48},{48,0},{1,17},{17,33},{33,49},{49,1},{2,18}... | collective-permute-start | bytes 2949128 | tf_op jit(solution)/shard_map/ppermute | solution.py:23
  91.6 24.5 %collective-permute-start.3 = (bf16[1280,3,128]{2,0,1:T(8,128)(2,1)S(1)}, bf16[1280,3,128]{2,0,1:T(8,128)(2,1)S(1)}, u32[]{:S(2)}, u32[]{:S(2)}) collective-permute-start(bf16[1280,3,128]{2,0,1:T(8,128)(2,1)S(1)} %bitcast.71), channel_id=1, source_target_pairs={{0,48},{16,0},{32,16},{48,32},{1,49},{17,1},{33,17},{49,33},{2,50}... | collective-permute-start | bytes 2949128 | tf_op jit(solution)/shard_map/ppermute | solution.py:24
  94.1 24.8 %collective-permute-start.6 = (bf16[1280,3,128]{2,0,1:T(8,128)(2,1)S(1)}, bf16[1280,3,128]{2,0,1:T(8,128)(2,1)}, u32[]{:S(2)}, u32[]{:S(2)}) collective-permute-start(bf16[1280,3,128]{2,0,1:T(8,128)(2,1)S(1)} %bitcast.72), channel_id=1, source_target_pairs={{0,64},{64,0},{1,65},{65,1},{2,66},{66,2},{3,67},{67,3},{4,68},{68... | collective-permute-start | bytes 2949128 | tf_op jit(solution)/shard_map/ppermute | solution.py:64
  116.1 13.4 %collective-permute-start.4 = (bf16[640,3,128]{2,0,1:T(8,128)(2,1)S(1)}, bf16[640,3,128]{2,0,1:T(8,128)(2,1)S(1)}, u32[]{:S(2)}, u32[]{:S(2)}) collective-permute-start(bf16[640,3,128]{2,0,1:T(8,128)(2,1)S(1)} %slice.40), channel_id=1, source_target_pairs={{0,16},{16,32},{32,48},{48,0},{1,17},{17,33},{33,49},{49,1},{2,18}... | collective-permute-start | bytes 1474568 | tf_op jit(solution)/shard_map/ppermute | solution.py:29
  116.2 14.2 %collective-permute-start.5 = (bf16[640,3,128]{2,0,1:T(8,128)(2,1)S(1)}, bf16[640,3,128]{2,0,1:T(8,128)(2,1)S(1)}, u32[]{:S(2)}, u32[]{:S(2)}) collective-permute-start(bf16[640,3,128]{2,0,1:T(8,128)(2,1)S(1)} %slice.41), channel_id=1, source_target_pairs={{0,48},{16,0},{32,16},{48,32},{1,49},{17,1},{33,17},{49,33},{2,50}... | collective-permute-start | bytes 1474568 | tf_op jit(solution)/shard_map/ppermute | solution.py:30
  118.9 31.6 %collective-permute-start.7 = (bf16[1280,3,128]{2,0,1:T(8,128)(2,1)}, bf16[1280,3,128]{2,0,1:T(8,128)(2,1)S(1)}, u32[]{:S(2)}, u32[]{:S(2)}) collective-permute-start(bf16[1280,3,128]{2,0,1:T(8,128)(2,1)} %collective-permute-done.6), channel_id=1, source_target_pairs={{0,16},{16,32},{32,48},{48,0},{1,17},{17,33},{33,49},{49,1},{2,18}... | collective-permute-start | bytes 2949128 | tf_op jit(solution)/shard_map/ppermute | solution.py:23
  118.9 31.7 %collective-permute-start.8 = (bf16[1280,3,128]{2,0,1:T(8,128)(2,1)}, bf16[1280,3,128]{2,0,1:T(8,128)(2,1)S(1)}, u32[]{:S(2)}, u32[]{:S(2)}) collective-permute-start(bf16[1280,3,128]{2,0,1:T(8,128)(2,1)} %collective-permute-done.6), channel_id=1, source_target_pairs={{0,48},{16,0},{32,16},{48,32},{1,49},{17,1},{33,17},{49,33},{2,50}... | collective-permute-start | bytes 2949128 | tf_op jit(solution)/shard_map/ppermute | solution.py:24
  150.6 12.6 %collective-permute-start.9 = (bf16[640,3,128]{2,0,1:T(8,128)(2,1)S(1)}, bf16[640,3,128]{2,0,1:T(8,128)(2,1)S(1)}, u32[]{:S(2)}, u32[]{:S(2)}) collective-permute-start(bf16[640,3,128]{2,0,1:T(8,128)(2,1)S(1)} %slice.42), channel_id=1, source_target_pairs={{0,16},{16,32},{32,48},{48,0},{1,17},{17,33},{33,49},{49,1},{2,18}... | collective-permute-start | bytes 1474568 | tf_op jit(solution)/shard_map/ppermute | solution.py:29
  150.7 13.4 %collective-permute-start.10 = (bf16[640,3,128]{2,0,1:T(8,128)(2,1)S(1)}, bf16[640,3,128]{2,0,1:T(8,128)(2,1)S(1)}, u32[]{:S(2)}, u32[]{:S(2)}) collective-permute-start(bf16[640,3,128]{2,0,1:T(8,128)(2,1)S(1)} %slice.43), channel_id=1, source_target_pairs={{0,48},{16,0},{32,16},{48,32},{1,49},{17,1},{33,17},{49,33},{2,50}... | collective-permute-start | bytes 1474568 | tf_op jit(solution)/shard_map/ppermute | solution.py:30
Sparse Core Ops, SparseCore 0:
  85.0 81.6 all-gather.1

commit v16 on v13

--- a/solution.py
+++ b/solution.py
@@ -63,17 +63,17 @@
     spread_b = jnp.where(me_core == 0, jnp.stack([keep, got]), jnp.stack([got, keep]))
     first_zh = lax.axis_index("zh") == 0
     pair_a = jnp.where(first_zh, jnp.stack([spread_a, other_a]), jnp.stack([other_a, spread_a]))
-    block_a = lax.all_gather(pair_a, ("x", "core"), axis=0, tiled=True)
+    block_a = lax.all_gather(pair_a, ("core", "x"), axis=0, tiled=True)
     spread_b = spread_b.reshape(n_col * local_aux, nocc, cols_b)
     other_b = lax.ppermute(spread_b, "zl", [(k, (k + 1) % n_zl) for k in range(n_zl)])
     me_zl = lax.axis_index("zl")
     block_b = jnp.zeros((n_zl, n_y) + spread_b.shape, spread_b.dtype)
     block_b = ring_into(block_b, me_zl, spread_b, "y")
     block_b = ring_into(block_b, (me_zl + 1) % n_zl, other_b, "y")
-    block_a = block_a.reshape(n_x, n_core, n_zh, n_zl, n_y, local_aux, nocc, rows_a)
+    block_a = block_a.reshape(n_core, n_x, n_zh, n_zl, n_y, local_aux, nocc, rows_a)
     block_b = block_b.reshape(n_zl, n_y, n_core, n_x, n_zh, local_aux, nocc, cols_b)
     gram = jnp.einsum(
-        "xchzypia,zycxhpjb->ijab",
+        "cxhzypia,zycxhpjb->ijab",
         block_a,
         block_b,
         preferred_element_type=jnp.float32,

time: 170 us -> 170 us (level)
  no operation moved by 1% of the time
where the time goes in v16:
time: 170 us
  waiting for transfers between devices  67.3 us (40%)
  local copies, waits for them, and re-layouts  28 us (16%)
  starting transfers between devices  20.9 us (12%)
  blocking collectives  20.5 us (12%)
  between operations  13.8 us (8%)
  matrix products  11.8 us (7%)
  other arithmetic  7.4 us (4%)
    ppermute x2, waiting for transfers between devices, ring_into(): go_right = lax.ppermute(go_right, axis, right)  28.7 us
    all_to_all x1, waiting for transfers between devices, shards(): lax.all_to_all(factors.reshape(local_aux, nocc, n_x * n_zh, n_core, cols_...  22.4 us
    all_to_all x1, blocking collectives, shards(): lax.all_to_all(factors.reshape(local_aux, nocc, n_row, rows_a), ('zl', 'y...  20.5 us
    ppermute x2, waiting for transfers between devices, ring_into(): from_left = lax.ppermute(go_right[:half], axis, right)  13.4 us
    dot_general x1, matrix products, shards(): jnp.einsum('cxhzypia,zycxhpjb->ijab', block_a, block_b, preferred_element...  11.8 us
    dynamic_update_slice x10, local copies, waits for them, and re-layouts, put(): return lax.dynamic_update_slice(buf, piece[None, None], start)  10.9 us
    ppermute x2, starting transfers between devices, ring_into(): from_right = lax.ppermute(go_left[half:], axis, left)  5.62 us
    broadcast_in_dim x1, local copies, waits for them, and re-layouts, shards(): block_b = jnp.zeros((n_zl, n_y) + spread_b.shape, spread_b.dtype)  5.48 us
  transfers between devices with their start and end apart: 13, of which 6 were waited for; matrix products, arithmetic and copies ran while one was open for 16% of the time, Pallas kernels for 0%

profile of v16, /device:TPU:1, one launch (start us, length us, event | category | flops | bytes accessed | tf_op | source)
XLA Modules:
  0.0 169.7 jit_solution(13791559770877310439)
XLA Ops:
  6.5 0.0 copy-start
  6.5 1.3 copy.51
  7.8 20.5 %all_to_all.33 = bf16[80,3,8,256]{3,0,1,2:T(8,128)(2,1)S(1)} all-to-all(bf16[80,3,8,256]{3,0,1,2:T(8,128)(2,1)S(1)} %bitcast.79), channel_id=1, replica_groups=mesh['zl'=2,'y'=4,'x'=4,'zh'=2,'core'=2] {'zl','y'}, dimensions={2} | all-to-all | bytes 1966080 | tf_op jit(solution)/shard_map/all_to_all | solution.py:49
  28.3 0.1 copy.24
  28.4 0.0 copy-start.2
  28.4 0.0 copy-start.4
  28.4 0.0 copy-start.3
  28.4 3.4 %collective-permute-start = (bf16[640,3,256]{2,0,1:T(8,128)(2,1)S(1)}, bf16[640,3,256]{2,0,1:T(8,128)(2,1)}, u32[]{:S(2)}, u32[]{:S(2)}) collective-permute-start(bf16[640,3,256]{2,0,1:T(8,128)(2,1)S(1)} %bitcast.80), channel_id=1, source_target_pairs={{0,2},{2,0},{1,3},{3,1},{4,6},{6,4},{5,7},{7,5},{8,10},{10,8},{9,1... | collective-permute-start | bytes 2949128 | tf_op jit(solution)/shard_map/ppermute | solution.py:53
  31.8 2.9 %reshape.117 = bf16[80,3,8,2,128]{4,3,2,0,1:T(2,128)(2,1)S(1)} reshape(bf16[80,3,2048]{2,0,1:T(8,128)(2,1)} %param.7) | data formatting | bytes 1966080 | tf_op jit(solution)/shard_map/reshape | solution.py:55
  34.7 1.6 copy.25
  36.3 4.2 %all-to-all-start.1 = ((bf16[80,3,8,2,128]{4,3,0,1,2:T(2,128)(2,1)}), bf16[80,3,8,2,128]{4,3,0,1,2:T(2,128)(2,1)S(1)}, u32[]{:S(2)}, u32[]{:S(2)}) async-start(bf16[80,3,8,2,128]{4,3,0,1,2:T(2,128)(2,1)} %copy.25), calls=%async_computation.1 | async-start | bytes 1966080 | tf_op jit(solution)/shard_map/all_to_all | solution.py:54
  40.5 0.0 all-gather.2.cloned.1.call-start
  40.5 22.4 %all-to-all-done.1 = bf16[80,3,8,2,128]{4,3,0,1,2:T(2,128)(2,1)S(1)} async-done(((bf16[80,3,8,2,128]{4,3,0,1,2:T(2,128)(2,1)}), bf16[80,3,8,2,128]{4,3,0,1,2:T(2,128)(2,1)S(1)}, u32[]{:S(2)}, u32[]{:S(2)}) %all-to-all-start.1) | async-done | bytes 983072 | tf_op jit(solution)/shard_map/all_to_all | solution.py:54
  62.9 0.1 copy.26
  63.1 0.0 collective-permute-done
  63.1 3.1 %maximum_select_fusion = bf16[2,640,3,256]{3,1,2,0:T(8,128)(2,1)} fusion(bf16[1,640,3,256]{3,1,2,0:T(8,128)(2,1)} %bitcast.27, bf16[1,640,3,256]{3,1,2,0:T(8,128)(2,1)S(1)} %bitcast.81, pred[]{:T(512)S(6)} %eq.18), kind=kLoop, calls=%fused_computation.8 | loop fusion | flops 2949120 | bytes 3932161 | tf_op jit(solution)/shard_map/jit(_where)/select_n | solution.py:65
  66.2 0.0 all-gather.2.cloned.1.call-update
  66.2 0.2 dynamic-slice_bitcast_fusion.2
  66.5 2.2 %collective-permute-start.1 = (bf16[640,3,128]{2,0,1:T(8,128)(2,1)S(1)}, bf16[640,3,128]{2,0,1:T(8,128)(2,1)S(1)}, u32[]{:S(2)}, u32[]{:S(2)}) collective-permute-start(bf16[640,3,128]{2,0,1:T(8,128)(2,1)S(1)} %get-tuple-element.13), channel_id=1, source_target_pairs={{0,1},{1,0},{2,3},{3,2},{4,5},{5,4},{6,7},{7,6},{8,9},{9,8},{10,11... | collective-permute-start | bytes 1474568 | tf_op jit(solution)/shard_map/ppermute | solution.py:62
  68.6 0.0 copy-done.2
  68.6 0.7 fusion.10
  69.3 1.9 %fusion.8 = (s32[16]{0:T(128)S(1)}, s32[16]{0:T(128)S(1)}) fusion(s32[16,2]{0,1:T(2,128)S(1)} %copy-done.3, s32[]{:T(128)} %bitcast.36, s32[]{:T(128)} %bitcast.38, s32[]{:T(128)} %bitcast.37), kind=kLoop, calls=%fused_computation.42 | loop fusion | flops 320 | bytes 268 | tf_op jit(solution)/shard_map/select_n | solution.py:86
  71.3 0.0 collective-permute-done.1
  71.3 0.3 maximum_select_fusion.1
  71.5 0.3 collective-permute-start.2
  71.8 2.5 %collective-permute-start.3 = (bf16[1280,3,128]{2,0,1:T(8,128)(2,1)S(1)}, bf16[1280,3,128]{2,0,1:T(8,128)(2,1)S(1)}, u32[]{:S(2)}, u32[]{:S(2)}) collective-permute-start(bf16[1280,3,128]{2,0,1:T(8,128)(2,1)S(1)} %bitcast.74), channel_id=1, source_target_pairs={{0,48},{16,0},{32,16},{48,32},{1,49},{17,1},{33,17},{49,33},{2,50}... | collective-permute-start | bytes 2949128 | tf_op jit(solution)/shard_map/ppermute | solution.py:24
  74.3 0.0 collective-permute-start.6
  74.4 0.8 dynamic_slice.16
  75.2 0.8 dynamic_slice.15
  75.9 0.7 gather_fusion.1
  76.6 0.7 gather_fusion.2
  77.3 0.7 gather_fusion.3
  78.0 0.1 broadcast_add_fusion
  78.1 5.5 %broadcast_in_dim.53 = bf16[2,4,1280,3,128]{4,2,3,1,0:T(8,128)(2,1)} broadcast(bf16[]{:T(256)} %constant.91.clone.1), dimensions={} | broadcast | bytes 7864322 | tf_op jit(solution)/shard_map/broadcast_in_dim | solution.py:70
  83.6 1.0 constant_dynamic-update-slice_fusion
  84.6 11.6 %collective-permute-done.2 = bf16[1280,3,128]{2,0,1:T(8,128)(2,1)S(1)} collective-permute-done((bf16[1280,3,128]{2,0,1:T(8,128)(2,1)S(1)}, bf16[1280,3,128]{2,0,1:T(8,128)(2,1)S(1)}, u32[]{:S(2)}, u32[]{:S(2)}) %collective-permute-start.2) | collective-permute-done | bytes 983072 | tf_op jit(solution)/shard_map/ppermute | solution.py:23
  96.3 0.1 collective-permute-start.4
  96.3 0.0 collective-permute-done.3
  96.4 2.7 %collective-permute-start.5 = (bf16[640,3,128]{2,0,1:T(8,128)(2,1)S(1)}, bf16[640,3,128]{2,0,1:T(8,128)(2,1)S(1)}, u32[]{:S(2)}, u32[]{:S(2)}) collective-permute-start(bf16[640,3,128]{2,0,1:T(8,128)(2,1)S(1)} %slice.41), channel_id=1, source_target_pairs={{0,48},{16,0},{32,16},{48,32},{1,49},{17,1},{33,17},{49,33},{2,50}... | collective-permute-start | bytes 1474568 | tf_op jit(solution)/shard_map/ppermute | solution.py:30
  99.1 0.0 collective-permute-done.6
  99.1 0.0 collective-permute-start.7
  99.1 2.7 %collective-permute-start.8 = (bf16[1280,3,128]{2,0,1:T(8,128)(2,1)}, bf16[1280,3,128]{2,0,1:T(8,128)(2,1)S(1)}, u32[]{:S(2)}, u32[]{:S(2)}) collective-permute-start(bf16[1280,3,128]{2,0,1:T(8,128)(2,1)} %collective-permute-done.6), channel_id=1, source_target_pairs={{0,48},{16,0},{32,16},{48,32},{1,49},{17,1},{33,17},{49,33},{2,50}... | collective-permute-start | bytes 2949128 | tf_op jit(solution)/shard_map/ppermute | solution.py:24
  101.8 1.0 bitcast_dynamic-update-slice_fusion.4
  102.8 1.0 bitcast_dynamic-update-slice_fusion.3
  103.8 5.8 %collective-permute-done.4 = bf16[640,3,128]{2,0,1:T(8,128)(2,1)S(1)} collective-permute-done((bf16[640,3,128]{2,0,1:T(8,128)(2,1)S(1)}, bf16[640,3,128]{2,0,1:T(8,128)(2,1)S(1)}, u32[]{:S(2)}, u32[]{:S(2)}) %collective-permute-start.4) | collective-permute-done | bytes 491552 | tf_op jit(solution)/shard_map/ppermute | solution.py:29
  109.7 0.9 bitcast_dynamic-update-slice_fusion.8
  110.5 0.0 collective-permute-done.5
  110.5 0.9 bitcast_dynamic-update-slice_fusion.7
  111.4 2.2 %bitcast_dynamic-update-slice_fusion.2 = bf16[2,4,1280,3,128]{4,2,3,1,0:T(8,128)(2,1)} fusion(bf16[2,4,1280,3,128]{4,2,3,1,0:T(8,128)(2,1)} %bitcast_dynamic-update-slice_fusion.7, s32[]{:T(128)S(6)} %select_n.167, s32[]{:T(128)S(6)} %select_n.158, bf16[1280,3,128]{2,0,1:T(8,128)(2,1)} %collective-permute-done.6), kind=kLoop, calls=%fused_computation.15 | loop fusion | bytes 1966088 | tf_op jit(solution)/shard_map/dynamic_update_slice | solution.py:16
  113.6 17.1 %collective-permute-done.7 = bf16[1280,3,128]{2,0,1:T(8,128)(2,1)S(1)} collective-permute-done((bf16[1280,3,128]{2,0,1:T(8,128)(2,1)}, bf16[1280,3,128]{2,0,1:T(8,128)(2,1)S(1)}, u32[]{:S(2)}, u32[]{:S(2)}) %collective-permute-start.7) | collective-permute-done | bytes 983072 | tf_op jit(solution)/shard_map/ppermute | solution.py:23
  130.8 0.1 collective-permute-start.9
  130.8 0.0 collective-permute-done.8
  130.9 2.9 %collective-permute-start.10 = (bf16[640,3,128]{2,0,1:T(8,128)(2,1)S(1)}, bf16[640,3,128]{2,0,1:T(8,128)(2,1)S(1)}, u32[]{:S(2)}, u32[]{:S(2)}) collective-permute-start(bf16[640,3,128]{2,0,1:T(8,128)(2,1)S(1)} %slice.43), channel_id=1, source_target_pairs={{0,48},{16,0},{32,16},{48,32},{1,49},{17,1},{33,17},{49,33},{2,50}... | collective-permute-start | bytes 1474568 | tf_op jit(solution)/shard_map/ppermute | solution.py:30
  133.8 1.0 bitcast_dynamic-update-slice_fusion.1
  134.8 1.0 bitcast_dynamic-update-slice_fusion
  135.8 7.6 %collective-permute-done.9 = bf16[640,3,128]{2,0,1:T(8,128)(2,1)S(1)} collective-permute-done((bf16[640,3,128]{2,0,1:T(8,128)(2,1)S(1)}, bf16[640,3,128]{2,0,1:T(8,128)(2,1)S(1)}, u32[]{:S(2)}, u32[]{:S(2)}) %collective-permute-start.9) | collective-permute-done | bytes 491552 | tf_op jit(solution)/shard_map/ppermute | solution.py:29
  143.4 0.9 bitcast_dynamic-update-slice_fusion.6
  144.3 0.0 collective-permute-done.10
  144.3 0.9 bitcast_dynamic-update-slice_fusion.5
  145.2 2.8 %all-gather.2.cloned.1.call-done = bf16[16,640,3,256]{3,1,2,0:T(8,128)(2,1)} async-done(((bf16[2,640,3,256]{3,1,2,0:T(8,128)(2,1)}), bf16[16,640,3,256]{3,1,2,0:T(8,128)(2,1)}) %all-gather.2.cloned.1.call-update) | async-done | bytes 15728656 | tf_op jit(solution)/shard_map/all_gather | solution.py:66
  148.0 11.8 %fusion.3 = f32[3,3,256,128]{2,3,0,1:T(8,128)S(1)} fusion(bf16[2,4,2,2,4,80,3,256,1]{7,5,4,3,6,2,1,0,8:T(8,128)(2,1)} %bitcast.85, bf16[2,4,2,4,2,80,3,128,1]{7,5,4,3,2,6,1,0,8:T(8,128)(2,1)} %bitcast.24), kind=kOutput, calls=%fused_computation.9 | convolution fusion | flops 6039797760 | bytes 24772608 | tf_op jit(solution)/shard_map/cxhzypia,zycxhpjb->ijab/dot_general | solution.py:75
  159.8 0.4 copy.32
  160.2 0.7 gather_fusion
  160.9 1.9 %add_divide_fusion = f32[16,256,128]{2,1,0:T(8,128)} fusion(f32[16,256,128]{2,1,0:T(8,128)S(1)} %gather_fusion, f32[16]{0:T(128)S(1)} %gather_fusion.3, f32[16]{0:T(128)S(1)} %gather_fusion.2, f32[16]{0:T(128)S(1)} %gather_fusion.1, f32[256,128]{1,0:T(8,128)S(1)} %broadcast_add_fusion, pred[16]{0:T(512)(128)(4,1)S(1)} %get-tuple-element.9), kind=kLoop, calls=%fused_computation.7 | loop fusion | flops 3145728 | bytes 4325584 | tf_op jit(solution)/shard_map/div | solution.py:95
  (14 shorter events, 0.2 us)
Async XLA Ops:
  6.5 69.4 %copy-start = (f32[300]{0:T(512)S(1)}, f32[300]{0:T(512)}, u32[]{:S(2)}) copy-start(f32[300]{0:T(512)} %param.8) | copy-start | bytes 3604
  28.4 40.3 %copy-start.2 = (s32[3]{0:T(128)S(1)}, s32[3]{0:T(128)}, u32[]{:S(2)}) copy-start(s32[3]{0:T(128)} %param.10) | copy-start | bytes 40
  28.4 40.9 %copy-start.4 = (s32[16]{0:T(128)S(1)}, s32[16]{0:T(128)}, u32[]{:S(2)}) copy-start(s32[16]{0:T(128)} %param.12) | copy-start | bytes 196
  28.4 40.9 %copy-start.3 = (s32[16,2]{0,1:T(2,128)S(1)}, s32[16,2]{0,1:T(2,128)}, u32[]{:S(2)}) copy-start(s32[16,2]{0,1:T(2,128)} %param.11) | copy-start | bytes 388
  28.4 34.7 %collective-permute-start = (bf16[640,3,256]{2,0,1:T(8,128)(2,1)S(1)}, bf16[640,3,256]{2,0,1:T(8,128)(2,1)}, u32[]{:S(2)}, u32[]{:S(2)}) collective-permute-start(bf16[640,3,256]{2,0,1:T(8,128)(2,1)S(1)} %bitcast.80), channel_id=1, source_target_pairs={{0,2},{2,0},{1,3},{3,1},{4,6},{6,4},{5,7},{7,5},{8,10},{10,8},{9,1... | collective-permute-start | bytes 2949128 | tf_op jit(solution)/shard_map/ppermute | solution.py:53
  36.3 40.9 %copy-start.1 = (f32[4]{0:T(128)S(1)}, f32[4]{0:T(128)}, u32[]{:S(2)}) copy-start(f32[4]{0:T(128)} %param.13) | copy-start | bytes 52
  36.3 26.6 %all-to-all-start.1 = ((bf16[80,3,8,2,128]{4,3,0,1,2:T(2,128)(2,1)}), bf16[80,3,8,2,128]{4,3,0,1,2:T(2,128)(2,1)S(1)}, u32[]{:S(2)}, u32[]{:S(2)}) async-start(bf16[80,3,8,2,128]{4,3,0,1,2:T(2,128)(2,1)} %copy.25), calls=%async_computation.1 | async-start | bytes 1966080 | tf_op jit(solution)/shard_map/all_to_all | solution.py:54
  40.5 107.5 %all-gather.2.cloned.1.call-start = ((), (), s32[]{:S(2)}) async-start(), calls=%async_computation.2 | async-start | bytes 17694720 | tf_op jit(solution)/shard_map/all_gather | solution.py:66
  66.5 4.8 %collective-permute-start.1 = (bf16[640,3,128]{2,0,1:T(8,128)(2,1)S(1)}, bf16[640,3,128]{2,0,1:T(8,128)(2,1)S(1)}, u32[]{:S(2)}, u32[]{:S(2)}) collective-permute-start(bf16[640,3,128]{2,0,1:T(8,128)(2,1)S(1)} %get-tuple-element.13), channel_id=1, source_target_pairs={{0,1},{1,0},{2,3},{3,2},{4,5},{5,4},{6,7},{7,6},{8,9},{9,8},{10,11... | collective-permute-start | bytes 1474568 | tf_op jit(solution)/shard_map/ppermute | solution.py:62
  71.5 24.7 %collective-permute-start.2 = (bf16[1280,3,128]{2,0,1:T(8,128)(2,1)S(1)}, bf16[1280,3,128]{2,0,1:T(8,128)(2,1)S(1)}, u32[]{:S(2)}, u32[]{:S(2)}) collective-permute-start(bf16[1280,3,128]{2,0,1:T(8,128)(2,1)S(1)} %bitcast.73), channel_id=1, source_target_pairs={{0,16},{16,32},{32,48},{48,0},{1,17},{17,33},{33,49},{49,1},{2,18}... | collective-permute-start | bytes 2949128 | tf_op jit(solution)/shard_map/ppermute | solution.py:23
  71.8 24.5 %collective-permute-start.3 = (bf16[1280,3,128]{2,0,1:T(8,128)(2,1)S(1)}, bf16[1280,3,128]{2,0,1:T(8,128)(2,1)S(1)}, u32[]{:S(2)}, u32[]{:S(2)}) collective-permute-start(bf16[1280,3,128]{2,0,1:T(8,128)(2,1)S(1)} %bitcast.74), channel_id=1, source_target_pairs={{0,48},{16,0},{32,16},{48,32},{1,49},{17,1},{33,17},{49,33},{2,50}... | collective-permute-start | bytes 2949128 | tf_op jit(solution)/shard_map/ppermute | solution.py:24
  74.3 24.8 %collective-permute-start.6 = (bf16[1280,3,128]{2,0,1:T(8,128)(2,1)S(1)}, bf16[1280,3,128]{2,0,1:T(8,128)(2,1)}, u32[]{:S(2)}, u32[]{:S(2)}) collective-permute-start(bf16[1280,3,128]{2,0,1:T(8,128)(2,1)S(1)} %bitcast.75), channel_id=1, source_target_pairs={{0,64},{64,0},{1,65},{65,1},{2,66},{66,2},{3,67},{67,3},{4,68},{68... | collective-permute-start | bytes 2949128 | tf_op jit(solution)/shard_map/ppermute | solution.py:68
  96.3 13.4 %collective-permute-start.4 = (bf16[640,3,128]{2,0,1:T(8,128)(2,1)S(1)}, bf16[640,3,128]{2,0,1:T(8,128)(2,1)S(1)}, u32[]{:S(2)}, u32[]{:S(2)}) collective-permute-start(bf16[640,3,128]{2,0,1:T(8,128)(2,1)S(1)} %slice.40), channel_id=1, source_target_pairs={{0,16},{16,32},{32,48},{48,0},{1,17},{17,33},{33,49},{49,1},{2,18}... | collective-permute-start | bytes 1474568 | tf_op jit(solution)/shard_map/ppermute | solution.py:29
  96.4 14.2 %collective-permute-start.5 = (bf16[640,3,128]{2,0,1:T(8,128)(2,1)S(1)}, bf16[640,3,128]{2,0,1:T(8,128)(2,1)S(1)}, u32[]{:S(2)}, u32[]{:S(2)}) collective-permute-start(bf16[640,3,128]{2,0,1:T(8,128)(2,1)S(1)} %slice.41), channel_id=1, source_target_pairs={{0,48},{16,0},{32,16},{48,32},{1,49},{17,1},{33,17},{49,33},{2,50}... | collective-permute-start | bytes 1474568 | tf_op jit(solution)/shard_map/ppermute | solution.py:30
  99.1 31.6 %collective-permute-start.7 = (bf16[1280,3,128]{2,0,1:T(8,128)(2,1)}, bf16[1280,3,128]{2,0,1:T(8,128)(2,1)S(1)}, u32[]{:S(2)}, u32[]{:S(2)}) collective-permute-start(bf16[1280,3,128]{2,0,1:T(8,128)(2,1)} %collective-permute-done.6), channel_id=1, source_target_pairs={{0,16},{16,32},{32,48},{48,0},{1,17},{17,33},{33,49},{49,1},{2,18}... | collective-permute-start | bytes 2949128 | tf_op jit(solution)/shard_map/ppermute | solution.py:23
  99.1 31.7 %collective-permute-start.8 = (bf16[1280,3,128]{2,0,1:T(8,128)(2,1)}, bf16[1280,3,128]{2,0,1:T(8,128)(2,1)S(1)}, u32[]{:S(2)}, u32[]{:S(2)}) collective-permute-start(bf16[1280,3,128]{2,0,1:T(8,128)(2,1)} %collective-permute-done.6), channel_id=1, source_target_pairs={{0,48},{16,0},{32,16},{48,32},{1,49},{17,1},{33,17},{49,33},{2,50}... | collective-permute-start | bytes 2949128 | tf_op jit(solution)/shard_map/ppermute | solution.py:24
  130.8 12.6 %collective-permute-start.9 = (bf16[640,3,128]{2,0,1:T(8,128)(2,1)S(1)}, bf16[640,3,128]{2,0,1:T(8,128)(2,1)S(1)}, u32[]{:S(2)}, u32[]{:S(2)}) collective-permute-start(bf16[640,3,128]{2,0,1:T(8,128)(2,1)S(1)} %slice.42), channel_id=1, source_target_pairs={{0,16},{16,32},{32,48},{48,0},{1,17},{17,33},{33,49},{49,1},{2,18}... | collective-permute-start | bytes 1474568 | tf_op jit(solution)/shard_map/ppermute | solution.py:29
  130.9 13.4 %collective-permute-start.10 = (bf16[640,3,128]{2,0,1:T(8,128)(2,1)S(1)}, bf16[640,3,128]{2,0,1:T(8,128)(2,1)S(1)}, u32[]{:S(2)}, u32[]{:S(2)}) collective-permute-start(bf16[640,3,128]{2,0,1:T(8,128)(2,1)S(1)} %slice.43), channel_id=1, source_target_pairs={{0,48},{16,0},{32,16},{48,32},{1,49},{17,1},{33,17},{49,33},{2,50}... | collective-permute-start | bytes 1474568 | tf_op jit(solution)/shard_map/ppermute | solution.py:30
Sparse Core Ops, SparseCore 0:
  66.4 81.6 all-gather.1

commit v17 on v16

--- a/solution.py
+++ b/solution.py
@@ -73,14 +73,14 @@
     block_a = block_a.reshape(n_core, n_x, n_zh, n_zl, n_y, local_aux, nocc, rows_a)
     block_b = block_b.reshape(n_zl, n_y, n_core, n_x, n_zh, local_aux, nocc, cols_b)
     gram = jnp.einsum(
-        "cxhzypia,zycxhpjb->ijab",
+        "cxhzypia,zycxhpjb->iajb",
         block_a,
         block_b,
         preferred_element_type=jnp.float32,
-    ).reshape(nocc * nocc, rows_a, cols_b)
+    )
     first = pair_list[:, 0]
     second = pair_list[:, 1]
-    kernel = jnp.take(gram, first * nocc + second, axis=0)
+    kernel = gram[first, :, second, :]
     vir_a = lax.dynamic_slice_in_dim(vir_energy, row_index * rows_a, rows_a)
     vir_b = lax.dynamic_slice_in_dim(vir_energy, col_index * cols_b, cols_b)
     e_first = occ_energy[slab_orbitals[first]]

time: 170 us -> 172 us (1.012)
  matrix products: 11.8 us -> 13.9 us
    all_gather x1, waiting for transfers between devices: 2.81 us -> 5.18 us  [shards(): block_a = lax.all_gather(pair_a, ('core', 'x'), axis=0, tiled=True)]
    dot_general x1, matrix products: 11.8 us -> 13.9 us  [shards(): jnp.einsum('cxhzypia,zycxhpjb->iajb', block_a, block_b, preferred_element...]
    ppermute x2, waiting for transfers between devices: 28.7 us -> 26.9 us  [ring_into(): go_right = lax.ppermute(go_right, axis, right)]
  transfers between devices with their start and end apart: 13 -> 13, of which waited for: 6 -> 7; matrix products, arithmetic and copies ran while one was open for 16% -> 16% of each run, Pallas kernels for 0% -> 0%
where the time goes in v17:
time: 172 us; the launch traced here: 171 us
  waiting for transfers between devices  68.1 us (40%)
  local copies, waits for them, and re-layouts  27 us (16%)
  starting transfers between devices  21 us (12%)
  blocking collectives  20.5 us (12%)
  matrix products  13.9 us (8%)
  between operations  13.7 us (8%)
  other arithmetic  7.19 us (4%)
    ppermute x2, waiting for transfers between devices, ring_into(): go_right = lax.ppermute(go_right, axis, right)  26.9 us
    all_to_all x1, waiting for transfers between devices, shards(): lax.all_to_all(factors.reshape(local_aux, nocc, n_x * n_zh, n_core, cols_...  22.4 us
    all_to_all x1, blocking collectives, shards(): lax.all_to_all(factors.reshape(local_aux, nocc, n_row, rows_a), ('zl', 'y...  20.5 us
    dot_general x1, matrix products, shards(): jnp.einsum('cxhzypia,zycxhpjb->iajb', block_a, block_b, preferred_element...  13.9 us
    ppermute x2, waiting for transfers between devices, ring_into(): from_left = lax.ppermute(go_right[:half], axis, right)  12.7 us
    dynamic_update_slice x10, local copies, waits for them, and re-layouts, put(): return lax.dynamic_update_slice(buf, piece[None, None], start)  10.9 us
    ppermute x2, starting transfers between devices, ring_into(): from_right = lax.ppermute(go_left[half:], axis, left)  5.62 us
    all_gather x1, waiting for transfers between devices, shards(): block_a = lax.all_gather(pair_a, ('core', 'x'), axis=0, tiled=True)  5.18 us
  transfers between devices with their start and end apart: 13, of which 7 were waited for; matrix products, arithmetic and copies ran while one was open for 16% of the time, Pallas kernels for 0%

profile of v17, /device:TPU:1, one launch (start us, length us, event | category | flops | bytes accessed | tf_op | source)
XLA Modules:
  0.0 171.3 jit_solution(3192491769817855873)
XLA Ops:
  6.5 0.0 copy-start
  6.5 1.3 copy.42
  7.8 20.5 %all_to_all.33 = bf16[80,3,8,256]{3,0,1,2:T(8,128)(2,1)S(1)} all-to-all(bf16[80,3,8,256]{3,0,1,2:T(8,128)(2,1)S(1)} %bitcast.69), channel_id=1, replica_groups=mesh['zl'=2,'y'=4,'x'=4,'zh'=2,'core'=2] {'zl','y'}, dimensions={2} | all-to-all | bytes 1966080 | tf_op jit(solution)/shard_map/all_to_all | solution.py:49
  28.3 0.1 copy.18
  28.4 0.0 copy-start.2
  28.4 3.4 %collective-permute-start = (bf16[640,3,256]{2,0,1:T(8,128)(2,1)S(1)}, bf16[640,3,256]{2,0,1:T(8,128)(2,1)}, u32[]{:S(2)}, u32[]{:S(2)}) collective-permute-start(bf16[640,3,256]{2,0,1:T(8,128)(2,1)S(1)} %bitcast.70), channel_id=1, source_target_pairs={{0,2},{2,0},{1,3},{3,1},{4,6},{6,4},{5,7},{7,5},{8,10},{10,8},{9,1... | collective-permute-start | bytes 2949128 | tf_op jit(solution)/shard_map/ppermute | solution.py:53
  31.8 2.9 %reshape.110 = bf16[80,3,8,2,128]{4,3,2,0,1:T(2,128)(2,1)S(1)} reshape(bf16[80,3,2048]{2,0,1:T(8,128)(2,1)} %param.7) | data formatting | bytes 1966080 | tf_op jit(solution)/shard_map/reshape | solution.py:55
  34.7 1.6 copy.19
  36.3 4.2 %all-to-all-start.1 = ((bf16[80,3,8,2,128]{4,3,0,1,2:T(2,128)(2,1)}), bf16[80,3,8,2,128]{4,3,0,1,2:T(2,128)(2,1)S(1)}, u32[]{:S(2)}, u32[]{:S(2)}) async-start(bf16[80,3,8,2,128]{4,3,0,1,2:T(2,128)(2,1)} %copy.19), calls=%async_computation.1 | async-start | bytes 1966080 | tf_op jit(solution)/shard_map/all_to_all | solution.py:54
  40.5 0.0 copy-start.1
  40.5 0.0 all-gather.2.cloned.1.call-start
  40.5 22.4 %all-to-all-done.1 = bf16[80,3,8,2,128]{4,3,0,1,2:T(2,128)(2,1)S(1)} async-done(((bf16[80,3,8,2,128]{4,3,0,1,2:T(2,128)(2,1)}), bf16[80,3,8,2,128]{4,3,0,1,2:T(2,128)(2,1)S(1)}, u32[]{:S(2)}, u32[]{:S(2)}) %all-to-all-start.1) | async-done | bytes 983072 | tf_op jit(solution)/shard_map/all_to_all | solution.py:54
  62.9 0.1 copy.20
  63.0 0.0 collective-permute-done
  63.1 3.1 %maximum_select_fusion = bf16[2,640,3,256]{3,1,2,0:T(8,128)(2,1)} fusion(bf16[1,640,3,256]{3,1,2,0:T(8,128)(2,1)} %bitcast.8, bf16[1,640,3,256]{3,1,2,0:T(8,128)(2,1)S(1)} %bitcast.71, pred[]{:T(512)S(6)} %eq.17), kind=kLoop, calls=%fused_computation.8 | loop fusion | flops 2949120 | bytes 3932161 | tf_op jit(solution)/shard_map/jit(_where)/select_n | solution.py:65
  66.2 0.0 all-gather.2.cloned.1.call-update
  66.2 0.1 dynamic-slice_bitcast_fusion.1
  66.3 2.2 %collective-permute-start.1 = (bf16[640,3,128]{2,0,1:T(8,128)(2,1)S(1)}, bf16[640,3,128]{2,0,1:T(8,128)(2,1)S(1)}, u32[]{:S(2)}, u32[]{:S(2)}) collective-permute-start(bf16[640,3,128]{2,0,1:T(8,128)(2,1)S(1)} %get-tuple-element.10), channel_id=1, source_target_pairs={{0,1},{1,0},{2,3},{3,2},{4,5},{5,4},{6,7},{7,6},{8,9},{9,8},{10,11... | collective-permute-start | bytes 1474568 | tf_op jit(solution)/shard_map/ppermute | solution.py:62
  68.5 0.0 copy-done.2
  68.5 0.6 fusion.10
  69.1 0.9 collective-permute-done.1
  70.0 0.2 maximum_select_fusion.1
  70.1 0.1 copy.21
  70.2 0.3 collective-permute-start.2
  70.5 2.5 %collective-permute-start.3 = (bf16[1280,3,128]{2,0,1:T(8,128)(2,1)S(1)}, bf16[1280,3,128]{2,0,1:T(8,128)(2,1)S(1)}, u32[]{:S(2)}, u32[]{:S(2)}) collective-permute-start(bf16[1280,3,128]{2,0,1:T(8,128)(2,1)S(1)} %bitcast.64), channel_id=1, source_target_pairs={{0,48},{16,0},{32,16},{48,32},{1,49},{17,1},{33,17},{49,33},{2,50}... | collective-permute-start | bytes 2949128 | tf_op jit(solution)/shard_map/ppermute | solution.py:24
  73.0 0.0 collective-permute-start.6
  73.0 0.0 copy-done.3
  73.0 1.9 %fusion.8 = (s32[16]{0:T(128)S(1)}, s32[16]{0:T(128)S(1)}, s32[16]{0:T(128)S(1)}) fusion(s32[]{:T(128)} %bitcast.31, s32[]{:T(128)} %bitcast.33, s32[]{:T(128)} %bitcast.32, s32[16,2]{0,1:T(2,128)S(1)} %copy-done.3), kind=kLoop, calls=%fused_computation.37 | loop fusion | flops 400 | bytes 332 | tf_op jit(solution)/shard_map/select_n | solution.py:86
  74.9 0.8 dynamic_slice.16
  75.7 0.8 dynamic_slice.15
  76.5 0.7 gather_fusion.1
  77.1 0.7 gather_fusion.2
  77.9 0.7 gather_fusion.3
  78.5 0.1 broadcast_add_fusion
  78.6 5.0 %broadcast_in_dim.44 = bf16[2,4,1280,3,128]{4,2,3,1,0:T(8,128)(2,1)} broadcast(bf16[]{:T(256)} %constant.77.clone.1), dimensions={} | broadcast | bytes 7864322 | tf_op jit(solution)/shard_map/broadcast_in_dim | solution.py:70
  83.6 1.0 constant_dynamic-update-slice_fusion
  84.7 9.9 %collective-permute-done.2 = bf16[1280,3,128]{2,0,1:T(8,128)(2,1)S(1)} collective-permute-done((bf16[1280,3,128]{2,0,1:T(8,128)(2,1)S(1)}, bf16[1280,3,128]{2,0,1:T(8,128)(2,1)S(1)}, u32[]{:S(2)}, u32[]{:S(2)}) %collective-permute-start.2) | collective-permute-done | bytes 983072 | tf_op jit(solution)/shard_map/ppermute | solution.py:23
  94.6 0.1 collective-permute-start.4
  94.7 0.0 collective-permute-done.3
  94.7 2.7 %collective-permute-start.5 = (bf16[640,3,128]{2,0,1:T(8,128)(2,1)S(1)}, bf16[640,3,128]{2,0,1:T(8,128)(2,1)S(1)}, u32[]{:S(2)}, u32[]{:S(2)}) collective-permute-start(bf16[640,3,128]{2,0,1:T(8,128)(2,1)S(1)} %slice.41), channel_id=1, source_target_pairs={{0,48},{16,0},{32,16},{48,32},{1,49},{17,1},{33,17},{49,33},{2,50}... | collective-permute-start | bytes 1474568 | tf_op jit(solution)/shard_map/ppermute | solution.py:30
  97.4 0.0 collective-permute-done.6
  97.4 0.0 collective-permute-start.7
  97.4 2.7 %collective-permute-start.8 = (bf16[1280,3,128]{2,0,1:T(8,128)(2,1)}, bf16[1280,3,128]{2,0,1:T(8,128)(2,1)S(1)}, u32[]{:S(2)}, u32[]{:S(2)}) collective-permute-start(bf16[1280,3,128]{2,0,1:T(8,128)(2,1)} %collective-permute-done.6), channel_id=1, source_target_pairs={{0,48},{16,0},{32,16},{48,32},{1,49},{17,1},{33,17},{49,33},{2,50}... | collective-permute-start | bytes 2949128 | tf_op jit(solution)/shard_map/ppermute | solution.py:24
  100.1 1.0 bitcast_dynamic-update-slice_fusion.4
  101.1 1.0 bitcast_dynamic-update-slice_fusion.3
  102.2 5.5 %collective-permute-done.4 = bf16[640,3,128]{2,0,1:T(8,128)(2,1)S(1)} collective-permute-done((bf16[640,3,128]{2,0,1:T(8,128)(2,1)S(1)}, bf16[640,3,128]{2,0,1:T(8,128)(2,1)S(1)}, u32[]{:S(2)}, u32[]{:S(2)}) %collective-permute-start.4) | collective-permute-done | bytes 491552 | tf_op jit(solution)/shard_map/ppermute | solution.py:29
  107.6 0.9 bitcast_dynamic-update-slice_fusion.8
  108.5 0.0 collective-permute-done.5
  108.5 0.9 bitcast_dynamic-update-slice_fusion.7
  109.4 2.2 %bitcast_dynamic-update-slice_fusion.2 = bf16[2,4,1280,3,128]{4,2,3,1,0:T(8,128)(2,1)} fusion(bf16[2,4,1280,3,128]{4,2,3,1,0:T(8,128)(2,1)} %bitcast_dynamic-update-slice_fusion.7, s32[]{:T(128)S(6)} %select_n.159, s32[]{:T(128)S(6)} %select_n.150, bf16[1280,3,128]{2,0,1:T(8,128)(2,1)} %collective-permute-done.6), kind=kLoop, calls=%fused_computation.14 | loop fusion | bytes 1966088 | tf_op jit(solution)/shard_map/dynamic_update_slice | solution.py:16
  111.6 17.0 %collective-permute-done.7 = bf16[1280,3,128]{2,0,1:T(8,128)(2,1)S(1)} collective-permute-done((bf16[1280,3,128]{2,0,1:T(8,128)(2,1)}, bf16[1280,3,128]{2,0,1:T(8,128)(2,1)S(1)}, u32[]{:S(2)}, u32[]{:S(2)}) %collective-permute-start.7) | collective-permute-done | bytes 983072 | tf_op jit(solution)/shard_map/ppermute | solution.py:23
  128.7 0.1 collective-permute-start.9
  128.8 0.0 collective-permute-done.8
  128.9 2.9 %collective-permute-start.10 = (bf16[640,3,128]{2,0,1:T(8,128)(2,1)S(1)}, bf16[640,3,128]{2,0,1:T(8,128)(2,1)S(1)}, u32[]{:S(2)}, u32[]{:S(2)}) collective-permute-start(bf16[640,3,128]{2,0,1:T(8,128)(2,1)S(1)} %slice.43), channel_id=1, source_target_pairs={{0,48},{16,0},{32,16},{48,32},{1,49},{17,1},{33,17},{49,33},{2,50}... | collective-permute-start | bytes 1474568 | tf_op jit(solution)/shard_map/ppermute | solution.py:30
  131.8 1.0 bitcast_dynamic-update-slice_fusion.1
  132.8 1.0 bitcast_dynamic-update-slice_fusion
  133.8 7.2 %collective-permute-done.9 = bf16[640,3,128]{2,0,1:T(8,128)(2,1)S(1)} collective-permute-done((bf16[640,3,128]{2,0,1:T(8,128)(2,1)S(1)}, bf16[640,3,128]{2,0,1:T(8,128)(2,1)S(1)}, u32[]{:S(2)}, u32[]{:S(2)}) %collective-permute-start.9) | collective-permute-done | bytes 491552 | tf_op jit(solution)/shard_map/ppermute | solution.py:29
  141.0 0.9 bitcast_dynamic-update-slice_fusion.6
  141.9 0.0 collective-permute-done.10
  141.9 0.9 bitcast_dynamic-update-slice_fusion.5
  142.8 5.2 %all-gather.2.cloned.1.call-done = bf16[16,640,3,256]{3,1,2,0:T(8,128)(2,1)} async-done(((bf16[2,640,3,256]{3,1,2,0:T(8,128)(2,1)}), bf16[16,640,3,256]{3,1,2,0:T(8,128)(2,1)}) %all-gather.2.cloned.1.call-update) | async-done | bytes 15728656 | tf_op jit(solution)/shard_map/all_gather | solution.py:66
  148.0 13.9 %fusion.3 = f32[3,256,3,128]{3,1,2,0:T(8,128)S(1)} fusion(bf16[2,4,2,4,2,80,3,128,1]{7,5,4,3,2,6,1,0,8:T(8,128)(2,1)} %bitcast.27, bf16[2,4,2,2,4,80,3,256,1]{7,5,4,3,6,2,1,0,8:T(8,128)(2,1)} %bitcast.73), kind=kOutput, calls=%fused_computation.9 | convolution fusion | flops 6039797760 | bytes 24772608 | tf_op jit(solution)/shard_map/cxhzypia,zycxhpjb->iajb/dot_general | solution.py:75
  161.9 0.7 gather_fusion
  162.6 1.9 %add_divide_fusion = f32[16,256,128]{2,1,0:T(8,128)} fusion(f32[16,256,128]{2,1,0:T(8,128)S(1)} %gather_fusion, f32[16]{0:T(128)S(1)} %gather_fusion.3, f32[16]{0:T(128)S(1)} %gather_fusion.2, f32[16]{0:T(128)S(1)} %gather_fusion.1, f32[256,128]{1,0:T(8,128)S(1)} %broadcast_add_fusion), kind=kLoop, calls=%fused_computation.7 | loop fusion | flops 2621440 | bytes 4325568 | tf_op jit(solution)/shard_map/div | solution.py:95
  (12 shorter events, 0.2 us)
Async XLA Ops:
  6.5 69.9 %copy-start = (f32[300]{0:T(512)S(1)}, f32[300]{0:T(512)}, u32[]{:S(2)}) copy-start(f32[300]{0:T(512)} %param.8) | copy-start | bytes 3604
  28.4 40.1 %copy-start.2 = (s32[3]{0:T(128)S(1)}, s32[3]{0:T(128)}, u32[]{:S(2)}) copy-start(s32[3]{0:T(128)} %param.10) | copy-start | bytes 40
  28.4 34.7 %collective-permute-start = (bf16[640,3,256]{2,0,1:T(8,128)(2,1)S(1)}, bf16[640,3,256]{2,0,1:T(8,128)(2,1)}, u32[]{:S(2)}, u32[]{:S(2)}) collective-permute-start(bf16[640,3,256]{2,0,1:T(8,128)(2,1)S(1)} %bitcast.70), channel_id=1, source_target_pairs={{0,2},{2,0},{1,3},{3,1},{4,6},{6,4},{5,7},{7,5},{8,10},{10,8},{9,1... | collective-permute-start | bytes 2949128 | tf_op jit(solution)/shard_map/ppermute | solution.py:53
  36.3 36.6 %copy-start.3 = (s32[16,2]{0,1:T(2,128)S(1)}, s32[16,2]{0,1:T(2,128)}, u32[]{:S(2)}) copy-start(s32[16,2]{0,1:T(2,128)} %param.11) | copy-start | bytes 388
  36.3 26.6 %all-to-all-start.1 = ((bf16[80,3,8,2,128]{4,3,0,1,2:T(2,128)(2,1)}), bf16[80,3,8,2,128]{4,3,0,1,2:T(2,128)(2,1)S(1)}, u32[]{:S(2)}, u32[]{:S(2)}) async-start(bf16[80,3,8,2,128]{4,3,0,1,2:T(2,128)(2,1)} %copy.19), calls=%async_computation.1 | async-start | bytes 1966080 | tf_op jit(solution)/shard_map/all_to_all | solution.py:54
  40.5 37.4 %copy-start.4 = (s32[16]{0:T(128)S(1)}, s32[16]{0:T(128)}, u32[]{:S(2)}) copy-start(s32[16]{0:T(128)} %param.12) | copy-start | bytes 196
  40.5 37.4 %copy-start.1 = (f32[4]{0:T(128)S(1)}, f32[4]{0:T(128)}, u32[]{:S(2)}) copy-start(f32[4]{0:T(128)} %param.13) | copy-start | bytes 52
  40.5 107.5 %all-gather.2.cloned.1.call-start = ((), (), s32[]{:S(2)}) async-start(), calls=%async_computation.2 | async-start | bytes 17694720 | tf_op jit(solution)/shard_map/all_gather | solution.py:66
  66.3 3.7 %collective-permute-start.1 = (bf16[640,3,128]{2,0,1:T(8,128)(2,1)S(1)}, bf16[640,3,128]{2,0,1:T(8,128)(2,1)S(1)}, u32[]{:S(2)}, u32[]{:S(2)}) collective-permute-start(bf16[640,3,128]{2,0,1:T(8,128)(2,1)S(1)} %get-tuple-element.10), channel_id=1, source_target_pairs={{0,1},{1,0},{2,3},{3,2},{4,5},{5,4},{6,7},{7,6},{8,9},{9,8},{10,11... | collective-permute-start | bytes 1474568 | tf_op jit(solution)/shard_map/ppermute | solution.py:62
  70.2 24.3 %collective-permute-start.2 = (bf16[1280,3,128]{2,0,1:T(8,128)(2,1)S(1)}, bf16[1280,3,128]{2,0,1:T(8,128)(2,1)S(1)}, u32[]{:S(2)}, u32[]{:S(2)}) collective-permute-start(bf16[1280,3,128]{2,0,1:T(8,128)(2,1)S(1)} %bitcast.63), channel_id=1, source_target_pairs={{0,16},{16,32},{32,48},{48,0},{1,17},{17,33},{33,49},{49,1},{2,18}... | collective-permute-start | bytes 2949128 | tf_op jit(solution)/shard_map/ppermute | solution.py:23
  70.5 24.2 %collective-permute-start.3 = (bf16[1280,3,128]{2,0,1:T(8,128)(2,1)S(1)}, bf16[1280,3,128]{2,0,1:T(8,128)(2,1)S(1)}, u32[]{:S(2)}, u32[]{:S(2)}) collective-permute-start(bf16[1280,3,128]{2,0,1:T(8,128)(2,1)S(1)} %bitcast.64), channel_id=1, source_target_pairs={{0,48},{16,0},{32,16},{48,32},{1,49},{17,1},{33,17},{49,33},{2,50}... | collective-permute-start | bytes 2949128 | tf_op jit(solution)/shard_map/ppermute | solution.py:24
  73.0 24.5 %collective-permute-start.6 = (bf16[1280,3,128]{2,0,1:T(8,128)(2,1)S(1)}, bf16[1280,3,128]{2,0,1:T(8,128)(2,1)}, u32[]{:S(2)}, u32[]{:S(2)}) collective-permute-start(bf16[1280,3,128]{2,0,1:T(8,128)(2,1)S(1)} %bitcast.65), channel_id=1, source_target_pairs={{0,64},{64,0},{1,65},{65,1},{2,66},{66,2},{3,67},{67,3},{4,68},{68... | collective-permute-start | bytes 2949128 | tf_op jit(solution)/shard_map/ppermute | solution.py:68
  94.6 13.0 %collective-permute-start.4 = (bf16[640,3,128]{2,0,1:T(8,128)(2,1)S(1)}, bf16[640,3,128]{2,0,1:T(8,128)(2,1)S(1)}, u32[]{:S(2)}, u32[]{:S(2)}) collective-permute-start(bf16[640,3,128]{2,0,1:T(8,128)(2,1)S(1)} %slice.40), channel_id=1, source_target_pairs={{0,16},{16,32},{32,48},{48,0},{1,17},{17,33},{33,49},{49,1},{2,18}... | collective-permute-start | bytes 1474568 | tf_op jit(solution)/shard_map/ppermute | solution.py:29
  94.7 13.8 %collective-permute-start.5 = (bf16[640,3,128]{2,0,1:T(8,128)(2,1)S(1)}, bf16[640,3,128]{2,0,1:T(8,128)(2,1)S(1)}, u32[]{:S(2)}, u32[]{:S(2)}) collective-permute-start(bf16[640,3,128]{2,0,1:T(8,128)(2,1)S(1)} %slice.41), channel_id=1, source_target_pairs={{0,48},{16,0},{32,16},{48,32},{1,49},{17,1},{33,17},{49,33},{2,50}... | collective-permute-start | bytes 1474568 | tf_op jit(solution)/shard_map/ppermute | solution.py:30
  97.4 31.2 %collective-permute-start.7 = (bf16[1280,3,128]{2,0,1:T(8,128)(2,1)}, bf16[1280,3,128]{2,0,1:T(8,128)(2,1)S(1)}, u32[]{:S(2)}, u32[]{:S(2)}) collective-permute-start(bf16[1280,3,128]{2,0,1:T(8,128)(2,1)} %collective-permute-done.6), channel_id=1, source_target_pairs={{0,16},{16,32},{32,48},{48,0},{1,17},{17,33},{33,49},{49,1},{2,18}... | collective-permute-start | bytes 2949128 | tf_op jit(solution)/shard_map/ppermute | solution.py:23
  97.4 31.4 %collective-permute-start.8 = (bf16[1280,3,128]{2,0,1:T(8,128)(2,1)}, bf16[1280,3,128]{2,0,1:T(8,128)(2,1)S(1)}, u32[]{:S(2)}, u32[]{:S(2)}) collective-permute-start(bf16[1280,3,128]{2,0,1:T(8,128)(2,1)} %collective-permute-done.6), channel_id=1, source_target_pairs={{0,48},{16,0},{32,16},{48,32},{1,49},{17,1},{33,17},{49,33},{2,50}... | collective-permute-start | bytes 2949128 | tf_op jit(solution)/shard_map/ppermute | solution.py:24
  128.7 12.3 %collective-permute-start.9 = (bf16[640,3,128]{2,0,1:T(8,128)(2,1)S(1)}, bf16[640,3,128]{2,0,1:T(8,128)(2,1)S(1)}, u32[]{:S(2)}, u32[]{:S(2)}) collective-permute-start(bf16[640,3,128]{2,0,1:T(8,128)(2,1)S(1)} %slice.42), channel_id=1, source_target_pairs={{0,16},{16,32},{32,48},{48,0},{1,17},{17,33},{33,49},{49,1},{2,18}... | collective-permute-start | bytes 1474568 | tf_op jit(solution)/shard_map/ppermute | solution.py:29
  128.9 13.1 %collective-permute-start.10 = (bf16[640,3,128]{2,0,1:T(8,128)(2,1)S(1)}, bf16[640,3,128]{2,0,1:T(8,128)(2,1)S(1)}, u32[]{:S(2)}, u32[]{:S(2)}) collective-permute-start(bf16[640,3,128]{2,0,1:T(8,128)(2,1)S(1)} %slice.43), channel_id=1, source_target_pairs={{0,48},{16,0},{32,16},{48,32},{1,49},{17,1},{33,17},{49,33},{2,50}... | collective-permute-start | bytes 1474568 | tf_op jit(solution)/shard_map/ppermute | solution.py:30
Sparse Core Ops, SparseCore 0:
  66.3 81.6 all-gather.1
